TPU v7x, 128 devices: a whole 4x4x4 slice. The times are simulated.
128 devices in a mesh: blk: 8 (over y_lo, x), dp: 16 (over z, y_hi, core).
Axes of the slice: x: 4, y: 4 (y_hi: 2, y_lo: 2; y = y_hi * 2 + y_lo), z: 4, core: 2. Of those that a mesh axis runs over, the one named last changes fastest.
Arguments:
- train_grads: bfloat16 [8192, 8192], P(('blk', 'dp')), may hold values from -6 to 6
- train_scale: bfloat16 [8192], P(('blk', 'dp')), may hold values from 0.5 to 4
- train_class: int32 [8192], P(('blk', 'dp')), may hold values from 0 to 511
- test_grads: bfloat16 [8192, 8192], P(('blk', 'dp')), may hold values from -0.099609375 to 0.099609375
- test_class: int32 [8192], P(('blk', 'dp')), may hold values from 0 to 511
Outputs:
- train_attr: float32 [8192, 512], P(('blk', 'dp'))
- test_attr: float32 [8192], P(('blk', 'dp'))
All inputs are finite; a program needn't handle non-finite values.
Results may differ from a plain program's by a relative error of at most 0.0021.
Values may be sent and summed in bfloat16 or wider, within the bound.
No kernel may reach another device: no remote copies, remote signals or barrier semaphores. Data moves between devices by JAX's collectives and lax.ppermute only.
A program may use at most 128 MiB of HBM per device.

v0:
```python
import jax
import jax.numpy as jnp
from jax import lax
from jax.sharding import PartitionSpec as P

NCLS = 512


def indicator(labels):
    columns = lax.broadcasted_iota(jnp.int32, (labels.shape[0], NCLS), 1)
    return (labels[:, None] == columns).astype(jnp.bfloat16)


def weigh(grads, scale, tests):
    raw = lax.dot_general(
        grads, tests, (((1,), (1,)), ((), ())), preferred_element_type=jnp.float32
    )
    return jnp.tanh(scale.astype(jnp.float32)[:, None] * raw).astype(jnp.bfloat16)


def class_by_rows(weights, hot):
    return lax.dot_general(
        weights, hot, (((0,), (0,)), ((), ())), preferred_element_type=jnp.float32
    )


def local(train_grads, train_scale, train_class, test_grads, test_class):
    train_hot = indicator(train_class)
    test_hot = indicator(test_class)
    test_whole, hot_whole = (
        lax.all_gather(test_grads, "blk", axis=0, tiled=True),
        lax.all_gather(test_hot, "blk", axis=0, tiled=True),
    )
    hot_wide = hot_whole.astype(jnp.float32)
    grads = lax.all_gather(train_grads, "dp", axis=0, tiled=True)
    scale = lax.all_gather(train_scale, "dp", axis=0, tiled=True)
    hot = lax.all_gather(train_hot, "dp", axis=0, tiled=True)
    weights = weigh(grads, scale, test_whole)
    part = jnp.dot(weights, hot_whole, preferred_element_type=jnp.float32)
    per_class = class_by_rows(weights, hot)
    test_part = jnp.sum(per_class * hot_wide, axis=1)
    train_attr = lax.psum_scatter(part, "dp", scatter_dimension=0, tiled=True)
    test_attr = lax.psum_scatter(test_part, "blk", scatter_dimension=0, tiled=True)
    return (train_attr, test_attr)


def solution(mesh):
    in_specs = (
        P(("blk", "dp"), None),
        P(("blk", "dp")),
        P(("blk", "dp")),
        P(("blk", "dp"), None),
        P(("blk", "dp")),
    )
    out_specs = (P(("blk", "dp"), None), P(("blk", "dp")))
    return jax.shard_map(local, mesh=mesh, in_specs=in_specs, out_specs=out_specs, check_vma=False)
```

profile of v0, /device:TPU:0, one launch (start us, length us, event | category | flops | bytes accessed | tf_op | source)
XLA Modules:
  0.0 341.9 jit_solution(8928282868838127938)
XLA Ops:
  7.2 0.0 all-gather.6.cloned.1.call-start
  7.2 0.7 all-gather.6.cloned.1.call-update
  7.9 0.0 all-gather.4.cloned.1.call-start
  7.9 0.7 all-gather.4.cloned.1.call-update
  8.6 0.0 all-gather.8.cloned.1.call-start
  8.7 1.4 fusion.2
  10.1 0.0 all-gather.8.cloned.1.call-update
  10.1 0.0 reduce-scatter.2.cloned.1.call-start
  10.1 1.2 dynamic-slice
  12.0 0.8 dynamic-update-slice
  12.9 111.8 %all-reduce = bf16[1024]{0:T(1024)(128)(2,1)S(1)} all-reduce(bf16[1024]{0:T(1024)(128)(2,1)S(1)} %dynamic-update-slice), channel_id=1, replica_groups=mesh['blk'=8,'dp'=16] {'dp'}, use_global_device_ids=true, to_apply=%add | all-reduce | flops 1024 | bytes 4096
  124.7 0.7 fusion.1
  125.4 29.0 %all_gather.18 = bf16[512,512]{1,0:T(8,128)(2,1)S(1)} all-gather(bf16[64,512]{1,0:T(8,128)(2,1)S(1)} %fusion.1), channel_id=1, replica_groups=mesh['blk'=8,'dp'=16] {'blk'}, dimensions={0}, use_global_device_ids=true | all-gather | bytes 589824 | tf_op jit(solution)/shard_map/all_gather | solution.py:32
  154.4 0.0 copy-start
  154.4 0.0 all-gather.6.cloned.1.call-done
  154.4 61.8 %all-gather.4.cloned.1.call-done = bf16[1024,8192]{1,0:T(8,128)(2,1)} async-done(((bf16[64,8192]{1,0:T(8,128)(2,1)}), bf16[1024,8192]{1,0:T(8,128)(2,1)}) %all-gather.4.cloned.1.call-update) | async-done | bytes 16777232 | tf_op jit(solution)/shard_map/all_gather | solution.py:35
  216.2 14.9 %tanh_convert_fusion = bf16[1024,512]{1,0:T(8,128)(2,1)S(1)} fusion(bf16[1024,8192]{1,0:T(8,128)(2,1)} %all-gather.4.cloned.1.call-done, bf16[512,8192]{1,0:T(8,128)(2,1)} %all-gather.6.cloned.1.call-done, f32[1024]{0:T(1024)S(1)} %convert_element_type.15), kind=kOutput, calls=%fused_computation | convolution fusion | flops 8590983168 | bytes 26218496 | tf_op jit(solution)/shard_map/dot_general | solution.py:15
  231.1 2.0 fusion.3
  233.1 0.0 reduce-scatter.2.cloned.1.call-update
  233.1 0.2 copy.7
  233.4 0.0 copy-done
  233.4 0.6 dynamic-slice.1
  234.6 26.6 %all-gather.8.cloned.1.call-done = bf16[1024,512]{1,0:T(8,128)(2,1)} async-done(((bf16[64,512]{1,0:T(8,128)(2,1)}), bf16[1024,512]{1,0:T(8,128)(2,1)}) %all-gather.8.cloned.1.call-update) | async-done | bytes 1048592 | tf_op jit(solution)/shard_map/all_gather | solution.py:37
  261.3 2.0 fusion
  263.3 18.7 %all-reduce.1 = f32[512]{0:T(512)S(1)} all-reduce(f32[512]{0:T(512)S(1)} %fusion), channel_id=3, replica_groups=mesh['blk'=8,'dp'=16] {'blk'}, use_global_device_ids=true, to_apply=%region_2.0.clone | all-reduce | flops 512 | bytes 4096
  281.9 0.6 dynamic-slice.2
  282.5 52.9 %reduce-scatter.2.cloned.1.call-done = f32[64,512]{1,0:T(8,128)} async-done(((f32[1024,512]{1,0:T(8,128)}), f32[64,512]{1,0:T(8,128)}) %reduce-scatter.2.cloned.1.call-update) | async-done | bytes 131088 | tf_op jit(solution)/shard_map/reduce_scatter | solution.py:42
  (2 shorter events, 0.0 us)
Async XLA Ops:
  7.2 147.3 %all-gather.6.cloned.1.call-start = ((), (), s32[]{:S(2)}) async-start(), calls=%async_computation.2 | async-start | bytes 9437184 | tf_op jit(solution)/shard_map/all_gather | solution.py:31
  7.9 208.3 %all-gather.4.cloned.1.call-start = ((), (), s32[]{:S(2)}) async-start(), calls=%async_computation.1 | async-start | bytes 17825792 | tf_op jit(solution)/shard_map/all_gather | solution.py:35
  8.6 252.6 %all-gather.8.cloned.1.call-start = ((), (), s32[]{:S(2)}) async-start(), calls=%async_computation.4 | async-start | bytes 1114112 | tf_op jit(solution)/shard_map/all_gather | solution.py:37
  10.1 325.3 %reduce-scatter.2.cloned.1.call-start = ((), (), s32[]{:S(2)}) async-start(), calls=%async_computation.3 | async-start | bytes 2228224 | tf_op jit(solution)/shard_map/reduce_scatter | solution.py:42
  154.4 78.9 %copy-start = (u32[128]{0:T(128)S(1)}, u32[128]{0:T(128)}, u32[]{:S(2)}) copy-start(u32[128]{0:T(128)} %constant.15) | copy-start | bytes 1540
Sparse Core Ops, SparseCore 0:
  9.6 94.4 all-gather.5
  106.6 109.5 all-gather.3
  218.7 42.5 all-gather.7
  265.6 69.7 reduce-scatter.1
where the time goes:
time: 342 us
  blocking collectives  159 us (46%)
  waiting for transfers between devices  143 us (42%)
  matrix products  18.9 us (6%)
  between operations  15.1 us (4%)
  local copies, waits for them, and re-layouts  3.48 us (1%)
    unnamed x2, blocking collectives  130 us
    all_gather x1, waiting for transfers between devices, local(): grads = lax.all_gather(train_grads, 'dp', axis=0, tiled=True)  61.8 us
    reduce_scatter x1, waiting for transfers between devices, local(): train_attr = lax.psum_scatter(part, 'dp', scatter_dimension=0, tiled=True)  52.9 us
    all_gather x1, blocking collectives, local(): lax.all_gather(test_hot, 'blk', axis=0, tiled=True)  29 us
    all_gather x1, waiting for transfers between devices, local(): hot = lax.all_gather(train_hot, 'dp', axis=0, tiled=True)  26.6 us
    dot_general x1, matrix products, weigh(): lax.dot_general(grads, tests, (((1,), (1,)), ((), ())), preferred_element...  14.9 us
  transfers between devices with their start and end apart: 4, of which 3 were waited for; matrix products, arithmetic and copies ran while one was open for 7% of the time, Pallas kernels for 0%

commit v1 on v0

v1 whole, which is shorter than its diff:
```python
import jax
import jax.numpy as jnp
from jax import lax
from jax.sharding import PartitionSpec as P

NCLS = 512
PAD = 128


def indicator(labels):
    columns = lax.broadcasted_iota(jnp.int32, (labels.shape[0], NCLS), 1)
    return (labels[:, None] == columns).astype(jnp.bfloat16)


def with_side(grads, side, first):
    rows = grads.shape[0]
    cols = lax.broadcasted_iota(jnp.int32, (rows, PAD), 1)
    extra = jnp.zeros((rows, PAD), jnp.bfloat16)
    for k, v in enumerate(side):
        extra = jnp.where(cols == first + k, v[:, None].astype(jnp.bfloat16), extra)
    return jnp.concatenate([grads, extra], axis=1)


def split_class(c):
    return (c // 32, c % 32)


def join_class(x, k):
    hi = x[:, k].astype(jnp.int32)
    lo = x[:, k + 1].astype(jnp.int32)
    return hi * 32 + lo


def local(train_grads, train_scale, train_class, test_grads, test_class):
    k = train_grads.shape[1]
    tr = with_side(train_grads, (train_scale,) + split_class(train_class), 0)
    te = with_side(test_grads, split_class(test_class), 4)
    tr_all = lax.all_gather(tr, "blk", axis=0, tiled=True)
    te_all = lax.all_gather(te, "dp", axis=0, tiled=True)
    raw = lax.dot_general(
        tr_all, te_all, (((1,), (1,)), ((), ())), preferred_element_type=jnp.float32
    )
    scale = tr_all[:, k].astype(jnp.float32)
    weights = jnp.tanh(scale[:, None] * raw).astype(jnp.bfloat16)
    train_hot = indicator(join_class(tr_all, k + 1))
    test_hot = indicator(join_class(te_all, k + 4))
    part = jnp.dot(weights, test_hot, preferred_element_type=jnp.float32)
    per_class = lax.dot_general(
        weights, train_hot, (((0,), (0,)), ((), ())), preferred_element_type=jnp.float32
    )
    test_part = jnp.sum(per_class * test_hot.astype(jnp.float32), axis=1)
    train_attr = lax.psum_scatter(part, "blk", scatter_dimension=0, tiled=True)
    test_attr = lax.psum_scatter(test_part, "dp", scatter_dimension=0, tiled=True)
    return (train_attr, test_attr)


def solution(mesh):
    in_specs = (
        P(("blk", "dp"), None),
        P(("blk", "dp")),
        P(("blk", "dp")),
        P(("blk", "dp"), None),
        P(("blk", "dp")),
    )
    out_specs = (P(("blk", "dp"), None), P(("blk", "dp")))
    return jax.shard_map(local, mesh=mesh, in_specs=in_specs, out_specs=out_specs, check_vma=False)
```

time: 342 us -> 282 us (0.82)
  blocking collectives: 159 us -> 33.7 us
  waiting for transfers between devices: 143 us -> 205 us
  other arithmetic: 2.1 us -> 8.7 us
    all_gather x3 -> x2, waiting for transfers between devices: 88.4 us -> 205 us  [the longest x1 111 us: local(): te_all = lax.all_gather(te, 'dp', axis=0, tiled=True)]
    unnamed x2 -> x1, blocking collectives: 130 us -> 33.7 us
    reduce_scatter x1, waiting for transfers between devices: 52.9 us -> 0.01 us  [local(): train_attr = lax.psum_scatter(part, 'blk', scatter_dimension=0, tiled=True)]
    all_gather x1 -> x0, blocking collectives: 29 us -> none  [local(): lax.all_gather(test_hot, 'blk', axis=0, tiled=True)]
  transfers between devices with their start and end apart: 4 -> 3, of which waited for: 3 -> 2; matrix products, arithmetic and copies ran while one was open for 7% -> 2% of each run, Pallas kernels for 0% -> 0%
where the time goes in v1:
time: 282 us; the launch traced here: 281 us
  waiting for transfers between devices  205 us (73%)
  blocking collectives  33.7 us (12%)
  matrix products  17.9 us (6%)
  between operations  14.5 us (5%)
  other arithmetic  8.7 us (3%)
    all_gather x1, waiting for transfers between devices, local(): te_all = lax.all_gather(te, 'dp', axis=0, tiled=True)  111 us
    all_gather x1, waiting for transfers between devices, local(): tr_all = lax.all_gather(tr, 'blk', axis=0, tiled=True)  94.4 us
    unnamed x1, blocking collectives  33.7 us
    dot_general x1, matrix products, local(): lax.dot_general(tr_all, te_all, (((1,), (1,)), ((), ())), preferred_eleme...  15.2 us
  transfers between devices with their start and end apart: 3, of which 2 were waited for; matrix products, arithmetic and copies ran while one was open for 2% of the time, Pallas kernels for 0%

profile of v1, /device:TPU:0, one launch (start us, length us, event | category | flops | bytes accessed | tf_op | source)
XLA Modules:
  0.0 281.5 jit_solution(7258270787479759474)
XLA Ops:
  7.2 0.0 copy-start.1
  7.2 0.0 copy-start
  7.2 0.0 all-gather.3.cloned.1.call-start
  7.3 0.7 fusion.4
  8.0 0.7 select_select_fusion.1
  8.7 2.3 pad_maximum_fusion
  11.1 0.0 all-gather.3.cloned.1.call-update
  11.1 0.0 all-gather.5.cloned.1.call-start
  11.2 0.0 copy-done.1
  11.2 0.1 select_select_fusion
  11.3 0.0 copy-done
  11.3 1.1 pad_maximum_fusion.1
  12.4 0.0 all-gather.5.cloned.1.call-update
  12.4 0.0 reduce-scatter.2.cloned.1.call-start
  12.4 94.4 %all-gather.3.cloned.1.call-done = bf16[512,8320]{1,0:T(8,128)(2,1)} async-done(((bf16[64,8320]{1,0:T(8,128)(2,1)}), bf16[512,8320]{1,0:T(8,128)(2,1)}) %all-gather.3.cloned.1.call-update) | async-done | bytes 8519696 | tf_op jit(solution)/shard_map/all_gather | solution.py:38
  106.8 1.0 convert_reduce_fusion
  107.9 110.9 %all-gather.5.cloned.1.call-done = bf16[1024,8320]{1,0:T(8,128)(2,1)} async-done(((bf16[64,8320]{1,0:T(8,128)(2,1)}), bf16[1024,8320]{1,0:T(8,128)(2,1)}) %all-gather.5.cloned.1.call-update) | async-done | bytes 17039376 | tf_op jit(solution)/shard_map/all_gather | solution.py:39
  218.8 1.4 add_reduce_fusion
  220.2 15.2 %tanh_convert_fusion = bf16[512,1024]{1,0:T(8,128)(2,1)S(1)} fusion(bf16[512,8320]{1,0:T(8,128)(2,1)} %all-gather.3.cloned.1.call-done, bf16[1024,8320]{1,0:T(8,128)(2,1)} %all-gather.5.cloned.1.call-done, f32[512]{0:T(512)S(1)} %convert_reduce_fusion), kind=kOutput, calls=%fused_computation.4 | convolution fusion | flops 8725200896 | bytes 26609664 | tf_op jit(solution)/shard_map/dot_general | solution.py:40
  235.4 0.0 copy-start.2
  235.4 1.8 fusion.1
  237.2 0.0 reduce-scatter.2.cloned.1.call-update
  237.2 0.0 copy-done.2
  237.2 0.6 dynamic-slice
  238.5 1.3 add_reduce_fusion.1
  239.7 0.9 multiply_reduce_fusion
  240.6 33.7 %all-reduce = f32[1024]{0:T(1024)S(1)} all-reduce(f32[1024]{0:T(1024)S(1)} %multiply_reduce_fusion), channel_id=3, replica_groups=mesh['blk'=8,'dp'=16] {'dp'}, use_global_device_ids=true, to_apply=%region_2.3.clone | all-reduce | flops 1024 | bytes 8192
  274.4 0.6 dynamic-slice.1
  274.9 0.0 reduce-scatter.2.cloned.1.call-done
  (4 shorter events, 0.0 us)
Async XLA Ops:
  7.2 4.0 %copy-start.1 = (s32[64]{0:T(128)S(1)}, s32[64]{0:T(128)}, u32[]{:S(2)}) copy-start(s32[64]{0:T(128)} %param.9) | copy-start | bytes 772
  7.2 4.1 %copy-start = (bf16[64,8192]{1,0:T(8,128)(2,1)S(1)}, bf16[64,8192]{1,0:T(8,128)(2,1)}, u32[]{:S(2)}) copy-start(bf16[64,8192]{1,0:T(8,128)(2,1)} %param.8) | copy-start | bytes 3145732
  7.2 99.7 %all-gather.3.cloned.1.call-start = ((), (), s32[]{:S(2)}) async-start(), calls=%async_computation.1 | async-start | bytes 9584640 | tf_op jit(solution)/shard_map/all_gather | solution.py:38
  11.1 207.6 %all-gather.5.cloned.1.call-start = ((), (), s32[]{:S(2)}) async-start(), calls=%async_computation.2 | async-start | bytes 18104320 | tf_op jit(solution)/shard_map/all_gather | solution.py:39
  12.4 262.5 %reduce-scatter.2.cloned.1.call-start = ((), (), s32[]{:S(2)}) async-start(), calls=%async_computation.3 | async-start | bytes 1179648 | tf_op jit(solution)/shard_map/reduce_scatter | solution.py:52
  235.4 1.8 copy-start.2
Sparse Core Ops, SparseCore 0:
  11.2 95.5 all-gather.2
  109.3 109.3 all-gather.4
  237.3 36.6 reduce-scatter.1

commit v2 on v1

--- a/solution.py
+++ b/solution.py
@@ -31,20 +31,49 @@
     return hi * 32 + lo
 
 
+def blk_pieces(tr, nx, ny):
+    n = nx * ny
+    yl = lax.axis_index("blk") // nx
+
+    def at(y, x):
+        return y * nx + x % nx
+
+    partner = lax.ppermute(tr, "blk", [(at(y, x), at(1 - y, x)) for y in range(ny) for x in range(nx)])
+    unit = jnp.where(yl == 0, jnp.concatenate([tr, partner]), jnp.concatenate([partner, tr]))
+    right = [(at(y, x), at(y, x + 1)) for y in range(ny) for x in range(nx)]
+    left = [(at(y, x), at(y, x - 1)) for y in range(ny) for x in range(nx)]
+    from_left = lax.ppermute(unit, "blk", right)
+    from_right = lax.ppermute(unit, "blk", left)
+    rows = tr.shape[0]
+    far_a = lax.ppermute(from_left[:rows], "blk", right)
+    far_b = lax.ppermute(from_right[rows:], "blk", left)
+    far = jnp.concatenate([far_a, far_b])
+    return [unit, from_right, far, from_left]
+
+
 def local(train_grads, train_scale, train_class, test_grads, test_class):
     k = train_grads.shape[1]
+    rows = train_grads.shape[0]
+    nx, ny = 4, 2
     tr = with_side(train_grads, (train_scale,) + split_class(train_class), 0)
     te = with_side(test_grads, split_class(test_class), 4)
-    tr_all = lax.all_gather(tr, "blk", axis=0, tiled=True)
     te_all = lax.all_gather(te, "dp", axis=0, tiled=True)
-    raw = lax.dot_general(
-        tr_all, te_all, (((1,), (1,)), ((), ())), preferred_element_type=jnp.float32
-    )
-    scale = tr_all[:, k].astype(jnp.float32)
-    weights = jnp.tanh(scale[:, None] * raw).astype(jnp.bfloat16)
-    train_hot = indicator(join_class(tr_all, k + 1))
     test_hot = indicator(join_class(te_all, k + 4))
+    pieces = blk_pieces(tr, nx, ny)
+    ws, hots = [], []
+    for piece in pieces:
+        raw = lax.dot_general(
+            piece, te_all, (((1,), (1,)), ((), ())), preferred_element_type=jnp.float32
+        )
+        scale = piece[:, k].astype(jnp.float32)
+        ws.append(jnp.tanh(scale[:, None] * raw).astype(jnp.bfloat16))
+        hots.append(indicator(join_class(piece, k + 1)))
+    weights = jnp.concatenate(ws)
+    train_hot = jnp.concatenate(hots)
     part = jnp.dot(weights, test_hot, preferred_element_type=jnp.float32)
+    xc = lax.axis_index("blk") % nx
+    part = jnp.roll(part.reshape(nx, ny, rows, NCLS), xc, axis=0)
+    part = jnp.swapaxes(part, 0, 1).reshape(nx * ny * rows, NCLS)
     per_class = lax.dot_general(
         weights, train_hot, (((0,), (0,)), ((), ())), preferred_element_type=jnp.float32
     )

time: 282 us -> 234 us (0.83)
  waiting for transfers between devices: 205 us -> 106 us
  matrix products: 17.9 us -> 49.1 us
  starting transfers between devices: 0.12 us -> 8.61 us
  local copies, waits for them, and re-layouts: 1.19 us -> 7.53 us
  other arithmetic: 8.7 us -> 13.1 us
    all_gather x1, waiting for transfers between devices: 111 us -> 10.5 us  [local(): te_all = lax.all_gather(te, 'dp', axis=0, tiled=True)]
    ppermute x0 -> x5, waiting for transfers between devices: none -> 95.1 us  [the longest x1 43.4 us: blk_pieces(): from_left = lax.ppermute(unit, 'blk', right)]
    all_gather x1 -> x0, waiting for transfers between devices: 94.4 us -> none  [local(): tr_all = lax.all_gather(tr, 'blk', axis=0, tiled=True)]
    dot_general x1 -> x4, matrix products: 15.2 us -> 47.6 us  [local(): lax.dot_general(piece, te_all, (((1,), (1,)), ((), ())), preferred_elemen...]
    ppermute x0 -> x5, starting transfers between devices: none -> 8.53 us  [the longest x1 3.42 us: blk_pieces(): far_b = lax.ppermute(from_right[rows:], 'blk', left)]
  transfers between devices with their start and end apart: 3 -> 7, of which waited for: 2 -> 5; matrix products, arithmetic and copies ran while one was open for 2% -> 6% of each run, Pallas kernels for 0% -> 0%
where the time goes in v2:
time: 234 us; the launch traced here: 233 us
  waiting for transfers between devices  106 us (45%)
  matrix products  49.1 us (21%)
  blocking collectives  34.3 us (15%)
  between operations  15 us (6%)
  other arithmetic  13.1 us (6%)
  starting transfers between devices  8.61 us (4%)
  local copies, waits for them, and re-layouts  7.53 us (3%)
    dot_general x4, matrix products, local(): lax.dot_general(piece, te_all, (((1,), (1,)), ((), ())), preferred_elemen...  47.6 us
    ppermute x1, waiting for transfers between devices, blk_pieces(): from_left = lax.ppermute(unit, 'blk', right)  43.4 us
    ppermute x1, waiting for transfers between devices, blk_pieces(): lax.ppermute(tr, 'blk', [(at(y, x), at(1 - y, x)) for y in range(ny) for...  34.6 us
    unnamed x1, blocking collectives  34.3 us
    ppermute x1, waiting for transfers between devices, blk_pieces(): far_a = lax.ppermute(from_left[:rows], 'blk', right)  16.5 us
    all_gather x1, waiting for transfers between devices, local(): te_all = lax.all_gather(te, 'dp', axis=0, tiled=True)  10.5 us
  transfers between devices with their start and end apart: 7, of which 5 were waited for; matrix products, arithmetic and copies ran while one was open for 6% of the time, Pallas kernels for 0%

profile of v2, /device:TPU:0, one launch (start us, length us, event | category | flops | bytes accessed | tf_op | source)
XLA Modules:
  0.0 233.3 jit_solution(8272988910544852030)
XLA Ops:
  7.2 0.8 fusion.12
  8.1 2.3 pad_maximum_fusion.1
  10.7 1.7 collective-permute-start
  12.4 34.6 %collective-permute-done = bf16[64,8320]{1,0:T(8,128)(2,1)} collective-permute-done((bf16[64,8320]{1,0:T(8,128)(2,1)S(1)}, bf16[64,8320]{1,0:T(8,128)(2,1)}, u32[]{:S(2)}, u32[]{:S(2)}) %collective-permute-start) | collective-permute-done | bytes 1064992 | tf_op jit(solution)/shard_map/ppermute | solution.py:41
  47.0 2.5 %maximum_select_fusion = bf16[128,8320]{1,0:T(8,128)(2,1)S(1)} fusion(bf16[64,8320]{1,0:T(8,128)(2,1)} %collective-permute-done, bf16[64,128]{1,0:T(8,128)(2,1)S(1)} %select_select_fusion.1, bf16[64,8192]{1,0:T(8,128)(2,1)S(1)} %copy-done.2, pred[]{:T(512)S(6)} %eq.96), kind=kLoop, calls=%fused_computation | loop fusion | flops 13844480 | bytes 4259841 | tf_op jit(solution)/shard_map/jit(_where)/select_n | solution.py:42
  49.5 1.8 collective-permute-start.2
  51.3 1.5 collective-permute-start.1
  52.8 43.4 %collective-permute-done.2 = bf16[128,8320]{1,0:T(8,128)(2,1)S(1)} collective-permute-done((bf16[128,8320]{1,0:T(8,128)(2,1)S(1)}, bf16[128,8320]{1,0:T(8,128)(2,1)S(1)}, u32[]{:S(2)}, u32[]{:S(2)}) %collective-permute-start.2) | collective-permute-done | bytes 2129952 | tf_op jit(solution)/shard_map/ppermute | solution.py:45
  96.2 1.3 copy-done
  97.5 1.1 slice.66
  98.8 1.3 slice.67
  100.1 3.4 %collective-permute-start.4 = (bf16[64,8320]{1,0:T(8,128)(2,1)S(1)}, bf16[64,8320]{1,0:T(8,128)(2,1)S(1)}, u32[]{:S(2)}, u32[]{:S(2)}) collective-permute-start(bf16[64,8320]{1,0:T(8,128)(2,1)S(1)} %slice.67), channel_id=1, source_target_pairs={{0,48},{16,0},{32,16},{48,32},{64,112},{80,64},{96,80},{112,96},{1... | collective-permute-start | bytes 3194888 | tf_op jit(solution)/shard_map/ppermute | solution.py:49
  103.5 0.9 convert_reduce_fusion
  104.4 0.9 convert_reduce_fusion.2
  105.3 16.5 %collective-permute-done.3 = bf16[64,8320]{1,0:T(8,128)(2,1)S(1)} collective-permute-done((bf16[64,8320]{1,0:T(8,128)(2,1)}, bf16[64,8320]{1,0:T(8,128)(2,1)S(1)}, u32[]{:S(2)}, u32[]{:S(2)}) %collective-permute-start.3) | collective-permute-done | bytes 1064992 | tf_op jit(solution)/shard_map/ppermute | solution.py:48
  121.9 0.7 collective-permute-done.4
  122.7 1.3 copy-done.1
  124.1 10.5 %all-gather.2.cloned.1.call-done = bf16[1024,8320]{1,0:T(8,128)(2,1)} async-done(((bf16[64,8320]{1,0:T(8,128)(2,1)}), bf16[1024,8320]{1,0:T(8,128)(2,1)}) %all-gather.2.cloned.1.call-update) | async-done | bytes 17039376 | tf_op jit(solution)/shard_map/all_gather | solution.py:60
  134.6 1.4 add_reduce_fusion
  136.1 11.4 %tanh_convert_fusion.3 = bf16[128,1024]{1,0:T(8,128)(2,1)S(1)} fusion(f32[128]{0:T(128)S(1)} %convert_reduce_fusion.3, bf16[128,8320]{1,0:T(8,128)(2,1)S(1)} %maximum_select_fusion, bf16[1024,8320]{1,0:T(8,128)(2,1)} %all-gather.2.cloned.1.call-done), kind=kOutput, calls=%fused_computation.24 | convolution fusion | flops 2181300224 | bytes 19431936 | tf_op jit(solution)/shard_map/dot_general | solution.py:65
  147.5 12.1 %tanh_convert_fusion = bf16[128,1024]{1,0:T(8,128)(2,1)S(1)} fusion(f32[128]{0:T(128)S(1)} %convert_reduce_fusion, bf16[128,8320]{1,0:T(8,128)(2,1)} %copy-done, bf16[1024,8320]{1,0:T(8,128)(2,1)} %all-gather.2.cloned.1.call-done), kind=kOutput, calls=%fused_computation.21 | convolution fusion | flops 2181300224 | bytes 19431936 | tf_op jit(solution)/shard_map/dot_general | solution.py:65
  159.5 12.1 %tanh_convert_fusion.2 = bf16[128,1024]{1,0:T(8,128)(2,1)S(1)} fusion(f32[128]{0:T(128)S(1)} %convert_reduce_fusion.2, bf16[128,8320]{1,0:T(8,128)(2,1)} %collective-permute-done.1, bf16[1024,8320]{1,0:T(8,128)(2,1)} %all-gather.2.cloned.1.call-done), kind=kOutput, calls=%fused_computation.23 | convolution fusion | flops 2181300224 | bytes 19431936 | tf_op jit(solution)/shard_map/dot_general | solution.py:65
  171.6 12.1 %tanh_convert_fusion.1 = bf16[128,1024]{1,0:T(8,128)(2,1)S(1)} fusion(f32[128]{0:T(128)S(1)} %convert_reduce_fusion.1, bf16[128,8320]{1,0:T(8,128)(2,1)} %copy-done.1, bf16[1024,8320]{1,0:T(8,128)(2,1)} %all-gather.2.cloned.1.call-done), kind=kOutput, calls=%fused_computation.22 | convolution fusion | flops 2181300224 | bytes 19431936 | tf_op jit(solution)/shard_map/dot_general | solution.py:65
  183.6 0.8 fusion.1
  184.7 1.1 copy.9
  185.8 0.6 dynamic-slice
  187.4 1.0 add_reduce_fusion.1
  188.4 1.0 add_reduce_fusion.3
  189.7 1.0 add_reduce_fusion.2
  190.8 0.8 multiply_reduce_fusion
  191.6 34.3 %all-reduce = f32[1024]{0:T(1024)S(1)} all-reduce(f32[1024]{0:T(1024)S(1)} %multiply_reduce_fusion), channel_id=3, replica_groups=mesh['blk'=8,'dp'=16] {'dp'}, use_global_device_ids=true, to_apply=%region_2.3.clone | all-reduce | flops 1024 | bytes 8192
  225.9 0.6 dynamic-slice.1
  (31 shorter events, 1.7 us)
Async XLA Ops:
  7.2 3.3 %copy-start.3 = (bf16[64]{0:T(256)(128)(2,1)S(1)}, bf16[64]{0:T(256)(128)(2,1)}, u32[]{:S(2)}) copy-start(bf16[64]{0:T(256)(128)(2,1)} %param.6) | copy-start | bytes 388
  7.2 3.4 %copy-start.2 = (bf16[64,8192]{1,0:T(8,128)(2,1)S(1)}, bf16[64,8192]{1,0:T(8,128)(2,1)}, u32[]{:S(2)}) copy-start(bf16[64,8192]{1,0:T(8,128)(2,1)} %param.5) | copy-start | bytes 3145732
  7.2 127.4 %all-gather.2.cloned.1.call-start = ((), (), s32[]{:S(2)}) async-start(), calls=%async_computation.1 | async-start | bytes 18104320 | tf_op jit(solution)/shard_map/all_gather | solution.py:60
  10.4 216.1 %reduce-scatter.2.cloned.1.call-start = ((), (), s32[]{:S(2)}) async-start(), calls=%async_computation.2 | async-start | bytes 1179648 | tf_op jit(solution)/shard_map/reduce_scatter | solution.py:81
  10.7 36.3 %collective-permute-start = (bf16[64,8320]{1,0:T(8,128)(2,1)S(1)}, bf16[64,8320]{1,0:T(8,128)(2,1)}, u32[]{:S(2)}, u32[]{:S(2)}) collective-permute-start(bf16[64,8320]{1,0:T(8,128)(2,1)S(1)} %pad_maximum_fusion), channel_id=1, source_target_pairs={{0,64},{16,80},{32,96},{48,112},{64,0},{80,16},{96,32},{112,48},{1... | collective-permute-start | bytes 3194888 | tf_op jit(solution)/shard_map/ppermute | solution.py:41
  49.5 46.7 %collective-permute-start.2 = (bf16[128,8320]{1,0:T(8,128)(2,1)S(1)}, bf16[128,8320]{1,0:T(8,128)(2,1)S(1)}, u32[]{:S(2)}, u32[]{:S(2)}) collective-permute-start(bf16[128,8320]{1,0:T(8,128)(2,1)S(1)} %maximum_select_fusion), channel_id=1, source_target_pairs={{0,16},{16,32},{32,48},{48,0},{64,80},{80,96},{96,112},{112,64},{1... | collective-permute-start | bytes 6389768 | tf_op jit(solution)/shard_map/ppermute | solution.py:45
  51.3 47.4 %collective-permute-start.1 = (bf16[128,8320]{1,0:T(8,128)(2,1)S(1)}, bf16[128,8320]{1,0:T(8,128)(2,1)}, u32[]{:S(2)}, u32[]{:S(2)}) collective-permute-start(bf16[128,8320]{1,0:T(8,128)(2,1)S(1)} %maximum_select_fusion), channel_id=1, source_target_pairs={{0,48},{16,0},{32,16},{48,32},{64,112},{80,64},{96,80},{112,96},{1... | collective-permute-start | bytes 6389768 | tf_op jit(solution)/shard_map/ppermute | solution.py:46
  96.2 1.3 copy-start
  98.6 23.2 %collective-permute-start.3 = (bf16[64,8320]{1,0:T(8,128)(2,1)}, bf16[64,8320]{1,0:T(8,128)(2,1)S(1)}, u32[]{:S(2)}, u32[]{:S(2)}) collective-permute-start(bf16[64,8320]{1,0:T(8,128)(2,1)} %slice.66), channel_id=1, source_target_pairs={{0,16},{16,32},{32,48},{48,0},{64,80},{80,96},{96,112},{112,64},{1... | collective-permute-start | bytes 3194888 | tf_op jit(solution)/shard_map/ppermute | solution.py:48
  100.1 22.4 %collective-permute-start.4 = (bf16[64,8320]{1,0:T(8,128)(2,1)S(1)}, bf16[64,8320]{1,0:T(8,128)(2,1)S(1)}, u32[]{:S(2)}, u32[]{:S(2)}) collective-permute-start(bf16[64,8320]{1,0:T(8,128)(2,1)S(1)} %slice.67), channel_id=1, source_target_pairs={{0,48},{16,0},{32,16},{48,32},{64,112},{80,64},{96,80},{112,96},{1... | collective-permute-start | bytes 3194888 | tf_op jit(solution)/shard_map/ppermute | solution.py:49
  122.6 1.4 copy-start.1
  184.4 1.4 copy-start.4
Sparse Core Ops, SparseCore 0:
  10.5 124.0 all-gather.1
  185.9 36.8 reduce-scatter.1

commit v3 on v2

--- a/solution.py
+++ b/solution.py
@@ -60,16 +60,13 @@
     te_all = lax.all_gather(te, "dp", axis=0, tiled=True)
     test_hot = indicator(join_class(te_all, k + 4))
     pieces = blk_pieces(tr, nx, ny)
-    ws, hots = [], []
-    for piece in pieces:
-        raw = lax.dot_general(
-            piece, te_all, (((1,), (1,)), ((), ())), preferred_element_type=jnp.float32
-        )
-        scale = piece[:, k].astype(jnp.float32)
-        ws.append(jnp.tanh(scale[:, None] * raw).astype(jnp.bfloat16))
-        hots.append(indicator(join_class(piece, k + 1)))
-    weights = jnp.concatenate(ws)
-    train_hot = jnp.concatenate(hots)
+    train_all = jnp.concatenate(pieces)
+    raw = lax.dot_general(
+        train_all, te_all, (((1,), (1,)), ((), ())), preferred_element_type=jnp.float32
+    )
+    scale = train_all[:, k].astype(jnp.float32)
+    weights = jnp.tanh(scale[:, None] * raw).astype(jnp.bfloat16)
+    train_hot = indicator(join_class(train_all, k + 1))
     part = jnp.dot(weights, test_hot, preferred_element_type=jnp.float32)
     xc = lax.axis_index("blk") % nx
     part = jnp.roll(part.reshape(nx, ny, rows, NCLS), xc, axis=0)

time: 234 us -> 199 us (0.85)
  matrix products: 49.1 us -> 16.4 us
  other arithmetic: 13.1 us -> 10.1 us
  local copies, waits for them, and re-layouts: 7.53 us -> 10.4 us
    dot_general x4 -> x1, matrix products: 47.6 us -> 14.7 us  [local(): lax.dot_general(train_all, te_all, (((1,), (1,)), ((), ())), preferred_el...]
    unnamed x0 -> x1, other arithmetic: none -> 2.78 us
    select_n x1 -> x0, other arithmetic: 2.53 us -> none  [blk_pieces(): jnp.where(yl == 0, jnp.concatenate([tr, partner]), jnp.concatenate([partn...]
    unnamed x13 -> x11, local copies, waits for them, and re-layouts: 3.93 us -> 6.37 us
  transfers between devices with their start and end apart: 7 -> 7, of which waited for: 5 -> 4; matrix products, arithmetic and copies ran while one was open for 6% -> 8% of each run, Pallas kernels for 0% -> 0%
where the time goes in v3:
time: 199 us; the launch traced here: 198 us
  waiting for transfers between devices  104 us (52%)
  blocking collectives  33.7 us (17%)
  matrix products  16.4 us (8%)
  between operations  14.8 us (7%)
  local copies, waits for them, and re-layouts  10.4 us (5%)
  other arithmetic  10.1 us (5%)
  starting transfers between devices  8.43 us (4%)
    ppermute x1, waiting for transfers between devices, blk_pieces(): from_left = lax.ppermute(unit, 'blk', right)  43.7 us
    ppermute x1, waiting for transfers between devices, blk_pieces(): lax.ppermute(tr, 'blk', [(at(y, x), at(1 - y, x)) for y in range(ny) for...  34.5 us
    unnamed x1, blocking collectives  33.7 us
    ppermute x1, waiting for transfers between devices, blk_pieces(): far_a = lax.ppermute(from_left[:rows], 'blk', right)  15.4 us
    dot_general x1, matrix products, local(): lax.dot_general(train_all, te_all, (((1,), (1,)), ((), ())), preferred_el...  14.7 us
    all_gather x1, waiting for transfers between devices, local(): te_all = lax.all_gather(te, 'dp', axis=0, tiled=True)  10.1 us
    unnamed x11, local copies, waits for them, and re-layouts  6.37 us
  transfers between devices with their start and end apart: 7, of which 4 were waited for; matrix products, arithmetic and copies ran while one was open for 8% of the time, Pallas kernels for 0%

profile of v3, /device:TPU:0, one launch (start us, length us, event | category | flops | bytes accessed | tf_op | source)
XLA Modules:
  0.0 197.7 jit_solution(8587208275507298187)
XLA Ops:
  7.2 0.8 fusion.6
  8.0 0.1 select_select_fusion
  8.1 2.3 %pad_maximum_fusion.1 = bf16[64,8320]{1,0:T(8,128)(2,1)} fusion(bf16[64,128]{1,0:T(8,128)(2,1)S(1)} %select_select_fusion, bf16[64,8192]{1,0:T(8,128)(2,1)} %param.8), kind=kLoop, calls=%fused_computation.9 | loop fusion | flops 2129920 | bytes 2129920 | tf_op jit(solution)/shard_map/concatenate | solution.py:21
  10.5 0.1 select_select_fusion.1
  10.6 0.1 pad_maximum_fusion
  10.7 1.7 collective-permute-start
  12.5 34.5 %collective-permute-done = bf16[64,8320]{1,0:T(8,128)(2,1)S(1)} collective-permute-done((bf16[64,8320]{1,0:T(8,128)(2,1)S(1)}, bf16[64,8320]{1,0:T(8,128)(2,1)S(1)}, u32[]{:S(2)}, u32[]{:S(2)}) %collective-permute-start) | collective-permute-done | bytes 1064992 | tf_op jit(solution)/shard_map/ppermute | solution.py:41
  46.9 2.8 %constant_dynamic-update-slice_fusion.4 = (bf16[512,8320]{1,0:T(8,128)(2,1)}, bf16[128,8320]{1,0:T(8,128)(2,1)}) fusion(bf16[64,128]{1,0:T(8,128)(2,1)S(1)} %select_select_fusion.1, bf16[64,8192]{1,0:T(8,128)(2,1)S(1)} %copy-done, bf16[64,8320]{1,0:T(8,128)(2,1)S(1)} %collective-permute-done, pred[]{:T(512)S(6)} %eq.66), kind=kLoop, calls=%fused_computation.24 | loop fusion | flops 13844479 | bytes 6389761
  49.7 1.7 collective-permute-start.2
  51.5 1.5 collective-permute-start.1
  53.0 43.7 %collective-permute-done.2 = bf16[128,8320]{1,0:T(8,128)(2,1)S(1)} collective-permute-done((bf16[128,8320]{1,0:T(8,128)(2,1)}, bf16[128,8320]{1,0:T(8,128)(2,1)S(1)}, u32[]{:S(2)}, u32[]{:S(2)}) %collective-permute-start.2) | collective-permute-done | bytes 2129952 | tf_op jit(solution)/shard_map/ppermute | solution.py:45
  96.6 0.1 slice.28
  96.7 0.6 collective-permute-start.3
  97.4 1.3 slice.29
  98.7 2.7 %collective-permute-start.4 = (bf16[64,8320]{1,0:T(8,128)(2,1)S(1)}, bf16[64,8320]{1,0:T(8,128)(2,1)S(1)}, u32[]{:S(2)}, u32[]{:S(2)}) collective-permute-start(bf16[64,8320]{1,0:T(8,128)(2,1)S(1)} %slice.29), channel_id=1, source_target_pairs={{0,48},{16,0},{32,16},{48,32},{64,112},{80,64},{96,80},{112,96},{1... | collective-permute-start | bytes 3194888 | tf_op jit(solution)/shard_map/ppermute | solution.py:49
  101.4 3.1 %constant_dynamic-update-slice_fusion.3 = bf16[512,8320]{1,0:T(8,128)(2,1)} fusion(bf16[512,8320]{1,0:T(8,128)(2,1)} %get-tuple-element.2, bf16[128,8320]{1,0:T(8,128)(2,1)} %collective-permute-done.1), kind=kLoop, calls=%fused_computation.23 | loop fusion | bytes 4259840
  104.5 15.4 %collective-permute-done.3 = bf16[64,8320]{1,0:T(8,128)(2,1)S(1)} collective-permute-done((bf16[64,8320]{1,0:T(8,128)(2,1)S(1)}, bf16[64,8320]{1,0:T(8,128)(2,1)S(1)}, u32[]{:S(2)}, u32[]{:S(2)}) %collective-permute-start.3) | collective-permute-done | bytes 1064992 | tf_op jit(solution)/shard_map/ppermute | solution.py:48
  119.9 1.1 constant_dynamic-update-slice_fusion.2
  120.9 1.1 constant_dynamic-update-slice_fusion.1
  122.0 1.5 constant_dynamic-update-slice_fusion
  123.5 1.0 convert_reduce_fusion
  124.5 10.1 %all-gather.2.cloned.1.call-done = bf16[1024,8320]{1,0:T(8,128)(2,1)} async-done(((bf16[64,8320]{1,0:T(8,128)(2,1)}), bf16[1024,8320]{1,0:T(8,128)(2,1)}) %all-gather.2.cloned.1.call-update) | async-done | bytes 17039376 | tf_op jit(solution)/shard_map/all_gather | solution.py:60
  134.7 14.7 %fusion.10 = f32[512,1024]{1,0:T(8,128)S(1)} fusion(bf16[512,8320]{1,0:T(8,128)(2,1)} %constant_dynamic-update-slice_fusion, bf16[1024,8320]{1,0:T(8,128)(2,1)} %all-gather.2.cloned.1.call-done), kind=kOutput, calls=%fused_computation.44 | convolution fusion | flops 8724152320 | bytes 27656192 | tf_op jit(solution)/shard_map/dot_general | solution.py:64
  149.3 1.5 add_reduce_fusion
  150.8 0.8 fusion.1
  151.7 0.3 fusion.3
  151.9 1.1 copy.9
  153.1 0.6 dynamic-slice
  154.3 1.3 add_reduce_fusion.1
  155.6 0.9 multiply_reduce_fusion
  156.5 33.7 %all-reduce = f32[1024]{0:T(1024)S(1)} all-reduce(f32[1024]{0:T(1024)S(1)} %multiply_reduce_fusion), channel_id=3, replica_groups=mesh['blk'=8,'dp'=16] {'dp'}, use_global_device_ids=true, to_apply=%region_2.3.clone | all-reduce | flops 1024 | bytes 8192
  190.2 0.6 dynamic-slice.1
  (16 shorter events, 0.2 us)
Async XLA Ops:
  7.2 3.4 %copy-start.1 = (bf16[64]{0:T(256)(128)(2,1)S(1)}, bf16[64]{0:T(256)(128)(2,1)}, u32[]{:S(2)}) copy-start(bf16[64]{0:T(256)(128)(2,1)} %param.6) | copy-start | bytes 388
  7.2 3.5 %copy-start = (bf16[64,8192]{1,0:T(8,128)(2,1)S(1)}, bf16[64,8192]{1,0:T(8,128)(2,1)}, u32[]{:S(2)}) copy-start(bf16[64,8192]{1,0:T(8,128)(2,1)} %param.5) | copy-start | bytes 3145732
  7.2 127.5 %all-gather.2.cloned.1.call-start = ((), (), s32[]{:S(2)}) async-start(), calls=%async_computation.1 | async-start | bytes 18104320 | tf_op jit(solution)/shard_map/all_gather | solution.py:60
  10.4 180.4 %reduce-scatter.2.cloned.1.call-start = ((), (), s32[]{:S(2)}) async-start(), calls=%async_computation.2 | async-start | bytes 1179648 | tf_op jit(solution)/shard_map/reduce_scatter | solution.py:78
  10.7 36.2 %collective-permute-start = (bf16[64,8320]{1,0:T(8,128)(2,1)S(1)}, bf16[64,8320]{1,0:T(8,128)(2,1)S(1)}, u32[]{:S(2)}, u32[]{:S(2)}) collective-permute-start(bf16[64,8320]{1,0:T(8,128)(2,1)S(1)} %pad_maximum_fusion), channel_id=1, source_target_pairs={{0,64},{16,80},{32,96},{48,112},{64,0},{80,16},{96,32},{112,48},{1... | collective-permute-start | bytes 3194888 | tf_op jit(solution)/shard_map/ppermute | solution.py:41
  49.7 46.9 %collective-permute-start.2 = (bf16[128,8320]{1,0:T(8,128)(2,1)}, bf16[128,8320]{1,0:T(8,128)(2,1)S(1)}, u32[]{:S(2)}, u32[]{:S(2)}) collective-permute-start(bf16[128,8320]{1,0:T(8,128)(2,1)} %get-tuple-element.3), channel_id=1, source_target_pairs={{0,16},{16,32},{32,48},{48,0},{64,80},{80,96},{96,112},{112,64},{1... | collective-permute-start | bytes 6389768 | tf_op jit(solution)/shard_map/ppermute | solution.py:45
  51.5 45.9 %collective-permute-start.1 = (bf16[128,8320]{1,0:T(8,128)(2,1)}, bf16[128,8320]{1,0:T(8,128)(2,1)}, u32[]{:S(2)}, u32[]{:S(2)}) collective-permute-start(bf16[128,8320]{1,0:T(8,128)(2,1)} %get-tuple-element.3), channel_id=1, source_target_pairs={{0,48},{16,0},{32,16},{48,32},{64,112},{80,64},{96,80},{112,96},{1... | collective-permute-start | bytes 6389768 | tf_op jit(solution)/shard_map/ppermute | solution.py:46
  96.7 23.1 %collective-permute-start.3 = (bf16[64,8320]{1,0:T(8,128)(2,1)S(1)}, bf16[64,8320]{1,0:T(8,128)(2,1)S(1)}, u32[]{:S(2)}, u32[]{:S(2)}) collective-permute-start(bf16[64,8320]{1,0:T(8,128)(2,1)S(1)} %slice.28), channel_id=1, source_target_pairs={{0,16},{16,32},{32,48},{48,0},{64,80},{80,96},{96,112},{112,64},{1... | collective-permute-start | bytes 3194888 | tf_op jit(solution)/shard_map/ppermute | solution.py:48
  98.7 22.2 %collective-permute-start.4 = (bf16[64,8320]{1,0:T(8,128)(2,1)S(1)}, bf16[64,8320]{1,0:T(8,128)(2,1)S(1)}, u32[]{:S(2)}, u32[]{:S(2)}) collective-permute-start(bf16[64,8320]{1,0:T(8,128)(2,1)S(1)} %slice.29), channel_id=1, source_target_pairs={{0,48},{16,0},{32,16},{48,32},{64,112},{80,64},{96,80},{112,96},{1... | collective-permute-start | bytes 3194888 | tf_op jit(solution)/shard_map/ppermute | solution.py:49
  151.6 1.4 copy-start.2
Sparse Core Ops, SparseCore 0:
  10.6 124.0 all-gather.1
  153.2 36.6 reduce-scatter.1

commit v4 on v1

v4 whole, which is shorter than its diff:
```python
import jax
import jax.numpy as jnp
from jax import lax
from jax.sharding import PartitionSpec as P

NCLS = 512
PAD = 128
AXES = ("blk", "dp")


def indicator(labels):
    columns = lax.broadcasted_iota(jnp.int32, (labels.shape[0], NCLS), 1)
    return (labels[:, None] == columns).astype(jnp.bfloat16)


def with_side(grads, side, first):
    rows = grads.shape[0]
    cols = lax.broadcasted_iota(jnp.int32, (rows, PAD), 1)
    extra = jnp.zeros((rows, PAD), jnp.bfloat16)
    for k, v in enumerate(side):
        extra = jnp.where(cols == first + k, v[:, None].astype(jnp.bfloat16), extra)
    return jnp.concatenate([grads, extra], axis=1)


def split_class(c):
    return (c // 32, c % 32)


def join_class(x, k):
    hi = x[:, k].astype(jnp.int32)
    lo = x[:, k + 1].astype(jnp.int32)
    return hi * 32 + lo


def coords(L):
    blk, dp = divmod(L, 16)
    yl, x = divmod(blk, 4)
    z, r = divmod(dp, 4)
    yh, c = divmod(r, 2)
    return [x, 2 * yh + yl, z], c


def lin(v, c):
    x, y, z = v
    return ((y % 2) * 4 + x) * 16 + z * 4 + (y // 2) * 2 + c


def train_mate(v):
    return v ^ 1


def test_mate(v):
    return ((((v - 1) % 4) ^ 1) + 1) % 4


def mate_pairs(n, axis, mate):
    out = []
    for L in range(n):
        v, c = coords(L)
        w = list(v)
        w[axis] = mate(v[axis])
        out.append((L, lin(w, c)))
    return out


def core_pairs(n):
    return [(L, L ^ 1) for L in range(n)]


def cube_gather(shard, mate, n):
    cols = shard.shape[1]
    tiles = cols // 128
    cut = [0, (tiles // 3) * 128, (2 * tiles // 3) * 128, cols]
    parts = []
    for p in range(3):
        order = [(p + s) % 3 for s in range(3)]
        buf = [shard[:, cut[p]:cut[p + 1]]]
        labs = [0]
        for a in order:
            got = lax.ppermute(buf, AXES, mate_pairs(n, a, mate))
            buf = buf + list(got)
            labs = labs + [o ^ (1 << a) for o in labs]
        parts.append({o: b for o, b in zip(labs, buf)})
    return jnp.concatenate(
        [jnp.concatenate([parts[p][o] for p in range(3)], axis=1) for o in range(8)]
    )


def cube_reduce(blocks, mate, n):
    blocks = list(blocks)
    live = list(range(8))
    for a in range(3):
        send = [o for o in live if o & (1 << a)]
        keep = [o for o in live if not o & (1 << a)]
        got = lax.ppermute([blocks[o] for o in send], AXES, mate_pairs(n, a, mate))
        for o, g in zip(send, got):
            blocks[o ^ (1 << a)] = blocks[o ^ (1 << a)] + g
        live = keep
    return blocks[0]


def local(train_grads, train_scale, train_class, test_grads, test_class):
    n = 128
    k = train_grads.shape[1]
    rows = train_grads.shape[0]
    tr = with_side(train_grads, (train_scale,) + split_class(train_class), 0)
    te = with_side(test_grads, split_class(test_class), 4)
    te_all = cube_gather(te, test_mate, n)
    tr_mine = cube_gather(tr, train_mate, n)
    tr_other = lax.ppermute(tr_mine, AXES, core_pairs(n))
    test_hot = indicator(join_class(te_all, k + 4))

    def weigh(t):
        raw = lax.dot_general(
            t, te_all, (((1,), (1,)), ((), ())), preferred_element_type=jnp.float32
        )
        scale = t[:, k].astype(jnp.float32)
        w = jnp.tanh(scale[:, None] * raw).astype(jnp.bfloat16)
        hot = indicator(join_class(t, k + 1))
        part = jnp.dot(w, test_hot, preferred_element_type=jnp.float32)
        per_class = lax.dot_general(
            w, hot, (((0,), (0,)), ((), ())), preferred_element_type=jnp.float32
        )
        return part, per_class

    part_m, pc_m = weigh(tr_mine)
    part_o, pc_o = weigh(tr_other)
    part = part_m + lax.ppermute(part_o, AXES, core_pairs(n))
    train_attr = cube_reduce(
        [part[o * rows:(o + 1) * rows] for o in range(8)], train_mate, n
    )
    test_part = jnp.sum((pc_m + pc_o) * test_hot.astype(jnp.float32), axis=1)
    test_attr = cube_reduce(
        [test_part[o * rows:(o + 1) * rows] for o in range(8)], test_mate, n
    )
    return (train_attr, test_attr)


def solution(mesh):
    in_specs = (
        P(AXES, None),
        P(AXES),
        P(AXES),
        P(AXES, None),
        P(AXES),
    )
    out_specs = (P(AXES, None), P(AXES))
    return jax.shard_map(local, mesh=mesh, in_specs=in_specs, out_specs=out_specs, check_vma=False)
```

time: 282 us -> 232 us (0.82)
  waiting for transfers between devices: 205 us -> 104 us
  starting transfers between devices: 0.12 us -> 94.4 us
  blocking collectives: 33.7 us -> 0 us
  between operations: 14.5 us -> 1.04 us
    all_gather x2 -> x0, waiting for transfers between devices: 205 us -> none  [the longest x1 111 us: local(): te_all = lax.all_gather(te, 'dp', axis=0, tiled=True)]
    ppermute x0 -> x58, waiting for transfers between devices: none -> 104 us  [the longest x42 93.3 us: cube_gather(): got = lax.ppermute(buf, AXES, mate_pairs(n, a, mate))]
    ppermute x0 -> x58, starting transfers between devices: none -> 94.4 us  [the longest x42 78.9 us: cube_gather(): got = lax.ppermute(buf, AXES, mate_pairs(n, a, mate))]
    unnamed x1 -> x0, blocking collectives: 33.7 us -> none
    concatenate x2, other arithmetic: 3.41 us -> 0.26 us  [cube_gather(): jnp.concatenate([jnp.concatenate([parts[p][o] for p in range(3)], axis=1)...]
    dot_general x3 -> x6, matrix products: 17.9 us -> 20 us  [the longest x2 17.8 us: weigh(): lax.dot_general(t, te_all, (((1,), (1,)), ((), ())), preferred_element_ty...]
  transfers between devices with their start and end apart: 3 -> 58, of which waited for: 2 -> 26; matrix products, arithmetic and copies ran while one was open for 2% -> 6% of each run, Pallas kernels for 0% -> 0%
where the time goes in v4:
time: 232 us
  waiting for transfers between devices  104 us (45%)
  starting transfers between devices  94.4 us (41%)
  matrix products  20 us (9%)
  other arithmetic  8.96 us (4%)
  local copies, waits for them, and re-layouts  3.27 us (1%)
    ppermute x42, waiting for transfers between devices, cube_gather(): got = lax.ppermute(buf, AXES, mate_pairs(n, a, mate))  93.3 us
    ppermute x42, starting transfers between devices, cube_gather(): got = lax.ppermute(buf, AXES, mate_pairs(n, a, mate))  78.9 us
    dot_general x2, matrix products, weigh(): lax.dot_general(t, te_all, (((1,), (1,)), ((), ())), preferred_element_ty...  17.8 us
    ppermute x14, starting transfers between devices, cube_reduce(): got = lax.ppermute([blocks[o] for o in send], AXES, mate_pairs(n, a, mate))  15.4 us
    ppermute x14, waiting for transfers between devices, cube_reduce(): got = lax.ppermute([blocks[o] for o in send], AXES, mate_pairs(n, a, mate))  10.7 us
  transfers between devices with their start and end apart: 58, of which 26 were waited for; matrix products, arithmetic and copies ran while one was open for 6% of the time, Pallas kernels for 0%

profile of v4, /device:TPU:0, one launch (start us, length us, event | category | flops | bytes accessed | tf_op | source)
XLA Modules:
  0.0 231.7 jit_solution(15784176432920590820)
XLA Ops:
  9.5 19.0 %collective-permute-done = bf16[64,2688]{1,0:T(8,128)(2,1)S(1)} collective-permute-done((bf16[64,2688]{1,0:T(8,128)(2,1)S(1)}, bf16[64,2688]{1,0:T(8,128)(2,1)S(1)}, u32[]{:S(2)}, u32[]{:S(2)}) %collective-permute-start) | collective-permute-done | bytes 344096 | tf_op jit(solution)/shard_map/ppermute | solution.py:80
  32.6 5.0 %collective-permute-done.3 = bf16[64,2688]{1,0:T(8,128)(2,1)S(1)} collective-permute-done((bf16[64,2688]{1,0:T(8,128)(2,1)S(1)}, bf16[64,2688]{1,0:T(8,128)(2,1)S(1)}, u32[]{:S(2)}, u32[]{:S(2)}) %collective-permute-start.3) | collective-permute-done | bytes 344096 | tf_op jit(solution)/shard_map/ppermute | solution.py:80
  41.4 7.2 %collective-permute-done.6 = bf16[64,2688]{1,0:T(8,128)(2,1)S(1)} collective-permute-done((bf16[64,2688]{1,0:T(8,128)(2,1)S(1)}, bf16[64,2688]{1,0:T(8,128)(2,1)S(1)}, u32[]{:S(2)}, u32[]{:S(2)}) %collective-permute-start.6) | collective-permute-done | bytes 344096 | tf_op jit(solution)/shard_map/ppermute | solution.py:80
  50.7 2.8 %collective-permute-start.22 = (bf16[64,2816]{1,0:T(8,128)(2,1)S(1)}, bf16[64,2816]{1,0:T(8,128)(2,1)S(1)}, u32[]{:S(2)}, u32[]{:S(2)}) collective-permute-start(bf16[64,2816]{1,0:T(8,128)(2,1)S(1)} %get-tuple-element.10), channel_id=1, source_target_pairs={{0,48},{1,49},{2,50},{3,51},{4,52},{5,53},{6,54},{7,55},{8,56},{9,... | collective-permute-start | bytes 1081352 | tf_op jit(solution)/shard_map/ppermute | solution.py:80
  53.4 3.1 %collective-permute-start.25 = (bf16[64,2816]{1,0:T(8,128)(2,1)S(1)}, bf16[64,2816]{1,0:T(8,128)(2,1)S(1)}, u32[]{:S(2)}, u32[]{:S(2)}) collective-permute-start(bf16[64,2816]{1,0:T(8,128)(2,1)S(1)} %get-tuple-element.10), channel_id=1, source_target_pairs={{0,66},{1,67},{2,64},{3,65},{4,70},{5,71},{6,68},{7,69},{8,74},{9,... | collective-permute-start | bytes 1081352 | tf_op jit(solution)/shard_map/ppermute | solution.py:80
  60.8 4.3 %collective-permute-done.12 = bf16[64,2688]{1,0:T(8,128)(2,1)S(1)} collective-permute-done((bf16[64,2688]{1,0:T(8,128)(2,1)S(1)}, bf16[64,2688]{1,0:T(8,128)(2,1)S(1)}, u32[]{:S(2)}, u32[]{:S(2)}) %collective-permute-start.12) | collective-permute-done | bytes 344096 | tf_op jit(solution)/shard_map/ppermute | solution.py:80
  69.8 3.5 %collective-permute-done.13 = bf16[64,2816]{1,0:T(8,128)(2,1)S(1)} collective-permute-done((bf16[64,2816]{1,0:T(8,128)(2,1)S(1)}, bf16[64,2816]{1,0:T(8,128)(2,1)S(1)}, u32[]{:S(2)}, u32[]{:S(2)}) %collective-permute-start.13) | collective-permute-done | bytes 360480 | tf_op jit(solution)/shard_map/ppermute | solution.py:80
  78.2 4.5 %collective-permute-done.16 = bf16[64,2816]{1,0:T(8,128)(2,1)S(1)} collective-permute-done((bf16[64,2816]{1,0:T(8,128)(2,1)S(1)}, bf16[64,2816]{1,0:T(8,128)(2,1)S(1)}, u32[]{:S(2)}, u32[]{:S(2)}) %collective-permute-start.16) | collective-permute-done | bytes 360480 | tf_op jit(solution)/shard_map/ppermute | solution.py:80
  86.4 2.8 %collective-permute-start.23 = (bf16[64,2816]{1,0:T(8,128)(2,1)S(1)}, bf16[64,2816]{1,0:T(8,128)(2,1)S(1)}, u32[]{:S(2)}, u32[]{:S(2)}) collective-permute-start(bf16[64,2816]{1,0:T(8,128)(2,1)S(1)} %get-tuple-element.11), channel_id=1, source_target_pairs={{0,48},{1,49},{2,50},{3,51},{4,52},{5,53},{6,54},{7,55},{8,56},{9,... | collective-permute-start | bytes 1081352 | tf_op jit(solution)/shard_map/ppermute | solution.py:80
  90.2 2.8 %collective-permute-start.21 = (bf16[64,2688]{1,0:T(8,128)(2,1)S(1)}, bf16[64,2688]{1,0:T(8,128)(2,1)S(1)}, u32[]{:S(2)}, u32[]{:S(2)}) collective-permute-start(bf16[64,2688]{1,0:T(8,128)(2,1)S(1)} %slice.103), channel_id=1, source_target_pairs={{0,48},{1,49},{2,50},{3,51},{4,52},{5,53},{6,54},{7,55},{8,56},{9,... | collective-permute-start | bytes 1032200 | tf_op jit(solution)/shard_map/ppermute | solution.py:80
  93.3 7.3 %collective-permute-done.21 = bf16[64,2688]{1,0:T(8,128)(2,1)S(1)} collective-permute-done((bf16[64,2688]{1,0:T(8,128)(2,1)S(1)}, bf16[64,2688]{1,0:T(8,128)(2,1)S(1)}, u32[]{:S(2)}, u32[]{:S(2)}) %collective-permute-start.21) | collective-permute-done | bytes 344096 | tf_op jit(solution)/shard_map/ppermute | solution.py:80
  100.6 2.9 %collective-permute-start.26 = (bf16[64,2816]{1,0:T(8,128)(2,1)S(1)}, bf16[64,2816]{1,0:T(8,128)(2,1)S(1)}, u32[]{:S(2)}, u32[]{:S(2)}) collective-permute-start(bf16[64,2816]{1,0:T(8,128)(2,1)S(1)} %get-tuple-element.11), channel_id=1, source_target_pairs={{0,66},{1,67},{2,64},{3,65},{4,70},{5,71},{6,68},{7,69},{8,74},{9,... | collective-permute-start | bytes 1081352 | tf_op jit(solution)/shard_map/ppermute | solution.py:80
  103.8 3.9 %collective-permute-start.32 = (bf16[64,2816]{1,0:T(8,128)(2,1)S(1)}, bf16[64,2816]{1,0:T(8,128)(2,1)S(1)}, u32[]{:S(2)}, u32[]{:S(2)}) collective-permute-start(bf16[64,2816]{1,0:T(8,128)(2,1)S(1)} %get-tuple-element.11), channel_id=1, source_target_pairs={{0,12},{1,13},{2,14},{3,15},{4,8},{5,9},{6,10},{7,11},{8,4},{9,5},... | collective-permute-start | bytes 1081352 | tf_op jit(solution)/shard_map/ppermute | solution.py:80
  107.9 8.6 %collective-permute-done.24 = bf16[64,2688]{1,0:T(8,128)(2,1)S(1)} collective-permute-done((bf16[64,2688]{1,0:T(8,128)(2,1)S(1)}, bf16[64,2688]{1,0:T(8,128)(2,1)S(1)}, u32[]{:S(2)}, u32[]{:S(2)}) %collective-permute-start.24) | collective-permute-done | bytes 344096 | tf_op jit(solution)/shard_map/ppermute | solution.py:80
  116.5 3.0 %collective-permute-start.27 = (bf16[64,2688]{1,0:T(8,128)(2,1)S(1)}, bf16[64,2688]{1,0:T(8,128)(2,1)S(1)}, u32[]{:S(2)}, u32[]{:S(2)}) collective-permute-start(bf16[64,2688]{1,0:T(8,128)(2,1)S(1)} %collective-permute-done.21), channel_id=1, source_target_pairs={{0,66},{1,67},{2,64},{3,65},{4,70},{5,71},{6,68},{7,69},{8,74},{9,... | collective-permute-start | bytes 1032200 | tf_op jit(solution)/shard_map/ppermute | solution.py:80
  119.8 3.3 %collective-permute-start.28 = (bf16[64,2816]{1,0:T(8,128)(2,1)S(1)}, bf16[64,2816]{1,0:T(8,128)(2,1)S(1)}, u32[]{:S(2)}, u32[]{:S(2)}) collective-permute-start(bf16[64,2816]{1,0:T(8,128)(2,1)S(1)} %collective-permute-done.25), channel_id=1, source_target_pairs={{0,48},{1,49},{2,50},{3,51},{4,52},{5,53},{6,54},{7,55},{8,56},{9,... | collective-permute-start | bytes 1081352 | tf_op jit(solution)/shard_map/ppermute | solution.py:80
  125.8 4.1 %collective-permute-start.31 = (bf16[64,2816]{1,0:T(8,128)(2,1)S(1)}, bf16[64,2816]{1,0:T(8,128)(2,1)S(1)}, u32[]{:S(2)}, u32[]{:S(2)}) collective-permute-start(bf16[64,2816]{1,0:T(8,128)(2,1)S(1)} %get-tuple-element.10), channel_id=1, source_target_pairs={{0,12},{1,13},{2,14},{3,15},{4,8},{5,9},{6,10},{7,11},{8,4},{9,5},... | collective-permute-start | bytes 1081352 | tf_op jit(solution)/shard_map/ppermute | solution.py:80
  133.9 12.7 %collective-permute-done.30 = bf16[64,2688]{1,0:T(8,128)(2,1)S(1)} collective-permute-done((bf16[64,2688]{1,0:T(8,128)(2,1)S(1)}, bf16[64,2688]{1,0:T(8,128)(2,1)S(1)}, u32[]{:S(2)}, u32[]{:S(2)}) %collective-permute-start.30) | collective-permute-done | bytes 344096 | tf_op jit(solution)/shard_map/ppermute | solution.py:80
  146.6 3.2 %collective-permute-start.36 = (bf16[64,2688]{1,0:T(8,128)(2,1)S(1)}, bf16[64,2688]{1,0:T(8,128)(2,1)S(1)}, u32[]{:S(2)}, u32[]{:S(2)}) collective-permute-start(bf16[64,2688]{1,0:T(8,128)(2,1)S(1)} %collective-permute-done.24), channel_id=1, source_target_pairs={{0,12},{1,13},{2,14},{3,15},{4,8},{5,9},{6,10},{7,11},{8,4},{9,5},... | collective-permute-start | bytes 1032200 | tf_op jit(solution)/shard_map/ppermute | solution.py:80
  154.0 3.2 %collective-permute-start.37 = (bf16[64,2816]{1,0:T(8,128)(2,1)S(1)}, bf16[64,2816]{1,0:T(8,128)(2,1)S(1)}, u32[]{:S(2)}, u32[]{:S(2)}) collective-permute-start(bf16[64,2816]{1,0:T(8,128)(2,1)S(1)} %collective-permute-done.25), channel_id=1, source_target_pairs={{0,12},{1,13},{2,14},{3,15},{4,8},{5,9},{6,10},{7,11},{8,4},{9,5},... | collective-permute-start | bytes 1081352 | tf_op jit(solution)/shard_map/ppermute | solution.py:80
  157.2 3.8 %collective-permute-done.35 = bf16[64,2816]{1,0:T(8,128)(2,1)S(1)} collective-permute-done((bf16[64,2816]{1,0:T(8,128)(2,1)S(1)}, bf16[64,2816]{1,0:T(8,128)(2,1)S(1)}, u32[]{:S(2)}, u32[]{:S(2)}) %collective-permute-start.35) | collective-permute-done | bytes 360480 | tf_op jit(solution)/shard_map/ppermute | solution.py:80
  161.0 2.8 %collective-permute-start.38 = (bf16[64,2816]{1,0:T(8,128)(2,1)S(1)}, bf16[64,2816]{1,0:T(8,128)(2,1)S(1)}, u32[]{:S(2)}, u32[]{:S(2)}) collective-permute-start(bf16[64,2816]{1,0:T(8,128)(2,1)S(1)} %collective-permute-done.32), channel_id=1, source_target_pairs={{0,66},{1,67},{2,64},{3,65},{4,70},{5,71},{6,68},{7,69},{8,74},{9,... | collective-permute-start | bytes 1081352 | tf_op jit(solution)/shard_map/ppermute | solution.py:80
  166.4 3.0 %collective-permute-start.41 = (bf16[64,2816]{1,0:T(8,128)(2,1)S(1)}, bf16[64,2816]{1,0:T(8,128)(2,1)S(1)}, u32[]{:S(2)}, u32[]{:S(2)}) collective-permute-start(bf16[64,2816]{1,0:T(8,128)(2,1)S(1)} %collective-permute-done.35), channel_id=1, source_target_pairs={{0,66},{1,67},{2,64},{3,65},{4,70},{5,71},{6,68},{7,69},{8,74},{9,... | collective-permute-start | bytes 1081352 | tf_op jit(solution)/shard_map/ppermute | solution.py:80
  169.4 2.7 %collective-permute-start.40 = (bf16[64,2816]{1,0:T(8,128)(2,1)S(1)}, bf16[64,2816]{1,0:T(8,128)(2,1)S(1)}, u32[]{:S(2)}, u32[]{:S(2)}) collective-permute-start(bf16[64,2816]{1,0:T(8,128)(2,1)S(1)} %collective-permute-done.37), channel_id=1, source_target_pairs={{0,48},{1,49},{2,50},{3,51},{4,52},{5,53},{6,54},{7,55},{8,56},{9,... | collective-permute-start | bytes 1081352 | tf_op jit(solution)/shard_map/ppermute | solution.py:80
  175.1 3.0 %collective-permute-done.40 = bf16[64,2816]{1,0:T(8,128)(2,1)S(1)} collective-permute-done((bf16[64,2816]{1,0:T(8,128)(2,1)S(1)}, bf16[64,2816]{1,0:T(8,128)(2,1)S(1)}, u32[]{:S(2)}, u32[]{:S(2)}) %collective-permute-start.40) | collective-permute-done | bytes 360480 | tf_op jit(solution)/shard_map/ppermute | solution.py:80
  178.4 3.1 %copy-done.2 = bf16[512,8320]{1,0:T(8,128)(2,1)} copy-done((bf16[512,8320]{1,0:T(8,128)(2,1)}, bf16[512,8320]{1,0:T(8,128)(2,1)S(1)}, u32[]{:S(2)}) %copy-start.2) | copy-done | bytes 8519704
  181.5 9.7 %fusion.22 = f32[512,512]{1,0:T(8,128)S(1)} fusion(bf16[512,8320]{1,0:T(8,128)(2,1)} %collective-permute-done.42, bf16[512,8320]{1,0:T(8,128)(2,1)} %copy-done.2), kind=kOutput, calls=%fused_computation.77 | convolution fusion | flops 4362076160 | bytes 18087936 | tf_op jit(solution)/shard_map/dot_general | solution.py:114
  192.8 8.1 %fusion.2 = bf16[512,512]{1,0:T(8,128)(2,1)S(1)} fusion(bf16[512,8320]{1,0:T(8,128)(2,1)S(1)} %maximum_dynamic-update-slice_fusion, bf16[512,8320]{1,0:T(8,128)(2,1)} %copy-done.2, f32[512]{0:T(512)S(1)} %convert_reduce_fusion.1), kind=kOutput, calls=%fused_computation.5 | convolution fusion | flops 4362600448 | bytes 17565696 | tf_op jit(solution)/shard_map/dot_general | solution.py:114
  203.7 2.8 %collective-permute-start.52 = (f32[64]{0:T(128)S(1)}, f32[64]{0:T(128)S(1)}, u32[]{:S(2)}, u32[]{:S(2)}) collective-permute-start(f32[64]{0:T(128)S(1)} %get-tuple-element.15), channel_id=1, source_target_pairs={{0,48},{1,49},{2,50},{3,51},{4,52},{5,53},{6,54},{7,55},{8,56},{9,... | collective-permute-start | bytes 776 | tf_op jit(solution)/shard_map/ppermute | solution.py:95
  207.0 2.7 %collective-permute-start.54 = (f32[64]{0:T(128)S(1)}, f32[64]{0:T(128)S(1)}, u32[]{:S(2)}, u32[]{:S(2)}) collective-permute-start(f32[64]{0:T(128)S(1)} %get-tuple-element.14), channel_id=1, source_target_pairs={{0,48},{1,49},{2,50},{3,51},{4,52},{5,53},{6,54},{7,55},{8,56},{9,... | collective-permute-start | bytes 776 | tf_op jit(solution)/shard_map/ppermute | solution.py:95
  213.2 3.9 %collective-permute-done.45 = f32[64,512]{1,0:T(8,128)S(1)} collective-permute-done((f32[64,512]{1,0:T(8,128)S(1)}, f32[64,512]{1,0:T(8,128)S(1)}, u32[]{:S(2)}, u32[]{:S(2)}) %collective-permute-start.45) | collective-permute-done | bytes 131104 | tf_op jit(solution)/shard_map/ppermute | solution.py:95
  218.9 3.3 %collective-permute-start.57 = (f32[64]{0:T(128)S(1)}, f32[64]{0:T(128)S(1)}, u32[]{:S(2)}, u32[]{:S(2)}) collective-permute-start(f32[64]{0:T(128)S(1)} %add_add_fusion), channel_id=1, source_target_pairs={{0,12},{1,13},{2,14},{3,15},{4,8},{5,9},{6,10},{7,11},{8,4},{9,5},... | collective-permute-start | bytes 776 | tf_op jit(solution)/shard_map/ppermute | solution.py:95
  (142 shorter events, 74.5 us)
Async XLA Ops:
  3.4 28.9 %collective-permute-start.1 = (bf16[64,2816]{1,0:T(8,128)(2,1)S(1)}, bf16[64,2816]{1,0:T(8,128)(2,1)S(1)}, u32[]{:S(2)}, u32[]{:S(2)}) collective-permute-start(bf16[64,2816]{1,0:T(8,128)(2,1)S(1)} %get-tuple-element.8), channel_id=1, source_target_pairs={{0,16},{1,17},{2,18},{3,19},{4,20},{5,21},{6,22},{7,23},{8,24},{9,... | collective-permute-start | bytes 1081352 | tf_op jit(solution)/shard_map/ppermute | solution.py:80
  5.1 34.3 %collective-permute-start.4 = (bf16[64,2816]{1,0:T(8,128)(2,1)S(1)}, bf16[64,2816]{1,0:T(8,128)(2,1)S(1)}, u32[]{:S(2)}, u32[]{:S(2)}) collective-permute-start(bf16[64,2816]{1,0:T(8,128)(2,1)S(1)} %get-tuple-element.8), channel_id=1, source_target_pairs={{0,64},{1,65},{2,66},{3,67},{4,68},{5,69},{6,70},{7,71},{8,72},{9,... | collective-permute-start | bytes 1081352 | tf_op jit(solution)/shard_map/ppermute | solution.py:80
  6.6 23.8 %collective-permute-start.2 = (bf16[64,2816]{1,0:T(8,128)(2,1)S(1)}, bf16[64,2816]{1,0:T(8,128)(2,1)S(1)}, u32[]{:S(2)}, u32[]{:S(2)}) collective-permute-start(bf16[64,2816]{1,0:T(8,128)(2,1)S(1)} %get-tuple-element.9), channel_id=1, source_target_pairs={{0,16},{1,17},{2,18},{3,19},{4,20},{5,21},{6,22},{7,23},{8,24},{9,... | collective-permute-start | bytes 1081352 | tf_op jit(solution)/shard_map/ppermute | solution.py:80
  7.2 32.4 %collective-permute-start.5 = (bf16[64,2816]{1,0:T(8,128)(2,1)S(1)}, bf16[64,2816]{1,0:T(8,128)(2,1)S(1)}, u32[]{:S(2)}, u32[]{:S(2)}) collective-permute-start(bf16[64,2816]{1,0:T(8,128)(2,1)S(1)} %get-tuple-element.9), channel_id=1, source_target_pairs={{0,64},{1,65},{2,66},{3,67},{4,68},{5,69},{6,70},{7,71},{8,72},{9,... | collective-permute-start | bytes 1081352 | tf_op jit(solution)/shard_map/ppermute | solution.py:80
  7.6 21.0 %collective-permute-start = (bf16[64,2688]{1,0:T(8,128)(2,1)S(1)}, bf16[64,2688]{1,0:T(8,128)(2,1)S(1)}, u32[]{:S(2)}, u32[]{:S(2)}) collective-permute-start(bf16[64,2688]{1,0:T(8,128)(2,1)S(1)} %slice.98), channel_id=1, source_target_pairs={{0,16},{1,17},{2,18},{3,19},{4,20},{5,21},{6,22},{7,23},{8,24},{9,... | collective-permute-start | bytes 1032200 | tf_op jit(solution)/shard_map/ppermute | solution.py:80
  30.4 28.2 %collective-permute-start.11 = (bf16[64,2816]{1,0:T(8,128)(2,1)S(1)}, bf16[64,2816]{1,0:T(8,128)(2,1)S(1)}, u32[]{:S(2)}, u32[]{:S(2)}) collective-permute-start(bf16[64,2816]{1,0:T(8,128)(2,1)S(1)} %get-tuple-element.9), channel_id=1, source_target_pairs={{0,4},{1,5},{2,6},{3,7},{4,0},{5,1},{6,2},{7,3},{8,12},{9,13},{10,... | collective-permute-start | bytes 1081352 | tf_op jit(solution)/shard_map/ppermute | solution.py:80
  32.3 27.8 %collective-permute-start.10 = (bf16[64,2816]{1,0:T(8,128)(2,1)S(1)}, bf16[64,2816]{1,0:T(8,128)(2,1)S(1)}, u32[]{:S(2)}, u32[]{:S(2)}) collective-permute-start(bf16[64,2816]{1,0:T(8,128)(2,1)S(1)} %get-tuple-element.8), channel_id=1, source_target_pairs={{0,4},{1,5},{2,6},{3,7},{4,0},{5,1},{6,2},{7,3},{8,12},{9,13},{10,... | collective-permute-start | bytes 1081352 | tf_op jit(solution)/shard_map/ppermute | solution.py:80
  39.3 14.1 %collective-permute-start.8 = (bf16[64,2816]{1,0:T(8,128)(2,1)S(1)}, bf16[64,2816]{1,0:T(8,128)(2,1)S(1)}, u32[]{:S(2)}, u32[]{:S(2)}) collective-permute-start(bf16[64,2816]{1,0:T(8,128)(2,1)S(1)} %collective-permute-done.2), channel_id=1, source_target_pairs={{0,64},{1,65},{2,66},{3,67},{4,68},{5,69},{6,70},{7,71},{8,72},{9,... | collective-permute-start | bytes 1081352 | tf_op jit(solution)/shard_map/ppermute | solution.py:80
  39.6 11.1 %collective-permute-start.7 = (bf16[64,2816]{1,0:T(8,128)(2,1)S(1)}, bf16[64,2816]{1,0:T(8,128)(2,1)S(1)}, u32[]{:S(2)}, u32[]{:S(2)}) collective-permute-start(bf16[64,2816]{1,0:T(8,128)(2,1)S(1)} %collective-permute-done.4), channel_id=1, source_target_pairs={{0,16},{1,17},{2,18},{3,19},{4,20},{5,21},{6,22},{7,23},{8,24},{9,... | collective-permute-start | bytes 1081352 | tf_op jit(solution)/shard_map/ppermute | solution.py:80
  50.7 53.2 %collective-permute-start.22 = (bf16[64,2816]{1,0:T(8,128)(2,1)S(1)}, bf16[64,2816]{1,0:T(8,128)(2,1)S(1)}, u32[]{:S(2)}, u32[]{:S(2)}) collective-permute-start(bf16[64,2816]{1,0:T(8,128)(2,1)S(1)} %get-tuple-element.10), channel_id=1, source_target_pairs={{0,48},{1,49},{2,50},{3,51},{4,52},{5,53},{6,54},{7,55},{8,56},{9,... | collective-permute-start | bytes 1081352 | tf_op jit(solution)/shard_map/ppermute | solution.py:80
  53.4 66.0 %collective-permute-start.25 = (bf16[64,2816]{1,0:T(8,128)(2,1)S(1)}, bf16[64,2816]{1,0:T(8,128)(2,1)S(1)}, u32[]{:S(2)}, u32[]{:S(2)}) collective-permute-start(bf16[64,2816]{1,0:T(8,128)(2,1)S(1)} %get-tuple-element.10), channel_id=1, source_target_pairs={{0,66},{1,67},{2,64},{3,65},{4,70},{5,71},{6,68},{7,69},{8,74},{9,... | collective-permute-start | bytes 1081352 | tf_op jit(solution)/shard_map/ppermute | solution.py:80
  60.1 13.1 %collective-permute-start.13 = (bf16[64,2816]{1,0:T(8,128)(2,1)S(1)}, bf16[64,2816]{1,0:T(8,128)(2,1)S(1)}, u32[]{:S(2)}, u32[]{:S(2)}) collective-permute-start(bf16[64,2816]{1,0:T(8,128)(2,1)S(1)} %collective-permute-done.10), channel_id=1, source_target_pairs={{0,16},{1,17},{2,18},{3,19},{4,20},{5,21},{6,22},{7,23},{8,24},{9,... | collective-permute-start | bytes 1081352 | tf_op jit(solution)/shard_map/ppermute | solution.py:80
  65.2 11.1 %collective-permute-start.15 = (bf16[64,2688]{1,0:T(8,128)(2,1)S(1)}, bf16[64,2688]{1,0:T(8,128)(2,1)S(1)}, u32[]{:S(2)}, u32[]{:S(2)}) collective-permute-start(bf16[64,2688]{1,0:T(8,128)(2,1)S(1)} %collective-permute-done.3), channel_id=1, source_target_pairs={{0,4},{1,5},{2,6},{3,7},{4,0},{5,1},{6,2},{7,3},{8,12},{9,13},{10,... | collective-permute-start | bytes 1032200 | tf_op jit(solution)/shard_map/ppermute | solution.py:80
  69.4 13.4 %collective-permute-start.16 = (bf16[64,2816]{1,0:T(8,128)(2,1)S(1)}, bf16[64,2816]{1,0:T(8,128)(2,1)S(1)}, u32[]{:S(2)}, u32[]{:S(2)}) collective-permute-start(bf16[64,2816]{1,0:T(8,128)(2,1)S(1)} %collective-permute-done.4), channel_id=1, source_target_pairs={{0,4},{1,5},{2,6},{3,7},{4,0},{5,1},{6,2},{7,3},{8,12},{9,13},{10,... | collective-permute-start | bytes 1081352 | tf_op jit(solution)/shard_map/ppermute | solution.py:80
  73.2 11.5 %collective-permute-start.17 = (bf16[64,2816]{1,0:T(8,128)(2,1)S(1)}, bf16[64,2816]{1,0:T(8,128)(2,1)S(1)}, u32[]{:S(2)}, u32[]{:S(2)}) collective-permute-start(bf16[64,2816]{1,0:T(8,128)(2,1)S(1)} %collective-permute-done.11), channel_id=1, source_target_pairs={{0,64},{1,65},{2,66},{3,67},{4,68},{5,69},{6,70},{7,71},{8,72},{9,... | collective-permute-start | bytes 1081352 | tf_op jit(solution)/shard_map/ppermute | solution.py:80
  86.4 17.1 %collective-permute-start.23 = (bf16[64,2816]{1,0:T(8,128)(2,1)S(1)}, bf16[64,2816]{1,0:T(8,128)(2,1)S(1)}, u32[]{:S(2)}, u32[]{:S(2)}) collective-permute-start(bf16[64,2816]{1,0:T(8,128)(2,1)S(1)} %get-tuple-element.11), channel_id=1, source_target_pairs={{0,48},{1,49},{2,50},{3,51},{4,52},{5,53},{6,54},{7,55},{8,56},{9,... | collective-permute-start | bytes 1081352 | tf_op jit(solution)/shard_map/ppermute | solution.py:80
  93.1 88.4 %collective-permute-start.42 = (bf16[512,8320]{1,0:T(8,128)(2,1)S(1)}, bf16[512,8320]{1,0:T(8,128)(2,1)}, u32[]{:S(2)}, u32[]{:S(2)}) collective-permute-start(bf16[512,8320]{1,0:T(8,128)(2,1)S(1)} %maximum_dynamic-update-slice_fusion), channel_id=1, source_target_pairs={{0,1},{1,0},{2,3},{3,2},{4,5},{5,4},{6,7},{7,6},{8,9},{9,8},{10,11... | collective-permute-start | bytes 25559048 | tf_op jit(solution)/shard_map/ppermute | solution.py:110
  100.6 19.2 %collective-permute-start.26 = (bf16[64,2816]{1,0:T(8,128)(2,1)S(1)}, bf16[64,2816]{1,0:T(8,128)(2,1)S(1)}, u32[]{:S(2)}, u32[]{:S(2)}) collective-permute-start(bf16[64,2816]{1,0:T(8,128)(2,1)S(1)} %get-tuple-element.11), channel_id=1, source_target_pairs={{0,66},{1,67},{2,64},{3,65},{4,70},{5,71},{6,68},{7,69},{8,74},{9,... | collective-permute-start | bytes 1081352 | tf_op jit(solution)/shard_map/ppermute | solution.py:80
  103.5 13.0 %collective-permute-start.24 = (bf16[64,2688]{1,0:T(8,128)(2,1)S(1)}, bf16[64,2688]{1,0:T(8,128)(2,1)S(1)}, u32[]{:S(2)}, u32[]{:S(2)}) collective-permute-start(bf16[64,2688]{1,0:T(8,128)(2,1)S(1)} %slice.103), channel_id=1, source_target_pairs={{0,66},{1,67},{2,64},{3,65},{4,70},{5,71},{6,68},{7,69},{8,74},{9,... | collective-permute-start | bytes 1032200 | tf_op jit(solution)/shard_map/ppermute | solution.py:80
  103.8 46.0 %collective-permute-start.32 = (bf16[64,2816]{1,0:T(8,128)(2,1)S(1)}, bf16[64,2816]{1,0:T(8,128)(2,1)S(1)}, u32[]{:S(2)}, u32[]{:S(2)}) collective-permute-start(bf16[64,2816]{1,0:T(8,128)(2,1)S(1)} %get-tuple-element.11), channel_id=1, source_target_pairs={{0,12},{1,13},{2,14},{3,15},{4,8},{5,9},{6,10},{7,11},{8,4},{9,5},... | collective-permute-start | bytes 1081352 | tf_op jit(solution)/shard_map/ppermute | solution.py:80
  119.5 13.2 %collective-permute-start.29 = (bf16[64,2816]{1,0:T(8,128)(2,1)S(1)}, bf16[64,2816]{1,0:T(8,128)(2,1)S(1)}, u32[]{:S(2)}, u32[]{:S(2)}) collective-permute-start(bf16[64,2816]{1,0:T(8,128)(2,1)S(1)} %collective-permute-done.23), channel_id=1, source_target_pairs={{0,66},{1,67},{2,64},{3,65},{4,70},{5,71},{6,68},{7,69},{8,74},{9,... | collective-permute-start | bytes 1081352 | tf_op jit(solution)/shard_map/ppermute | solution.py:80
  125.8 26.6 %collective-permute-start.31 = (bf16[64,2816]{1,0:T(8,128)(2,1)S(1)}, bf16[64,2816]{1,0:T(8,128)(2,1)S(1)}, u32[]{:S(2)}, u32[]{:S(2)}) collective-permute-start(bf16[64,2816]{1,0:T(8,128)(2,1)S(1)} %get-tuple-element.10), channel_id=1, source_target_pairs={{0,12},{1,13},{2,14},{3,15},{4,8},{5,9},{6,10},{7,11},{8,4},{9,5},... | collective-permute-start | bytes 1081352 | tf_op jit(solution)/shard_map/ppermute | solution.py:80
  129.9 16.7 %collective-permute-start.30 = (bf16[64,2688]{1,0:T(8,128)(2,1)S(1)}, bf16[64,2688]{1,0:T(8,128)(2,1)S(1)}, u32[]{:S(2)}, u32[]{:S(2)}) collective-permute-start(bf16[64,2688]{1,0:T(8,128)(2,1)S(1)} %slice.103), channel_id=1, source_target_pairs={{0,12},{1,13},{2,14},{3,15},{4,8},{5,9},{6,10},{7,11},{8,4},{9,5},... | collective-permute-start | bytes 1032200 | tf_op jit(solution)/shard_map/ppermute | solution.py:80
  132.7 21.3 %collective-permute-start.33 = (bf16[64,2688]{1,0:T(8,128)(2,1)S(1)}, bf16[64,2688]{1,0:T(8,128)(2,1)S(1)}, u32[]{:S(2)}, u32[]{:S(2)}) collective-permute-start(bf16[64,2688]{1,0:T(8,128)(2,1)S(1)} %collective-permute-done.21), channel_id=1, source_target_pairs={{0,12},{1,13},{2,14},{3,15},{4,8},{5,9},{6,10},{7,11},{8,4},{9,5},... | collective-permute-start | bytes 1032200 | tf_op jit(solution)/shard_map/ppermute | solution.py:80
  146.6 19.7 %collective-permute-start.36 = (bf16[64,2688]{1,0:T(8,128)(2,1)S(1)}, bf16[64,2688]{1,0:T(8,128)(2,1)S(1)}, u32[]{:S(2)}, u32[]{:S(2)}) collective-permute-start(bf16[64,2688]{1,0:T(8,128)(2,1)S(1)} %collective-permute-done.24), channel_id=1, source_target_pairs={{0,12},{1,13},{2,14},{3,15},{4,8},{5,9},{6,10},{7,11},{8,4},{9,5},... | collective-permute-start | bytes 1032200 | tf_op jit(solution)/shard_map/ppermute | solution.py:80
  149.9 11.2 %collective-permute-start.35 = (bf16[64,2816]{1,0:T(8,128)(2,1)S(1)}, bf16[64,2816]{1,0:T(8,128)(2,1)S(1)}, u32[]{:S(2)}, u32[]{:S(2)}) collective-permute-start(bf16[64,2816]{1,0:T(8,128)(2,1)S(1)} %collective-permute-done.32), channel_id=1, source_target_pairs={{0,48},{1,49},{2,50},{3,51},{4,52},{5,53},{6,54},{7,55},{8,56},{9,... | collective-permute-start | bytes 1081352 | tf_op jit(solution)/shard_map/ppermute | solution.py:80
  152.3 13.9 %collective-permute-start.34 = (bf16[64,2816]{1,0:T(8,128)(2,1)S(1)}, bf16[64,2816]{1,0:T(8,128)(2,1)S(1)}, u32[]{:S(2)}, u32[]{:S(2)}) collective-permute-start(bf16[64,2816]{1,0:T(8,128)(2,1)S(1)} %collective-permute-done.31), channel_id=1, source_target_pairs={{0,48},{1,49},{2,50},{3,51},{4,52},{5,53},{6,54},{7,55},{8,56},{9,... | collective-permute-start | bytes 1081352 | tf_op jit(solution)/shard_map/ppermute | solution.py:80
  154.0 15.4 %collective-permute-start.37 = (bf16[64,2816]{1,0:T(8,128)(2,1)S(1)}, bf16[64,2816]{1,0:T(8,128)(2,1)S(1)}, u32[]{:S(2)}, u32[]{:S(2)}) collective-permute-start(bf16[64,2816]{1,0:T(8,128)(2,1)S(1)} %collective-permute-done.25), channel_id=1, source_target_pairs={{0,12},{1,13},{2,14},{3,15},{4,8},{5,9},{6,10},{7,11},{8,4},{9,5},... | collective-permute-start | bytes 1081352 | tf_op jit(solution)/shard_map/ppermute | solution.py:80
  161.0 11.1 %collective-permute-start.38 = (bf16[64,2816]{1,0:T(8,128)(2,1)S(1)}, bf16[64,2816]{1,0:T(8,128)(2,1)S(1)}, u32[]{:S(2)}, u32[]{:S(2)}) collective-permute-start(bf16[64,2816]{1,0:T(8,128)(2,1)S(1)} %collective-permute-done.32), channel_id=1, source_target_pairs={{0,66},{1,67},{2,64},{3,65},{4,70},{5,71},{6,68},{7,69},{8,74},{9,... | collective-permute-start | bytes 1081352 | tf_op jit(solution)/shard_map/ppermute | solution.py:80
  192.7 17.5 %collective-permute-start.43 = (f32[512,512]{1,0:T(8,128)S(1)}, f32[512,512]{1,0:T(8,128)S(1)}, u32[]{:S(2)}, u32[]{:S(2)}) collective-permute-start(f32[512,512]{1,0:T(8,128)S(1)} %fusion.5), channel_id=1, source_target_pairs={{0,1},{1,0},{2,3},{3,2},{4,5},{5,4},{6,7},{7,6},{8,9},{9,8},{10,11... | collective-permute-start | bytes 3145736 | tf_op jit(solution)/shard_map/ppermute | solution.py:128
  207.0 11.8 %collective-permute-start.54 = (f32[64]{0:T(128)S(1)}, f32[64]{0:T(128)S(1)}, u32[]{:S(2)}, u32[]{:S(2)}) collective-permute-start(f32[64]{0:T(128)S(1)} %get-tuple-element.14), channel_id=1, source_target_pairs={{0,48},{1,49},{2,50},{3,51},{4,52},{5,53},{6,54},{7,55},{8,56},{9,... | collective-permute-start | bytes 776 | tf_op jit(solution)/shard_map/ppermute | solution.py:95
  209.7 16.3 %collective-permute-start.51 = (f32[64]{0:T(128)S(1)}, f32[64]{0:T(128)S(1)}, u32[]{:S(2)}, u32[]{:S(2)}) collective-permute-start(f32[64]{0:T(128)S(1)} %get-tuple-element.12), channel_id=1, source_target_pairs={{0,48},{1,49},{2,50},{3,51},{4,52},{5,53},{6,54},{7,55},{8,56},{9,... | collective-permute-start | bytes 776 | tf_op jit(solution)/shard_map/ppermute | solution.py:95
  (32 other events, 253.3 us)

commit v5 on v4

--- a/solution.py
+++ b/solution.py
@@ -74,13 +74,14 @@
     parts = []
     for p in range(3):
         order = [(p + s) % 3 for s in range(3)]
-        buf = [shard[:, cut[p]:cut[p + 1]]]
+        buf = shard[:, cut[p]:cut[p + 1]]
         labs = [0]
         for a in order:
             got = lax.ppermute(buf, AXES, mate_pairs(n, a, mate))
-            buf = buf + list(got)
+            buf = jnp.concatenate([buf, got])
             labs = labs + [o ^ (1 << a) for o in labs]
-        parts.append({o: b for o, b in zip(labs, buf)})
+        rows = shard.shape[0]
+        parts.append({o: buf[i * rows:(i + 1) * rows] for i, o in enumerate(labs)})
     return jnp.concatenate(
         [jnp.concatenate([parts[p][o] for p in range(3)], axis=1) for o in range(8)]
     )
@@ -92,9 +93,12 @@
     for a in range(3):
         send = [o for o in live if o & (1 << a)]
         keep = [o for o in live if not o & (1 << a)]
-        got = lax.ppermute([blocks[o] for o in send], AXES, mate_pairs(n, a, mate))
-        for o, g in zip(send, got):
-            blocks[o ^ (1 << a)] = blocks[o ^ (1 << a)] + g
+        rows = blocks[0].shape[0]
+        got = lax.ppermute(
+            jnp.concatenate([blocks[o] for o in send]), AXES, mate_pairs(n, a, mate)
+        )
+        for i, o in enumerate(send):
+            blocks[o ^ (1 << a)] = blocks[o ^ (1 << a)] + got[i * rows:(i + 1) * rows]
         live = keep
     return blocks[0]
 

time: 232 us -> 166 us (0.72)
  starting transfers between devices: 94.4 us -> 38 us
  waiting for transfers between devices: 104 us -> 87.3 us
  other arithmetic: 8.96 us -> 18.7 us
    ppermute x42 -> x18, starting transfers between devices: 78.9 us -> 31.7 us  [cube_gather(): got = lax.ppermute(buf, AXES, mate_pairs(n, a, mate))]
    ppermute x42 -> x18, waiting for transfers between devices: 93.3 us -> 66.6 us  [cube_gather(): got = lax.ppermute(buf, AXES, mate_pairs(n, a, mate))]
    ppermute x14 -> x6, waiting for transfers between devices: 10.7 us -> 20.7 us  [cube_reduce(): lax.ppermute(jnp.concatenate([blocks[o] for o in send]), AXES, mate_pairs...]
    ppermute x14 -> x6, starting transfers between devices: 15.4 us -> 5.88 us  [cube_reduce(): lax.ppermute(jnp.concatenate([blocks[o] for o in send]), AXES, mate_pairs...]
    unnamed x14, other arithmetic: 1.7 us -> 8.3 us
    unnamed x8 -> x6, local copies, waits for them, and re-layouts: 3.1 us -> 0.02 us
  transfers between devices with their start and end apart: 58 -> 26, of which waited for: 26 -> 17; matrix products, arithmetic and copies ran while one was open for 6% -> 15% of each run, Pallas kernels for 0% -> 0%
where the time goes in v5:
time: 166 us
  waiting for transfers between devices  87.3 us (53%)
  starting transfers between devices  38 us (23%)
  matrix products  20.1 us (12%)
  other arithmetic  18.7 us (11%)
    ppermute x18, waiting for transfers between devices, cube_gather(): got = lax.ppermute(buf, AXES, mate_pairs(n, a, mate))  66.6 us
    ppermute x18, starting transfers between devices, cube_gather(): got = lax.ppermute(buf, AXES, mate_pairs(n, a, mate))  31.7 us
    ppermute x6, waiting for transfers between devices, cube_reduce(): lax.ppermute(jnp.concatenate([blocks[o] for o in send]), AXES, mate_pairs...  20.7 us
    dot_general x2, matrix products, weigh(): lax.dot_general(t, te_all, (((1,), (1,)), ((), ())), preferred_element_ty...  17.8 us
    unnamed x14, other arithmetic  8.3 us
    ppermute x6, starting transfers between devices, cube_reduce(): lax.ppermute(jnp.concatenate([blocks[o] for o in send]), AXES, mate_pairs...  5.88 us
  transfers between devices with their start and end apart: 26, of which 17 were waited for; matrix products, arithmetic and copies ran while one was open for 15% of the time, Pallas kernels for 0%

profile of v5, /device:TPU:0, one launch (start us, length us, event | category | flops | bytes accessed | tf_op | source)
XLA Modules:
  0.0 166.1 jit_solution(3883628012543592640)
XLA Ops:
  2.2 1.1 fusion.23
  3.4 1.7 %collective-permute-start.1 = (bf16[64,2816]{1,0:T(8,128)(2,1)S(1)}, bf16[64,2816]{1,0:T(8,128)(2,1)S(1)}, u32[]{:S(2)}, u32[]{:S(2)}) collective-permute-start(bf16[64,2816]{1,0:T(8,128)(2,1)S(1)} %get-tuple-element.32), channel_id=1, source_target_pairs={{0,64},{1,65},{2,66},{3,67},{4,68},{5,69},{6,70},{7,71},{8,72},{9,... | collective-permute-start | bytes 1081352 | tf_op jit(solution)/shard_map/ppermute | solution.py:80
  5.1 1.9 %collective-permute-start.4 = (bf16[64,2816]{1,0:T(8,128)(2,1)S(1)}, bf16[64,2816]{1,0:T(8,128)(2,1)S(1)}, u32[]{:S(2)}, u32[]{:S(2)}) collective-permute-start(bf16[64,2816]{1,0:T(8,128)(2,1)S(1)} %get-tuple-element.33), channel_id=1, source_target_pairs={{0,4},{1,5},{2,6},{3,7},{4,0},{5,1},{6,2},{7,3},{8,12},{9,13},{10,... | collective-permute-start | bytes 1081352 | tf_op jit(solution)/shard_map/ppermute | solution.py:80
  7.1 1.6 collective-permute-start
  8.8 2.3 %collective-permute-start.10 = (bf16[64,2816]{1,0:T(8,128)(2,1)S(1)}, bf16[64,2816]{1,0:T(8,128)(2,1)S(1)}, u32[]{:S(2)}, u32[]{:S(2)}) collective-permute-start(bf16[64,2816]{1,0:T(8,128)(2,1)S(1)} %get-tuple-element.34), channel_id=1, source_target_pairs={{0,66},{1,67},{2,64},{3,65},{4,70},{5,71},{6,68},{7,69},{8,74},{9,... | collective-permute-start | bytes 1081352 | tf_op jit(solution)/shard_map/ppermute | solution.py:80
  11.1 2.5 %collective-permute-start.13 = (bf16[64,2816]{1,0:T(8,128)(2,1)S(1)}, bf16[64,2816]{1,0:T(8,128)(2,1)S(1)}, u32[]{:S(2)}, u32[]{:S(2)}) collective-permute-start(bf16[64,2816]{1,0:T(8,128)(2,1)S(1)} %get-tuple-element.35), channel_id=1, source_target_pairs={{0,12},{1,13},{2,14},{3,15},{4,8},{5,9},{6,10},{7,11},{8,4},{9,5},... | collective-permute-start | bytes 1081352 | tf_op jit(solution)/shard_map/ppermute | solution.py:80
  14.8 1.6 collective-permute-done
  16.4 2.8 %collective-permute-start.9 = (bf16[64,2688]{1,0:T(8,128)(2,1)S(1)}, bf16[64,2688]{1,0:T(8,128)(2,1)S(1)}, u32[]{:S(2)}, u32[]{:S(2)}) collective-permute-start(bf16[64,2688]{1,0:T(8,128)(2,1)S(1)} %slice.265), channel_id=1, source_target_pairs={{0,48},{1,49},{2,50},{3,51},{4,52},{5,53},{6,54},{7,55},{8,56},{9,... | collective-permute-start | bytes 1032200 | tf_op jit(solution)/shard_map/ppermute | solution.py:80
  19.2 6.7 %collective-permute-done.9 = bf16[64,2688]{1,0:T(8,128)(2,1)S(1)} collective-permute-done((bf16[64,2688]{1,0:T(8,128)(2,1)S(1)}, bf16[64,2688]{1,0:T(8,128)(2,1)S(1)}, u32[]{:S(2)}, u32[]{:S(2)}) %collective-permute-start.9) | collective-permute-done | bytes 344096 | tf_op jit(solution)/shard_map/ppermute | solution.py:80
  26.4 3.1 %collective-permute-start.15 = (bf16[128,2688]{1,0:T(8,128)(2,1)S(1)}, bf16[128,2688]{1,0:T(8,128)(2,1)S(1)}, u32[]{:S(2)}, u32[]{:S(2)}) collective-permute-start(bf16[128,2688]{1,0:T(8,128)(2,1)S(1)} %pad_maximum_fusion.11), channel_id=1, source_target_pairs={{0,66},{1,67},{2,64},{3,65},{4,70},{5,71},{6,68},{7,69},{8,74},{9,... | collective-permute-start | bytes 2064392 | tf_op jit(solution)/shard_map/ppermute | solution.py:80
  30.6 3.8 %collective-permute-start.11 = (bf16[128,2816]{1,0:T(8,128)(2,1)S(1)}, bf16[128,2816]{1,0:T(8,128)(2,1)S(1)}, u32[]{:S(2)}, u32[]{:S(2)}) collective-permute-start(bf16[128,2816]{1,0:T(8,128)(2,1)S(1)} %pad_maximum_fusion.8), channel_id=1, source_target_pairs={{0,12},{1,13},{2,14},{3,15},{4,8},{5,9},{6,10},{7,11},{8,4},{9,5},... | collective-permute-start | bytes 2162696 | tf_op jit(solution)/shard_map/ppermute | solution.py:80
  34.4 6.3 %collective-permute-done.6 = bf16[128,2688]{1,0:T(8,128)(2,1)S(1)} collective-permute-done((bf16[128,2688]{1,0:T(8,128)(2,1)S(1)}, bf16[128,2688]{1,0:T(8,128)(2,1)S(1)}, u32[]{:S(2)}, u32[]{:S(2)}) %collective-permute-start.6) | collective-permute-done | bytes 688160 | tf_op jit(solution)/shard_map/ppermute | solution.py:80
  40.7 2.8 %collective-permute-start.14 = (bf16[128,2816]{1,0:T(8,128)(2,1)S(1)}, bf16[128,2816]{1,0:T(8,128)(2,1)S(1)}, u32[]{:S(2)}, u32[]{:S(2)}) collective-permute-start(bf16[128,2816]{1,0:T(8,128)(2,1)S(1)} %pad_maximum_fusion.9), channel_id=1, source_target_pairs={{0,48},{1,49},{2,50},{3,51},{4,52},{5,53},{6,54},{7,55},{8,56},{9,... | collective-permute-start | bytes 2162696 | tf_op jit(solution)/shard_map/ppermute | solution.py:80
  44.5 2.1 %collective-permute-done.2 = bf16[128,2816]{1,0:T(8,128)(2,1)S(1)} collective-permute-done((bf16[128,2816]{1,0:T(8,128)(2,1)S(1)}, bf16[128,2816]{1,0:T(8,128)(2,1)S(1)}, u32[]{:S(2)}, u32[]{:S(2)}) %collective-permute-start.2) | collective-permute-done | bytes 720928 | tf_op jit(solution)/shard_map/ppermute | solution.py:80
  46.6 2.5 %collective-permute-start.17 = (bf16[256,2688]{1,0:T(8,128)(2,1)S(1)}, bf16[256,2688]{1,0:T(8,128)(2,1)S(1)}, u32[]{:S(2)}, u32[]{:S(2)}) collective-permute-start(bf16[256,2688]{1,0:T(8,128)(2,1)S(1)} %pad_maximum_fusion.5), channel_id=1, source_target_pairs={{0,12},{1,13},{2,14},{3,15},{4,8},{5,9},{6,10},{7,11},{8,4},{9,5},... | collective-permute-start | bytes 4128776 | tf_op jit(solution)/shard_map/ppermute | solution.py:80
  49.2 1.6 collective-permute-start.3
  51.3 5.7 %collective-permute-done.14 = bf16[128,2816]{1,0:T(8,128)(2,1)S(1)} collective-permute-done((bf16[128,2816]{1,0:T(8,128)(2,1)S(1)}, bf16[128,2816]{1,0:T(8,128)(2,1)S(1)}, u32[]{:S(2)}, u32[]{:S(2)}) %collective-permute-start.14) | collective-permute-done | bytes 720928 | tf_op jit(solution)/shard_map/ppermute | solution.py:80
  57.0 2.8 %collective-permute-start.12 = (bf16[256,2816]{1,0:T(8,128)(2,1)S(1)}, bf16[256,2816]{1,0:T(8,128)(2,1)S(1)}, u32[]{:S(2)}, u32[]{:S(2)}) collective-permute-start(bf16[256,2816]{1,0:T(8,128)(2,1)S(1)} %pad_maximum_fusion.2), channel_id=1, source_target_pairs={{0,48},{1,49},{2,50},{3,51},{4,52},{5,53},{6,54},{7,55},{8,56},{9,... | collective-permute-start | bytes 4325384 | tf_op jit(solution)/shard_map/ppermute | solution.py:80
  60.0 14.1 %collective-permute-done.8 = bf16[256,2688]{1,0:T(8,128)(2,1)S(1)} collective-permute-done((bf16[256,2688]{1,0:T(8,128)(2,1)S(1)}, bf16[256,2688]{1,0:T(8,128)(2,1)S(1)}, u32[]{:S(2)}, u32[]{:S(2)}) %collective-permute-start.8) | collective-permute-done | bytes 1376288 | tf_op jit(solution)/shard_map/ppermute | solution.py:80
  74.5 2.0 %collective-permute-done.17 = bf16[256,2688]{1,0:T(8,128)(2,1)S(1)} collective-permute-done((bf16[256,2688]{1,0:T(8,128)(2,1)S(1)}, bf16[256,2688]{1,0:T(8,128)(2,1)S(1)}, u32[]{:S(2)}, u32[]{:S(2)}) %collective-permute-start.17) | collective-permute-done | bytes 1376288 | tf_op jit(solution)/shard_map/ppermute | solution.py:80
  78.9 8.5 %collective-permute-done.12 = bf16[256,2816]{1,0:T(8,128)(2,1)S(1)} collective-permute-done((bf16[256,2816]{1,0:T(8,128)(2,1)S(1)}, bf16[256,2816]{1,0:T(8,128)(2,1)S(1)}, u32[]{:S(2)}, u32[]{:S(2)}) %collective-permute-start.12) | collective-permute-done | bytes 1441824 | tf_op jit(solution)/shard_map/ppermute | solution.py:80
  87.6 18.6 %collective-permute-done.16 = bf16[256,2816]{1,0:T(8,128)(2,1)S(1)} collective-permute-done((bf16[256,2816]{1,0:T(8,128)(2,1)S(1)}, bf16[256,2816]{1,0:T(8,128)(2,1)S(1)}, u32[]{:S(2)}, u32[]{:S(2)}) %collective-permute-start.16) | collective-permute-done | bytes 1441824 | tf_op jit(solution)/shard_map/ppermute | solution.py:80
  113.7 1.2 add_reduce_fusion.2
  114.9 9.7 %fusion.32 = f32[512,512]{1,0:T(8,128)S(1)} fusion(bf16[512,8320]{1,0:T(8,128)(2,1)} %collective-permute-done.18, bf16[512,8320]{1,0:T(8,128)(2,1)} %maximum_dynamic-update-slice_fusion.8), kind=kOutput, calls=%fused_computation.105 | convolution fusion | flops 4362076160 | bytes 18087936 | tf_op jit(solution)/shard_map/dot_general | solution.py:118
  126.4 8.1 %fusion.2 = bf16[512,512]{1,0:T(8,128)(2,1)S(1)} fusion(bf16[512,8320]{1,0:T(8,128)(2,1)S(1)} %maximum_dynamic-update-slice_fusion, bf16[512,8320]{1,0:T(8,128)(2,1)} %maximum_dynamic-update-slice_fusion.8, f32[512]{0:T(512)S(1)} %convert_reduce_fusion.1), kind=kOutput, calls=%fused_computation.11 | convolution fusion | flops 4362600448 | bytes 17565696 | tf_op jit(solution)/shard_map/dot_general | solution.py:118
  135.4 1.2 add_reduce_fusion
  138.1 2.2 %collective-permute-start.23 = (f32[256]{0:T(256)S(1)}, f32[256]{0:T(256)S(1)}, u32[]{:S(2)}, u32[]{:S(2)}) collective-permute-start(f32[256]{0:T(256)S(1)} %pad_maximum_fusion.16), channel_id=1, source_target_pairs={{0,48},{1,49},{2,50},{3,51},{4,52},{5,53},{6,54},{7,55},{8,56},{9,... | collective-permute-start | bytes 3080 | tf_op jit(solution)/shard_map/ppermute | solution.py:97
  140.3 2.6 %collective-permute-done.23 = f32[256]{0:T(256)S(1)} collective-permute-done((f32[256]{0:T(256)S(1)}, f32[256]{0:T(256)S(1)}, u32[]{:S(2)}, u32[]{:S(2)}) %collective-permute-start.23) | collective-permute-done | bytes 1056 | tf_op jit(solution)/shard_map/ppermute | solution.py:97
  143.0 9.3 %collective-permute-done.20 = f32[256,512]{1,0:T(8,128)S(1)} collective-permute-done((f32[256,512]{1,0:T(8,128)S(1)}, f32[256,512]{1,0:T(8,128)S(1)}, u32[]{:S(2)}, u32[]{:S(2)}) %collective-permute-start.20) | collective-permute-done | bytes 524320 | tf_op jit(solution)/shard_map/ppermute | solution.py:97
  152.8 4.5 %collective-permute-done.24 = f32[128]{0:T(128)S(1)} collective-permute-done((f32[128]{0:T(128)S(1)}, f32[128]{0:T(128)S(1)}, u32[]{:S(2)}, u32[]{:S(2)}) %collective-permute-start.24) | collective-permute-done | bytes 544 | tf_op jit(solution)/shard_map/ppermute | solution.py:97
  157.4 2.5 %collective-permute-start.25 = (f32[64]{0:T(128)S(1)}, f32[64]{0:T(128)S(1)}, u32[]{:S(2)}, u32[]{:S(2)}) collective-permute-start(f32[64]{0:T(128)S(1)} %slice_add_fusion.6), channel_id=1, source_target_pairs={{0,12},{1,13},{2,14},{3,15},{4,8},{5,9},{6,10},{7,11},{8,4},{9,5},... | collective-permute-start | bytes 776 | tf_op jit(solution)/shard_map/ppermute | solution.py:97
  162.6 2.8 %collective-permute-done.22 = f32[64,512]{1,0:T(8,128)S(1)} collective-permute-done((f32[64,512]{1,0:T(8,128)S(1)}, f32[64,512]{1,0:T(8,128)S(1)}, u32[]{:S(2)}, u32[]{:S(2)}) %collective-permute-start.22) | collective-permute-done | bytes 131104 | tf_op jit(solution)/shard_map/ppermute | solution.py:97
  (104 shorter events, 24.9 us)
Async XLA Ops:
  0.6 6.4 %copy-start = (bf16[64,8192]{1,0:T(8,128)(2,1)S(1)}, bf16[64,8192]{1,0:T(8,128)(2,1)}, u32[]{:S(2)}) copy-start(bf16[64,8192]{1,0:T(8,128)(2,1)} %param.5) | copy-start | bytes 3145732
  0.6 8.0 %copy-start.2 = (s32[64]{0:T(128)S(1)}, s32[64]{0:T(128)}, u32[]{:S(2)}) copy-start(s32[64]{0:T(128)} %param.9) | copy-start | bytes 772
  0.7 8.1 %copy-start.1 = (bf16[64,8192]{1,0:T(8,128)(2,1)S(1)}, bf16[64,8192]{1,0:T(8,128)(2,1)}, u32[]{:S(2)}) copy-start(bf16[64,8192]{1,0:T(8,128)(2,1)} %param.8) | copy-start | bytes 3145732
  3.4 23.0 %collective-permute-start.1 = (bf16[64,2816]{1,0:T(8,128)(2,1)S(1)}, bf16[64,2816]{1,0:T(8,128)(2,1)S(1)}, u32[]{:S(2)}, u32[]{:S(2)}) collective-permute-start(bf16[64,2816]{1,0:T(8,128)(2,1)S(1)} %get-tuple-element.32), channel_id=1, source_target_pairs={{0,64},{1,65},{2,66},{3,67},{4,68},{5,69},{6,70},{7,71},{8,72},{9,... | collective-permute-start | bytes 1081352 | tf_op jit(solution)/shard_map/ppermute | solution.py:80
  5.1 24.5 %collective-permute-start.4 = (bf16[64,2816]{1,0:T(8,128)(2,1)S(1)}, bf16[64,2816]{1,0:T(8,128)(2,1)S(1)}, u32[]{:S(2)}, u32[]{:S(2)}) collective-permute-start(bf16[64,2816]{1,0:T(8,128)(2,1)S(1)} %get-tuple-element.33), channel_id=1, source_target_pairs={{0,4},{1,5},{2,6},{3,7},{4,0},{5,1},{6,2},{7,3},{8,12},{9,13},{10,... | collective-permute-start | bytes 1081352 | tf_op jit(solution)/shard_map/ppermute | solution.py:80
  7.1 9.3 %collective-permute-start = (bf16[64,2688]{1,0:T(8,128)(2,1)S(1)}, bf16[64,2688]{1,0:T(8,128)(2,1)S(1)}, u32[]{:S(2)}, u32[]{:S(2)}) collective-permute-start(bf16[64,2688]{1,0:T(8,128)(2,1)S(1)} %slice.242), channel_id=1, source_target_pairs={{0,16},{1,17},{2,18},{3,19},{4,20},{5,21},{6,22},{7,23},{8,24},{9,... | collective-permute-start | bytes 1032200 | tf_op jit(solution)/shard_map/ppermute | solution.py:80
  8.8 4.9 %slice-start = ((bf16[64,8192]{1,0:T(8,128)(2,1)}), bf16[64,5504]{1,0:T(8,128)(2,1)S(1)}, s32[]{:S(2)}) async-start(bf16[64,8192]{1,0:T(8,128)(2,1)} %param.5), calls=%async_computation | async-start | bytes 1409024 | tf_op jit(solution)/shard_map/slice | solution.py:77
  8.8 21.3 %collective-permute-start.10 = (bf16[64,2816]{1,0:T(8,128)(2,1)S(1)}, bf16[64,2816]{1,0:T(8,128)(2,1)S(1)}, u32[]{:S(2)}, u32[]{:S(2)}) collective-permute-start(bf16[64,2816]{1,0:T(8,128)(2,1)S(1)} %get-tuple-element.34), channel_id=1, source_target_pairs={{0,66},{1,67},{2,64},{3,65},{4,70},{5,71},{6,68},{7,69},{8,74},{9,... | collective-permute-start | bytes 1081352 | tf_op jit(solution)/shard_map/ppermute | solution.py:80
  11.1 2.6 %slice-start.1 = ((bf16[64,8192]{1,0:T(8,128)(2,1)}), bf16[64,5504]{1,0:T(8,128)(2,1)S(1)}, s32[]{:S(2)}) async-start(bf16[64,8192]{1,0:T(8,128)(2,1)} %param.8), calls=%async_computation.1 | async-start | bytes 1409024 | tf_op jit(solution)/shard_map/slice | solution.py:77
  11.1 19.5 %collective-permute-start.13 = (bf16[64,2816]{1,0:T(8,128)(2,1)S(1)}, bf16[64,2816]{1,0:T(8,128)(2,1)S(1)}, u32[]{:S(2)}, u32[]{:S(2)}) collective-permute-start(bf16[64,2816]{1,0:T(8,128)(2,1)S(1)} %get-tuple-element.35), channel_id=1, source_target_pairs={{0,12},{1,13},{2,14},{3,15},{4,8},{5,9},{6,10},{7,11},{8,4},{9,5},... | collective-permute-start | bytes 1081352 | tf_op jit(solution)/shard_map/ppermute | solution.py:80
  16.4 9.5 %collective-permute-start.9 = (bf16[64,2688]{1,0:T(8,128)(2,1)S(1)}, bf16[64,2688]{1,0:T(8,128)(2,1)S(1)}, u32[]{:S(2)}, u32[]{:S(2)}) collective-permute-start(bf16[64,2688]{1,0:T(8,128)(2,1)S(1)} %slice.265), channel_id=1, source_target_pairs={{0,48},{1,49},{2,50},{3,51},{4,52},{5,53},{6,54},{7,55},{8,56},{9,... | collective-permute-start | bytes 1032200 | tf_op jit(solution)/shard_map/ppermute | solution.py:80
  25.9 14.8 %collective-permute-start.6 = (bf16[128,2688]{1,0:T(8,128)(2,1)S(1)}, bf16[128,2688]{1,0:T(8,128)(2,1)S(1)}, u32[]{:S(2)}, u32[]{:S(2)}) collective-permute-start(bf16[128,2688]{1,0:T(8,128)(2,1)S(1)} %pad_maximum_fusion.10), channel_id=1, source_target_pairs={{0,64},{1,65},{2,66},{3,67},{4,68},{5,69},{6,70},{7,71},{8,72},{9,... | collective-permute-start | bytes 2064392 | tf_op jit(solution)/shard_map/ppermute | solution.py:80
  26.4 17.2 %collective-permute-start.15 = (bf16[128,2688]{1,0:T(8,128)(2,1)S(1)}, bf16[128,2688]{1,0:T(8,128)(2,1)S(1)}, u32[]{:S(2)}, u32[]{:S(2)}) collective-permute-start(bf16[128,2688]{1,0:T(8,128)(2,1)S(1)} %pad_maximum_fusion.11), channel_id=1, source_target_pairs={{0,66},{1,67},{2,64},{3,65},{4,70},{5,71},{6,68},{7,69},{8,74},{9,... | collective-permute-start | bytes 2064392 | tf_op jit(solution)/shard_map/ppermute | solution.py:80
  29.6 17.0 %collective-permute-start.2 = (bf16[128,2816]{1,0:T(8,128)(2,1)S(1)}, bf16[128,2816]{1,0:T(8,128)(2,1)S(1)}, u32[]{:S(2)}, u32[]{:S(2)}) collective-permute-start(bf16[128,2816]{1,0:T(8,128)(2,1)S(1)} %pad_maximum_fusion.6), channel_id=1, source_target_pairs={{0,4},{1,5},{2,6},{3,7},{4,0},{5,1},{6,2},{7,3},{8,12},{9,13},{10,... | collective-permute-start | bytes 2162696 | tf_op jit(solution)/shard_map/ppermute | solution.py:80
  30.2 19.0 %collective-permute-start.5 = (bf16[128,2816]{1,0:T(8,128)(2,1)S(1)}, bf16[128,2816]{1,0:T(8,128)(2,1)S(1)}, u32[]{:S(2)}, u32[]{:S(2)}) collective-permute-start(bf16[128,2816]{1,0:T(8,128)(2,1)S(1)} %pad_maximum_fusion.7), channel_id=1, source_target_pairs={{0,16},{1,17},{2,18},{3,19},{4,20},{5,21},{6,22},{7,23},{8,24},{9,... | collective-permute-start | bytes 2162696 | tf_op jit(solution)/shard_map/ppermute | solution.py:80
  30.6 20.4 %collective-permute-start.11 = (bf16[128,2816]{1,0:T(8,128)(2,1)S(1)}, bf16[128,2816]{1,0:T(8,128)(2,1)S(1)}, u32[]{:S(2)}, u32[]{:S(2)}) collective-permute-start(bf16[128,2816]{1,0:T(8,128)(2,1)S(1)} %pad_maximum_fusion.8), channel_id=1, source_target_pairs={{0,12},{1,13},{2,14},{3,15},{4,8},{5,9},{6,10},{7,11},{8,4},{9,5},... | collective-permute-start | bytes 2162696 | tf_op jit(solution)/shard_map/ppermute | solution.py:80
  40.7 16.3 %collective-permute-start.14 = (bf16[128,2816]{1,0:T(8,128)(2,1)S(1)}, bf16[128,2816]{1,0:T(8,128)(2,1)S(1)}, u32[]{:S(2)}, u32[]{:S(2)}) collective-permute-start(bf16[128,2816]{1,0:T(8,128)(2,1)S(1)} %pad_maximum_fusion.9), channel_id=1, source_target_pairs={{0,48},{1,49},{2,50},{3,51},{4,52},{5,53},{6,54},{7,55},{8,56},{9,... | collective-permute-start | bytes 2162696 | tf_op jit(solution)/shard_map/ppermute | solution.py:80
  43.6 30.5 %collective-permute-start.8 = (bf16[256,2688]{1,0:T(8,128)(2,1)S(1)}, bf16[256,2688]{1,0:T(8,128)(2,1)S(1)}, u32[]{:S(2)}, u32[]{:S(2)}) collective-permute-start(bf16[256,2688]{1,0:T(8,128)(2,1)S(1)} %pad_maximum_fusion.4), channel_id=1, source_target_pairs={{0,4},{1,5},{2,6},{3,7},{4,0},{5,1},{6,2},{7,3},{8,12},{9,13},{10,... | collective-permute-start | bytes 4128776 | tf_op jit(solution)/shard_map/ppermute | solution.py:80
  46.6 29.9 %collective-permute-start.17 = (bf16[256,2688]{1,0:T(8,128)(2,1)S(1)}, bf16[256,2688]{1,0:T(8,128)(2,1)S(1)}, u32[]{:S(2)}, u32[]{:S(2)}) collective-permute-start(bf16[256,2688]{1,0:T(8,128)(2,1)S(1)} %pad_maximum_fusion.5), channel_id=1, source_target_pairs={{0,12},{1,13},{2,14},{3,15},{4,8},{5,9},{6,10},{7,11},{8,4},{9,5},... | collective-permute-start | bytes 4128776 | tf_op jit(solution)/shard_map/ppermute | solution.py:80
  49.2 28.2 %collective-permute-start.3 = (bf16[256,2816]{1,0:T(8,128)(2,1)S(1)}, bf16[256,2816]{1,0:T(8,128)(2,1)S(1)}, u32[]{:S(2)}, u32[]{:S(2)}) collective-permute-start(bf16[256,2816]{1,0:T(8,128)(2,1)S(1)} %pad_maximum_fusion), channel_id=1, source_target_pairs={{0,16},{1,17},{2,18},{3,19},{4,20},{5,21},{6,22},{7,23},{8,24},{9,... | collective-permute-start | bytes 4325384 | tf_op jit(solution)/shard_map/ppermute | solution.py:80
  51.0 26.7 %collective-permute-start.7 = (bf16[256,2816]{1,0:T(8,128)(2,1)S(1)}, bf16[256,2816]{1,0:T(8,128)(2,1)S(1)}, u32[]{:S(2)}, u32[]{:S(2)}) collective-permute-start(bf16[256,2816]{1,0:T(8,128)(2,1)S(1)} %pad_maximum_fusion.1), channel_id=1, source_target_pairs={{0,64},{1,65},{2,66},{3,67},{4,68},{5,69},{6,70},{7,71},{8,72},{9,... | collective-permute-start | bytes 4325384 | tf_op jit(solution)/shard_map/ppermute | solution.py:80
  57.0 30.4 %collective-permute-start.12 = (bf16[256,2816]{1,0:T(8,128)(2,1)S(1)}, bf16[256,2816]{1,0:T(8,128)(2,1)S(1)}, u32[]{:S(2)}, u32[]{:S(2)}) collective-permute-start(bf16[256,2816]{1,0:T(8,128)(2,1)S(1)} %pad_maximum_fusion.2), channel_id=1, source_target_pairs={{0,48},{1,49},{2,50},{3,51},{4,52},{5,53},{6,54},{7,55},{8,56},{9,... | collective-permute-start | bytes 4325384 | tf_op jit(solution)/shard_map/ppermute | solution.py:80
  74.1 32.1 %collective-permute-start.16 = (bf16[256,2816]{1,0:T(8,128)(2,1)S(1)}, bf16[256,2816]{1,0:T(8,128)(2,1)S(1)}, u32[]{:S(2)}, u32[]{:S(2)}) collective-permute-start(bf16[256,2816]{1,0:T(8,128)(2,1)S(1)} %pad_maximum_fusion.3), channel_id=1, source_target_pairs={{0,66},{1,67},{2,64},{3,65},{4,70},{5,71},{6,68},{7,69},{8,74},{9,... | collective-permute-start | bytes 4325384 | tf_op jit(solution)/shard_map/ppermute | solution.py:80
  78.8 36.1 %collective-permute-start.18 = (bf16[512,8320]{1,0:T(8,128)(2,1)S(1)}, bf16[512,8320]{1,0:T(8,128)(2,1)}, u32[]{:S(2)}, u32[]{:S(2)}) collective-permute-start(bf16[512,8320]{1,0:T(8,128)(2,1)S(1)} %maximum_dynamic-update-slice_fusion), channel_id=1, source_target_pairs={{0,1},{1,0},{2,3},{3,2},{4,5},{5,4},{6,7},{7,6},{8,9},{9,8},{10,11... | collective-permute-start | bytes 25559048 | tf_op jit(solution)/shard_map/ppermute | solution.py:114
  126.2 11.1 %collective-permute-start.19 = (f32[512,512]{1,0:T(8,128)S(1)}, f32[512,512]{1,0:T(8,128)S(1)}, u32[]{:S(2)}, u32[]{:S(2)}) collective-permute-start(f32[512,512]{1,0:T(8,128)S(1)} %fusion.5), channel_id=1, source_target_pairs={{0,1},{1,0},{2,3},{3,2},{4,5},{5,4},{6,7},{7,6},{8,9},{9,8},{10,11... | collective-permute-start | bytes 3145736 | tf_op jit(solution)/shard_map/ppermute | solution.py:132
  137.9 14.4 %collective-permute-start.20 = (f32[256,512]{1,0:T(8,128)S(1)}, f32[256,512]{1,0:T(8,128)S(1)}, u32[]{:S(2)}, u32[]{:S(2)}) collective-permute-start(f32[256,512]{1,0:T(8,128)S(1)} %pad_maximum_fusion.12), channel_id=1, source_target_pairs={{0,16},{1,17},{2,18},{3,19},{4,20},{5,21},{6,22},{7,23},{8,24},{9,... | collective-permute-start | bytes 1572872 | tf_op jit(solution)/shard_map/ppermute | solution.py:97
  138.1 4.8 %collective-permute-start.23 = (f32[256]{0:T(256)S(1)}, f32[256]{0:T(256)S(1)}, u32[]{:S(2)}, u32[]{:S(2)}) collective-permute-start(f32[256]{0:T(256)S(1)} %pad_maximum_fusion.16), channel_id=1, source_target_pairs={{0,48},{1,49},{2,50},{3,51},{4,52},{5,53},{6,54},{7,55},{8,56},{9,... | collective-permute-start | bytes 3080 | tf_op jit(solution)/shard_map/ppermute | solution.py:97
  152.4 8.0 %collective-permute-start.21 = (f32[128,512]{1,0:T(8,128)S(1)}, f32[128,512]{1,0:T(8,128)S(1)}, u32[]{:S(2)}, u32[]{:S(2)}) collective-permute-start(f32[128,512]{1,0:T(8,128)S(1)} %pad_maximum_fusion.15), channel_id=1, source_target_pairs={{0,64},{1,65},{2,66},{3,67},{4,68},{5,69},{6,70},{7,71},{8,72},{9,... | collective-permute-start | bytes 786440 | tf_op jit(solution)/shard_map/ppermute | solution.py:97
  152.5 4.8 %collective-permute-start.24 = (f32[128]{0:T(128)S(1)}, f32[128]{0:T(128)S(1)}, u32[]{:S(2)}, u32[]{:S(2)}) collective-permute-start(f32[128]{0:T(128)S(1)} %pad_maximum_fusion.17), channel_id=1, source_target_pairs={{0,66},{1,67},{2,64},{3,65},{4,70},{5,71},{6,68},{7,69},{8,74},{9,... | collective-permute-start | bytes 1544 | tf_op jit(solution)/shard_map/ppermute | solution.py:97
  157.4 4.8 %collective-permute-start.25 = (f32[64]{0:T(128)S(1)}, f32[64]{0:T(128)S(1)}, u32[]{:S(2)}, u32[]{:S(2)}) collective-permute-start(f32[64]{0:T(128)S(1)} %slice_add_fusion.6), channel_id=1, source_target_pairs={{0,12},{1,13},{2,14},{3,15},{4,8},{5,9},{6,10},{7,11},{8,4},{9,5},... | collective-permute-start | bytes 776 | tf_op jit(solution)/shard_map/ppermute | solution.py:97
  160.4 5.0 %collective-permute-start.22 = (f32[64,512]{1,0:T(8,128)S(1)}, f32[64,512]{1,0:T(8,128)S(1)}, u32[]{:S(2)}, u32[]{:S(2)}) collective-permute-start(f32[64,512]{1,0:T(8,128)S(1)} %slice_add_fusion), channel_id=1, source_target_pairs={{0,4},{1,5},{2,6},{3,7},{4,0},{5,1},{6,2},{7,3},{8,12},{9,13},{10,... | collective-permute-start | bytes 393224 | tf_op jit(solution)/shard_map/ppermute | solution.py:97

commit v6 on v5

--- a/solution.py
+++ b/solution.py
@@ -67,8 +67,9 @@
     return [(L, L ^ 1) for L in range(n)]
 
 
-def cube_gather(shard, mate, n):
+def cube_parts(shard, mate, n):
     cols = shard.shape[1]
+    rows = shard.shape[0]
     tiles = cols // 128
     cut = [0, (tiles // 3) * 128, (2 * tiles // 3) * 128, cols]
     parts = []
@@ -80,27 +81,25 @@
             got = lax.ppermute(buf, AXES, mate_pairs(n, a, mate))
             buf = jnp.concatenate([buf, got])
             labs = labs + [o ^ (1 << a) for o in labs]
-        rows = shard.shape[0]
-        parts.append({o: buf[i * rows:(i + 1) * rows] for i, o in enumerate(labs)})
-    return jnp.concatenate(
-        [jnp.concatenate([parts[p][o] for p in range(3)], axis=1) for o in range(8)]
-    )
+        at = {o: i for i, o in enumerate(labs)}
+        parts.append(jnp.concatenate([buf[at[o] * rows:(at[o] + 1) * rows] for o in range(8)]))
+    return parts
+
+
+def offset_pairs(n, o, mate):
+    out = []
+    for L in range(n):
+        v, c = coords(L)
+        w = [mate(v[a]) if o & (1 << a) else v[a] for a in range(3)]
+        out.append((L, lin(w, c)))
+    return out
 
 
 def cube_reduce(blocks, mate, n):
-    blocks = list(blocks)
-    live = list(range(8))
-    for a in range(3):
-        send = [o for o in live if o & (1 << a)]
-        keep = [o for o in live if not o & (1 << a)]
-        rows = blocks[0].shape[0]
-        got = lax.ppermute(
-            jnp.concatenate([blocks[o] for o in send]), AXES, mate_pairs(n, a, mate)
-        )
-        for i, o in enumerate(send):
-            blocks[o ^ (1 << a)] = blocks[o ^ (1 << a)] + got[i * rows:(i + 1) * rows]
-        live = keep
-    return blocks[0]
+    total = blocks[0]
+    for o in range(1, 8):
+        total = total + lax.ppermute(blocks[o], AXES, offset_pairs(n, o, mate))
+    return total
 
 
 def local(train_grads, train_scale, train_class, test_grads, test_class):
@@ -109,9 +108,12 @@
     rows = train_grads.shape[0]
     tr = with_side(train_grads, (train_scale,) + split_class(train_class), 0)
     te = with_side(test_grads, split_class(test_class), 4)
-    te_all = cube_gather(te, test_mate, n)
-    tr_mine = cube_gather(tr, train_mate, n)
-    tr_other = lax.ppermute(tr_mine, AXES, core_pairs(n))
+    te_all = jnp.concatenate(cube_parts(te, test_mate, n), axis=1)
+    tr_parts = cube_parts(tr, train_mate, n)
+    tr_mine = jnp.concatenate(tr_parts, axis=1)
+    tr_other = jnp.concatenate(
+        [lax.ppermute(t, AXES, core_pairs(n)) for t in tr_parts], axis=1
+    )
     test_hot = indicator(join_class(te_all, k + 4))
 
     def weigh(t):

time: 166 us -> 195 us (1.17)
  matrix products: 20.1 us -> 36.5 us
  local copies, waits for them, and re-layouts: 1.06 us -> 12.5 us
  other arithmetic: 18.7 us -> 8.99 us
  starting transfers between devices: 38 us -> 44.8 us
  waiting for transfers between devices: 87.3 us -> 90.4 us
    dot_general x2, matrix products: 17.8 us -> 32.1 us  [weigh(): lax.dot_general(t, te_all, (((1,), (1,)), ((), ())), preferred_element_ty...]
    unnamed x6 -> x46, local copies, waits for them, and re-layouts: 0.02 us -> 10.5 us
    unnamed x14 -> x0, other arithmetic: 8.3 us -> none
    ppermute x25 -> x35, starting transfers between devices: 37.7 us -> 44.7 us  [the longest x18 24.1 us: cube_parts(): got = lax.ppermute(buf, AXES, mate_pairs(n, a, mate))]
    ppermute x25 -> x35, waiting for transfers between devices: 87.3 us -> 90.4 us  [the longest x18 73.9 us: cube_parts(): got = lax.ppermute(buf, AXES, mate_pairs(n, a, mate))]
    dot_general x2, matrix products: 1.02 us -> 3.24 us  [weigh(): part = jnp.dot(w, test_hot, preferred_element_type=jnp.float32)]
  transfers between devices with their start and end apart: 26 -> 36, of which waited for: 17 -> 14; matrix products, arithmetic and copies ran while one was open for 15% -> 16% of each run, Pallas kernels for 0% -> 0%
where the time goes in v6:
time: 195 us; the launch traced here: 194 us
  waiting for transfers between devices  90.4 us (46%)
  starting transfers between devices  44.8 us (23%)
  matrix products  36.5 us (19%)
  local copies, waits for them, and re-layouts  12.5 us (6%)
  other arithmetic  8.99 us (5%)
    ppermute x18, waiting for transfers between devices, cube_parts(): got = lax.ppermute(buf, AXES, mate_pairs(n, a, mate))  73.9 us
    dot_general x2, matrix products, weigh(): lax.dot_general(t, te_all, (((1,), (1,)), ((), ())), preferred_element_ty...  32.1 us
    ppermute x18, starting transfers between devices, cube_parts(): got = lax.ppermute(buf, AXES, mate_pairs(n, a, mate))  24.1 us
    ppermute x14, starting transfers between devices, cube_reduce(): total = total + lax.ppermute(blocks[o], AXES, offset_pairs(n, o, mate))  19.8 us
    ppermute x14, waiting for transfers between devices, cube_reduce(): total = total + lax.ppermute(blocks[o], AXES, offset_pairs(n, o, mate))  11.3 us
    unnamed x46, local copies, waits for them, and re-layouts  10.5 us
    ppermute x3, waiting for transfers between devices, local(): lax.ppermute(t, AXES, core_pairs(n))  5.16 us
  transfers between devices with their start and end apart: 36, of which 14 were waited for; matrix products, arithmetic and copies ran while one was open for 16% of the time, Pallas kernels for 0%

profile of v6, /device:TPU:0, one launch (start us, length us, event | category | flops | bytes accessed | tf_op | source)
XLA Modules:
  0.0 194.4 jit_solution(12397440925291903658)
XLA Ops:
  1.5 1.9 fusion.51
  3.4 3.1 %collective-permute-start.12 = (bf16[64,2816]{1,0:T(8,128)(2,1)S(1)}, bf16[64,2816]{1,0:T(8,128)(2,1)S(1)}, u32[]{:S(2)}, u32[]{:S(2)}) collective-permute-start(bf16[64,2816]{1,0:T(8,128)(2,1)S(1)} %get-tuple-element.13), channel_id=1, source_target_pairs={{0,66},{1,67},{2,64},{3,65},{4,70},{5,71},{6,68},{7,69},{8,74},{9,... | collective-permute-start | bytes 1081352 | tf_op jit(solution)/shard_map/ppermute | solution.py:81
  6.5 4.0 %collective-permute-start.15 = (bf16[64,2816]{1,0:T(8,128)(2,1)S(1)}, bf16[64,2816]{1,0:T(8,128)(2,1)S(1)}, u32[]{:S(2)}, u32[]{:S(2)}) collective-permute-start(bf16[64,2816]{1,0:T(8,128)(2,1)S(1)} %get-tuple-element.16), channel_id=1, source_target_pairs={{0,12},{1,13},{2,14},{3,15},{4,8},{5,9},{6,10},{7,11},{8,4},{9,5},... | collective-permute-start | bytes 1081352 | tf_op jit(solution)/shard_map/ppermute | solution.py:81
  11.6 2.8 %collective-permute-start.9 = (bf16[64,2688]{1,0:T(8,128)(2,1)S(1)}, bf16[64,2688]{1,0:T(8,128)(2,1)S(1)}, u32[]{:S(2)}, u32[]{:S(2)}) collective-permute-start(bf16[64,2688]{1,0:T(8,128)(2,1)S(1)} %slice.194), channel_id=1, source_target_pairs={{0,48},{1,49},{2,50},{3,51},{4,52},{5,53},{6,54},{7,55},{8,56},{9,... | collective-permute-start | bytes 1032200 | tf_op jit(solution)/shard_map/ppermute | solution.py:81
  15.6 6.5 %collective-permute-done.9 = bf16[64,2688]{1,0:T(8,128)(2,1)S(1)} collective-permute-done((bf16[64,2688]{1,0:T(8,128)(2,1)S(1)}, bf16[64,2688]{1,0:T(8,128)(2,1)S(1)}, u32[]{:S(2)}, u32[]{:S(2)}) %collective-permute-start.9) | collective-permute-done | bytes 344096 | tf_op jit(solution)/shard_map/ppermute | solution.py:81
  22.4 8.0 %collective-permute-done.3 = bf16[64,2688]{1,0:T(8,128)(2,1)S(1)} collective-permute-done((bf16[64,2688]{1,0:T(8,128)(2,1)S(1)}, bf16[64,2688]{1,0:T(8,128)(2,1)S(1)}, u32[]{:S(2)}, u32[]{:S(2)}) %collective-permute-start.3) | collective-permute-done | bytes 344096 | tf_op jit(solution)/shard_map/ppermute | solution.py:81
  31.9 2.8 %collective-permute-start.16 = (bf16[128,2816]{1,0:T(8,128)(2,1)S(1)}, bf16[128,2816]{1,0:T(8,128)(2,1)S(1)}, u32[]{:S(2)}, u32[]{:S(2)}) collective-permute-start(bf16[128,2816]{1,0:T(8,128)(2,1)S(1)} %pad_maximum_fusion.11), channel_id=1, source_target_pairs={{0,48},{1,49},{2,50},{3,51},{4,52},{5,53},{6,54},{7,55},{8,56},{9,... | collective-permute-start | bytes 2162696 | tf_op jit(solution)/shard_map/ppermute | solution.py:81
  35.0 11.4 %collective-permute-done.10 = bf16[128,2688]{1,0:T(8,128)(2,1)S(1)} collective-permute-done((bf16[128,2688]{1,0:T(8,128)(2,1)S(1)}, bf16[128,2688]{1,0:T(8,128)(2,1)S(1)}, u32[]{:S(2)}, u32[]{:S(2)}) %collective-permute-start.10) | collective-permute-done | bytes 688160 | tf_op jit(solution)/shard_map/ppermute | solution.py:81
  48.3 2.9 %collective-permute-start.14 = (bf16[256,2816]{1,0:T(8,128)(2,1)S(1)}, bf16[256,2816]{1,0:T(8,128)(2,1)S(1)}, u32[]{:S(2)}, u32[]{:S(2)}) collective-permute-start(bf16[256,2816]{1,0:T(8,128)(2,1)S(1)} %pad_maximum_fusion.4), channel_id=1, source_target_pairs={{0,48},{1,49},{2,50},{3,51},{4,52},{5,53},{6,54},{7,55},{8,56},{9,... | collective-permute-start | bytes 4325384 | tf_op jit(solution)/shard_map/ppermute | solution.py:81
  52.5 3.2 %collective-permute-start.17 = (bf16[256,2816]{1,0:T(8,128)(2,1)S(1)}, bf16[256,2816]{1,0:T(8,128)(2,1)S(1)}, u32[]{:S(2)}, u32[]{:S(2)}) collective-permute-start(bf16[256,2816]{1,0:T(8,128)(2,1)S(1)} %pad_maximum_fusion.5), channel_id=1, source_target_pairs={{0,66},{1,67},{2,64},{3,65},{4,70},{5,71},{6,68},{7,69},{8,74},{9,... | collective-permute-start | bytes 4325384 | tf_op jit(solution)/shard_map/ppermute | solution.py:81
  55.9 6.7 %collective-permute-done.1 = bf16[128,2816]{1,0:T(8,128)(2,1)S(1)} collective-permute-done((bf16[128,2816]{1,0:T(8,128)(2,1)S(1)}, bf16[128,2816]{1,0:T(8,128)(2,1)S(1)}, u32[]{:S(2)}, u32[]{:S(2)}) %collective-permute-start.1) | collective-permute-done | bytes 720928 | tf_op jit(solution)/shard_map/ppermute | solution.py:81
  63.0 16.2 %collective-permute-done.5 = bf16[256,2688]{1,0:T(8,128)(2,1)S(1)} collective-permute-done((bf16[256,2688]{1,0:T(8,128)(2,1)S(1)}, bf16[256,2688]{1,0:T(8,128)(2,1)S(1)}, u32[]{:S(2)}, u32[]{:S(2)}) %collective-permute-start.5) | collective-permute-done | bytes 1376288 | tf_op jit(solution)/shard_map/ppermute | solution.py:81
  79.2 1.7 collective-permute-start.2
  81.1 10.7 %collective-permute-done.8 = bf16[256,2816]{1,0:T(8,128)(2,1)S(1)} collective-permute-done((bf16[256,2816]{1,0:T(8,128)(2,1)S(1)}, bf16[256,2816]{1,0:T(8,128)(2,1)S(1)}, u32[]{:S(2)}, u32[]{:S(2)}) %collective-permute-start.8) | collective-permute-done | bytes 1441824 | tf_op jit(solution)/shard_map/ppermute | solution.py:81
  97.2 12.8 %collective-permute-done.2 = bf16[256,2816]{1,0:T(8,128)(2,1)S(1)} collective-permute-done((bf16[256,2816]{1,0:T(8,128)(2,1)S(1)}, bf16[256,2816]{1,0:T(8,128)(2,1)S(1)}, u32[]{:S(2)}, u32[]{:S(2)}) %collective-permute-start.2) | collective-permute-done | bytes 1441824 | tf_op jit(solution)/shard_map/ppermute | solution.py:81
  111.5 2.4 %copy-done.6 = bf16[512,2816]{1,0:T(8,128)(2,1)S(1)} copy-done((bf16[512,2816]{1,0:T(8,128)(2,1)S(1)}, bf16[512,2816]{1,0:T(8,128)(2,1)}, u32[]{:S(2)}) %copy-start.6) | copy-done | bytes 2883608
  114.3 5.2 %collective-permute-done.18 = bf16[512,2816]{1,0:T(8,128)(2,1)S(1)} collective-permute-done((bf16[512,2816]{1,0:T(8,128)(2,1)S(1)}, bf16[512,2816]{1,0:T(8,128)(2,1)S(1)}, u32[]{:S(2)}, u32[]{:S(2)}) %collective-permute-start.18) | collective-permute-done | bytes 2883616 | tf_op jit(solution)/shard_map/ppermute | solution.py:115
  121.0 1.5 copy-done.9
  122.6 14.0 %tanh_convert_fusion = bf16[512,512]{1,0:T(8,128)(2,1)S(1)} fusion(f32[512]{0:T(512)S(1)} %convert_reduce_fusion, bf16[512,2816]{1,0:T(8,128)(2,1)} %copy-done.5, bf16[512,2816]{1,0:T(8,128)(2,1)} %collective-permute-done.20, bf16[512,2688]{1,0:T(8,128)(2,1)} %copy-done.9, bf16[512,2816]{1,0:T(8,128)(2,1)} %copy-done.4, bf16[512,2816]{1,0:T(8,128)(2,1)} %copy-done.7, ...), kind=kOutput, calls=%fused_computation.35 | convolution fusion | flops 4439277568 | bytes 17565696 | tf_op jit(solution)/shard_map/dot_general | solution.py:120
  136.6 1.5 fusion.30
  138.2 18.2 %fusion.25 = bf16[512,512]{1,0:T(8,128)(2,1)S(1)} fusion(bf16[512,2816]{1,0:T(8,128)(2,1)} %copy-done.3, bf16[512,2816]{1,0:T(8,128)(2,1)} %slice_dynamic-update-slice_fusion.12, bf16[256,2688]{1,0:T(8,128)(2,1)} %copy-done.1, bf16[128,2688]{1,0:T(8,128)(2,1)S(1)} %collective-permute-done.4, bf16[64,2688]{1,0:T(8,128)(2,1)S(1)} %collective-permute-done.3, ...), kind=kOutput, calls=%fused_computation.31 | convolution fusion | flops 4464836608 | bytes 17565696 | tf_op jit(solution)/shard_map/dot_general | solution.py:120
  160.0 1.7 convolution_add_fusion.1
  162.9 2.1 %collective-permute-start.30 = (f32[64]{0:T(128)S(1)}, f32[64]{0:T(128)S(1)}, u32[]{:S(2)}, u32[]{:S(2)}) collective-permute-start(f32[64]{0:T(128)S(1)} %get-tuple-element.27), channel_id=1, source_target_pairs={{0,66},{1,67},{2,64},{3,65},{4,70},{5,71},{6,68},{7,69},{8,74},{9,... | collective-permute-start | bytes 776 | tf_op jit(solution)/shard_map/ppermute | solution.py:101
  165.0 3.8 %collective-permute-start.31 = (f32[64]{0:T(128)S(1)}, f32[64]{0:T(128)S(1)}, u32[]{:S(2)}, u32[]{:S(2)}) collective-permute-start(f32[64]{0:T(128)S(1)} %get-tuple-element.26), channel_id=1, source_target_pairs={{0,114},{1,115},{2,112},{3,113},{4,118},{5,119},{6,116},{7,117},{8... | collective-permute-start | bytes 776 | tf_op jit(solution)/shard_map/ppermute | solution.py:101
  168.8 1.9 collective-permute-start.32
  170.7 1.5 collective-permute-start.33
  172.2 3.5 %collective-permute-start.34 = (f32[64]{0:T(128)S(1)}, f32[64]{0:T(128)S(1)}, u32[]{:S(2)}, u32[]{:S(2)}) collective-permute-start(f32[64]{0:T(128)S(1)} %get-tuple-element.23), channel_id=1, source_target_pairs={{0,78},{1,79},{2,76},{3,77},{4,74},{5,75},{6,72},{7,73},{8,70},{9,... | collective-permute-start | bytes 776 | tf_op jit(solution)/shard_map/ppermute | solution.py:101
  175.7 4.1 %collective-permute-start.35 = (f32[64]{0:T(128)S(1)}, f32[64]{0:T(128)S(1)}, u32[]{:S(2)}, u32[]{:S(2)}) collective-permute-start(f32[64]{0:T(128)S(1)} %get-tuple-element.22), channel_id=1, source_target_pairs={{0,126},{1,127},{2,124},{3,125},{4,122},{5,123},{6,120},{7,121},{8... | collective-permute-start | bytes 776 | tf_op jit(solution)/shard_map/ppermute | solution.py:101
  179.9 4.7 %collective-permute-done.35 = f32[64]{0:T(128)S(1)} collective-permute-done((f32[64]{0:T(128)S(1)}, f32[64]{0:T(128)S(1)}, u32[]{:S(2)}, u32[]{:S(2)}) %collective-permute-start.35) | collective-permute-done | bytes 288 | tf_op jit(solution)/shard_map/ppermute | solution.py:101
  184.7 1.9 collective-permute-start.28
  187.1 5.0 %collective-permute-done.26 = f32[64,512]{1,0:T(8,128)S(1)} collective-permute-done((f32[64,512]{1,0:T(8,128)S(1)}, f32[64,512]{1,0:T(8,128)S(1)}, u32[]{:S(2)}, u32[]{:S(2)}) %collective-permute-start.26) | collective-permute-done | bytes 131104 | tf_op jit(solution)/shard_map/ppermute | solution.py:101
  192.1 1.5 collective-permute-done.27
  (129 shorter events, 23.6 us)
Async XLA Ops:
  3.4 27.4 %collective-permute-start.12 = (bf16[64,2816]{1,0:T(8,128)(2,1)S(1)}, bf16[64,2816]{1,0:T(8,128)(2,1)S(1)}, u32[]{:S(2)}, u32[]{:S(2)}) collective-permute-start(bf16[64,2816]{1,0:T(8,128)(2,1)S(1)} %get-tuple-element.13), channel_id=1, source_target_pairs={{0,66},{1,67},{2,64},{3,65},{4,70},{5,71},{6,68},{7,69},{8,74},{9,... | collective-permute-start | bytes 1081352 | tf_op jit(solution)/shard_map/ppermute | solution.py:81
  6.5 24.7 %collective-permute-start.15 = (bf16[64,2816]{1,0:T(8,128)(2,1)S(1)}, bf16[64,2816]{1,0:T(8,128)(2,1)S(1)}, u32[]{:S(2)}, u32[]{:S(2)}) collective-permute-start(bf16[64,2816]{1,0:T(8,128)(2,1)S(1)} %get-tuple-element.16), channel_id=1, source_target_pairs={{0,12},{1,13},{2,14},{3,15},{4,8},{5,9},{6,10},{7,11},{8,4},{9,5},... | collective-permute-start | bytes 1081352 | tf_op jit(solution)/shard_map/ppermute | solution.py:81
  11.6 10.5 %collective-permute-start.9 = (bf16[64,2688]{1,0:T(8,128)(2,1)S(1)}, bf16[64,2688]{1,0:T(8,128)(2,1)S(1)}, u32[]{:S(2)}, u32[]{:S(2)}) collective-permute-start(bf16[64,2688]{1,0:T(8,128)(2,1)S(1)} %slice.194), channel_id=1, source_target_pairs={{0,48},{1,49},{2,50},{3,51},{4,52},{5,53},{6,54},{7,55},{8,56},{9,... | collective-permute-start | bytes 1032200 | tf_op jit(solution)/shard_map/ppermute | solution.py:81
  15.4 16.5 %collective-permute-start.6 = (bf16[64,2816]{1,0:T(8,128)(2,1)S(1)}, bf16[64,2816]{1,0:T(8,128)(2,1)S(1)}, u32[]{:S(2)}, u32[]{:S(2)}) collective-permute-start(bf16[64,2816]{1,0:T(8,128)(2,1)S(1)} %get-tuple-element.17), channel_id=1, source_target_pairs={{0,64},{1,65},{2,66},{3,67},{4,68},{5,69},{6,70},{7,71},{8,72},{9,... | collective-permute-start | bytes 1081352 | tf_op jit(solution)/shard_map/ppermute | solution.py:81
  15.5 19.3 %collective-permute-start = (bf16[64,2816]{1,0:T(8,128)(2,1)S(1)}, bf16[64,2816]{1,0:T(8,128)(2,1)S(1)}, u32[]{:S(2)}, u32[]{:S(2)}) collective-permute-start(bf16[64,2816]{1,0:T(8,128)(2,1)S(1)} %get-tuple-element.20), channel_id=1, source_target_pairs={{0,4},{1,5},{2,6},{3,7},{4,0},{5,1},{6,2},{7,3},{8,12},{9,13},{10,... | collective-permute-start | bytes 1081352 | tf_op jit(solution)/shard_map/ppermute | solution.py:81
  22.1 8.3 %collective-permute-start.3 = (bf16[64,2688]{1,0:T(8,128)(2,1)S(1)}, bf16[64,2688]{1,0:T(8,128)(2,1)S(1)}, u32[]{:S(2)}, u32[]{:S(2)}) collective-permute-start(bf16[64,2688]{1,0:T(8,128)(2,1)S(1)} %slice.186), channel_id=1, source_target_pairs={{0,16},{1,17},{2,18},{3,19},{4,20},{5,21},{6,22},{7,23},{8,24},{9,... | collective-permute-start | bytes 1032200 | tf_op jit(solution)/shard_map/ppermute | solution.py:81
  30.4 16.0 %collective-permute-start.10 = (bf16[128,2688]{1,0:T(8,128)(2,1)S(1)}, bf16[128,2688]{1,0:T(8,128)(2,1)S(1)}, u32[]{:S(2)}, u32[]{:S(2)}) collective-permute-start(bf16[128,2688]{1,0:T(8,128)(2,1)S(1)} %pad_maximum_fusion.13), channel_id=1, source_target_pairs={{0,66},{1,67},{2,64},{3,65},{4,70},{5,71},{6,68},{7,69},{8,74},{9,... | collective-permute-start | bytes 2064392 | tf_op jit(solution)/shard_map/ppermute | solution.py:81
  30.8 16.0 %collective-permute-start.4 = (bf16[128,2688]{1,0:T(8,128)(2,1)S(1)}, bf16[128,2688]{1,0:T(8,128)(2,1)S(1)}, u32[]{:S(2)}, u32[]{:S(2)}) collective-permute-start(bf16[128,2688]{1,0:T(8,128)(2,1)S(1)} %pad_maximum_fusion.12), channel_id=1, source_target_pairs={{0,64},{1,65},{2,66},{3,67},{4,68},{5,69},{6,70},{7,71},{8,72},{9,... | collective-permute-start | bytes 2064392 | tf_op jit(solution)/shard_map/ppermute | solution.py:81
  31.2 16.9 %collective-permute-start.13 = (bf16[128,2816]{1,0:T(8,128)(2,1)S(1)}, bf16[128,2816]{1,0:T(8,128)(2,1)S(1)}, u32[]{:S(2)}, u32[]{:S(2)}) collective-permute-start(bf16[128,2816]{1,0:T(8,128)(2,1)S(1)} %pad_maximum_fusion.10), channel_id=1, source_target_pairs={{0,12},{1,13},{2,14},{3,15},{4,8},{5,9},{6,10},{7,11},{8,4},{9,5},... | collective-permute-start | bytes 2162696 | tf_op jit(solution)/shard_map/ppermute | solution.py:81
  31.9 16.3 %collective-permute-start.16 = (bf16[128,2816]{1,0:T(8,128)(2,1)S(1)}, bf16[128,2816]{1,0:T(8,128)(2,1)S(1)}, u32[]{:S(2)}, u32[]{:S(2)}) collective-permute-start(bf16[128,2816]{1,0:T(8,128)(2,1)S(1)} %pad_maximum_fusion.11), channel_id=1, source_target_pairs={{0,48},{1,49},{2,50},{3,51},{4,52},{5,53},{6,54},{7,55},{8,56},{9,... | collective-permute-start | bytes 2162696 | tf_op jit(solution)/shard_map/ppermute | solution.py:81
  34.9 17.7 %collective-permute-start.7 = (bf16[128,2816]{1,0:T(8,128)(2,1)S(1)}, bf16[128,2816]{1,0:T(8,128)(2,1)S(1)}, u32[]{:S(2)}, u32[]{:S(2)}) collective-permute-start(bf16[128,2816]{1,0:T(8,128)(2,1)S(1)} %pad_maximum_fusion.9), channel_id=1, source_target_pairs={{0,4},{1,5},{2,6},{3,7},{4,0},{5,1},{6,2},{7,3},{8,12},{9,13},{10,... | collective-permute-start | bytes 2162696 | tf_op jit(solution)/shard_map/ppermute | solution.py:81
  46.4 16.2 %collective-permute-start.1 = (bf16[128,2816]{1,0:T(8,128)(2,1)S(1)}, bf16[128,2816]{1,0:T(8,128)(2,1)S(1)}, u32[]{:S(2)}, u32[]{:S(2)}) collective-permute-start(bf16[128,2816]{1,0:T(8,128)(2,1)S(1)} %pad_maximum_fusion.8), channel_id=1, source_target_pairs={{0,16},{1,17},{2,18},{3,19},{4,20},{5,21},{6,22},{7,23},{8,24},{9,... | collective-permute-start | bytes 2162696 | tf_op jit(solution)/shard_map/ppermute | solution.py:81
  46.8 72.8 %collective-permute-start.11 = (bf16[256,2688]{1,0:T(8,128)(2,1)S(1)}, bf16[256,2688]{1,0:T(8,128)(2,1)}, u32[]{:S(2)}, u32[]{:S(2)}) collective-permute-start(bf16[256,2688]{1,0:T(8,128)(2,1)S(1)} %pad_maximum_fusion.7), channel_id=1, source_target_pairs={{0,12},{1,13},{2,14},{3,15},{4,8},{5,9},{6,10},{7,11},{8,4},{9,5},... | collective-permute-start | bytes 4128776 | tf_op jit(solution)/shard_map/ppermute | solution.py:81
  48.1 31.1 %collective-permute-start.5 = (bf16[256,2688]{1,0:T(8,128)(2,1)S(1)}, bf16[256,2688]{1,0:T(8,128)(2,1)S(1)}, u32[]{:S(2)}, u32[]{:S(2)}) collective-permute-start(bf16[256,2688]{1,0:T(8,128)(2,1)S(1)} %pad_maximum_fusion.6), channel_id=1, source_target_pairs={{0,4},{1,5},{2,6},{3,7},{4,0},{5,1},{6,2},{7,3},{8,12},{9,13},{10,... | collective-permute-start | bytes 4128776 | tf_op jit(solution)/shard_map/ppermute | solution.py:81
  48.3 63.2 %collective-permute-start.14 = (bf16[256,2816]{1,0:T(8,128)(2,1)S(1)}, bf16[256,2816]{1,0:T(8,128)(2,1)S(1)}, u32[]{:S(2)}, u32[]{:S(2)}) collective-permute-start(bf16[256,2816]{1,0:T(8,128)(2,1)S(1)} %pad_maximum_fusion.4), channel_id=1, source_target_pairs={{0,48},{1,49},{2,50},{3,51},{4,52},{5,53},{6,54},{7,55},{8,56},{9,... | collective-permute-start | bytes 4325384 | tf_op jit(solution)/shard_map/ppermute | solution.py:81
  52.5 57.7 %collective-permute-start.17 = (bf16[256,2816]{1,0:T(8,128)(2,1)S(1)}, bf16[256,2816]{1,0:T(8,128)(2,1)S(1)}, u32[]{:S(2)}, u32[]{:S(2)}) collective-permute-start(bf16[256,2816]{1,0:T(8,128)(2,1)S(1)} %pad_maximum_fusion.5), channel_id=1, source_target_pairs={{0,66},{1,67},{2,64},{3,65},{4,70},{5,71},{6,68},{7,69},{8,74},{9,... | collective-permute-start | bytes 4325384 | tf_op jit(solution)/shard_map/ppermute | solution.py:81
  62.6 29.3 %collective-permute-start.8 = (bf16[256,2816]{1,0:T(8,128)(2,1)S(1)}, bf16[256,2816]{1,0:T(8,128)(2,1)S(1)}, u32[]{:S(2)}, u32[]{:S(2)}) collective-permute-start(bf16[256,2816]{1,0:T(8,128)(2,1)S(1)} %pad_maximum_fusion.3), channel_id=1, source_target_pairs={{0,16},{1,17},{2,18},{3,19},{4,20},{5,21},{6,22},{7,23},{8,24},{9,... | collective-permute-start | bytes 4325384 | tf_op jit(solution)/shard_map/ppermute | solution.py:81
  79.2 30.9 %collective-permute-start.2 = (bf16[256,2816]{1,0:T(8,128)(2,1)S(1)}, bf16[256,2816]{1,0:T(8,128)(2,1)S(1)}, u32[]{:S(2)}, u32[]{:S(2)}) collective-permute-start(bf16[256,2816]{1,0:T(8,128)(2,1)S(1)} %pad_maximum_fusion.2), channel_id=1, source_target_pairs={{0,64},{1,65},{2,66},{3,67},{4,68},{5,69},{6,70},{7,71},{8,72},{9,... | collective-permute-start | bytes 4325384 | tf_op jit(solution)/shard_map/ppermute | solution.py:81
  91.9 27.7 %collective-permute-start.19 = (bf16[512,2688]{1,0:T(8,128)(2,1)S(1)}, bf16[512,2688]{1,0:T(8,128)(2,1)S(1)}, u32[]{:S(2)}, u32[]{:S(2)}) collective-permute-start(bf16[512,2688]{1,0:T(8,128)(2,1)S(1)} %pad_maximum_fusion.1), channel_id=1, source_target_pairs={{0,1},{1,0},{2,3},{3,2},{4,5},{5,4},{6,7},{7,6},{8,9},{9,8},{10,11... | collective-permute-start | bytes 8257544 | tf_op jit(solution)/shard_map/ppermute | solution.py:115
  110.1 12.5 %collective-permute-start.20 = (bf16[512,2816]{1,0:T(8,128)(2,1)}, bf16[512,2816]{1,0:T(8,128)(2,1)}, u32[]{:S(2)}, u32[]{:S(2)}) collective-permute-start(bf16[512,2816]{1,0:T(8,128)(2,1)} %slice_dynamic-update-slice_fusion.12), channel_id=1, source_target_pairs={{0,1},{1,0},{2,3},{3,2},{4,5},{5,4},{6,7},{7,6},{8,9},{9,8},{10,11... | collective-permute-start | bytes 8650760 | tf_op jit(solution)/shard_map/ppermute | solution.py:115
  110.3 9.2 %collective-permute-start.18 = (bf16[512,2816]{1,0:T(8,128)(2,1)S(1)}, bf16[512,2816]{1,0:T(8,128)(2,1)S(1)}, u32[]{:S(2)}, u32[]{:S(2)}) collective-permute-start(bf16[512,2816]{1,0:T(8,128)(2,1)S(1)} %slice_dynamic-update-slice_fusion.18), channel_id=1, source_target_pairs={{0,1},{1,0},{2,3},{3,2},{4,5},{5,4},{6,7},{7,6},{8,9},{9,8},{10,11... | collective-permute-start | bytes 8650760 | tf_op jit(solution)/shard_map/ppermute | solution.py:115
  138.1 21.9 %collective-permute-start.21 = (f32[512,512]{1,0:T(8,128)}, f32[512,512]{1,0:T(8,128)}, u32[]{:S(2)}, u32[]{:S(2)}) collective-permute-start(f32[512,512]{1,0:T(8,128)} %fusion.30), channel_id=1, source_target_pairs={{0,1},{1,0},{2,3},{3,2},{4,5},{5,4},{6,7},{7,6},{8,9},{9,8},{10,11... | collective-permute-start | bytes 3145736 | tf_op jit(solution)/shard_map/ppermute | solution.py:134
  161.8 22.8 %collective-permute-start.22 = (f32[64,512]{1,0:T(8,128)S(1)}, f32[64,512]{1,0:T(8,128)S(1)}, u32[]{:S(2)}, u32[]{:S(2)}) collective-permute-start(f32[64,512]{1,0:T(8,128)S(1)} %get-tuple-element.6), channel_id=1, source_target_pairs={{0,16},{1,17},{2,18},{3,19},{4,20},{5,21},{6,22},{7,23},{8,24},{9,... | collective-permute-start | bytes 393224 | tf_op jit(solution)/shard_map/ppermute | solution.py:101
  161.9 22.7 %collective-permute-start.23 = (f32[64,512]{1,0:T(8,128)S(1)}, f32[64,512]{1,0:T(8,128)S(1)}, u32[]{:S(2)}, u32[]{:S(2)}) collective-permute-start(f32[64,512]{1,0:T(8,128)S(1)} %get-tuple-element.12), channel_id=1, source_target_pairs={{0,64},{1,65},{2,66},{3,67},{4,68},{5,69},{6,70},{7,71},{8,72},{9,... | collective-permute-start | bytes 393224 | tf_op jit(solution)/shard_map/ppermute | solution.py:101
  162.9 7.8 %collective-permute-start.30 = (f32[64]{0:T(128)S(1)}, f32[64]{0:T(128)S(1)}, u32[]{:S(2)}, u32[]{:S(2)}) collective-permute-start(f32[64]{0:T(128)S(1)} %get-tuple-element.27), channel_id=1, source_target_pairs={{0,66},{1,67},{2,64},{3,65},{4,70},{5,71},{6,68},{7,69},{8,74},{9,... | collective-permute-start | bytes 776 | tf_op jit(solution)/shard_map/ppermute | solution.py:101
  170.7 9.1 %collective-permute-start.33 = (f32[64]{0:T(128)S(1)}, f32[64]{0:T(128)S(1)}, u32[]{:S(2)}, u32[]{:S(2)}) collective-permute-start(f32[64]{0:T(128)S(1)} %get-tuple-element.24), channel_id=1, source_target_pairs={{0,60},{1,61},{2,62},{3,63},{4,56},{5,57},{6,58},{7,59},{8,52},{9,... | collective-permute-start | bytes 776 | tf_op jit(solution)/shard_map/ppermute | solution.py:101
  172.2 7.6 %collective-permute-start.34 = (f32[64]{0:T(128)S(1)}, f32[64]{0:T(128)S(1)}, u32[]{:S(2)}, u32[]{:S(2)}) collective-permute-start(f32[64]{0:T(128)S(1)} %get-tuple-element.23), channel_id=1, source_target_pairs={{0,78},{1,79},{2,76},{3,77},{4,74},{5,75},{6,72},{7,73},{8,70},{9,... | collective-permute-start | bytes 776 | tf_op jit(solution)/shard_map/ppermute | solution.py:101
  175.7 9.0 %collective-permute-start.35 = (f32[64]{0:T(128)S(1)}, f32[64]{0:T(128)S(1)}, u32[]{:S(2)}, u32[]{:S(2)}) collective-permute-start(f32[64]{0:T(128)S(1)} %get-tuple-element.22), channel_id=1, source_target_pairs={{0,126},{1,127},{2,124},{3,125},{4,122},{5,123},{6,120},{7,121},{8... | collective-permute-start | bytes 776 | tf_op jit(solution)/shard_map/ppermute | solution.py:101
  179.8 7.3 %collective-permute-start.24 = (f32[64,512]{1,0:T(8,128)S(1)}, f32[64,512]{1,0:T(8,128)S(1)}, u32[]{:S(2)}, u32[]{:S(2)}) collective-permute-start(f32[64,512]{1,0:T(8,128)S(1)} %get-tuple-element.11), channel_id=1, source_target_pairs={{0,80},{1,81},{2,82},{3,83},{4,84},{5,85},{6,86},{7,87},{8,88},{9,... | collective-permute-start | bytes 393224 | tf_op jit(solution)/shard_map/ppermute | solution.py:101
  184.6 7.5 %collective-permute-start.26 = (f32[64,512]{1,0:T(8,128)S(1)}, f32[64,512]{1,0:T(8,128)S(1)}, u32[]{:S(2)}, u32[]{:S(2)}) collective-permute-start(f32[64,512]{1,0:T(8,128)S(1)} %get-tuple-element.9), channel_id=1, source_target_pairs={{0,20},{1,21},{2,22},{3,23},{4,16},{5,17},{6,18},{7,19},{8,28},{9,... | collective-permute-start | bytes 393224 | tf_op jit(solution)/shard_map/ppermute | solution.py:101
  184.6 9.0 %collective-permute-start.27 = (f32[64,512]{1,0:T(8,128)S(1)}, f32[64,512]{1,0:T(8,128)S(1)}, u32[]{:S(2)}, u32[]{:S(2)}) collective-permute-start(f32[64,512]{1,0:T(8,128)S(1)} %get-tuple-element.8), channel_id=1, source_target_pairs={{0,68},{1,69},{2,70},{3,71},{4,64},{5,65},{6,66},{7,67},{8,76},{9,... | collective-permute-start | bytes 393224 | tf_op jit(solution)/shard_map/ppermute | solution.py:101
  184.7 9.0 %collective-permute-start.28 = (f32[64,512]{1,0:T(8,128)S(1)}, f32[64,512]{1,0:T(8,128)S(1)}, u32[]{:S(2)}, u32[]{:S(2)}) collective-permute-start(f32[64,512]{1,0:T(8,128)S(1)} %get-tuple-element.7), channel_id=1, source_target_pairs={{0,84},{1,85},{2,86},{3,87},{4,80},{5,81},{6,82},{7,83},{8,92},{9,... | collective-permute-start | bytes 393224 | tf_op jit(solution)/shard_map/ppermute | solution.py:101
  (15 other events, 182.8 us)

commit v7 on v5

--- a/solution.py
+++ b/solution.py
@@ -5,7 +5,8 @@
 
 NCLS = 512
 PAD = 128
-AXES = ("blk", "dp")
+AXES = ("y_lo", "x_hi", "x_lo", "z_hi", "z_lo", "y_hi", "core")
+CUBE = ("y_lo", "x_lo", "z_lo", "core")
 
 
 def indicator(labels):
@@ -110,8 +111,7 @@
     tr = with_side(train_grads, (train_scale,) + split_class(train_class), 0)
     te = with_side(test_grads, split_class(test_class), 4)
     te_all = cube_gather(te, test_mate, n)
-    tr_mine = cube_gather(tr, train_mate, n)
-    tr_other = lax.ppermute(tr_mine, AXES, core_pairs(n))
+    tr_all = lax.all_gather(tr, CUBE, axis=0, tiled=True)
     test_hot = indicator(join_class(te_all, k + 4))
 
     def weigh(t):
@@ -127,13 +127,9 @@
         )
         return part, per_class
 
-    part_m, pc_m = weigh(tr_mine)
-    part_o, pc_o = weigh(tr_other)
-    part = part_m + lax.ppermute(part_o, AXES, core_pairs(n))
-    train_attr = cube_reduce(
-        [part[o * rows:(o + 1) * rows] for o in range(8)], train_mate, n
-    )
-    test_part = jnp.sum((pc_m + pc_o) * test_hot.astype(jnp.float32), axis=1)
+    part, per_class = weigh(tr_all)
+    train_attr = lax.psum_scatter(part, CUBE, scatter_dimension=0, tiled=True)
+    test_part = jnp.sum(per_class * test_hot.astype(jnp.float32), axis=1)
     test_attr = cube_reduce(
         [test_part[o * rows:(o + 1) * rows] for o in range(8)], test_mate, n
     )
@@ -141,6 +137,7 @@
 
 
 def solution(mesh):
+    fine = jax.sharding.Mesh(mesh.devices.reshape((2,) * 7), AXES)
     in_specs = (
         P(AXES, None),
         P(AXES),
@@ -149,4 +146,4 @@
         P(AXES),
     )
     out_specs = (P(AXES, None), P(AXES))
-    return jax.shard_map(local, mesh=mesh, in_specs=in_specs, out_specs=out_specs, check_vma=False)
+    return jax.shard_map(local, mesh=fine, in_specs=in_specs, out_specs=out_specs, check_vma=False)

time: 166 us -> 195 us (1.17)
  waiting for transfers between devices: 87.3 us -> 119 us
  between operations: 1.12 us -> 14.3 us
  other arithmetic: 18.7 us -> 8.92 us
  starting transfers between devices: 38 us -> 29.7 us
  local copies, waits for them, and re-layouts: 1.06 us -> 3.85 us
    reduce_scatter x0 -> x1, waiting for transfers between devices: none -> 45 us  [local(): train_attr = lax.psum_scatter(part, CUBE, scatter_dimension=0, tiled=True)]
    all_gather x0 -> x1, waiting for transfers between devices: none -> 19.9 us  [local(): tr_all = lax.all_gather(tr, CUBE, axis=0, tiled=True)]
    ppermute x18 -> x9, waiting for transfers between devices: 66.6 us -> 48.2 us  [cube_gather(): got = lax.ppermute(buf, AXES, mate_pairs(n, a, mate))]
    ppermute x6 -> x3, waiting for transfers between devices: 20.7 us -> 6.3 us  [cube_reduce(): lax.ppermute(jnp.concatenate([blocks[o] for o in send]), AXES, mate_pairs...]
    ppermute x18 -> x9, starting transfers between devices: 31.7 us -> 21.6 us  [cube_gather(): got = lax.ppermute(buf, AXES, mate_pairs(n, a, mate))]
    unnamed x14 -> x7, other arithmetic: 8.3 us -> 0.86 us
    unnamed x6, local copies, waits for them, and re-layouts: 0.02 us -> 3.32 us
    dot_general x2 -> x1, matrix products: 17.8 us -> 15.2 us  [weigh(): lax.dot_general(t, te_all, (((1,), (1,)), ((), ())), preferred_element_ty...]
  transfers between devices with their start and end apart: 26 -> 14, of which waited for: 17 -> 11; matrix products, arithmetic and copies ran while one was open for 15% -> 3% of each run, Pallas kernels for 0% -> 0%
where the time goes in v7:
time: 195 us
  waiting for transfers between devices  119 us (61%)
  starting transfers between devices  29.7 us (15%)
  matrix products  18.4 us (9%)
  between operations  14.3 us (7%)
  other arithmetic  8.92 us (5%)
  local copies, waits for them, and re-layouts  3.85 us (2%)
    ppermute x9, waiting for transfers between devices, cube_gather(): got = lax.ppermute(buf, AXES, mate_pairs(n, a, mate))  48.2 us
    reduce_scatter x1, waiting for transfers between devices, local(): train_attr = lax.psum_scatter(part, CUBE, scatter_dimension=0, tiled=True)  45 us
    ppermute x9, starting transfers between devices, cube_gather(): got = lax.ppermute(buf, AXES, mate_pairs(n, a, mate))  21.6 us
    all_gather x1, waiting for transfers between devices, local(): tr_all = lax.all_gather(tr, CUBE, axis=0, tiled=True)  19.9 us
    dot_general x1, matrix products, weigh(): lax.dot_general(t, te_all, (((1,), (1,)), ((), ())), preferred_element_ty...  15.2 us
    ppermute x3, starting transfers between devices, cube_reduce(): lax.ppermute(jnp.concatenate([blocks[o] for o in send]), AXES, mate_pairs...  8.01 us
    ppermute x3, waiting for transfers between devices, cube_reduce(): lax.ppermute(jnp.concatenate([blocks[o] for o in send]), AXES, mate_pairs...  6.3 us
  transfers between devices with their start and end apart: 14, of which 11 were waited for; matrix products, arithmetic and copies ran while one was open for 3% of the time, Pallas kernels for 0%

profile of v7, /device:TPU:0, one launch (start us, length us, event | category | flops | bytes accessed | tf_op | source)
XLA Modules:
  0.0 194.6 jit_solution(11146954028574961510)
XLA Ops:
  7.3 0.7 fusion.7
  8.0 0.7 select_select_fusion.1
  8.7 2.3 %pad_maximum_fusion.3 = bf16[64,8320]{1,0:T(8,128)(2,1)} fusion(bf16[64,128]{1,0:T(8,128)(2,1)S(1)} %select_select_fusion.1, bf16[64,8192]{1,0:T(8,128)(2,1)} %param.5), kind=kLoop, calls=%fused_computation.8 | loop fusion | flops 2129920 | bytes 2129920 | tf_op jit(solution)/shard_map/concatenate | solution.py:23
  11.3 3.2 %collective-permute-start.1 = (bf16[64,2816]{1,0:T(8,128)(2,1)S(1)}, bf16[64,2816]{1,0:T(8,128)(2,1)S(1)}, u32[]{:S(2)}, u32[]{:S(2)}) collective-permute-start(bf16[64,2816]{1,0:T(8,128)(2,1)S(1)} %get-tuple-element.14), channel_id=1, source_target_pairs={{0,66},{1,67},{2,64},{3,65},{4,70},{5,71},{6,68},{7,69},{8,74},{9,... | collective-permute-start | bytes 1081352 | tf_op jit(solution)/shard_map/ppermute | solution.py:81
  14.5 4.0 %collective-permute-start.4 = (bf16[64,2816]{1,0:T(8,128)(2,1)S(1)}, bf16[64,2816]{1,0:T(8,128)(2,1)S(1)}, u32[]{:S(2)}, u32[]{:S(2)}) collective-permute-start(bf16[64,2816]{1,0:T(8,128)(2,1)S(1)} %get-tuple-element.15), channel_id=1, source_target_pairs={{0,12},{1,13},{2,14},{3,15},{4,8},{5,9},{6,10},{7,11},{8,4},{9,5},... | collective-permute-start | bytes 1081352 | tf_op jit(solution)/shard_map/ppermute | solution.py:81
  18.6 2.8 %collective-permute-start = (bf16[64,2688]{1,0:T(8,128)(2,1)S(1)}, bf16[64,2688]{1,0:T(8,128)(2,1)S(1)}, u32[]{:S(2)}, u32[]{:S(2)}) collective-permute-start(bf16[64,2688]{1,0:T(8,128)(2,1)S(1)} %slice.126), channel_id=1, source_target_pairs={{0,48},{1,49},{2,50},{3,51},{4,52},{5,53},{6,54},{7,55},{8,56},{9,... | collective-permute-start | bytes 1032200 | tf_op jit(solution)/shard_map/ppermute | solution.py:81
  21.5 7.6 %collective-permute-done = bf16[64,2688]{1,0:T(8,128)(2,1)S(1)} collective-permute-done((bf16[64,2688]{1,0:T(8,128)(2,1)S(1)}, bf16[64,2688]{1,0:T(8,128)(2,1)S(1)}, u32[]{:S(2)}, u32[]{:S(2)}) %collective-permute-start) | collective-permute-done | bytes 344096 | tf_op jit(solution)/shard_map/ppermute | solution.py:81
  29.1 0.5 collective-permute-start.6
  29.6 0.4 collective-permute-start.2
  30.1 2.8 %collective-permute-start.5 = (bf16[128,2816]{1,0:T(8,128)(2,1)S(1)}, bf16[128,2816]{1,0:T(8,128)(2,1)S(1)}, u32[]{:S(2)}, u32[]{:S(2)}) collective-permute-start(bf16[128,2816]{1,0:T(8,128)(2,1)S(1)} %pad_maximum_fusion.5), channel_id=1, source_target_pairs={{0,48},{1,49},{2,50},{3,51},{4,52},{5,53},{6,54},{7,55},{8,56},{9,... | collective-permute-start | bytes 2162696 | tf_op jit(solution)/shard_map/ppermute | solution.py:81
  32.9 13.2 %collective-permute-done.6 = bf16[128,2688]{1,0:T(8,128)(2,1)S(1)} collective-permute-done((bf16[128,2688]{1,0:T(8,128)(2,1)S(1)}, bf16[128,2688]{1,0:T(8,128)(2,1)S(1)}, u32[]{:S(2)}, u32[]{:S(2)}) %collective-permute-start.6) | collective-permute-done | bytes 688160 | tf_op jit(solution)/shard_map/ppermute | solution.py:81
  46.2 0.7 collective-permute-start.8
  47.3 2.8 %collective-permute-start.3 = (bf16[256,2816]{1,0:T(8,128)(2,1)S(1)}, bf16[256,2816]{1,0:T(8,128)(2,1)S(1)}, u32[]{:S(2)}, u32[]{:S(2)}) collective-permute-start(bf16[256,2816]{1,0:T(8,128)(2,1)S(1)} %pad_maximum_fusion), channel_id=1, source_target_pairs={{0,48},{1,49},{2,50},{3,51},{4,52},{5,53},{6,54},{7,55},{8,56},{9,... | collective-permute-start | bytes 4325384 | tf_op jit(solution)/shard_map/ppermute | solution.py:81
  50.2 4.4 %collective-permute-start.7 = (bf16[256,2816]{1,0:T(8,128)(2,1)S(1)}, bf16[256,2816]{1,0:T(8,128)(2,1)S(1)}, u32[]{:S(2)}, u32[]{:S(2)}) collective-permute-start(bf16[256,2816]{1,0:T(8,128)(2,1)S(1)} %pad_maximum_fusion.1), channel_id=1, source_target_pairs={{0,66},{1,67},{2,64},{3,65},{4,70},{5,71},{6,68},{7,69},{8,74},{9,... | collective-permute-start | bytes 4325384 | tf_op jit(solution)/shard_map/ppermute | solution.py:81
  54.8 22.3 %collective-permute-done.8 = bf16[256,2688]{1,0:T(8,128)(2,1)S(1)} collective-permute-done((bf16[256,2688]{1,0:T(8,128)(2,1)S(1)}, bf16[256,2688]{1,0:T(8,128)(2,1)S(1)}, u32[]{:S(2)}, u32[]{:S(2)}) %collective-permute-start.8) | collective-permute-done | bytes 1376288 | tf_op jit(solution)/shard_map/ppermute | solution.py:81
  77.1 2.3 %collective-permute-done.3 = bf16[256,2816]{1,0:T(8,128)(2,1)S(1)} collective-permute-done((bf16[256,2816]{1,0:T(8,128)(2,1)S(1)}, bf16[256,2816]{1,0:T(8,128)(2,1)S(1)}, u32[]{:S(2)}, u32[]{:S(2)}) %collective-permute-start.3) | collective-permute-done | bytes 1441824 | tf_op jit(solution)/shard_map/ppermute | solution.py:81
  79.5 2.6 %collective-permute-done.7 = bf16[256,2816]{1,0:T(8,128)(2,1)S(1)} collective-permute-done((bf16[256,2816]{1,0:T(8,128)(2,1)S(1)}, bf16[256,2816]{1,0:T(8,128)(2,1)S(1)}, u32[]{:S(2)}, u32[]{:S(2)}) %collective-permute-start.7) | collective-permute-done | bytes 1441824 | tf_op jit(solution)/shard_map/ppermute | solution.py:81
  83.1 3.3 %copy-done.1 = bf16[512,8320]{1,0:T(8,128)(2,1)} copy-done((bf16[512,8320]{1,0:T(8,128)(2,1)}, bf16[512,8320]{1,0:T(8,128)(2,1)S(1)}, u32[]{:S(2)}) %copy-start.1) | copy-done | bytes 8519704
  86.7 19.9 %all-gather.2.cloned.1.call-done = bf16[1024,8320]{1,0:T(8,128)(2,1)} async-done(((bf16[64,8320]{1,0:T(8,128)(2,1)}), bf16[1024,8320]{1,0:T(8,128)(2,1)}) %all-gather.2.cloned.1.call-update) | async-done | bytes 17039376 | tf_op jit(solution)/shard_map/all_gather | solution.py:114
  106.6 1.1 convert_reduce_fusion
  107.7 15.2 %tanh_convert_fusion = bf16[1024,512]{1,0:T(8,128)(2,1)S(1)} fusion(bf16[1024,8320]{1,0:T(8,128)(2,1)} %all-gather.2.cloned.1.call-done, bf16[512,8320]{1,0:T(8,128)(2,1)} %copy-done.1, f32[1024]{0:T(1024)S(1)} %convert_reduce_fusion), kind=kOutput, calls=%fused_computation.1 | convolution fusion | flops 8725200896 | bytes 26611712 | tf_op jit(solution)/shard_map/dot_general | solution.py:118
  122.9 2.1 %fusion.5 = f32[1024,512]{1,0:T(8,128)} fusion(bf16[1024,512]{1,0:T(8,128)(2,1)S(1)} %tanh_convert_fusion, s32[512]{0:T(512)S(1)} %add_reduce_fusion.1), kind=kOutput, calls=%fused_computation.20 | convolution fusion | flops 537133056 | bytes 3147776 | tf_op jit(solution)/shard_map/dot_general | solution.py:124
  125.0 1.4 add_reduce_fusion
  126.5 1.1 fusion.2
  127.7 2.5 %collective-permute-start.9 = (f32[256]{0:T(256)S(1)}, f32[256]{0:T(256)S(1)}, u32[]{:S(2)}, u32[]{:S(2)}) collective-permute-start(f32[256]{0:T(256)S(1)} %pad_maximum_fusion.8), channel_id=1, source_target_pairs={{0,48},{1,49},{2,50},{3,51},{4,52},{5,53},{6,54},{7,55},{8,56},{9,... | collective-permute-start | bytes 3080 | tf_op jit(solution)/shard_map/ppermute | solution.py:98
  130.2 2.3 %collective-permute-done.9 = f32[256]{0:T(256)S(1)} collective-permute-done((f32[256]{0:T(256)S(1)}, f32[256]{0:T(256)S(1)}, u32[]{:S(2)}, u32[]{:S(2)}) %collective-permute-start.9) | collective-permute-done | bytes 1056 | tf_op jit(solution)/shard_map/ppermute | solution.py:98
  132.7 2.7 %collective-permute-start.10 = (f32[128]{0:T(128)S(1)}, f32[128]{0:T(128)S(1)}, u32[]{:S(2)}, u32[]{:S(2)}) collective-permute-start(f32[128]{0:T(128)S(1)} %pad_maximum_fusion.9), channel_id=1, source_target_pairs={{0,66},{1,67},{2,64},{3,65},{4,70},{5,71},{6,68},{7,69},{8,74},{9,... | collective-permute-start | bytes 1544 | tf_op jit(solution)/shard_map/ppermute | solution.py:98
  135.3 2.1 %collective-permute-done.10 = f32[128]{0:T(128)S(1)} collective-permute-done((f32[128]{0:T(128)S(1)}, f32[128]{0:T(128)S(1)}, u32[]{:S(2)}, u32[]{:S(2)}) %collective-permute-start.10) | collective-permute-done | bytes 544 | tf_op jit(solution)/shard_map/ppermute | solution.py:98
  137.5 2.9 %collective-permute-start.11 = (f32[64]{0:T(128)S(1)}, f32[64]{0:T(128)S(1)}, u32[]{:S(2)}, u32[]{:S(2)}) collective-permute-start(f32[64]{0:T(128)S(1)} %slice_add_fusion), channel_id=1, source_target_pairs={{0,12},{1,13},{2,14},{3,15},{4,8},{5,9},{6,10},{7,11},{8,4},{9,5},... | collective-permute-start | bytes 776 | tf_op jit(solution)/shard_map/ppermute | solution.py:98
  140.4 1.9 collective-permute-done.11
  142.2 0.5 add_add_fusion
  142.8 45.0 %reduce-scatter.2.cloned.1.call-done = f32[64,512]{1,0:T(8,128)} async-done(((f32[1024,512]{1,0:T(8,128)}), f32[64,512]{1,0:T(8,128)}) %reduce-scatter.2.cloned.1.call-update) | async-done | bytes 131088 | tf_op jit(solution)/shard_map/reduce_scatter | solution.py:131
  (48 shorter events, 3.1 us)
Async XLA Ops:
  7.2 4.0 %copy-start.2 = (s32[64]{0:T(128)S(1)}, s32[64]{0:T(128)}, u32[]{:S(2)}) copy-start(s32[64]{0:T(128)} %param.9) | copy-start | bytes 772
  7.2 4.1 %copy-start = (bf16[64,8192]{1,0:T(8,128)(2,1)S(1)}, bf16[64,8192]{1,0:T(8,128)(2,1)}, u32[]{:S(2)}) copy-start(bf16[64,8192]{1,0:T(8,128)(2,1)} %param.8) | copy-start | bytes 3145732
  7.2 99.4 %all-gather.2.cloned.1.call-start = ((), (), s32[]{:S(2)}) async-start(), calls=%async_computation.1 | async-start | bytes 18104320 | tf_op jit(solution)/shard_map/all_gather | solution.py:114
  11.1 176.7 %reduce-scatter.2.cloned.1.call-start = ((), (), s32[]{:S(2)}) async-start(), calls=%async_computation.2 | async-start | bytes 2228224 | tf_op jit(solution)/shard_map/reduce_scatter | solution.py:131
  11.1 10.3 %slice-start = ((bf16[64,8192]{1,0:T(8,128)(2,1)}), bf16[64,5504]{1,0:T(8,128)(2,1)S(1)}, s32[]{:S(2)}) async-start(bf16[64,8192]{1,0:T(8,128)(2,1)} %param.8), calls=%async_computation.3 | async-start | bytes 1409024 | tf_op jit(solution)/shard_map/slice | solution.py:78
  11.3 18.3 %collective-permute-start.1 = (bf16[64,2816]{1,0:T(8,128)(2,1)S(1)}, bf16[64,2816]{1,0:T(8,128)(2,1)S(1)}, u32[]{:S(2)}, u32[]{:S(2)}) collective-permute-start(bf16[64,2816]{1,0:T(8,128)(2,1)S(1)} %get-tuple-element.14), channel_id=1, source_target_pairs={{0,66},{1,67},{2,64},{3,65},{4,70},{5,71},{6,68},{7,69},{8,74},{9,... | collective-permute-start | bytes 1081352 | tf_op jit(solution)/shard_map/ppermute | solution.py:81
  14.5 15.5 %collective-permute-start.4 = (bf16[64,2816]{1,0:T(8,128)(2,1)S(1)}, bf16[64,2816]{1,0:T(8,128)(2,1)S(1)}, u32[]{:S(2)}, u32[]{:S(2)}) collective-permute-start(bf16[64,2816]{1,0:T(8,128)(2,1)S(1)} %get-tuple-element.15), channel_id=1, source_target_pairs={{0,12},{1,13},{2,14},{3,15},{4,8},{5,9},{6,10},{7,11},{8,4},{9,5},... | collective-permute-start | bytes 1081352 | tf_op jit(solution)/shard_map/ppermute | solution.py:81
  18.6 10.5 %collective-permute-start = (bf16[64,2688]{1,0:T(8,128)(2,1)S(1)}, bf16[64,2688]{1,0:T(8,128)(2,1)S(1)}, u32[]{:S(2)}, u32[]{:S(2)}) collective-permute-start(bf16[64,2688]{1,0:T(8,128)(2,1)S(1)} %slice.126), channel_id=1, source_target_pairs={{0,48},{1,49},{2,50},{3,51},{4,52},{5,53},{6,54},{7,55},{8,56},{9,... | collective-permute-start | bytes 1032200 | tf_op jit(solution)/shard_map/ppermute | solution.py:81
  29.1 17.0 %collective-permute-start.6 = (bf16[128,2688]{1,0:T(8,128)(2,1)S(1)}, bf16[128,2688]{1,0:T(8,128)(2,1)S(1)}, u32[]{:S(2)}, u32[]{:S(2)}) collective-permute-start(bf16[128,2688]{1,0:T(8,128)(2,1)S(1)} %pad_maximum_fusion.6), channel_id=1, source_target_pairs={{0,66},{1,67},{2,64},{3,65},{4,70},{5,71},{6,68},{7,69},{8,74},{9,... | collective-permute-start | bytes 2064392 | tf_op jit(solution)/shard_map/ppermute | solution.py:81
  29.6 17.6 %collective-permute-start.2 = (bf16[128,2816]{1,0:T(8,128)(2,1)S(1)}, bf16[128,2816]{1,0:T(8,128)(2,1)S(1)}, u32[]{:S(2)}, u32[]{:S(2)}) collective-permute-start(bf16[128,2816]{1,0:T(8,128)(2,1)S(1)} %pad_maximum_fusion.4), channel_id=1, source_target_pairs={{0,12},{1,13},{2,14},{3,15},{4,8},{5,9},{6,10},{7,11},{8,4},{9,5},... | collective-permute-start | bytes 2162696 | tf_op jit(solution)/shard_map/ppermute | solution.py:81
  30.1 20.1 %collective-permute-start.5 = (bf16[128,2816]{1,0:T(8,128)(2,1)S(1)}, bf16[128,2816]{1,0:T(8,128)(2,1)S(1)}, u32[]{:S(2)}, u32[]{:S(2)}) collective-permute-start(bf16[128,2816]{1,0:T(8,128)(2,1)S(1)} %pad_maximum_fusion.5), channel_id=1, source_target_pairs={{0,48},{1,49},{2,50},{3,51},{4,52},{5,53},{6,54},{7,55},{8,56},{9,... | collective-permute-start | bytes 2162696 | tf_op jit(solution)/shard_map/ppermute | solution.py:81
  46.2 30.8 %collective-permute-start.8 = (bf16[256,2688]{1,0:T(8,128)(2,1)S(1)}, bf16[256,2688]{1,0:T(8,128)(2,1)S(1)}, u32[]{:S(2)}, u32[]{:S(2)}) collective-permute-start(bf16[256,2688]{1,0:T(8,128)(2,1)S(1)} %pad_maximum_fusion.2), channel_id=1, source_target_pairs={{0,12},{1,13},{2,14},{3,15},{4,8},{5,9},{6,10},{7,11},{8,4},{9,5},... | collective-permute-start | bytes 4128776 | tf_op jit(solution)/shard_map/ppermute | solution.py:81
  47.3 32.1 %collective-permute-start.3 = (bf16[256,2816]{1,0:T(8,128)(2,1)S(1)}, bf16[256,2816]{1,0:T(8,128)(2,1)S(1)}, u32[]{:S(2)}, u32[]{:S(2)}) collective-permute-start(bf16[256,2816]{1,0:T(8,128)(2,1)S(1)} %pad_maximum_fusion), channel_id=1, source_target_pairs={{0,48},{1,49},{2,50},{3,51},{4,52},{5,53},{6,54},{7,55},{8,56},{9,... | collective-permute-start | bytes 4325384 | tf_op jit(solution)/shard_map/ppermute | solution.py:81
  50.2 31.8 %collective-permute-start.7 = (bf16[256,2816]{1,0:T(8,128)(2,1)S(1)}, bf16[256,2816]{1,0:T(8,128)(2,1)S(1)}, u32[]{:S(2)}, u32[]{:S(2)}) collective-permute-start(bf16[256,2816]{1,0:T(8,128)(2,1)S(1)} %pad_maximum_fusion.1), channel_id=1, source_target_pairs={{0,66},{1,67},{2,64},{3,65},{4,70},{5,71},{6,68},{7,69},{8,74},{9,... | collective-permute-start | bytes 4325384 | tf_op jit(solution)/shard_map/ppermute | solution.py:81
  83.1 3.3 %copy-start.1 = (bf16[512,8320]{1,0:T(8,128)(2,1)}, bf16[512,8320]{1,0:T(8,128)(2,1)S(1)}, u32[]{:S(2)}) copy-start(bf16[512,8320]{1,0:T(8,128)(2,1)S(1)} %maximum_dynamic-update-slice_fusion) | copy-start | bytes 25559044
  127.7 4.8 %collective-permute-start.9 = (f32[256]{0:T(256)S(1)}, f32[256]{0:T(256)S(1)}, u32[]{:S(2)}, u32[]{:S(2)}) collective-permute-start(f32[256]{0:T(256)S(1)} %pad_maximum_fusion.8), channel_id=1, source_target_pairs={{0,48},{1,49},{2,50},{3,51},{4,52},{5,53},{6,54},{7,55},{8,56},{9,... | collective-permute-start | bytes 3080 | tf_op jit(solution)/shard_map/ppermute | solution.py:98
  132.7 4.8 %collective-permute-start.10 = (f32[128]{0:T(128)S(1)}, f32[128]{0:T(128)S(1)}, u32[]{:S(2)}, u32[]{:S(2)}) collective-permute-start(f32[128]{0:T(128)S(1)} %pad_maximum_fusion.9), channel_id=1, source_target_pairs={{0,66},{1,67},{2,64},{3,65},{4,70},{5,71},{6,68},{7,69},{8,74},{9,... | collective-permute-start | bytes 1544 | tf_op jit(solution)/shard_map/ppermute | solution.py:98
  137.5 4.8 %collective-permute-start.11 = (f32[64]{0:T(128)S(1)}, f32[64]{0:T(128)S(1)}, u32[]{:S(2)}, u32[]{:S(2)}) collective-permute-start(f32[64]{0:T(128)S(1)} %slice_add_fusion), channel_id=1, source_target_pairs={{0,12},{1,13},{2,14},{3,15},{4,8},{5,9},{6,10},{7,11},{8,4},{9,5},... | collective-permute-start | bytes 776 | tf_op jit(solution)/shard_map/ppermute | solution.py:98
Sparse Core Ops, SparseCore 0:
  11.2 95.3 all-gather.1
  125.2 62.5 reduce-scatter.1

commit v8 on v5

--- a/solution.py
+++ b/solution.py
@@ -6,6 +6,8 @@
 NCLS = 512
 PAD = 128
 AXES = ("blk", "dp")
+THREE = ((0, 1, 2), (1, 2, 0), (2, 0, 1))
+TWO = ((0, 1, 2), (2, 0, 1))
 
 
 def indicator(labels):
@@ -67,13 +69,13 @@
     return [(L, L ^ 1) for L in range(n)]
 
 
-def cube_gather(shard, mate, n):
+def cube_gather(shard, mate, n, orders):
     cols = shard.shape[1]
     tiles = cols // 128
-    cut = [0, (tiles // 3) * 128, (2 * tiles // 3) * 128, cols]
+    m = len(orders)
+    cut = [(tiles * p // m) * 128 for p in range(m)] + [cols]
     parts = []
-    for p in range(3):
-        order = [(p + s) % 3 for s in range(3)]
+    for p, order in enumerate(orders):
         buf = shard[:, cut[p]:cut[p + 1]]
         labs = [0]
         for a in order:
@@ -83,7 +85,7 @@
         rows = shard.shape[0]
         parts.append({o: buf[i * rows:(i + 1) * rows] for i, o in enumerate(labs)})
     return jnp.concatenate(
-        [jnp.concatenate([parts[p][o] for p in range(3)], axis=1) for o in range(8)]
+        [jnp.concatenate([parts[p][o] for p in range(m)], axis=1) for o in range(8)]
     )
 
 
@@ -109,8 +111,8 @@
     rows = train_grads.shape[0]
     tr = with_side(train_grads, (train_scale,) + split_class(train_class), 0)
     te = with_side(test_grads, split_class(test_class), 4)
-    te_all = cube_gather(te, test_mate, n)
-    tr_mine = cube_gather(tr, train_mate, n)
+    te_all = cube_gather(te, test_mate, n, TWO)
+    tr_mine = cube_gather(tr, train_mate, n, THREE)
     tr_other = lax.ppermute(tr_mine, AXES, core_pairs(n))
     test_hot = indicator(join_class(te_all, k + 4))
 

time: 166 us -> 158 us (0.952)
  starting transfers between devices: 38 us -> 29.3 us
    ppermute x18 -> x15, starting transfers between devices: 31.7 us -> 23.7 us  [cube_gather(): got = lax.ppermute(buf, AXES, mate_pairs(n, a, mate))]
    ppermute x18 -> x15, waiting for transfers between devices: 66.6 us -> 66.5 us  [cube_gather(): got = lax.ppermute(buf, AXES, mate_pairs(n, a, mate))]
  transfers between devices with their start and end apart: 26 -> 23, of which waited for: 17 -> 17; matrix products, arithmetic and copies ran while one was open for 15% -> 16% of each run, Pallas kernels for 0% -> 0%
where the time goes in v8:
time: 158 us
  waiting for transfers between devices  87.8 us (56%)
  starting transfers between devices  29.3 us (19%)
  matrix products  20 us (13%)
  other arithmetic  18.8 us (12%)
    ppermute x15, waiting for transfers between devices, cube_gather(): got = lax.ppermute(buf, AXES, mate_pairs(n, a, mate))  66.5 us
    ppermute x15, starting transfers between devices, cube_gather(): got = lax.ppermute(buf, AXES, mate_pairs(n, a, mate))  23.7 us
    ppermute x6, waiting for transfers between devices, cube_reduce(): lax.ppermute(jnp.concatenate([blocks[o] for o in send]), AXES, mate_pairs...  21.4 us
    dot_general x2, matrix products, weigh(): lax.dot_general(t, te_all, (((1,), (1,)), ((), ())), preferred_element_ty...  17.8 us
    unnamed x14, other arithmetic  8.38 us
    ppermute x6, starting transfers between devices, cube_reduce(): lax.ppermute(jnp.concatenate([blocks[o] for o in send]), AXES, mate_pairs...  5.21 us
  transfers between devices with their start and end apart: 23, of which 17 were waited for; matrix products, arithmetic and copies ran while one was open for 16% of the time, Pallas kernels for 0%

profile of v8, /device:TPU:0, one launch (start us, length us, event | category | flops | bytes accessed | tf_op | source)
XLA Modules:
  0.0 158.1 jit_solution(14945276229073394686)
XLA Ops:
  2.2 1.1 fusion.23
  3.4 1.7 %collective-permute-start.1 = (bf16[64,2816]{1,0:T(8,128)(2,1)S(1)}, bf16[64,2816]{1,0:T(8,128)(2,1)S(1)}, u32[]{:S(2)}, u32[]{:S(2)}) collective-permute-start(bf16[64,2816]{1,0:T(8,128)(2,1)S(1)} %get-tuple-element.30), channel_id=1, source_target_pairs={{0,64},{1,65},{2,66},{3,67},{4,68},{5,69},{6,70},{7,71},{8,72},{9,... | collective-permute-start | bytes 1081352 | tf_op jit(solution)/shard_map/ppermute | solution.py:82
  5.1 1.9 %collective-permute-start.4 = (bf16[64,2816]{1,0:T(8,128)(2,1)S(1)}, bf16[64,2816]{1,0:T(8,128)(2,1)S(1)}, u32[]{:S(2)}, u32[]{:S(2)}) collective-permute-start(bf16[64,2816]{1,0:T(8,128)(2,1)S(1)} %get-tuple-element.31), channel_id=1, source_target_pairs={{0,4},{1,5},{2,6},{3,7},{4,0},{5,1},{6,2},{7,3},{8,12},{9,13},{10,... | collective-permute-start | bytes 1081352 | tf_op jit(solution)/shard_map/ppermute | solution.py:82
  7.1 1.6 collective-permute-start
  8.8 2.6 %collective-permute-start.10 = (bf16[64,4224]{1,0:T(8,128)(2,1)S(1)}, bf16[64,4224]{1,0:T(8,128)(2,1)S(1)}, u32[]{:S(2)}, u32[]{:S(2)}) collective-permute-start(bf16[64,4224]{1,0:T(8,128)(2,1)S(1)} %pad_maximum_fusion.10), channel_id=1, source_target_pairs={{0,12},{1,13},{2,14},{3,15},{4,8},{5,9},{6,10},{7,11},{8,4},{9,5},... | collective-permute-start | bytes 1622024 | tf_op jit(solution)/shard_map/ppermute | solution.py:82
  11.5 2.2 %collective-permute-start.9 = (bf16[64,4096]{1,0:T(8,128)(2,1)S(1)}, bf16[64,4096]{1,0:T(8,128)(2,1)S(1)}, u32[]{:S(2)}, u32[]{:S(2)}) collective-permute-start(bf16[64,4096]{1,0:T(8,128)(2,1)S(1)} %slice.239), channel_id=1, source_target_pairs={{0,48},{1,49},{2,50},{3,51},{4,52},{5,53},{6,54},{7,55},{8,56},{9,... | collective-permute-start | bytes 1572872 | tf_op jit(solution)/shard_map/ppermute | solution.py:82
  14.8 1.6 %collective-permute-done = bf16[64,2688]{1,0:T(8,128)(2,1)S(1)} collective-permute-done((bf16[64,2688]{1,0:T(8,128)(2,1)S(1)}, bf16[64,2688]{1,0:T(8,128)(2,1)S(1)}, u32[]{:S(2)}, u32[]{:S(2)}) %collective-permute-start) | collective-permute-done | bytes 344096 | tf_op jit(solution)/shard_map/ppermute | solution.py:82
  17.5 1.6 collective-permute-start.5
  19.0 6.3 %collective-permute-done.9 = bf16[64,4096]{1,0:T(8,128)(2,1)S(1)} collective-permute-done((bf16[64,4096]{1,0:T(8,128)(2,1)S(1)}, bf16[64,4096]{1,0:T(8,128)(2,1)S(1)}, u32[]{:S(2)}, u32[]{:S(2)}) %collective-permute-start.9) | collective-permute-done | bytes 524320 | tf_op jit(solution)/shard_map/ppermute | solution.py:82
  25.4 2.3 %collective-permute-start.12 = (bf16[128,4096]{1,0:T(8,128)(2,1)S(1)}, bf16[128,4096]{1,0:T(8,128)(2,1)S(1)}, u32[]{:S(2)}, u32[]{:S(2)}) collective-permute-start(bf16[128,4096]{1,0:T(8,128)(2,1)S(1)} %pad_maximum_fusion.6), channel_id=1, source_target_pairs={{0,66},{1,67},{2,64},{3,65},{4,70},{5,71},{6,68},{7,69},{8,74},{9,... | collective-permute-start | bytes 3145736 | tf_op jit(solution)/shard_map/ppermute | solution.py:82
  27.7 2.2 %collective-permute-start.11 = (bf16[128,4224]{1,0:T(8,128)(2,1)S(1)}, bf16[128,4224]{1,0:T(8,128)(2,1)S(1)}, u32[]{:S(2)}, u32[]{:S(2)}) collective-permute-start(bf16[128,4224]{1,0:T(8,128)(2,1)S(1)} %pad_maximum_fusion.5), channel_id=1, source_target_pairs={{0,48},{1,49},{2,50},{3,51},{4,52},{5,53},{6,54},{7,55},{8,56},{9,... | collective-permute-start | bytes 3244040 | tf_op jit(solution)/shard_map/ppermute | solution.py:82
  29.9 2.3 %collective-permute-done.6 = bf16[128,2688]{1,0:T(8,128)(2,1)S(1)} collective-permute-done((bf16[128,2688]{1,0:T(8,128)(2,1)S(1)}, bf16[128,2688]{1,0:T(8,128)(2,1)S(1)}, u32[]{:S(2)}, u32[]{:S(2)}) %collective-permute-start.6) | collective-permute-done | bytes 688160 | tf_op jit(solution)/shard_map/ppermute | solution.py:82
  34.1 1.6 collective-permute-start.3
  35.7 2.8 %collective-permute-start.7 = (bf16[256,2816]{1,0:T(8,128)(2,1)S(1)}, bf16[256,2816]{1,0:T(8,128)(2,1)S(1)}, u32[]{:S(2)}, u32[]{:S(2)}) collective-permute-start(bf16[256,2816]{1,0:T(8,128)(2,1)S(1)} %pad_maximum_fusion.3), channel_id=1, source_target_pairs={{0,64},{1,65},{2,66},{3,67},{4,68},{5,69},{6,70},{7,71},{8,72},{9,... | collective-permute-start | bytes 4325384 | tf_op jit(solution)/shard_map/ppermute | solution.py:82
  38.6 10.9 %collective-permute-done.12 = bf16[128,4096]{1,0:T(8,128)(2,1)S(1)} collective-permute-done((bf16[128,4096]{1,0:T(8,128)(2,1)S(1)}, bf16[128,4096]{1,0:T(8,128)(2,1)S(1)}, u32[]{:S(2)}, u32[]{:S(2)}) %collective-permute-start.12) | collective-permute-done | bytes 1048608 | tf_op jit(solution)/shard_map/ppermute | solution.py:82
  50.5 1.8 %collective-permute-done.11 = bf16[128,4224]{1,0:T(8,128)(2,1)S(1)} collective-permute-done((bf16[128,4224]{1,0:T(8,128)(2,1)S(1)}, bf16[128,4224]{1,0:T(8,128)(2,1)S(1)}, u32[]{:S(2)}, u32[]{:S(2)}) %collective-permute-start.11) | collective-permute-done | bytes 1081376 | tf_op jit(solution)/shard_map/ppermute | solution.py:82
  52.4 1.1 collective-permute-start.13
  54.7 8.0 %collective-permute-done.8 = bf16[256,2688]{1,0:T(8,128)(2,1)S(1)} collective-permute-done((bf16[256,2688]{1,0:T(8,128)(2,1)S(1)}, bf16[256,2688]{1,0:T(8,128)(2,1)S(1)}, u32[]{:S(2)}, u32[]{:S(2)}) %collective-permute-start.8) | collective-permute-done | bytes 1376288 | tf_op jit(solution)/shard_map/ppermute | solution.py:82
  62.8 1.7 %collective-permute-done.3 = bf16[256,2816]{1,0:T(8,128)(2,1)S(1)} collective-permute-done((bf16[256,2816]{1,0:T(8,128)(2,1)S(1)}, bf16[256,2816]{1,0:T(8,128)(2,1)S(1)}, u32[]{:S(2)}, u32[]{:S(2)}) %collective-permute-start.3) | collective-permute-done | bytes 1441824 | tf_op jit(solution)/shard_map/ppermute | solution.py:82
  67.0 28.4 %collective-permute-done.14 = bf16[256,4096]{1,0:T(8,128)(2,1)S(1)} collective-permute-done((bf16[256,4096]{1,0:T(8,128)(2,1)S(1)}, bf16[256,4096]{1,0:T(8,128)(2,1)S(1)}, u32[]{:S(2)}, u32[]{:S(2)}) %collective-permute-start.14) | collective-permute-done | bytes 2097184 | tf_op jit(solution)/shard_map/ppermute | solution.py:82
  95.6 3.7 %collective-permute-done.13 = bf16[256,4224]{1,0:T(8,128)(2,1)S(1)} collective-permute-done((bf16[256,4224]{1,0:T(8,128)(2,1)S(1)}, bf16[256,4224]{1,0:T(8,128)(2,1)S(1)}, u32[]{:S(2)}, u32[]{:S(2)}) %collective-permute-start.13) | collective-permute-done | bytes 2162720 | tf_op jit(solution)/shard_map/ppermute | solution.py:82
  103.7 1.1 maximum_dynamic-update-slice_fusion.9
  105.8 1.2 add_reduce_fusion.2
  107.1 9.7 %fusion.29 = f32[512,512]{1,0:T(8,128)S(1)} fusion(bf16[512,8320]{1,0:T(8,128)(2,1)} %collective-permute-done.15, bf16[512,8320]{1,0:T(8,128)(2,1)} %maximum_dynamic-update-slice_fusion.8), kind=kOutput, calls=%fused_computation.100 | convolution fusion | flops 4362076160 | bytes 18087936 | tf_op jit(solution)/shard_map/dot_general | solution.py:120
  118.6 8.1 %fusion.2 = bf16[512,512]{1,0:T(8,128)(2,1)S(1)} fusion(bf16[512,8320]{1,0:T(8,128)(2,1)S(1)} %maximum_dynamic-update-slice_fusion, bf16[512,8320]{1,0:T(8,128)(2,1)} %maximum_dynamic-update-slice_fusion.8, f32[512]{0:T(512)S(1)} %convert_reduce_fusion.1), kind=kOutput, calls=%fused_computation.10 | convolution fusion | flops 4362600448 | bytes 17565696 | tf_op jit(solution)/shard_map/dot_general | solution.py:120
  127.3 1.2 add_reduce_fusion
  130.0 2.1 %collective-permute-start.20 = (f32[256]{0:T(256)S(1)}, f32[256]{0:T(256)S(1)}, u32[]{:S(2)}, u32[]{:S(2)}) collective-permute-start(f32[256]{0:T(256)S(1)} %pad_maximum_fusion.14), channel_id=1, source_target_pairs={{0,48},{1,49},{2,50},{3,51},{4,52},{5,53},{6,54},{7,55},{8,56},{9,... | collective-permute-start | bytes 3080 | tf_op jit(solution)/shard_map/ppermute | solution.py:99
  132.1 2.7 %collective-permute-done.20 = f32[256]{0:T(256)S(1)} collective-permute-done((f32[256]{0:T(256)S(1)}, f32[256]{0:T(256)S(1)}, u32[]{:S(2)}, u32[]{:S(2)}) %collective-permute-start.20) | collective-permute-done | bytes 1056 | tf_op jit(solution)/shard_map/ppermute | solution.py:99
  134.9 9.3 %collective-permute-done.17 = f32[256,512]{1,0:T(8,128)S(1)} collective-permute-done((f32[256,512]{1,0:T(8,128)S(1)}, f32[256,512]{1,0:T(8,128)S(1)}, u32[]{:S(2)}, u32[]{:S(2)}) %collective-permute-start.17) | collective-permute-done | bytes 524320 | tf_op jit(solution)/shard_map/ppermute | solution.py:99
  145.5 3.7 %collective-permute-done.21 = f32[128]{0:T(128)S(1)} collective-permute-done((f32[128]{0:T(128)S(1)}, f32[128]{0:T(128)S(1)}, u32[]{:S(2)}, u32[]{:S(2)}) %collective-permute-start.21) | collective-permute-done | bytes 544 | tf_op jit(solution)/shard_map/ppermute | solution.py:99
  150.0 2.2 %collective-permute-done.18 = f32[128,512]{1,0:T(8,128)S(1)} collective-permute-done((f32[128,512]{1,0:T(8,128)S(1)}, f32[128,512]{1,0:T(8,128)S(1)}, u32[]{:S(2)}, u32[]{:S(2)}) %collective-permute-start.18) | collective-permute-done | bytes 262176 | tf_op jit(solution)/shard_map/ppermute | solution.py:99
  154.5 2.8 %collective-permute-done.19 = f32[64,512]{1,0:T(8,128)S(1)} collective-permute-done((f32[64,512]{1,0:T(8,128)S(1)}, f32[64,512]{1,0:T(8,128)S(1)}, u32[]{:S(2)}, u32[]{:S(2)}) %collective-permute-start.19) | collective-permute-done | bytes 131104 | tf_op jit(solution)/shard_map/ppermute | solution.py:99
  (92 shorter events, 25.6 us)
Async XLA Ops:
  0.6 6.4 %copy-start = (bf16[64,8192]{1,0:T(8,128)(2,1)S(1)}, bf16[64,8192]{1,0:T(8,128)(2,1)}, u32[]{:S(2)}) copy-start(bf16[64,8192]{1,0:T(8,128)(2,1)} %param.5) | copy-start | bytes 3145732
  0.6 8.0 %copy-start.2 = (s32[64]{0:T(128)S(1)}, s32[64]{0:T(128)}, u32[]{:S(2)}) copy-start(s32[64]{0:T(128)} %param.9) | copy-start | bytes 772
  0.7 8.1 %copy-start.1 = (bf16[64,8192]{1,0:T(8,128)(2,1)S(1)}, bf16[64,8192]{1,0:T(8,128)(2,1)}, u32[]{:S(2)}) copy-start(bf16[64,8192]{1,0:T(8,128)(2,1)} %param.8) | copy-start | bytes 3145732
  3.4 13.6 %collective-permute-start.1 = (bf16[64,2816]{1,0:T(8,128)(2,1)S(1)}, bf16[64,2816]{1,0:T(8,128)(2,1)S(1)}, u32[]{:S(2)}, u32[]{:S(2)}) collective-permute-start(bf16[64,2816]{1,0:T(8,128)(2,1)S(1)} %get-tuple-element.30), channel_id=1, source_target_pairs={{0,64},{1,65},{2,66},{3,67},{4,68},{5,69},{6,70},{7,71},{8,72},{9,... | collective-permute-start | bytes 1081352 | tf_op jit(solution)/shard_map/ppermute | solution.py:82
  5.1 12.3 %collective-permute-start.4 = (bf16[64,2816]{1,0:T(8,128)(2,1)S(1)}, bf16[64,2816]{1,0:T(8,128)(2,1)S(1)}, u32[]{:S(2)}, u32[]{:S(2)}) collective-permute-start(bf16[64,2816]{1,0:T(8,128)(2,1)S(1)} %get-tuple-element.31), channel_id=1, source_target_pairs={{0,4},{1,5},{2,6},{3,7},{4,0},{5,1},{6,2},{7,3},{8,12},{9,13},{10,... | collective-permute-start | bytes 1081352 | tf_op jit(solution)/shard_map/ppermute | solution.py:82
  7.1 9.3 %collective-permute-start = (bf16[64,2688]{1,0:T(8,128)(2,1)S(1)}, bf16[64,2688]{1,0:T(8,128)(2,1)S(1)}, u32[]{:S(2)}, u32[]{:S(2)}) collective-permute-start(bf16[64,2688]{1,0:T(8,128)(2,1)S(1)} %slice.218), channel_id=1, source_target_pairs={{0,16},{1,17},{2,18},{3,19},{4,20},{5,21},{6,22},{7,23},{8,24},{9,... | collective-permute-start | bytes 1032200 | tf_op jit(solution)/shard_map/ppermute | solution.py:82
  8.8 5.9 %slice-start = ((bf16[64,8192]{1,0:T(8,128)(2,1)}), bf16[64,5504]{1,0:T(8,128)(2,1)S(1)}, s32[]{:S(2)}) async-start(bf16[64,8192]{1,0:T(8,128)(2,1)} %param.5), calls=%async_computation | async-start | bytes 1409024 | tf_op jit(solution)/shard_map/slice | solution.py:79
  8.8 18.8 %collective-permute-start.10 = (bf16[64,4224]{1,0:T(8,128)(2,1)S(1)}, bf16[64,4224]{1,0:T(8,128)(2,1)S(1)}, u32[]{:S(2)}, u32[]{:S(2)}) collective-permute-start(bf16[64,4224]{1,0:T(8,128)(2,1)S(1)} %pad_maximum_fusion.10), channel_id=1, source_target_pairs={{0,12},{1,13},{2,14},{3,15},{4,8},{5,9},{6,10},{7,11},{8,4},{9,5},... | collective-permute-start | bytes 1622024 | tf_op jit(solution)/shard_map/ppermute | solution.py:82
  11.5 13.8 %collective-permute-start.9 = (bf16[64,4096]{1,0:T(8,128)(2,1)S(1)}, bf16[64,4096]{1,0:T(8,128)(2,1)S(1)}, u32[]{:S(2)}, u32[]{:S(2)}) collective-permute-start(bf16[64,4096]{1,0:T(8,128)(2,1)S(1)} %slice.239), channel_id=1, source_target_pairs={{0,48},{1,49},{2,50},{3,51},{4,52},{5,53},{6,54},{7,55},{8,56},{9,... | collective-permute-start | bytes 1572872 | tf_op jit(solution)/shard_map/ppermute | solution.py:82
  16.5 15.8 %collective-permute-start.6 = (bf16[128,2688]{1,0:T(8,128)(2,1)S(1)}, bf16[128,2688]{1,0:T(8,128)(2,1)S(1)}, u32[]{:S(2)}, u32[]{:S(2)}) collective-permute-start(bf16[128,2688]{1,0:T(8,128)(2,1)S(1)} %pad_maximum_fusion.9), channel_id=1, source_target_pairs={{0,64},{1,65},{2,66},{3,67},{4,68},{5,69},{6,70},{7,71},{8,72},{9,... | collective-permute-start | bytes 2064392 | tf_op jit(solution)/shard_map/ppermute | solution.py:82
  17.0 16.9 %collective-permute-start.2 = (bf16[128,2816]{1,0:T(8,128)(2,1)S(1)}, bf16[128,2816]{1,0:T(8,128)(2,1)S(1)}, u32[]{:S(2)}, u32[]{:S(2)}) collective-permute-start(bf16[128,2816]{1,0:T(8,128)(2,1)S(1)} %pad_maximum_fusion.7), channel_id=1, source_target_pairs={{0,4},{1,5},{2,6},{3,7},{4,0},{5,1},{6,2},{7,3},{8,12},{9,13},{10,... | collective-permute-start | bytes 2162696 | tf_op jit(solution)/shard_map/ppermute | solution.py:82
  17.5 18.2 %collective-permute-start.5 = (bf16[128,2816]{1,0:T(8,128)(2,1)S(1)}, bf16[128,2816]{1,0:T(8,128)(2,1)S(1)}, u32[]{:S(2)}, u32[]{:S(2)}) collective-permute-start(bf16[128,2816]{1,0:T(8,128)(2,1)S(1)} %pad_maximum_fusion.8), channel_id=1, source_target_pairs={{0,16},{1,17},{2,18},{3,19},{4,20},{5,21},{6,22},{7,23},{8,24},{9,... | collective-permute-start | bytes 2162696 | tf_op jit(solution)/shard_map/ppermute | solution.py:82
  25.4 24.1 %collective-permute-start.12 = (bf16[128,4096]{1,0:T(8,128)(2,1)S(1)}, bf16[128,4096]{1,0:T(8,128)(2,1)S(1)}, u32[]{:S(2)}, u32[]{:S(2)}) collective-permute-start(bf16[128,4096]{1,0:T(8,128)(2,1)S(1)} %pad_maximum_fusion.6), channel_id=1, source_target_pairs={{0,66},{1,67},{2,64},{3,65},{4,70},{5,71},{6,68},{7,69},{8,74},{9,... | collective-permute-start | bytes 3145736 | tf_op jit(solution)/shard_map/ppermute | solution.py:82
  27.7 24.6 %collective-permute-start.11 = (bf16[128,4224]{1,0:T(8,128)(2,1)S(1)}, bf16[128,4224]{1,0:T(8,128)(2,1)S(1)}, u32[]{:S(2)}, u32[]{:S(2)}) collective-permute-start(bf16[128,4224]{1,0:T(8,128)(2,1)S(1)} %pad_maximum_fusion.5), channel_id=1, source_target_pairs={{0,48},{1,49},{2,50},{3,51},{4,52},{5,53},{6,54},{7,55},{8,56},{9,... | collective-permute-start | bytes 3244040 | tf_op jit(solution)/shard_map/ppermute | solution.py:82
  32.3 30.4 %collective-permute-start.8 = (bf16[256,2688]{1,0:T(8,128)(2,1)S(1)}, bf16[256,2688]{1,0:T(8,128)(2,1)S(1)}, u32[]{:S(2)}, u32[]{:S(2)}) collective-permute-start(bf16[256,2688]{1,0:T(8,128)(2,1)S(1)} %pad_maximum_fusion.4), channel_id=1, source_target_pairs={{0,4},{1,5},{2,6},{3,7},{4,0},{5,1},{6,2},{7,3},{8,12},{9,13},{10,... | collective-permute-start | bytes 4128776 | tf_op jit(solution)/shard_map/ppermute | solution.py:82
  34.1 30.5 %collective-permute-start.3 = (bf16[256,2816]{1,0:T(8,128)(2,1)S(1)}, bf16[256,2816]{1,0:T(8,128)(2,1)S(1)}, u32[]{:S(2)}, u32[]{:S(2)}) collective-permute-start(bf16[256,2816]{1,0:T(8,128)(2,1)S(1)} %pad_maximum_fusion.2), channel_id=1, source_target_pairs={{0,16},{1,17},{2,18},{3,19},{4,20},{5,21},{6,22},{7,23},{8,24},{9,... | collective-permute-start | bytes 4325384 | tf_op jit(solution)/shard_map/ppermute | solution.py:82
  35.7 29.7 %collective-permute-start.7 = (bf16[256,2816]{1,0:T(8,128)(2,1)S(1)}, bf16[256,2816]{1,0:T(8,128)(2,1)S(1)}, u32[]{:S(2)}, u32[]{:S(2)}) collective-permute-start(bf16[256,2816]{1,0:T(8,128)(2,1)S(1)} %pad_maximum_fusion.3), channel_id=1, source_target_pairs={{0,64},{1,65},{2,66},{3,67},{4,68},{5,69},{6,70},{7,71},{8,72},{9,... | collective-permute-start | bytes 4325384 | tf_op jit(solution)/shard_map/ppermute | solution.py:82
  49.7 45.7 %collective-permute-start.14 = (bf16[256,4096]{1,0:T(8,128)(2,1)S(1)}, bf16[256,4096]{1,0:T(8,128)(2,1)S(1)}, u32[]{:S(2)}, u32[]{:S(2)}) collective-permute-start(bf16[256,4096]{1,0:T(8,128)(2,1)S(1)} %pad_maximum_fusion.1), channel_id=1, source_target_pairs={{0,12},{1,13},{2,14},{3,15},{4,8},{5,9},{6,10},{7,11},{8,4},{9,5},... | collective-permute-start | bytes 6291464 | tf_op jit(solution)/shard_map/ppermute | solution.py:82
  52.4 46.8 %collective-permute-start.13 = (bf16[256,4224]{1,0:T(8,128)(2,1)S(1)}, bf16[256,4224]{1,0:T(8,128)(2,1)S(1)}, u32[]{:S(2)}, u32[]{:S(2)}) collective-permute-start(bf16[256,4224]{1,0:T(8,128)(2,1)S(1)} %pad_maximum_fusion), channel_id=1, source_target_pairs={{0,66},{1,67},{2,64},{3,65},{4,70},{5,71},{6,68},{7,69},{8,74},{9,... | collective-permute-start | bytes 6488072 | tf_op jit(solution)/shard_map/ppermute | solution.py:82
  66.5 40.5 %collective-permute-start.15 = (bf16[512,8320]{1,0:T(8,128)(2,1)S(1)}, bf16[512,8320]{1,0:T(8,128)(2,1)}, u32[]{:S(2)}, u32[]{:S(2)}) collective-permute-start(bf16[512,8320]{1,0:T(8,128)(2,1)S(1)} %maximum_dynamic-update-slice_fusion), channel_id=1, source_target_pairs={{0,1},{1,0},{2,3},{3,2},{4,5},{5,4},{6,7},{7,6},{8,9},{9,8},{10,11... | collective-permute-start | bytes 25559048 | tf_op jit(solution)/shard_map/ppermute | solution.py:116
  118.3 10.9 %collective-permute-start.16 = (f32[512,512]{1,0:T(8,128)S(1)}, f32[512,512]{1,0:T(8,128)S(1)}, u32[]{:S(2)}, u32[]{:S(2)}) collective-permute-start(f32[512,512]{1,0:T(8,128)S(1)} %fusion.5), channel_id=1, source_target_pairs={{0,1},{1,0},{2,3},{3,2},{4,5},{5,4},{6,7},{7,6},{8,9},{9,8},{10,11... | collective-permute-start | bytes 3145736 | tf_op jit(solution)/shard_map/ppermute | solution.py:134
  129.8 14.4 %collective-permute-start.17 = (f32[256,512]{1,0:T(8,128)S(1)}, f32[256,512]{1,0:T(8,128)S(1)}, u32[]{:S(2)}, u32[]{:S(2)}) collective-permute-start(f32[256,512]{1,0:T(8,128)S(1)} %pad_maximum_fusion.11), channel_id=1, source_target_pairs={{0,16},{1,17},{2,18},{3,19},{4,20},{5,21},{6,22},{7,23},{8,24},{9,... | collective-permute-start | bytes 1572872 | tf_op jit(solution)/shard_map/ppermute | solution.py:99
  130.0 4.8 %collective-permute-start.20 = (f32[256]{0:T(256)S(1)}, f32[256]{0:T(256)S(1)}, u32[]{:S(2)}, u32[]{:S(2)}) collective-permute-start(f32[256]{0:T(256)S(1)} %pad_maximum_fusion.14), channel_id=1, source_target_pairs={{0,48},{1,49},{2,50},{3,51},{4,52},{5,53},{6,54},{7,55},{8,56},{9,... | collective-permute-start | bytes 3080 | tf_op jit(solution)/shard_map/ppermute | solution.py:99
  144.3 8.0 %collective-permute-start.18 = (f32[128,512]{1,0:T(8,128)S(1)}, f32[128,512]{1,0:T(8,128)S(1)}, u32[]{:S(2)}, u32[]{:S(2)}) collective-permute-start(f32[128,512]{1,0:T(8,128)S(1)} %pad_maximum_fusion.13), channel_id=1, source_target_pairs={{0,64},{1,65},{2,66},{3,67},{4,68},{5,69},{6,70},{7,71},{8,72},{9,... | collective-permute-start | bytes 786440 | tf_op jit(solution)/shard_map/ppermute | solution.py:99
  144.4 4.8 %collective-permute-start.21 = (f32[128]{0:T(128)S(1)}, f32[128]{0:T(128)S(1)}, u32[]{:S(2)}, u32[]{:S(2)}) collective-permute-start(f32[128]{0:T(128)S(1)} %pad_maximum_fusion.15), channel_id=1, source_target_pairs={{0,66},{1,67},{2,64},{3,65},{4,70},{5,71},{6,68},{7,69},{8,74},{9,... | collective-permute-start | bytes 1544 | tf_op jit(solution)/shard_map/ppermute | solution.py:99
  149.3 4.8 %collective-permute-start.22 = (f32[64]{0:T(128)S(1)}, f32[64]{0:T(128)S(1)}, u32[]{:S(2)}, u32[]{:S(2)}) collective-permute-start(f32[64]{0:T(128)S(1)} %slice_add_fusion.6), channel_id=1, source_target_pairs={{0,12},{1,13},{2,14},{3,15},{4,8},{5,9},{6,10},{7,11},{8,4},{9,5},... | collective-permute-start | bytes 776 | tf_op jit(solution)/shard_map/ppermute | solution.py:99
  152.3 5.0 %collective-permute-start.19 = (f32[64,512]{1,0:T(8,128)S(1)}, f32[64,512]{1,0:T(8,128)S(1)}, u32[]{:S(2)}, u32[]{:S(2)}) collective-permute-start(f32[64,512]{1,0:T(8,128)S(1)} %slice_add_fusion), channel_id=1, source_target_pairs={{0,4},{1,5},{2,6},{3,7},{4,0},{5,1},{6,2},{7,3},{8,12},{9,13},{10,... | collective-permute-start | bytes 393224 | tf_op jit(solution)/shard_map/ppermute | solution.py:99

commit v9 on v8

--- a/solution.py
+++ b/solution.py
@@ -5,7 +5,8 @@
 
 NCLS = 512
 PAD = 128
-AXES = ("blk", "dp")
+AXES = ("y_lo", "x_hi", "x_lo", "z_hi", "z_lo", "y_hi", "core")
+CUBE = ("y_lo", "x_lo", "z_lo")
 THREE = ((0, 1, 2), (1, 2, 0), (2, 0, 1))
 TWO = ((0, 1, 2), (2, 0, 1))
 
@@ -69,24 +70,37 @@
     return [(L, L ^ 1) for L in range(n)]
 
 
+def column_cuts(cols, m):
+    tiles = cols // 128
+    return [(tiles * p // m) * 128 for p in range(m)] + [cols]
+
+
+def chain(part, mate, n, order):
+    rows = part.shape[0]
+    buf = part
+    labs = [0]
+    for a in order:
+        got = lax.ppermute(buf, AXES, mate_pairs(n, a, mate))
+        buf = jnp.concatenate([buf, got])
+        labs = labs + [o ^ (1 << a) for o in labs]
+    at = {o: i for i, o in enumerate(labs)}
+    return jnp.concatenate([buf[at[o] * rows:(at[o] + 1) * rows] for o in range(8)])
+
+
 def cube_gather(shard, mate, n, orders):
-    cols = shard.shape[1]
-    tiles = cols // 128
-    m = len(orders)
-    cut = [(tiles * p // m) * 128 for p in range(m)] + [cols]
-    parts = []
-    for p, order in enumerate(orders):
-        buf = shard[:, cut[p]:cut[p + 1]]
-        labs = [0]
-        for a in order:
-            got = lax.ppermute(buf, AXES, mate_pairs(n, a, mate))
-            buf = jnp.concatenate([buf, got])
-            labs = labs + [o ^ (1 << a) for o in labs]
-        rows = shard.shape[0]
-        parts.append({o: buf[i * rows:(i + 1) * rows] for i, o in enumerate(labs)})
+    cut = column_cuts(shard.shape[1], len(orders))
     return jnp.concatenate(
-        [jnp.concatenate([parts[p][o] for p in range(m)], axis=1) for o in range(8)]
+        [chain(shard[:, cut[p]:cut[p + 1]], mate, n, order) for p, order in enumerate(orders)],
+        axis=1,
     )
+
+
+def sc_train_part(part):
+    rows, cols = part.shape
+    g = lax.all_gather(part, CUBE, axis=0, tiled=True).reshape(2, 2, 2, rows, cols)
+    for axis, name in enumerate(CUBE):
+        g = jnp.where(lax.axis_index(name) == 1, jnp.flip(g, axis), g)
+    return g.transpose(2, 0, 1, 3, 4).reshape(8 * rows, cols)
 
 
 def cube_reduce(blocks, mate, n):
@@ -111,9 +125,14 @@
     rows = train_grads.shape[0]
     tr = with_side(train_grads, (train_scale,) + split_class(train_class), 0)
     te = with_side(test_grads, split_class(test_class), 4)
-    te_all = cube_gather(te, test_mate, n, TWO)
-    tr_mine = cube_gather(tr, train_mate, n, THREE)
-    tr_other = lax.ppermute(tr_mine, AXES, core_pairs(n))
+    te_all = cube_gather(te, test_mate, n, THREE)
+    cut = column_cuts(tr.shape[1], 3)
+    tr_parts = [chain(tr[:, cut[p]:cut[p + 1]], train_mate, n, THREE[p]) for p in range(2)]
+    tr_parts.append(sc_train_part(tr[:, cut[2]:]))
+    tr_mine = jnp.concatenate(tr_parts, axis=1)
+    tr_other = jnp.concatenate(
+        [lax.ppermute(t, AXES, core_pairs(n)) for t in tr_parts], axis=1
+    )
     test_hot = indicator(join_class(te_all, k + 4))
 
     def weigh(t):
@@ -143,6 +162,7 @@
 
 
 def solution(mesh):
+    fine = jax.sharding.Mesh(mesh.devices.reshape((2,) * 7), AXES)
     in_specs = (
         P(AXES, None),
         P(AXES),
@@ -151,4 +171,4 @@
         P(AXES),
     )
     out_specs = (P(AXES, None), P(AXES))
-    return jax.shard_map(local, mesh=mesh, in_specs=in_specs, out_specs=out_specs, check_vma=False)
+    return jax.shard_map(local, mesh=fine, in_specs=in_specs, out_specs=out_specs, check_vma=False)

time: 158 us -> 221 us (1.40)
  local copies, waits for them, and re-layouts: 1.1 us -> 18.3 us
  waiting for transfers between devices: 87.8 us -> 104 us
  between operations: 1.03 us -> 14.5 us
  matrix products: 20 us -> 31 us
  starting transfers between devices: 29.3 us -> 39.9 us
  other arithmetic: 18.8 us -> 12.8 us
    ppermute x16 -> x18, waiting for transfers between devices: 66.5 us -> 87.3 us  [the longest x15 85.6 us: chain(): got = lax.ppermute(buf, AXES, mate_pairs(n, a, mate))]
    unnamed x6 -> x58, local copies, waits for them, and re-layouts: 0.01 us -> 12.5 us
    unnamed x14 -> x0, other arithmetic: 8.38 us -> none
    dot_general x2, matrix products: 17.8 us -> 24.6 us  [weigh(): lax.dot_general(t, te_all, (((1,), (1,)), ((), ())), preferred_element_ty...]
    ppermute x16 -> x18, starting transfers between devices: 23.8 us -> 29.5 us  [the longest x15 28.8 us: chain(): got = lax.ppermute(buf, AXES, mate_pairs(n, a, mate))]
    ppermute x6, starting transfers between devices: 5.21 us -> 10.2 us  [cube_reduce(): lax.ppermute(jnp.concatenate([blocks[o] for o in send]), AXES, mate_pairs...]
    ppermute x6, waiting for transfers between devices: 21.4 us -> 16.9 us  [cube_reduce(): lax.ppermute(jnp.concatenate([blocks[o] for o in send]), AXES, mate_pairs...]
  transfers between devices with their start and end apart: 23 -> 26, of which waited for: 17 -> 11; matrix products, arithmetic and copies ran while one was open for 16% -> 17% of each run, Pallas kernels for 0% -> 0%
where the time goes in v9:
time: 221 us
  waiting for transfers between devices  104 us (47%)
  starting transfers between devices  39.9 us (18%)
  matrix products  31 us (14%)
  local copies, waits for them, and re-layouts  18.3 us (8%)
  between operations  14.5 us (7%)
  other arithmetic  12.8 us (6%)
    ppermute x15, waiting for transfers between devices, chain(): got = lax.ppermute(buf, AXES, mate_pairs(n, a, mate))  85.6 us
    ppermute x15, starting transfers between devices, chain(): got = lax.ppermute(buf, AXES, mate_pairs(n, a, mate))  28.8 us
    dot_general x2, matrix products, weigh(): lax.dot_general(t, te_all, (((1,), (1,)), ((), ())), preferred_element_ty...  24.6 us
    ppermute x6, waiting for transfers between devices, cube_reduce(): lax.ppermute(jnp.concatenate([blocks[o] for o in send]), AXES, mate_pairs...  16.9 us
    unnamed x58, local copies, waits for them, and re-layouts  12.5 us
    ppermute x6, starting transfers between devices, cube_reduce(): lax.ppermute(jnp.concatenate([blocks[o] for o in send]), AXES, mate_pairs...  10.2 us
  transfers between devices with their start and end apart: 26, of which 11 were waited for; matrix products, arithmetic and copies ran while one was open for 17% of the time, Pallas kernels for 0%

profile of v9, /device:TPU:0, one launch (start us, length us, event | category | flops | bytes accessed | tf_op | source)
XLA Modules:
  0.0 220.7 jit_solution(2287431569920150164)
XLA Ops:
  8.1 2.1 fusion.46
  10.2 3.1 %collective-permute-start.9 = (bf16[64,2816]{1,0:T(8,128)(2,1)S(1)}, bf16[64,2816]{1,0:T(8,128)(2,1)S(1)}, u32[]{:S(2)}, u32[]{:S(2)}) collective-permute-start(bf16[64,2816]{1,0:T(8,128)(2,1)S(1)} %get-tuple-element.10), channel_id=1, source_target_pairs={{0,66},{1,67},{2,64},{3,65},{4,70},{5,71},{6,68},{7,69},{8,74},{9,... | collective-permute-start | bytes 1081352 | tf_op jit(solution)/shard_map/ppermute | solution.py:83
  13.3 4.0 %collective-permute-start.12 = (bf16[64,2816]{1,0:T(8,128)(2,1)S(1)}, bf16[64,2816]{1,0:T(8,128)(2,1)S(1)}, u32[]{:S(2)}, u32[]{:S(2)}) collective-permute-start(bf16[64,2816]{1,0:T(8,128)(2,1)S(1)} %get-tuple-element.13), channel_id=1, source_target_pairs={{0,12},{1,13},{2,14},{3,15},{4,8},{5,9},{6,10},{7,11},{8,4},{9,5},... | collective-permute-start | bytes 1081352 | tf_op jit(solution)/shard_map/ppermute | solution.py:83
  18.3 1.6 collective-permute-start
  22.1 2.2 collective-permute-start.6
  24.3 3.3 %collective-permute-done = bf16[64,2688]{1,0:T(8,128)(2,1)S(1)} collective-permute-done((bf16[64,2688]{1,0:T(8,128)(2,1)S(1)}, bf16[64,2688]{1,0:T(8,128)(2,1)S(1)}, u32[]{:S(2)}, u32[]{:S(2)}) %collective-permute-start) | collective-permute-done | bytes 344096 | tf_op jit(solution)/shard_map/ppermute | solution.py:83
  27.9 4.4 %collective-permute-done.6 = bf16[64,2688]{1,0:T(8,128)(2,1)S(1)} collective-permute-done((bf16[64,2688]{1,0:T(8,128)(2,1)S(1)}, bf16[64,2688]{1,0:T(8,128)(2,1)S(1)}, u32[]{:S(2)}, u32[]{:S(2)}) %collective-permute-start.6) | collective-permute-done | bytes 344096 | tf_op jit(solution)/shard_map/ppermute | solution.py:83
  33.8 2.2 collective-permute-start.13
  36.1 8.9 %collective-permute-done.1 = bf16[128,2688]{1,0:T(8,128)(2,1)S(1)} collective-permute-done((bf16[128,2688]{1,0:T(8,128)(2,1)S(1)}, bf16[128,2688]{1,0:T(8,128)(2,1)S(1)}, u32[]{:S(2)}, u32[]{:S(2)}) %collective-permute-start.1) | collective-permute-done | bytes 688160 | tf_op jit(solution)/shard_map/ppermute | solution.py:83
  45.1 7.6 %collective-permute-start.2 = (bf16[256,2688]{1,0:T(8,128)(2,1)S(1)}, bf16[256,2688]{1,0:T(8,128)(2,1)S(1)}, u32[]{:S(2)}, u32[]{:S(2)}) collective-permute-start(bf16[256,2688]{1,0:T(8,128)(2,1)S(1)} %pad_maximum_fusion.5), channel_id=1, source_target_pairs={{0,4},{1,5},{2,6},{3,7},{4,0},{5,1},{6,2},{7,3},{8,12},{9,13},{10,... | collective-permute-start | bytes 4128776 | tf_op jit(solution)/shard_map/ppermute | solution.py:83
  54.7 2.4 %collective-permute-start.11 = (bf16[256,2816]{1,0:T(8,128)(2,1)S(1)}, bf16[256,2816]{1,0:T(8,128)(2,1)S(1)}, u32[]{:S(2)}, u32[]{:S(2)}) collective-permute-start(bf16[256,2816]{1,0:T(8,128)(2,1)S(1)} %pad_maximum_fusion.3), channel_id=1, source_target_pairs={{0,48},{1,49},{2,50},{3,51},{4,52},{5,53},{6,54},{7,55},{8,56},{9,... | collective-permute-start | bytes 4325384 | tf_op jit(solution)/shard_map/ppermute | solution.py:83
  57.1 28.7 %collective-permute-done.4 = bf16[128,2816]{1,0:T(8,128)(2,1)S(1)} collective-permute-done((bf16[128,2816]{1,0:T(8,128)(2,1)S(1)}, bf16[128,2816]{1,0:T(8,128)(2,1)S(1)}, u32[]{:S(2)}, u32[]{:S(2)}) %collective-permute-start.4) | collective-permute-done | bytes 720928 | tf_op jit(solution)/shard_map/ppermute | solution.py:83
  87.6 1.9 collective-permute-start.14
  89.5 40.2 %collective-permute-done.2 = bf16[256,2688]{1,0:T(8,128)(2,1)S(1)} collective-permute-done((bf16[256,2688]{1,0:T(8,128)(2,1)S(1)}, bf16[256,2688]{1,0:T(8,128)(2,1)S(1)}, u32[]{:S(2)}, u32[]{:S(2)}) %collective-permute-start.2) | collective-permute-done | bytes 1376288 | tf_op jit(solution)/shard_map/ppermute | solution.py:83
  129.8 1.8 pad_maximum_fusion.1
  140.7 2.0 copy.9
  148.2 1.7 collective-permute-done.15
  151.5 14.2 %tanh_convert_fusion = bf16[512,512]{1,0:T(8,128)(2,1)S(1)} fusion(f32[512]{0:T(512)S(1)} %convert_reduce_fusion, bf16[512,2816]{1,0:T(8,128)(2,1)} %copy-done.17, bf16[512,2816]{1,0:T(8,128)(2,1)} %collective-permute-done.17, bf16[512,2688]{1,0:T(8,128)(2,1)} %collective-permute-done.16, bf16[512,2816]{1,0:T(8,128)(2,1)} %copy-done.16, ...), kind=kOutput, calls=%fused_computation.37 | convolution fusion | flops 4439277568 | bytes 17565696 | tf_op jit(solution)/shard_map/dot_general | solution.py:139
  168.0 10.4 %fusion.25 = bf16[512,512]{1,0:T(8,128)(2,1)} fusion(bf16[512,2816]{1,0:T(8,128)(2,1)S(1)} %bitcast.10, bf16[512,2816]{1,0:T(8,128)(2,1)} %slice_dynamic-update-slice_fusion.12, bf16[256,2688]{1,0:T(8,128)(2,1)} %copy-done.10, bf16[128,2688]{1,0:T(8,128)(2,1)} %copy-done.6, bf16[64,2688]{1,0:T(8,128)(2,1)} %copy-done.2, bf16[64,2688]{1,0:T(8,128)(2,1)S(1)} %slice.198, ...), kind=kOutput, calls=%fused_computation.33 | convolution fusion | flops 4464836608 | bytes 17565696 | tf_op jit(solution)/shard_map/dot_general | solution.py:139
  178.7 1.6 fusion.31
  181.5 1.6 fusion.28
  183.2 1.7 convolution_add_fusion.1
  185.0 1.6 collective-permute-start.19
  186.7 2.1 collective-permute-start.22
  188.8 2.7 %collective-permute-done.22 = f32[256]{0:T(256)S(1)} collective-permute-done((f32[256]{0:T(256)S(1)}, f32[256]{0:T(256)S(1)}, u32[]{:S(2)}, u32[]{:S(2)}) %collective-permute-start.22) | collective-permute-done | bytes 1056 | tf_op jit(solution)/shard_map/ppermute | solution.py:113
  191.6 7.7 %collective-permute-done.19 = f32[256,512]{1,0:T(8,128)S(1)} collective-permute-done((f32[256,512]{1,0:T(8,128)S(1)}, f32[256,512]{1,0:T(8,128)S(1)}, u32[]{:S(2)}, u32[]{:S(2)}) %collective-permute-start.19) | collective-permute-done | bytes 524320 | tf_op jit(solution)/shard_map/ppermute | solution.py:113
  199.4 1.6 collective-permute-start.20
  201.0 2.1 collective-permute-start.23
  203.1 2.7 %collective-permute-done.23 = f32[128]{0:T(128)S(1)} collective-permute-done((f32[128]{0:T(128)S(1)}, f32[128]{0:T(128)S(1)}, u32[]{:S(2)}, u32[]{:S(2)}) %collective-permute-start.23) | collective-permute-done | bytes 544 | tf_op jit(solution)/shard_map/ppermute | solution.py:113
  205.9 2.2 collective-permute-start.24
  208.8 1.8 collective-permute-done.24
  211.1 2.0 collective-permute-done.21
  (131 shorter events, 32.1 us)
Async XLA Ops:
  7.2 133.6 %all-gather.2.cloned.1.call-start = ((), (), s32[]{:S(2)}) async-start(), calls=%async_computation | async-start | bytes 3244032 | tf_op jit(solution)/shard_map/all_gather | solution.py:100
  10.2 23.1 %collective-permute-start.9 = (bf16[64,2816]{1,0:T(8,128)(2,1)S(1)}, bf16[64,2816]{1,0:T(8,128)(2,1)S(1)}, u32[]{:S(2)}, u32[]{:S(2)}) collective-permute-start(bf16[64,2816]{1,0:T(8,128)(2,1)S(1)} %get-tuple-element.10), channel_id=1, source_target_pairs={{0,66},{1,67},{2,64},{3,65},{4,70},{5,71},{6,68},{7,69},{8,74},{9,... | collective-permute-start | bytes 1081352 | tf_op jit(solution)/shard_map/ppermute | solution.py:83
  13.3 20.5 %collective-permute-start.12 = (bf16[64,2816]{1,0:T(8,128)(2,1)S(1)}, bf16[64,2816]{1,0:T(8,128)(2,1)S(1)}, u32[]{:S(2)}, u32[]{:S(2)}) collective-permute-start(bf16[64,2816]{1,0:T(8,128)(2,1)S(1)} %get-tuple-element.13), channel_id=1, source_target_pairs={{0,12},{1,13},{2,14},{3,15},{4,8},{5,9},{6,10},{7,11},{8,4},{9,5},... | collective-permute-start | bytes 1081352 | tf_op jit(solution)/shard_map/ppermute | solution.py:83
  18.3 9.3 %collective-permute-start = (bf16[64,2688]{1,0:T(8,128)(2,1)S(1)}, bf16[64,2688]{1,0:T(8,128)(2,1)S(1)}, u32[]{:S(2)}, u32[]{:S(2)}) collective-permute-start(bf16[64,2688]{1,0:T(8,128)(2,1)S(1)} %slice.198), channel_id=1, source_target_pairs={{0,16},{1,17},{2,18},{3,19},{4,20},{5,21},{6,22},{7,23},{8,24},{9,... | collective-permute-start | bytes 1032200 | tf_op jit(solution)/shard_map/ppermute | solution.py:83
  21.0 15.0 %collective-permute-start.3 = (bf16[64,2816]{1,0:T(8,128)(2,1)S(1)}, bf16[64,2816]{1,0:T(8,128)(2,1)S(1)}, u32[]{:S(2)}, u32[]{:S(2)}) collective-permute-start(bf16[64,2816]{1,0:T(8,128)(2,1)S(1)} %get-tuple-element.14), channel_id=1, source_target_pairs={{0,64},{1,65},{2,66},{3,67},{4,68},{5,69},{6,70},{7,71},{8,72},{9,... | collective-permute-start | bytes 1081352 | tf_op jit(solution)/shard_map/ppermute | solution.py:83
  22.1 63.8 %copy-start = (bf16[64,2688]{1,0:T(8,128)(2,1)}, bf16[64,2688]{1,0:T(8,128)(2,1)S(1)}, u32[]{:S(2)}) copy-start(bf16[64,2688]{1,0:T(8,128)(2,1)S(1)} %slice.206) | copy-start | bytes 1032196
  22.1 10.1 %collective-permute-start.6 = (bf16[64,2688]{1,0:T(8,128)(2,1)S(1)}, bf16[64,2688]{1,0:T(8,128)(2,1)S(1)}, u32[]{:S(2)}, u32[]{:S(2)}) collective-permute-start(bf16[64,2688]{1,0:T(8,128)(2,1)S(1)} %slice.206), channel_id=1, source_target_pairs={{0,48},{1,49},{2,50},{3,51},{4,52},{5,53},{6,54},{7,55},{8,56},{9,... | collective-permute-start | bytes 1032200 | tf_op jit(solution)/shard_map/ppermute | solution.py:83
  27.6 102.1 %copy-start.2 = (bf16[64,2688]{1,0:T(8,128)(2,1)}, bf16[64,2688]{1,0:T(8,128)(2,1)S(1)}, u32[]{:S(2)}) copy-start(bf16[64,2688]{1,0:T(8,128)(2,1)S(1)} %collective-permute-done) | copy-start | bytes 1032196
  27.7 17.4 %collective-permute-start.1 = (bf16[128,2688]{1,0:T(8,128)(2,1)S(1)}, bf16[128,2688]{1,0:T(8,128)(2,1)S(1)}, u32[]{:S(2)}, u32[]{:S(2)}) collective-permute-start(bf16[128,2688]{1,0:T(8,128)(2,1)S(1)} %pad_maximum_fusion.10), channel_id=1, source_target_pairs={{0,64},{1,65},{2,66},{3,67},{4,68},{5,69},{6,70},{7,71},{8,72},{9,... | collective-permute-start | bytes 2064392 | tf_op jit(solution)/shard_map/ppermute | solution.py:83
  32.3 20.5 %copy-start.11 = (bf16[64,2688]{1,0:T(8,128)(2,1)}, bf16[64,2688]{1,0:T(8,128)(2,1)S(1)}, u32[]{:S(2)}) copy-start(bf16[64,2688]{1,0:T(8,128)(2,1)S(1)} %collective-permute-done.6) | copy-start | bytes 1032196
  32.3 20.4 %collective-permute-start.7 = (bf16[128,2688]{1,0:T(8,128)(2,1)S(1)}, bf16[128,2688]{1,0:T(8,128)(2,1)S(1)}, u32[]{:S(2)}, u32[]{:S(2)}) collective-permute-start(bf16[128,2688]{1,0:T(8,128)(2,1)S(1)} %pad_maximum_fusion.11), channel_id=1, source_target_pairs={{0,66},{1,67},{2,64},{3,65},{4,70},{5,71},{6,68},{7,69},{8,74},{9,... | collective-permute-start | bytes 2064392 | tf_op jit(solution)/shard_map/ppermute | solution.py:83
  33.4 21.3 %collective-permute-start.10 = (bf16[128,2816]{1,0:T(8,128)(2,1)S(1)}, bf16[128,2816]{1,0:T(8,128)(2,1)S(1)}, u32[]{:S(2)}, u32[]{:S(2)}) collective-permute-start(bf16[128,2816]{1,0:T(8,128)(2,1)S(1)} %pad_maximum_fusion.8), channel_id=1, source_target_pairs={{0,12},{1,13},{2,14},{3,15},{4,8},{5,9},{6,10},{7,11},{8,4},{9,5},... | collective-permute-start | bytes 2162696 | tf_op jit(solution)/shard_map/ppermute | solution.py:83
  33.8 53.7 %collective-permute-start.13 = (bf16[128,2816]{1,0:T(8,128)(2,1)S(1)}, bf16[128,2816]{1,0:T(8,128)(2,1)S(1)}, u32[]{:S(2)}, u32[]{:S(2)}) collective-permute-start(bf16[128,2816]{1,0:T(8,128)(2,1)S(1)} %pad_maximum_fusion.9), channel_id=1, source_target_pairs={{0,48},{1,49},{2,50},{3,51},{4,52},{5,53},{6,54},{7,55},{8,56},{9,... | collective-permute-start | bytes 2162696 | tf_op jit(solution)/shard_map/ppermute | solution.py:83
  36.0 49.9 %collective-permute-start.4 = (bf16[128,2816]{1,0:T(8,128)(2,1)S(1)}, bf16[128,2816]{1,0:T(8,128)(2,1)S(1)}, u32[]{:S(2)}, u32[]{:S(2)}) collective-permute-start(bf16[128,2816]{1,0:T(8,128)(2,1)S(1)} %pad_maximum_fusion.7), channel_id=1, source_target_pairs={{0,4},{1,5},{2,6},{3,7},{4,0},{5,1},{6,2},{7,3},{8,12},{9,13},{10,... | collective-permute-start | bytes 2162696 | tf_op jit(solution)/shard_map/ppermute | solution.py:83
  45.0 86.5 %copy-start.6 = (bf16[128,2688]{1,0:T(8,128)(2,1)}, bf16[128,2688]{1,0:T(8,128)(2,1)S(1)}, u32[]{:S(2)}) copy-start(bf16[128,2688]{1,0:T(8,128)(2,1)S(1)} %collective-permute-done.1) | copy-start | bytes 2064388
  45.1 84.6 %collective-permute-start.2 = (bf16[256,2688]{1,0:T(8,128)(2,1)S(1)}, bf16[256,2688]{1,0:T(8,128)(2,1)S(1)}, u32[]{:S(2)}, u32[]{:S(2)}) collective-permute-start(bf16[256,2688]{1,0:T(8,128)(2,1)S(1)} %pad_maximum_fusion.5), channel_id=1, source_target_pairs={{0,4},{1,5},{2,6},{3,7},{4,0},{5,1},{6,2},{7,3},{8,12},{9,13},{10,... | collective-permute-start | bytes 4128776 | tf_op jit(solution)/shard_map/ppermute | solution.py:83
  54.1 95.9 %collective-permute-start.8 = (bf16[256,2688]{1,0:T(8,128)(2,1)}, bf16[256,2688]{1,0:T(8,128)(2,1)}, u32[]{:S(2)}, u32[]{:S(2)}) collective-permute-start(bf16[256,2688]{1,0:T(8,128)(2,1)} %pad_maximum_fusion.6), channel_id=1, source_target_pairs={{0,12},{1,13},{2,14},{3,15},{4,8},{5,9},{6,10},{7,11},{8,4},{9,5},... | collective-permute-start | bytes 4128776 | tf_op jit(solution)/shard_map/ppermute | solution.py:83
  54.6 31.4 %copy-start.4 = (bf16[128,2816]{1,0:T(8,128)(2,1)}, bf16[128,2816]{1,0:T(8,128)(2,1)S(1)}, u32[]{:S(2)}) copy-start(bf16[128,2816]{1,0:T(8,128)(2,1)S(1)} %collective-permute-done.10) | copy-start | bytes 2162692
  54.7 34.8 %copy-start.15 = (bf16[512,2816]{1,0:T(8,128)(2,1)S(1)}, bf16[512,2816]{1,0:T(8,128)(2,1)}, u32[]{:S(2)}) copy-start(bf16[512,2816]{1,0:T(8,128)(2,1)} %get-tuple-element.12) | copy-start | bytes 8650756
  54.7 83.3 %collective-permute-start.11 = (bf16[256,2816]{1,0:T(8,128)(2,1)S(1)}, bf16[256,2816]{1,0:T(8,128)(2,1)S(1)}, u32[]{:S(2)}, u32[]{:S(2)}) collective-permute-start(bf16[256,2816]{1,0:T(8,128)(2,1)S(1)} %pad_maximum_fusion.3), channel_id=1, source_target_pairs={{0,48},{1,49},{2,50},{3,51},{4,52},{5,53},{6,54},{7,55},{8,56},{9,... | collective-permute-start | bytes 4325384 | tf_op jit(solution)/shard_map/ppermute | solution.py:83
  86.0 45.6 %collective-permute-start.5 = (bf16[256,2816]{1,0:T(8,128)(2,1)S(1)}, bf16[256,2816]{1,0:T(8,128)(2,1)S(1)}, u32[]{:S(2)}, u32[]{:S(2)}) collective-permute-start(bf16[256,2816]{1,0:T(8,128)(2,1)S(1)} %pad_maximum_fusion.2), channel_id=1, source_target_pairs={{0,16},{1,17},{2,18},{3,19},{4,20},{5,21},{6,22},{7,23},{8,24},{9,... | collective-permute-start | bytes 4325384 | tf_op jit(solution)/shard_map/ppermute | solution.py:83
  87.6 50.0 %collective-permute-start.14 = (bf16[256,2816]{1,0:T(8,128)(2,1)S(1)}, bf16[256,2816]{1,0:T(8,128)(2,1)S(1)}, u32[]{:S(2)}, u32[]{:S(2)}) collective-permute-start(bf16[256,2816]{1,0:T(8,128)(2,1)S(1)} %pad_maximum_fusion.4), channel_id=1, source_target_pairs={{0,66},{1,67},{2,64},{3,65},{4,70},{5,71},{6,68},{7,69},{8,74},{9,... | collective-permute-start | bytes 4325384 | tf_op jit(solution)/shard_map/ppermute | solution.py:83
  131.6 18.4 %collective-permute-start.16 = (bf16[512,2688]{1,0:T(8,128)(2,1)}, bf16[512,2688]{1,0:T(8,128)(2,1)}, u32[]{:S(2)}, u32[]{:S(2)}) collective-permute-start(bf16[512,2688]{1,0:T(8,128)(2,1)} %pad_maximum_fusion.1), channel_id=1, source_target_pairs={{0,1},{1,0},{2,3},{3,2},{4,5},{5,4},{6,7},{7,6},{8,9},{9,8},{10,11... | collective-permute-start | bytes 8257544 | tf_op jit(solution)/shard_map/ppermute | solution.py:134
  137.0 14.4 %collective-permute-start.17 = (bf16[512,2816]{1,0:T(8,128)(2,1)}, bf16[512,2816]{1,0:T(8,128)(2,1)}, u32[]{:S(2)}, u32[]{:S(2)}) collective-permute-start(bf16[512,2816]{1,0:T(8,128)(2,1)} %slice_dynamic-update-slice_fusion.12), channel_id=1, source_target_pairs={{0,1},{1,0},{2,3},{3,2},{4,5},{5,4},{6,7},{7,6},{8,9},{9,8},{10,11... | collective-permute-start | bytes 8650760 | tf_op jit(solution)/shard_map/ppermute | solution.py:134
  144.3 5.5 %collective-permute-start.15 = (bf16[512,2816]{1,0:T(8,128)(2,1)S(1)}, bf16[512,2816]{1,0:T(8,128)(2,1)S(1)}, u32[]{:S(2)}, u32[]{:S(2)}) collective-permute-start(bf16[512,2816]{1,0:T(8,128)(2,1)S(1)} %bitcast.8), channel_id=1, source_target_pairs={{0,1},{1,0},{2,3},{3,2},{4,5},{5,4},{6,7},{7,6},{8,9},{9,8},{10,11... | collective-permute-start | bytes 8650760 | tf_op jit(solution)/shard_map/ppermute | solution.py:134
  167.9 15.3 %collective-permute-start.18 = (f32[512,512]{1,0:T(8,128)}, f32[512,512]{1,0:T(8,128)}, u32[]{:S(2)}, u32[]{:S(2)}) collective-permute-start(f32[512,512]{1,0:T(8,128)} %fusion.30), channel_id=1, source_target_pairs={{0,1},{1,0},{2,3},{3,2},{4,5},{5,4},{6,7},{7,6},{8,9},{9,8},{10,11... | collective-permute-start | bytes 3145736 | tf_op jit(solution)/shard_map/ppermute | solution.py:153
  185.0 14.3 %collective-permute-start.19 = (f32[256,512]{1,0:T(8,128)S(1)}, f32[256,512]{1,0:T(8,128)S(1)}, u32[]{:S(2)}, u32[]{:S(2)}) collective-permute-start(f32[256,512]{1,0:T(8,128)S(1)} %pad_maximum_fusion.12), channel_id=1, source_target_pairs={{0,16},{1,17},{2,18},{3,19},{4,20},{5,21},{6,22},{7,23},{8,24},{9,... | collective-permute-start | bytes 1572872 | tf_op jit(solution)/shard_map/ppermute | solution.py:113
  186.7 4.8 %collective-permute-start.22 = (f32[256]{0:T(256)S(1)}, f32[256]{0:T(256)S(1)}, u32[]{:S(2)}, u32[]{:S(2)}) collective-permute-start(f32[256]{0:T(256)S(1)} %pad_maximum_fusion.16), channel_id=1, source_target_pairs={{0,48},{1,49},{2,50},{3,51},{4,52},{5,53},{6,54},{7,55},{8,56},{9,... | collective-permute-start | bytes 3080 | tf_op jit(solution)/shard_map/ppermute | solution.py:113
  199.4 8.7 %collective-permute-start.20 = (f32[128,512]{1,0:T(8,128)S(1)}, f32[128,512]{1,0:T(8,128)S(1)}, u32[]{:S(2)}, u32[]{:S(2)}) collective-permute-start(f32[128,512]{1,0:T(8,128)S(1)} %pad_maximum_fusion.15), channel_id=1, source_target_pairs={{0,64},{1,65},{2,66},{3,67},{4,68},{5,69},{6,70},{7,71},{8,72},{9,... | collective-permute-start | bytes 786440 | tf_op jit(solution)/shard_map/ppermute | solution.py:113
  201.0 4.8 %collective-permute-start.23 = (f32[128]{0:T(128)S(1)}, f32[128]{0:T(128)S(1)}, u32[]{:S(2)}, u32[]{:S(2)}) collective-permute-start(f32[128]{0:T(128)S(1)} %pad_maximum_fusion.17), channel_id=1, source_target_pairs={{0,66},{1,67},{2,64},{3,65},{4,70},{5,71},{6,68},{7,69},{8,74},{9,... | collective-permute-start | bytes 1544 | tf_op jit(solution)/shard_map/ppermute | solution.py:113
  205.9 4.8 %collective-permute-start.24 = (f32[64]{0:T(128)S(1)}, f32[64]{0:T(128)S(1)}, u32[]{:S(2)}, u32[]{:S(2)}) collective-permute-start(f32[64]{0:T(128)S(1)} %slice_add_fusion.6), channel_id=1, source_target_pairs={{0,12},{1,13},{2,14},{3,15},{4,8},{5,9},{6,10},{7,11},{8,4},{9,5},... | collective-permute-start | bytes 776 | tf_op jit(solution)/shard_map/ppermute | solution.py:113
  208.1 5.0 %collective-permute-start.21 = (f32[64,512]{1,0:T(8,128)S(1)}, f32[64,512]{1,0:T(8,128)S(1)}, u32[]{:S(2)}, u32[]{:S(2)}) collective-permute-start(f32[64,512]{1,0:T(8,128)S(1)} %slice_add_fusion), channel_id=1, source_target_pairs={{0,4},{1,5},{2,6},{3,7},{4,0},{5,1},{6,2},{7,3},{8,12},{9,13},{10,... | collective-permute-start | bytes 393224 | tf_op jit(solution)/shard_map/ppermute | solution.py:113
  (14 other events, 71.5 us)
Sparse Core Ops, SparseCore 0:
  24.5 85.2 all-gather.1

commit v10 on v9

--- a/solution.py
+++ b/solution.py
@@ -5,8 +5,7 @@
 
 NCLS = 512
 PAD = 128
-AXES = ("y_lo", "x_hi", "x_lo", "z_hi", "z_lo", "y_hi", "core")
-CUBE = ("y_lo", "x_lo", "z_lo")
+AXES = ("blk", "dp")
 THREE = ((0, 1, 2), (1, 2, 0), (2, 0, 1))
 TWO = ((0, 1, 2), (2, 0, 1))
 
@@ -95,14 +94,6 @@
     )
 
 
-def sc_train_part(part):
-    rows, cols = part.shape
-    g = lax.all_gather(part, CUBE, axis=0, tiled=True).reshape(2, 2, 2, rows, cols)
-    for axis, name in enumerate(CUBE):
-        g = jnp.where(lax.axis_index(name) == 1, jnp.flip(g, axis), g)
-    return g.transpose(2, 0, 1, 3, 4).reshape(8 * rows, cols)
-
-
 def cube_reduce(blocks, mate, n):
     blocks = list(blocks)
     live = list(range(8))
@@ -125,36 +116,37 @@
     rows = train_grads.shape[0]
     tr = with_side(train_grads, (train_scale,) + split_class(train_class), 0)
     te = with_side(test_grads, split_class(test_class), 4)
-    te_all = cube_gather(te, test_mate, n, THREE)
-    cut = column_cuts(tr.shape[1], 3)
-    tr_parts = [chain(tr[:, cut[p]:cut[p + 1]], train_mate, n, THREE[p]) for p in range(2)]
-    tr_parts.append(sc_train_part(tr[:, cut[2]:]))
-    tr_mine = jnp.concatenate(tr_parts, axis=1)
-    tr_other = jnp.concatenate(
-        [lax.ppermute(t, AXES, core_pairs(n)) for t in tr_parts], axis=1
+    cut = column_cuts(te.shape[1], 3)
+    te_parts = [
+        chain(te[:, cut[p]:cut[p + 1]], test_mate, n, order) for p, order in enumerate(THREE)
+    ]
+    te_mine = jnp.concatenate(te_parts, axis=1)
+    te_other = jnp.concatenate(
+        [lax.ppermute(t, AXES, core_pairs(n)) for t in te_parts], axis=1
     )
-    test_hot = indicator(join_class(te_all, k + 4))
+    tr_all = cube_gather(tr, train_mate, n, TWO)
+    scale = tr_all[:, k].astype(jnp.float32)
+    train_hot = indicator(join_class(tr_all, k + 1))
 
     def weigh(t):
         raw = lax.dot_general(
-            t, te_all, (((1,), (1,)), ((), ())), preferred_element_type=jnp.float32
+            tr_all, t, (((1,), (1,)), ((), ())), preferred_element_type=jnp.float32
         )
-        scale = t[:, k].astype(jnp.float32)
         w = jnp.tanh(scale[:, None] * raw).astype(jnp.bfloat16)
-        hot = indicator(join_class(t, k + 1))
-        part = jnp.dot(w, test_hot, preferred_element_type=jnp.float32)
+        hot = indicator(join_class(t, k + 4))
+        part = jnp.dot(w, hot, preferred_element_type=jnp.float32)
         per_class = lax.dot_general(
-            w, hot, (((0,), (0,)), ((), ())), preferred_element_type=jnp.float32
+            w, train_hot, (((0,), (0,)), ((), ())), preferred_element_type=jnp.float32
         )
-        return part, per_class
+        test_part = jnp.sum(per_class * hot.astype(jnp.float32), axis=1)
+        return part, test_part
 
-    part_m, pc_m = weigh(tr_mine)
-    part_o, pc_o = weigh(tr_other)
-    part = part_m + lax.ppermute(part_o, AXES, core_pairs(n))
+    part_m, tp_m = weigh(te_mine)
+    part_o, tp_o = weigh(te_other)
     train_attr = cube_reduce(
-        [part[o * rows:(o + 1) * rows] for o in range(8)], train_mate, n
+        [(part_m + part_o)[o * rows:(o + 1) * rows] for o in range(8)], train_mate, n
     )
-    test_part = jnp.sum((pc_m + pc_o) * test_hot.astype(jnp.float32), axis=1)
+    test_part = tp_m + lax.ppermute(tp_o, AXES, core_pairs(n))
     test_attr = cube_reduce(
         [test_part[o * rows:(o + 1) * rows] for o in range(8)], test_mate, n
     )
@@ -162,7 +154,6 @@
 
 
 def solution(mesh):
-    fine = jax.sharding.Mesh(mesh.devices.reshape((2,) * 7), AXES)
     in_specs = (
         P(AXES, None),
         P(AXES),
@@ -171,4 +162,4 @@
         P(AXES),
     )
     out_specs = (P(AXES, None), P(AXES))
-    return jax.shard_map(local, mesh=fine, in_specs=in_specs, out_specs=out_specs, check_vma=False)
+    return jax.shard_map(local, mesh=mesh, in_specs=in_specs, out_specs=out_specs, check_vma=False)

time: 221 us -> 161 us (0.73)
  waiting for transfers between devices: 104 us -> 78.6 us
  starting transfers between devices: 39.9 us -> 26.1 us
  between operations: 14.5 us -> 0.93 us
  matrix products: 31 us -> 24.3 us
    ppermute x15, waiting for transfers between devices: 85.6 us -> 55.8 us  [chain(): got = lax.ppermute(buf, AXES, mate_pairs(n, a, mate))]
    ppermute x15, starting transfers between devices: 28.8 us -> 21.8 us  [chain(): got = lax.ppermute(buf, AXES, mate_pairs(n, a, mate))]
    dot_general x6, matrix products: 31 us -> 24.3 us  [the longest x2 20.1 us: weigh(): lax.dot_general(tr_all, t, (((1,), (1,)), ((), ())), preferred_element_ty...]
    ppermute x6, starting transfers between devices: 10.2 us -> 3.7 us  [cube_reduce(): lax.ppermute(jnp.concatenate([blocks[o] for o in send]), AXES, mate_pairs...]
    ppermute x6, waiting for transfers between devices: 16.9 us -> 22.2 us  [cube_reduce(): lax.ppermute(jnp.concatenate([blocks[o] for o in send]), AXES, mate_pairs...]
    unnamed x58 -> x30, local copies, waits for them, and re-layouts: 12.5 us -> 14.3 us
  transfers between devices with their start and end apart: 26 -> 25, of which waited for: 11 -> 15; matrix products, arithmetic and copies ran while one was open for 17% -> 23% of each run, Pallas kernels for 0% -> 0%
where the time goes in v10:
time: 161 us
  waiting for transfers between devices  78.6 us (49%)
  starting transfers between devices  26.1 us (16%)
  matrix products  24.3 us (15%)
  local copies, waits for them, and re-layouts  17.9 us (11%)
  other arithmetic  12.9 us (8%)
    ppermute x15, waiting for transfers between devices, chain(): got = lax.ppermute(buf, AXES, mate_pairs(n, a, mate))  55.8 us
    ppermute x6, waiting for transfers between devices, cube_reduce(): lax.ppermute(jnp.concatenate([blocks[o] for o in send]), AXES, mate_pairs...  22.2 us
    ppermute x15, starting transfers between devices, chain(): got = lax.ppermute(buf, AXES, mate_pairs(n, a, mate))  21.8 us
    dot_general x2, matrix products, weigh(): lax.dot_general(tr_all, t, (((1,), (1,)), ((), ())), preferred_element_ty...  20.1 us
    unnamed x30, local copies, waits for them, and re-layouts  14.3 us
    ppermute x6, starting transfers between devices, cube_reduce(): lax.ppermute(jnp.concatenate([blocks[o] for o in send]), AXES, mate_pairs...  3.7 us
    add x3, other arithmetic, join_class(): return hi * 32 + lo  3.66 us
  transfers between devices with their start and end apart: 25, of which 15 were waited for; matrix products, arithmetic and copies ran while one was open for 23% of the time, Pallas kernels for 0%

profile of v10, /device:TPU:0, one launch (start us, length us, event | category | flops | bytes accessed | tf_op | source)
XLA Modules:
  0.0 160.7 jit_solution(3096827448936138316)
XLA Ops:
  1.5 2.1 %fusion.53 = (bf16[64,2816]{1,0:T(8,128)(2,1)S(1)}, bf16[512,2816]{1,0:T(8,128)(2,1)}, bf16[512,2816]{1,0:T(8,128)(2,1)}, bf16[64,2816]{1,0:T(8,128)(2,1)S(1)}) fusion(bf16[64,8192]{1,0:T(8,128)(2,1)} %param.8, bf16[64,128]{1,0:T(8,128)(2,1)S(1)} %select_select_fusion), kind=kLoop, calls=%fused_computation.120 | loop fusion | flops 720894 | bytes 2867200 | tf_op jit(solution)/shard_map/slice | solution.py:121
  3.6 4.1 %collective-permute-start.12 = (bf16[64,2816]{1,0:T(8,128)(2,1)S(1)}, bf16[64,2816]{1,0:T(8,128)(2,1)S(1)}, u32[]{:S(2)}, u32[]{:S(2)}) collective-permute-start(bf16[64,2816]{1,0:T(8,128)(2,1)S(1)} %get-tuple-element.15), channel_id=1, source_target_pairs={{0,12},{1,13},{2,14},{3,15},{4,8},{5,9},{6,10},{7,11},{8,4},{9,5},... | collective-permute-start | bytes 1081352 | tf_op jit(solution)/shard_map/ppermute | solution.py:82
  7.7 3.0 %collective-permute-start.9 = (bf16[64,2816]{1,0:T(8,128)(2,1)S(1)}, bf16[64,2816]{1,0:T(8,128)(2,1)S(1)}, u32[]{:S(2)}, u32[]{:S(2)}) collective-permute-start(bf16[64,2816]{1,0:T(8,128)(2,1)S(1)} %get-tuple-element.12), channel_id=1, source_target_pairs={{0,66},{1,67},{2,64},{3,65},{4,70},{5,71},{6,68},{7,69},{8,74},{9,... | collective-permute-start | bytes 1081352 | tf_op jit(solution)/shard_map/ppermute | solution.py:82
  10.7 1.0 slice.199
  11.7 2.8 %collective-permute-start.6 = (bf16[64,2688]{1,0:T(8,128)(2,1)S(1)}, bf16[64,2688]{1,0:T(8,128)(2,1)S(1)}, u32[]{:S(2)}, u32[]{:S(2)}) collective-permute-start(bf16[64,2688]{1,0:T(8,128)(2,1)S(1)} %slice.199), channel_id=1, source_target_pairs={{0,48},{1,49},{2,50},{3,51},{4,52},{5,53},{6,54},{7,55},{8,56},{9,... | collective-permute-start | bytes 1032200 | tf_op jit(solution)/shard_map/ppermute | solution.py:82
  15.9 6.3 %collective-permute-done.6 = bf16[64,2688]{1,0:T(8,128)(2,1)S(1)} collective-permute-done((bf16[64,2688]{1,0:T(8,128)(2,1)S(1)}, bf16[64,2688]{1,0:T(8,128)(2,1)S(1)}, u32[]{:S(2)}, u32[]{:S(2)}) %collective-permute-start.6) | collective-permute-done | bytes 344096 | tf_op jit(solution)/shard_map/ppermute | solution.py:82
  22.7 2.8 %collective-permute-start.13 = (bf16[128,2816]{1,0:T(8,128)(2,1)S(1)}, bf16[128,2816]{1,0:T(8,128)(2,1)S(1)}, u32[]{:S(2)}, u32[]{:S(2)}) collective-permute-start(bf16[128,2816]{1,0:T(8,128)(2,1)S(1)} %pad_maximum_fusion.10), channel_id=1, source_target_pairs={{0,48},{1,49},{2,50},{3,51},{4,52},{5,53},{6,54},{7,55},{8,56},{9,... | collective-permute-start | bytes 2162696 | tf_op jit(solution)/shard_map/ppermute | solution.py:82
  26.0 2.6 %collective-permute-done.3 = bf16[64,4096]{1,0:T(8,128)(2,1)S(1)} collective-permute-done((bf16[64,4096]{1,0:T(8,128)(2,1)S(1)}, bf16[64,4096]{1,0:T(8,128)(2,1)S(1)}, u32[]{:S(2)}, u32[]{:S(2)}) %collective-permute-start.3) | collective-permute-done | bytes 524320 | tf_op jit(solution)/shard_map/ppermute | solution.py:82
  29.3 10.0 %collective-permute-done.7 = bf16[128,2688]{1,0:T(8,128)(2,1)S(1)} collective-permute-done((bf16[128,2688]{1,0:T(8,128)(2,1)S(1)}, bf16[128,2688]{1,0:T(8,128)(2,1)S(1)}, u32[]{:S(2)}, u32[]{:S(2)}) %collective-permute-start.7) | collective-permute-done | bytes 688160 | tf_op jit(solution)/shard_map/ppermute | solution.py:82
  40.3 3.0 %collective-permute-start.14 = (bf16[256,2816]{1,0:T(8,128)(2,1)S(1)}, bf16[256,2816]{1,0:T(8,128)(2,1)S(1)}, u32[]{:S(2)}, u32[]{:S(2)}) collective-permute-start(bf16[256,2816]{1,0:T(8,128)(2,1)S(1)} %pad_maximum_fusion.5), channel_id=1, source_target_pairs={{0,66},{1,67},{2,64},{3,65},{4,70},{5,71},{6,68},{7,69},{8,74},{9,... | collective-permute-start | bytes 4325384 | tf_op jit(solution)/shard_map/ppermute | solution.py:82
  43.2 1.6 collective-permute-done.10
  44.9 1.3 collective-permute-start.11
  46.9 4.9 %collective-permute-done.4 = bf16[128,4096]{1,0:T(8,128)(2,1)S(1)} collective-permute-done((bf16[128,4096]{1,0:T(8,128)(2,1)S(1)}, bf16[128,4096]{1,0:T(8,128)(2,1)S(1)}, u32[]{:S(2)}, u32[]{:S(2)}) %collective-permute-start.4) | collective-permute-done | bytes 1048608 | tf_op jit(solution)/shard_map/ppermute | solution.py:82
  52.0 1.5 collective-permute-start.5
  55.6 16.7 %collective-permute-done.8 = bf16[256,2688]{1,0:T(8,128)(2,1)S(1)} collective-permute-done((bf16[256,2688]{1,0:T(8,128)(2,1)S(1)}, bf16[256,2688]{1,0:T(8,128)(2,1)S(1)}, u32[]{:S(2)}, u32[]{:S(2)}) %collective-permute-start.8) | collective-permute-done | bytes 1376288 | tf_op jit(solution)/shard_map/ppermute | solution.py:82
  72.3 1.7 %pad_maximum_fusion.1 = bf16[512,2688]{1,0:T(8,128)(2,1)} fusion(bf16[256,2688]{1,0:T(8,128)(2,1)S(1)} %collective-permute-done.8, bf16[128,2688]{1,0:T(8,128)(2,1)S(1)} %collective-permute-done.7, bf16[64,2688]{1,0:T(8,128)(2,1)S(1)} %collective-permute-done.6, bf16[64,2688]{1,0:T(8,128)(2,1)S(1)} %slice.199), kind=kLoop, calls=%fused_computation.19 | loop fusion | flops 11010048 | bytes 5505024 | tf_op jit(solution)/shard_map/concatenate | solution.py:86
  84.6 1.2 add_reduce_fusion.2
  85.8 13.6 %collective-permute-done.2 = bf16[256,4224]{1,0:T(8,128)(2,1)S(1)} collective-permute-done((bf16[256,4224]{1,0:T(8,128)(2,1)S(1)}, bf16[256,4224]{1,0:T(8,128)(2,1)S(1)}, u32[]{:S(2)}, u32[]{:S(2)}) %collective-permute-start.2) | collective-permute-done | bytes 2162720 | tf_op jit(solution)/shard_map/ppermute | solution.py:82
  104.4 1.0 convert_reduce_fusion
  105.4 1.2 add_reduce_fusion
  106.7 9.2 %fusion.33 = bf16[512,512]{1,0:T(8,128)(2,1)S(1)} fusion(bf16[512,2816]{1,0:T(8,128)(2,1)} %slice_dynamic-update-slice_fusion.6, bf16[512,2816]{1,0:T(8,128)(2,1)} %slice_dynamic-update-slice_fusion.12, bf16[256,2688]{1,0:T(8,128)(2,1)S(1)} %collective-permute-done.8, bf16[128,2688]{1,0:T(8,128)(2,1)S(1)} %collective-permute-done.7, ...), kind=kOutput, calls=%fused_computation.33 | convolution fusion | flops 4456316928 | bytes 17565696 | tf_op jit(solution)/shard_map/dot_general | solution.py:132
  117.0 1.2 add_reduce_fusion.1
  118.3 10.8 %fusion.30 = bf16[512,512]{1,0:T(8,128)(2,1)} fusion(bf16[512,2816]{1,0:T(8,128)(2,1)} %collective-permute-done.17, bf16[512,2816]{1,0:T(8,128)(2,1)} %collective-permute-done.16, bf16[512,2688]{1,0:T(8,128)(2,1)} %collective-permute-done.15, f32[512]{0:T(512)S(1)} %convert_reduce_fusion, bf16[512,4224]{1,0:T(8,128)(2,1)} %slice_dynamic-update-slice_fusion, ...), kind=kOutput, calls=%fused_computation.32 | convolution fusion | flops 4430757888 | bytes 17565696 | tf_op jit(solution)/shard_map/dot_general | solution.py:132
  129.1 1.6 %fusion.37 = f32[512]{0:T(512)S(1)} fusion(bf16[512,512]{1,0:T(8,128)(2,1)} %fusion.30, s32[512]{0:T(512)S(1)} %add_reduce_fusion, s32[512]{0:T(512)S(1)} %add_reduce_fusion.1), kind=kOutput, calls=%fused_computation.35 | convolution fusion | flops 270007808 | bytes 530432 | tf_op jit(solution)/shard_map/dot_general | solution.py:138
  130.7 1.5 convolution_add_fusion
  134.2 4.3 %collective-permute-done.22 = f32[256]{0:T(256)S(1)} collective-permute-done((f32[256]{0:T(256)S(1)}, f32[256]{0:T(256)S(1)}, u32[]{:S(2)}, u32[]{:S(2)}) %collective-permute-start.22) | collective-permute-done | bytes 1056 | tf_op jit(solution)/shard_map/ppermute | solution.py:104
  138.6 8.3 %collective-permute-done.18 = f32[256,512]{1,0:T(8,128)S(1)} collective-permute-done((f32[256,512]{1,0:T(8,128)S(1)}, f32[256,512]{1,0:T(8,128)S(1)}, u32[]{:S(2)}, u32[]{:S(2)}) %collective-permute-start.18) | collective-permute-done | bytes 524320 | tf_op jit(solution)/shard_map/ppermute | solution.py:104
  146.9 1.3 collective-permute-start.19
  148.6 4.4 %collective-permute-done.23 = f32[128]{0:T(128)S(1)} collective-permute-done((f32[128]{0:T(128)S(1)}, f32[128]{0:T(128)S(1)}, u32[]{:S(2)}, u32[]{:S(2)}) %collective-permute-start.23) | collective-permute-done | bytes 544 | tf_op jit(solution)/shard_map/ppermute | solution.py:104
  153.3 1.6 %collective-permute-done.19 = f32[128,512]{1,0:T(8,128)S(1)} collective-permute-done((f32[128,512]{1,0:T(8,128)S(1)}, f32[128,512]{1,0:T(8,128)S(1)}, u32[]{:S(2)}, u32[]{:S(2)}) %collective-permute-start.19) | collective-permute-done | bytes 262176 | tf_op jit(solution)/shard_map/ppermute | solution.py:104
  155.9 2.0 %collective-permute-done.24 = f32[64]{0:T(128)S(1)} collective-permute-done((f32[64]{0:T(128)S(1)}, f32[64]{0:T(128)S(1)}, u32[]{:S(2)}, u32[]{:S(2)}) %collective-permute-start.24) | collective-permute-done | bytes 288 | tf_op jit(solution)/shard_map/ppermute | solution.py:104
  158.4 1.6 %collective-permute-done.20 = f32[64,512]{1,0:T(8,128)S(1)} collective-permute-done((f32[64,512]{1,0:T(8,128)S(1)}, f32[64,512]{1,0:T(8,128)S(1)}, u32[]{:S(2)}, u32[]{:S(2)}) %collective-permute-start.20) | collective-permute-done | bytes 131104 | tf_op jit(solution)/shard_map/ppermute | solution.py:104
  (96 shorter events, 29.4 us)
Async XLA Ops:
  0.6 13.9 %copy-start.5 = (s32[64]{0:T(128)S(1)}, s32[64]{0:T(128)}, u32[]{:S(2)}) copy-start(s32[64]{0:T(128)} %param.7) | copy-start | bytes 772
  0.6 14.0 %copy-start.4 = (bf16[64]{0:T(256)(128)(2,1)S(1)}, bf16[64]{0:T(256)(128)(2,1)}, u32[]{:S(2)}) copy-start(bf16[64]{0:T(256)(128)(2,1)} %param.6) | copy-start | bytes 388
  0.6 14.1 %copy-start = (bf16[64,8192]{1,0:T(8,128)(2,1)S(1)}, bf16[64,8192]{1,0:T(8,128)(2,1)}, u32[]{:S(2)}) copy-start(bf16[64,8192]{1,0:T(8,128)(2,1)} %param.5) | copy-start | bytes 3145732
  3.6 19.1 %collective-permute-start.12 = (bf16[64,2816]{1,0:T(8,128)(2,1)S(1)}, bf16[64,2816]{1,0:T(8,128)(2,1)S(1)}, u32[]{:S(2)}, u32[]{:S(2)}) collective-permute-start(bf16[64,2816]{1,0:T(8,128)(2,1)S(1)} %get-tuple-element.15), channel_id=1, source_target_pairs={{0,12},{1,13},{2,14},{3,15},{4,8},{5,9},{6,10},{7,11},{8,4},{9,5},... | collective-permute-start | bytes 1081352 | tf_op jit(solution)/shard_map/ppermute | solution.py:82
  7.7 17.9 %collective-permute-start.9 = (bf16[64,2816]{1,0:T(8,128)(2,1)S(1)}, bf16[64,2816]{1,0:T(8,128)(2,1)S(1)}, u32[]{:S(2)}, u32[]{:S(2)}) collective-permute-start(bf16[64,2816]{1,0:T(8,128)(2,1)S(1)} %get-tuple-element.12), channel_id=1, source_target_pairs={{0,66},{1,67},{2,64},{3,65},{4,70},{5,71},{6,68},{7,69},{8,74},{9,... | collective-permute-start | bytes 1081352 | tf_op jit(solution)/shard_map/ppermute | solution.py:82
  11.7 10.5 %collective-permute-start.6 = (bf16[64,2688]{1,0:T(8,128)(2,1)S(1)}, bf16[64,2688]{1,0:T(8,128)(2,1)S(1)}, u32[]{:S(2)}, u32[]{:S(2)}) collective-permute-start(bf16[64,2688]{1,0:T(8,128)(2,1)S(1)} %slice.199), channel_id=1, source_target_pairs={{0,48},{1,49},{2,50},{3,51},{4,52},{5,53},{6,54},{7,55},{8,56},{9,... | collective-permute-start | bytes 1032200 | tf_op jit(solution)/shard_map/ppermute | solution.py:82
  15.6 13.2 %collective-permute-start = (bf16[64,4224]{1,0:T(8,128)(2,1)S(1)}, bf16[64,4224]{1,0:T(8,128)(2,1)S(1)}, u32[]{:S(2)}, u32[]{:S(2)}) collective-permute-start(bf16[64,4224]{1,0:T(8,128)(2,1)S(1)} %get-tuple-element.3), channel_id=1, source_target_pairs={{0,4},{1,5},{2,6},{3,7},{4,0},{5,1},{6,2},{7,3},{8,12},{9,13},{10,... | collective-permute-start | bytes 1622024 | tf_op jit(solution)/shard_map/ppermute | solution.py:82
  15.6 12.9 %collective-permute-start.3 = (bf16[64,4096]{1,0:T(8,128)(2,1)S(1)}, bf16[64,4096]{1,0:T(8,128)(2,1)S(1)}, u32[]{:S(2)}, u32[]{:S(2)}) collective-permute-start(bf16[64,4096]{1,0:T(8,128)(2,1)S(1)} %slice.198), channel_id=1, source_target_pairs={{0,16},{1,17},{2,18},{3,19},{4,20},{5,21},{6,22},{7,23},{8,24},{9,... | collective-permute-start | bytes 1572872 | tf_op jit(solution)/shard_map/ppermute | solution.py:82
  22.3 17.0 %collective-permute-start.7 = (bf16[128,2688]{1,0:T(8,128)(2,1)S(1)}, bf16[128,2688]{1,0:T(8,128)(2,1)S(1)}, u32[]{:S(2)}, u32[]{:S(2)}) collective-permute-start(bf16[128,2688]{1,0:T(8,128)(2,1)S(1)} %pad_maximum_fusion.11), channel_id=1, source_target_pairs={{0,66},{1,67},{2,64},{3,65},{4,70},{5,71},{6,68},{7,69},{8,74},{9,... | collective-permute-start | bytes 2064392 | tf_op jit(solution)/shard_map/ppermute | solution.py:82
  22.7 17.5 %collective-permute-start.13 = (bf16[128,2816]{1,0:T(8,128)(2,1)S(1)}, bf16[128,2816]{1,0:T(8,128)(2,1)S(1)}, u32[]{:S(2)}, u32[]{:S(2)}) collective-permute-start(bf16[128,2816]{1,0:T(8,128)(2,1)S(1)} %pad_maximum_fusion.10), channel_id=1, source_target_pairs={{0,48},{1,49},{2,50},{3,51},{4,52},{5,53},{6,54},{7,55},{8,56},{9,... | collective-permute-start | bytes 2162696 | tf_op jit(solution)/shard_map/ppermute | solution.py:82
  25.6 19.2 %collective-permute-start.10 = (bf16[128,2816]{1,0:T(8,128)(2,1)S(1)}, bf16[128,2816]{1,0:T(8,128)(2,1)S(1)}, u32[]{:S(2)}, u32[]{:S(2)}) collective-permute-start(bf16[128,2816]{1,0:T(8,128)(2,1)S(1)} %pad_maximum_fusion.9), channel_id=1, source_target_pairs={{0,12},{1,13},{2,14},{3,15},{4,8},{5,9},{6,10},{7,11},{8,4},{9,5},... | collective-permute-start | bytes 2162696 | tf_op jit(solution)/shard_map/ppermute | solution.py:82
  28.6 23.2 %collective-permute-start.4 = (bf16[128,4096]{1,0:T(8,128)(2,1)S(1)}, bf16[128,4096]{1,0:T(8,128)(2,1)S(1)}, u32[]{:S(2)}, u32[]{:S(2)}) collective-permute-start(bf16[128,4096]{1,0:T(8,128)(2,1)S(1)} %pad_maximum_fusion.8), channel_id=1, source_target_pairs={{0,64},{1,65},{2,66},{3,67},{4,68},{5,69},{6,70},{7,71},{8,72},{9,... | collective-permute-start | bytes 3145736 | tf_op jit(solution)/shard_map/ppermute | solution.py:82
  28.9 24.6 %collective-permute-start.1 = (bf16[128,4224]{1,0:T(8,128)(2,1)S(1)}, bf16[128,4224]{1,0:T(8,128)(2,1)S(1)}, u32[]{:S(2)}, u32[]{:S(2)}) collective-permute-start(bf16[128,4224]{1,0:T(8,128)(2,1)S(1)} %pad_maximum_fusion.7), channel_id=1, source_target_pairs={{0,16},{1,17},{2,18},{3,19},{4,20},{5,21},{6,22},{7,23},{8,24},{9,... | collective-permute-start | bytes 3244040 | tf_op jit(solution)/shard_map/ppermute | solution.py:82
  39.4 32.9 %collective-permute-start.8 = (bf16[256,2688]{1,0:T(8,128)(2,1)S(1)}, bf16[256,2688]{1,0:T(8,128)(2,1)S(1)}, u32[]{:S(2)}, u32[]{:S(2)}) collective-permute-start(bf16[256,2688]{1,0:T(8,128)(2,1)S(1)} %pad_maximum_fusion.6), channel_id=1, source_target_pairs={{0,12},{1,13},{2,14},{3,15},{4,8},{5,9},{6,10},{7,11},{8,4},{9,5},... | collective-permute-start | bytes 4128776 | tf_op jit(solution)/shard_map/ppermute | solution.py:82
  40.3 33.8 %collective-permute-start.14 = (bf16[256,2816]{1,0:T(8,128)(2,1)S(1)}, bf16[256,2816]{1,0:T(8,128)(2,1)S(1)}, u32[]{:S(2)}, u32[]{:S(2)}) collective-permute-start(bf16[256,2816]{1,0:T(8,128)(2,1)S(1)} %pad_maximum_fusion.5), channel_id=1, source_target_pairs={{0,66},{1,67},{2,64},{3,65},{4,70},{5,71},{6,68},{7,69},{8,74},{9,... | collective-permute-start | bytes 4325384 | tf_op jit(solution)/shard_map/ppermute | solution.py:82
  44.9 34.2 %collective-permute-start.11 = (bf16[256,2816]{1,0:T(8,128)(2,1)S(1)}, bf16[256,2816]{1,0:T(8,128)(2,1)S(1)}, u32[]{:S(2)}, u32[]{:S(2)}) collective-permute-start(bf16[256,2816]{1,0:T(8,128)(2,1)S(1)} %pad_maximum_fusion.4), channel_id=1, source_target_pairs={{0,48},{1,49},{2,50},{3,51},{4,52},{5,53},{6,54},{7,55},{8,56},{9,... | collective-permute-start | bytes 4325384 | tf_op jit(solution)/shard_map/ppermute | solution.py:82
  51.8 1.9 %copy-start.1 = (bf16[128,4096]{1,0:T(8,128)(2,1)}, bf16[128,4096]{1,0:T(8,128)(2,1)S(1)}, u32[]{:S(2)}) copy-start(bf16[128,4096]{1,0:T(8,128)(2,1)S(1)} %collective-permute-done.4) | copy-start | bytes 3145732
  52.0 54.7 %collective-permute-start.5 = (bf16[256,4096]{1,0:T(8,128)(2,1)S(1)}, bf16[256,4096]{1,0:T(8,128)(2,1)}, u32[]{:S(2)}, u32[]{:S(2)}) collective-permute-start(bf16[256,4096]{1,0:T(8,128)(2,1)S(1)} %pad_maximum_fusion.3), channel_id=1, source_target_pairs={{0,4},{1,5},{2,6},{3,7},{4,0},{5,1},{6,2},{7,3},{8,12},{9,13},{10,... | collective-permute-start | bytes 6291464 | tf_op jit(solution)/shard_map/ppermute | solution.py:82
  53.7 45.6 %collective-permute-start.2 = (bf16[256,4224]{1,0:T(8,128)(2,1)S(1)}, bf16[256,4224]{1,0:T(8,128)(2,1)S(1)}, u32[]{:S(2)}, u32[]{:S(2)}) collective-permute-start(bf16[256,4224]{1,0:T(8,128)(2,1)S(1)} %pad_maximum_fusion.2), channel_id=1, source_target_pairs={{0,64},{1,65},{2,66},{3,67},{4,68},{5,69},{6,70},{7,71},{8,72},{9,... | collective-permute-start | bytes 6488072 | tf_op jit(solution)/shard_map/ppermute | solution.py:82
  74.0 44.2 %collective-permute-start.15 = (bf16[512,2688]{1,0:T(8,128)(2,1)}, bf16[512,2688]{1,0:T(8,128)(2,1)}, u32[]{:S(2)}, u32[]{:S(2)}) collective-permute-start(bf16[512,2688]{1,0:T(8,128)(2,1)} %pad_maximum_fusion.1), channel_id=1, source_target_pairs={{0,1},{1,0},{2,3},{3,2},{4,5},{5,4},{6,7},{7,6},{8,9},{9,8},{10,11... | collective-permute-start | bytes 8257544 | tf_op jit(solution)/shard_map/ppermute | solution.py:125
  78.6 38.4 %collective-permute-start.17 = (bf16[512,2816]{1,0:T(8,128)(2,1)}, bf16[512,2816]{1,0:T(8,128)(2,1)}, u32[]{:S(2)}, u32[]{:S(2)}) collective-permute-start(bf16[512,2816]{1,0:T(8,128)(2,1)} %slice_dynamic-update-slice_fusion.6), channel_id=1, source_target_pairs={{0,1},{1,0},{2,3},{3,2},{4,5},{5,4},{6,7},{7,6},{8,9},{9,8},{10,11... | collective-permute-start | bytes 8650760 | tf_op jit(solution)/shard_map/ppermute | solution.py:125
  84.6 33.7 %collective-permute-start.16 = (bf16[512,2816]{1,0:T(8,128)(2,1)}, bf16[512,2816]{1,0:T(8,128)(2,1)}, u32[]{:S(2)}, u32[]{:S(2)}) collective-permute-start(bf16[512,2816]{1,0:T(8,128)(2,1)} %slice_dynamic-update-slice_fusion.12), channel_id=1, source_target_pairs={{0,1},{1,0},{2,3},{3,2},{4,5},{5,4},{6,7},{7,6},{8,9},{9,8},{10,11... | collective-permute-start | bytes 8650760 | tf_op jit(solution)/shard_map/ppermute | solution.py:125
  100.2 6.5 %copy-start.2 = (bf16[128,4096]{1,0:T(8,128)(2,1)S(1)}, bf16[128,4096]{1,0:T(8,128)(2,1)}, u32[]{:S(2)}) copy-start(bf16[128,4096]{1,0:T(8,128)(2,1)} %copy-done.1) | copy-start | bytes 3145732
  115.9 2.4 %copy-start.3 = (bf16[128,4096]{1,0:T(8,128)(2,1)S(1)}, bf16[128,4096]{1,0:T(8,128)(2,1)}, u32[]{:S(2)}) copy-start(bf16[128,4096]{1,0:T(8,128)(2,1)} %copy-done.1) | copy-start | bytes 3145732
  132.3 1.2 collective-permute-start.21
  132.5 14.4 %collective-permute-start.18 = (f32[256,512]{1,0:T(8,128)S(1)}, f32[256,512]{1,0:T(8,128)S(1)}, u32[]{:S(2)}, u32[]{:S(2)}) collective-permute-start(f32[256,512]{1,0:T(8,128)S(1)} %pad_maximum_fusion.13), channel_id=1, source_target_pairs={{0,16},{1,17},{2,18},{3,19},{4,20},{5,21},{6,22},{7,23},{8,24},{9,... | collective-permute-start | bytes 1572872 | tf_op jit(solution)/shard_map/ppermute | solution.py:104
  133.7 4.8 %collective-permute-start.22 = (f32[256]{0:T(256)S(1)}, f32[256]{0:T(256)S(1)}, u32[]{:S(2)}, u32[]{:S(2)}) collective-permute-start(f32[256]{0:T(256)S(1)} %pad_maximum_fusion.16), channel_id=1, source_target_pairs={{0,48},{1,49},{2,50},{3,51},{4,52},{5,53},{6,54},{7,55},{8,56},{9,... | collective-permute-start | bytes 3080 | tf_op jit(solution)/shard_map/ppermute | solution.py:104
  146.9 8.0 %collective-permute-start.19 = (f32[128,512]{1,0:T(8,128)S(1)}, f32[128,512]{1,0:T(8,128)S(1)}, u32[]{:S(2)}, u32[]{:S(2)}) collective-permute-start(f32[128,512]{1,0:T(8,128)S(1)} %pad_maximum_fusion.15), channel_id=1, source_target_pairs={{0,64},{1,65},{2,66},{3,67},{4,68},{5,69},{6,70},{7,71},{8,72},{9,... | collective-permute-start | bytes 786440 | tf_op jit(solution)/shard_map/ppermute | solution.py:104
  148.3 4.8 %collective-permute-start.23 = (f32[128]{0:T(128)S(1)}, f32[128]{0:T(128)S(1)}, u32[]{:S(2)}, u32[]{:S(2)}) collective-permute-start(f32[128]{0:T(128)S(1)} %pad_maximum_fusion.17), channel_id=1, source_target_pairs={{0,66},{1,67},{2,64},{3,65},{4,70},{5,71},{6,68},{7,69},{8,74},{9,... | collective-permute-start | bytes 1544 | tf_op jit(solution)/shard_map/ppermute | solution.py:104
  153.1 4.8 %collective-permute-start.24 = (f32[64]{0:T(128)S(1)}, f32[64]{0:T(128)S(1)}, u32[]{:S(2)}, u32[]{:S(2)}) collective-permute-start(f32[64]{0:T(128)S(1)} %slice_add_fusion.6), channel_id=1, source_target_pairs={{0,12},{1,13},{2,14},{3,15},{4,8},{5,9},{6,10},{7,11},{8,4},{9,5},... | collective-permute-start | bytes 776 | tf_op jit(solution)/shard_map/ppermute | solution.py:104
  155.0 5.0 %collective-permute-start.20 = (f32[64,512]{1,0:T(8,128)S(1)}, f32[64,512]{1,0:T(8,128)S(1)}, u32[]{:S(2)}, u32[]{:S(2)}) collective-permute-start(f32[64,512]{1,0:T(8,128)S(1)} %slice_add_fusion), channel_id=1, source_target_pairs={{0,4},{1,5},{2,6},{3,7},{4,0},{5,1},{6,2},{7,3},{8,12},{9,13},{10,... | collective-permute-start | bytes 393224 | tf_op jit(solution)/shard_map/ppermute | solution.py:104

commit v11 on v10

--- a/solution.py
+++ b/solution.py
@@ -16,12 +16,13 @@
 
 
 def with_side(grads, side, first):
-    rows = grads.shape[0]
+    rows, k = grads.shape
     cols = lax.broadcasted_iota(jnp.int32, (rows, PAD), 1)
     extra = jnp.zeros((rows, PAD), jnp.bfloat16)
-    for k, v in enumerate(side):
-        extra = jnp.where(cols == first + k, v[:, None].astype(jnp.bfloat16), extra)
-    return jnp.concatenate([grads, extra], axis=1)
+    for j, v in enumerate(side):
+        extra = jnp.where(cols == first + j, v[:, None].astype(jnp.bfloat16), extra)
+    h = k // 2
+    return jnp.concatenate([grads[:, :h], extra, grads[:, h:], extra], axis=1)
 
 
 def split_class(c):
@@ -83,7 +84,20 @@
         buf = jnp.concatenate([buf, got])
         labs = labs + [o ^ (1 << a) for o in labs]
     at = {o: i for i, o in enumerate(labs)}
-    return jnp.concatenate([buf[at[o] * rows:(at[o] + 1) * rows] for o in range(8)])
+    return [buf[at[o] * rows:(at[o] + 1) * rows] for o in range(8)]
+
+
+def half_gather(shard, mate, n, orders):
+    r, cols = shard.shape
+    h = cols // 2
+    c = lax.axis_index(AXES) % 2
+    mine = lax.dynamic_slice_in_dim(shard, c * h, h, axis=1)
+    give = lax.dynamic_slice_in_dim(shard, (1 - c) * h, h, axis=1)
+    unit = jnp.concatenate([mine, lax.ppermute(give, AXES, core_pairs(n))])
+    cut = column_cuts(h, len(orders))
+    parts = [chain(unit[:, cut[p]:cut[p + 1]], mate, n, order) for p, order in enumerate(orders)]
+    blocks = [jnp.concatenate([parts[p][o] for p in range(len(orders))], axis=1) for o in range(8)]
+    return jnp.concatenate([b[:r] for b in blocks] + [b[r:] for b in blocks])
 
 
 def cube_gather(shard, mate, n, orders):
@@ -116,37 +130,32 @@
     rows = train_grads.shape[0]
     tr = with_side(train_grads, (train_scale,) + split_class(train_class), 0)
     te = with_side(test_grads, split_class(test_class), 4)
-    cut = column_cuts(te.shape[1], 3)
-    te_parts = [
-        chain(te[:, cut[p]:cut[p + 1]], test_mate, n, order) for p, order in enumerate(THREE)
-    ]
-    te_mine = jnp.concatenate(te_parts, axis=1)
-    te_other = jnp.concatenate(
-        [lax.ppermute(t, AXES, core_pairs(n)) for t in te_parts], axis=1
+    side = k // 2
+    te_all = half_gather(te, test_mate, n, THREE)
+    tr_all = half_gather(tr, train_mate, n, TWO)
+    half = 8 * rows
+
+    def partial(t):
+        return lax.dot_general(
+            t, te_all, (((1,), (1,)), ((), ())), preferred_element_type=jnp.float32
+        )
+
+    got = lax.ppermute(partial(tr_all[half:]), AXES, core_pairs(n))
+    raw = partial(tr_all[:half]) + jnp.concatenate([got[:, half:], got[:, :half]], axis=1)
+    tr_mine = tr_all[:half]
+    scale = tr_mine[:, side].astype(jnp.float32)
+    train_hot = indicator(join_class(tr_mine, side + 1))
+    test_hot = indicator(join_class(te_all, side + 4))
+    w = jnp.tanh(scale[:, None] * raw).astype(jnp.bfloat16)
+    part = jnp.dot(w, test_hot, preferred_element_type=jnp.float32)
+    per_class = lax.dot_general(
+        w, train_hot, (((0,), (0,)), ((), ())), preferred_element_type=jnp.float32
     )
-    tr_all = cube_gather(tr, train_mate, n, TWO)
-    scale = tr_all[:, k].astype(jnp.float32)
-    train_hot = indicator(join_class(tr_all, k + 1))
-
-    def weigh(t):
-        raw = lax.dot_general(
-            tr_all, t, (((1,), (1,)), ((), ())), preferred_element_type=jnp.float32
-        )
-        w = jnp.tanh(scale[:, None] * raw).astype(jnp.bfloat16)
-        hot = indicator(join_class(t, k + 4))
-        part = jnp.dot(w, hot, preferred_element_type=jnp.float32)
-        per_class = lax.dot_general(
-            w, train_hot, (((0,), (0,)), ((), ())), preferred_element_type=jnp.float32
-        )
-        test_part = jnp.sum(per_class * hot.astype(jnp.float32), axis=1)
-        return part, test_part
-
-    part_m, tp_m = weigh(te_mine)
-    part_o, tp_o = weigh(te_other)
+    tp = jnp.sum(per_class * test_hot.astype(jnp.float32), axis=1)
     train_attr = cube_reduce(
-        [(part_m + part_o)[o * rows:(o + 1) * rows] for o in range(8)], train_mate, n
+        [part[o * rows:(o + 1) * rows] for o in range(8)], train_mate, n
     )
-    test_part = tp_m + lax.ppermute(tp_o, AXES, core_pairs(n))
+    test_part = tp[:half] + lax.ppermute(tp[half:], AXES, core_pairs(n))
     test_attr = cube_reduce(
         [test_part[o * rows:(o + 1) * rows] for o in range(8)], test_mate, n
     )

time: 161 us -> 147 us (0.913)
  matrix products: 24.3 us -> 11.2 us
  local copies, waits for them, and re-layouts: 17.9 us -> 5.51 us
  waiting for transfers between devices: 78.6 us -> 87.5 us
  starting transfers between devices: 26.1 us -> 34.5 us
  other arithmetic: 12.9 us -> 6.94 us
    dot_general x6 -> x4, matrix products: 24.3 us -> 11.2 us  [the longest x2 9.58 us: partial(): lax.dot_general(t, te_all, (((1,), (1,)), ((), ())), preferred_element_ty...]
    unnamed x30 -> x25, local copies, waits for them, and re-layouts: 14.3 us -> 2.74 us
    ppermute x15, waiting for transfers between devices: 55.8 us -> 63 us  [chain(): got = lax.ppermute(buf, AXES, mate_pairs(n, a, mate))]
    ppermute x15, starting transfers between devices: 21.8 us -> 28.4 us  [chain(): got = lax.ppermute(buf, AXES, mate_pairs(n, a, mate))]
    ppermute x4, waiting for transfers between devices: 0.61 us -> 3.91 us  [the longest x1 3.37 us: local(): got = lax.ppermute(partial(tr_all[half:]), AXES, core_pairs(n))]
    add x3 -> x2, other arithmetic: 3.66 us -> 0.65 us  [join_class(): return hi * 32 + lo]
    concatenate x3 -> x1, local copies, waits for them, and re-layouts: 2.36 us -> 0.05 us  [half_gather(): return jnp.concatenate([b[:r] for b in blocks] + [b[r:] for b in blocks])]
    slice x1, other arithmetic: 2.06 us -> 0.05 us  [half_gather(): unit[:, cut[p]:cut[p + 1]]]
  transfers between devices with their start and end apart: 25 -> 25, of which waited for: 15 -> 20; matrix products, arithmetic and copies ran while one was open for 23% -> 5% of each run, Pallas kernels for 0% -> 0%
where the time goes in v11:
time: 147 us
  waiting for transfers between devices  87.5 us (60%)
  starting transfers between devices  34.5 us (23%)
  matrix products  11.2 us (8%)
  other arithmetic  6.94 us (5%)
  local copies, waits for them, and re-layouts  5.51 us (4%)
    ppermute x15, waiting for transfers between devices, chain(): got = lax.ppermute(buf, AXES, mate_pairs(n, a, mate))  63 us
    ppermute x15, starting transfers between devices, chain(): got = lax.ppermute(buf, AXES, mate_pairs(n, a, mate))  28.4 us
    ppermute x6, waiting for transfers between devices, cube_reduce(): lax.ppermute(jnp.concatenate([blocks[o] for o in send]), AXES, mate_pairs...  20.6 us
    dot_general x2, matrix products, partial(): lax.dot_general(t, te_all, (((1,), (1,)), ((), ())), preferred_element_ty...  9.58 us
    ppermute x6, starting transfers between devices, cube_reduce(): lax.ppermute(jnp.concatenate([blocks[o] for o in send]), AXES, mate_pairs...  5.64 us
    ppermute x1, waiting for transfers between devices, local(): got = lax.ppermute(partial(tr_all[half:]), AXES, core_pairs(n))  3.37 us
  transfers between devices with their start and end apart: 25, of which 20 were waited for; matrix products, arithmetic and copies ran while one was open for 5% of the time, Pallas kernels for 0%

profile of v11, /device:TPU:0, one launch (start us, length us, event | category | flops | bytes accessed | tf_op | source)
XLA Modules:
  0.0 147.1 jit_solution(15929005360058544522)
XLA Ops:
  0.7 1.3 fusion.43
  5.1 2.9 %collective-permute-start.8 = (bf16[128,1408]{1,0:T(8,128)(2,1)S(1)}, bf16[128,1408]{1,0:T(8,128)(2,1)S(1)}, u32[]{:S(2)}, u32[]{:S(2)}) collective-permute-start(bf16[128,1408]{1,0:T(8,128)(2,1)S(1)} %get-tuple-element.46), channel_id=1, source_target_pairs={{0,48},{1,49},{2,50},{3,51},{4,52},{5,53},{6,54},{7,55},{8,56},{9,... | collective-permute-start | bytes 1081352 | tf_op jit(solution)/shard_map/ppermute | solution.py:83
  8.0 4.0 %collective-permute-start.12 = (bf16[128,1408]{1,0:T(8,128)(2,1)S(1)}, bf16[128,1408]{1,0:T(8,128)(2,1)S(1)}, u32[]{:S(2)}, u32[]{:S(2)}) collective-permute-start(bf16[128,1408]{1,0:T(8,128)(2,1)S(1)} %get-tuple-element.47), channel_id=1, source_target_pairs={{0,12},{1,13},{2,14},{3,15},{4,8},{5,9},{6,10},{7,11},{8,4},{9,5},... | collective-permute-start | bytes 1081352 | tf_op jit(solution)/shard_map/ppermute | solution.py:83
  12.1 3.0 %collective-permute-start.9 = (bf16[128,1408]{1,0:T(8,128)(2,1)S(1)}, bf16[128,1408]{1,0:T(8,128)(2,1)S(1)}, u32[]{:S(2)}, u32[]{:S(2)}) collective-permute-start(bf16[128,1408]{1,0:T(8,128)(2,1)S(1)} %get-tuple-element.48), channel_id=1, source_target_pairs={{0,66},{1,67},{2,64},{3,65},{4,70},{5,71},{6,68},{7,69},{8,74},{9,... | collective-permute-start | bytes 1081352 | tf_op jit(solution)/shard_map/ppermute | solution.py:83
  16.9 3.2 %collective-permute-start.14 = (bf16[256,1408]{1,0:T(8,128)(2,1)S(1)}, bf16[256,1408]{1,0:T(8,128)(2,1)S(1)}, u32[]{:S(2)}, u32[]{:S(2)}) collective-permute-start(bf16[256,1408]{1,0:T(8,128)(2,1)S(1)} %pad_maximum_fusion.18), channel_id=1, source_target_pairs={{0,66},{1,67},{2,64},{3,65},{4,70},{5,71},{6,68},{7,69},{8,74},{9,... | collective-permute-start | bytes 2162696 | tf_op jit(solution)/shard_map/ppermute | solution.py:83
  20.6 2.4 %collective-permute-start.13 = (bf16[256,1408]{1,0:T(8,128)(2,1)S(1)}, bf16[256,1408]{1,0:T(8,128)(2,1)S(1)}, u32[]{:S(2)}, u32[]{:S(2)}) collective-permute-start(bf16[256,1408]{1,0:T(8,128)(2,1)S(1)} %pad_maximum_fusion.17), channel_id=1, source_target_pairs={{0,48},{1,49},{2,50},{3,51},{4,52},{5,53},{6,54},{7,55},{8,56},{9,... | collective-permute-start | bytes 2162696 | tf_op jit(solution)/shard_map/ppermute | solution.py:83
  23.0 1.6 %collective-permute-done.9 = bf16[128,1408]{1,0:T(8,128)(2,1)S(1)} collective-permute-done((bf16[128,1408]{1,0:T(8,128)(2,1)S(1)}, bf16[128,1408]{1,0:T(8,128)(2,1)S(1)}, u32[]{:S(2)}, u32[]{:S(2)}) %collective-permute-start.9) | collective-permute-done | bytes 360480 | tf_op jit(solution)/shard_map/ppermute | solution.py:83
  24.7 2.5 %collective-permute-start.10 = (bf16[256,1408]{1,0:T(8,128)(2,1)S(1)}, bf16[256,1408]{1,0:T(8,128)(2,1)S(1)}, u32[]{:S(2)}, u32[]{:S(2)}) collective-permute-start(bf16[256,1408]{1,0:T(8,128)(2,1)S(1)} %pad_maximum_fusion.16), channel_id=1, source_target_pairs={{0,12},{1,13},{2,14},{3,15},{4,8},{5,9},{6,10},{7,11},{8,4},{9,5},... | collective-permute-start | bytes 2162696 | tf_op jit(solution)/shard_map/ppermute | solution.py:83
  27.2 1.2 collective-permute-done.1
  29.3 1.8 %collective-permute-start.3 = (bf16[256,2176]{1,0:T(8,128)(2,1)S(1)}, bf16[256,2176]{1,0:T(8,128)(2,1)S(1)}, u32[]{:S(2)}, u32[]{:S(2)}) collective-permute-start(bf16[256,2176]{1,0:T(8,128)(2,1)S(1)} %pad_maximum_fusion.5), channel_id=1, source_target_pairs={{0,16},{1,17},{2,18},{3,19},{4,20},{5,21},{6,22},{7,23},{8,24},{9,... | collective-permute-start | bytes 3342344 | tf_op jit(solution)/shard_map/ppermute | solution.py:83
  31.1 7.6 %collective-permute-done.14 = bf16[256,1408]{1,0:T(8,128)(2,1)S(1)} collective-permute-done((bf16[256,1408]{1,0:T(8,128)(2,1)S(1)}, bf16[256,1408]{1,0:T(8,128)(2,1)S(1)}, u32[]{:S(2)}, u32[]{:S(2)}) %collective-permute-start.14) | collective-permute-done | bytes 720928 | tf_op jit(solution)/shard_map/ppermute | solution.py:83
  38.8 1.1 collective-permute-start.16
  40.0 3.0 %collective-permute-start.15 = (bf16[512,1408]{1,0:T(8,128)(2,1)S(1)}, bf16[512,1408]{1,0:T(8,128)(2,1)S(1)}, u32[]{:S(2)}, u32[]{:S(2)}) collective-permute-start(bf16[512,1408]{1,0:T(8,128)(2,1)S(1)} %pad_maximum_fusion.3), channel_id=1, source_target_pairs={{0,66},{1,67},{2,64},{3,65},{4,70},{5,71},{6,68},{7,69},{8,74},{9,... | collective-permute-start | bytes 4325384 | tf_op jit(solution)/shard_map/ppermute | solution.py:83
  43.9 2.2 %collective-permute-start.11 = (bf16[512,1408]{1,0:T(8,128)(2,1)S(1)}, bf16[512,1408]{1,0:T(8,128)(2,1)S(1)}, u32[]{:S(2)}, u32[]{:S(2)}) collective-permute-start(bf16[512,1408]{1,0:T(8,128)(2,1)S(1)} %pad_maximum_fusion.2), channel_id=1, source_target_pairs={{0,48},{1,49},{2,50},{3,51},{4,52},{5,53},{6,54},{7,55},{8,56},{9,... | collective-permute-start | bytes 4325384 | tf_op jit(solution)/shard_map/ppermute | solution.py:83
  46.2 5.7 %collective-permute-done.4 = bf16[256,2048]{1,0:T(8,128)(2,1)S(1)} collective-permute-done((bf16[256,2048]{1,0:T(8,128)(2,1)S(1)}, bf16[256,2048]{1,0:T(8,128)(2,1)S(1)}, u32[]{:S(2)}, u32[]{:S(2)}) %collective-permute-start.4) | collective-permute-done | bytes 1048608 | tf_op jit(solution)/shard_map/ppermute | solution.py:83
  52.4 1.6 %collective-permute-done.3 = bf16[256,2176]{1,0:T(8,128)(2,1)S(1)} collective-permute-done((bf16[256,2176]{1,0:T(8,128)(2,1)S(1)}, bf16[256,2176]{1,0:T(8,128)(2,1)S(1)}, u32[]{:S(2)}, u32[]{:S(2)}) %collective-permute-start.3) | collective-permute-done | bytes 1114144 | tf_op jit(solution)/shard_map/ppermute | solution.py:83
  54.1 1.5 %collective-permute-start.5 = (bf16[512,2176]{1,0:T(8,128)(2,1)S(1)}, bf16[512,2176]{1,0:T(8,128)(2,1)S(1)}, u32[]{:S(2)}, u32[]{:S(2)}) collective-permute-start(bf16[512,2176]{1,0:T(8,128)(2,1)S(1)} %pad_maximum_fusion), channel_id=1, source_target_pairs={{0,64},{1,65},{2,66},{3,67},{4,68},{5,69},{6,70},{7,71},{8,72},{9,... | collective-permute-start | bytes 6684680 | tf_op jit(solution)/shard_map/ppermute | solution.py:83
  55.8 0.9 fusion.26
  56.7 19.1 %collective-permute-done.11 = bf16[512,1408]{1,0:T(8,128)(2,1)S(1)} collective-permute-done((bf16[512,1408]{1,0:T(8,128)(2,1)S(1)}, bf16[512,1408]{1,0:T(8,128)(2,1)S(1)}, u32[]{:S(2)}, u32[]{:S(2)}) %collective-permute-start.11) | collective-permute-done | bytes 1441824 | tf_op jit(solution)/shard_map/ppermute | solution.py:83
  77.7 19.6 %collective-permute-done.6 = bf16[512,2048]{1,0:T(8,128)(2,1)S(1)} collective-permute-done((bf16[512,2048]{1,0:T(8,128)(2,1)S(1)}, bf16[512,2048]{1,0:T(8,128)(2,1)S(1)}, u32[]{:S(2)}, u32[]{:S(2)}) %collective-permute-start.6) | collective-permute-done | bytes 2097184 | tf_op jit(solution)/shard_map/ppermute | solution.py:83
  97.5 4.5 %collective-permute-done.5 = bf16[512,2176]{1,0:T(8,128)(2,1)S(1)} collective-permute-done((bf16[512,2176]{1,0:T(8,128)(2,1)S(1)}, bf16[512,2176]{1,0:T(8,128)(2,1)S(1)}, u32[]{:S(2)}, u32[]{:S(2)}) %collective-permute-start.5) | collective-permute-done | bytes 2228256 | tf_op jit(solution)/shard_map/ppermute | solution.py:83
  103.1 4.8 %fusion.50 = f32[512,1024]{1,0:T(8,128)S(1)} fusion(bf16[512,4224]{1,0:T(8,128)(2,1)S(1)} %get-tuple-element.32, bf16[1024,4224]{1,0:T(8,128)(2,1)S(1)} %slice_dynamic-update-slice_fusion), kind=kOutput, calls=%fused_computation.158 | convolution fusion | flops 4429185024 | bytes 15073280 | tf_op jit(solution)/shard_map/dot_general | solution.py:139
  108.7 3.4 %collective-permute-done.17 = f32[512,1024]{1,0:T(8,128)S(1)} collective-permute-done((f32[512,1024]{1,0:T(8,128)S(1)}, f32[512,1024]{1,0:T(8,128)S(1)}, u32[]{:S(2)}, u32[]{:S(2)}) %collective-permute-start.17) | collective-permute-done | bytes 2097184 | tf_op jit(solution)/shard_map/ppermute | solution.py:143
  112.3 4.8 %fusion.2 = bf16[512,1024]{1,0:T(8,128)(2,1)S(1)} fusion(f32[512,512]{1,0:T(8,128)S(1)} %get-tuple-element.11, f32[512,512]{1,0:T(8,128)S(1)} %get-tuple-element.10, f32[512]{0:T(512)S(1)} %convert_reduce_fusion, bf16[512,4224]{1,0:T(8,128)(2,1)S(1)} %get-tuple-element.33, bf16[1024,4224]{1,0:T(8,128)(2,1)S(1)} %slice_dynamic-update-slice_fusion), kind=kOutput, calls=%fused_computation.5 | convolution fusion | flops 4431282176 | bytes 16123904 | tf_op jit(solution)/shard_map/dot_general | solution.py:139
  119.1 1.7 %collective-permute-start.18 = (f32[256,512]{1,0:T(8,128)S(1)}, f32[256,512]{1,0:T(8,128)S(1)}, u32[]{:S(2)}, u32[]{:S(2)}) collective-permute-start(f32[256,512]{1,0:T(8,128)S(1)} %pad_maximum_fusion.28), channel_id=1, source_target_pairs={{0,16},{1,17},{2,18},{3,19},{4,20},{5,21},{6,22},{7,23},{8,24},{9,... | collective-permute-start | bytes 1572872 | tf_op jit(solution)/shard_map/ppermute | solution.py:118
  121.4 4.3 %collective-permute-done.22 = f32[256]{0:T(256)S(1)} collective-permute-done((f32[256]{0:T(256)S(1)}, f32[256]{0:T(256)S(1)}, u32[]{:S(2)}, u32[]{:S(2)}) %collective-permute-start.22) | collective-permute-done | bytes 1056 | tf_op jit(solution)/shard_map/ppermute | solution.py:118
  125.8 7.6 %collective-permute-done.18 = f32[256,512]{1,0:T(8,128)S(1)} collective-permute-done((f32[256,512]{1,0:T(8,128)S(1)}, f32[256,512]{1,0:T(8,128)S(1)}, u32[]{:S(2)}, u32[]{:S(2)}) %collective-permute-start.18) | collective-permute-done | bytes 524320 | tf_op jit(solution)/shard_map/ppermute | solution.py:118
  133.4 1.3 collective-permute-start.19
  135.2 4.3 %collective-permute-done.23 = f32[128]{0:T(128)S(1)} collective-permute-done((f32[128]{0:T(128)S(1)}, f32[128]{0:T(128)S(1)}, u32[]{:S(2)}, u32[]{:S(2)}) %collective-permute-start.23) | collective-permute-done | bytes 544 | tf_op jit(solution)/shard_map/ppermute | solution.py:118
  141.3 0.9 collective-permute-start.20
  142.2 2.1 %collective-permute-done.24 = f32[64]{0:T(128)S(1)} collective-permute-done((f32[64]{0:T(128)S(1)}, f32[64]{0:T(128)S(1)}, u32[]{:S(2)}, u32[]{:S(2)}) %collective-permute-start.24) | collective-permute-done | bytes 288 | tf_op jit(solution)/shard_map/ppermute | solution.py:118
  144.9 1.5 %collective-permute-done.20 = f32[64,512]{1,0:T(8,128)S(1)} collective-permute-done((f32[64,512]{1,0:T(8,128)S(1)}, f32[64,512]{1,0:T(8,128)S(1)}, u32[]{:S(2)}, u32[]{:S(2)}) %collective-permute-start.20) | collective-permute-done | bytes 131104 | tf_op jit(solution)/shard_map/ppermute | solution.py:118
  (114 shorter events, 18.3 us)
Async XLA Ops:
  2.7 1.2 copy-start
  2.8 1.2 copy-start.1
  3.0 2.0 %collective-permute-start.7 = (bf16[64,4224]{1,0:T(8,128)(2,1)S(1)}, bf16[64,4224]{1,0:T(8,128)(2,1)S(1)}, u32[]{:S(2)}, u32[]{:S(2)}) collective-permute-start(bf16[64,4224]{1,0:T(8,128)(2,1)S(1)} %get-tuple-element.49), channel_id=1, source_target_pairs={{0,1},{1,0},{2,3},{3,2},{4,5},{5,4},{6,7},{7,6},{8,9},{9,8},{10,11... | collective-permute-start | bytes 1622024 | tf_op jit(solution)/shard_map/ppermute | solution.py:96
  4.4 10.7 %collective-permute-start = (bf16[64,4224]{1,0:T(8,128)(2,1)S(1)}, bf16[64,4224]{1,0:T(8,128)(2,1)S(1)}, u32[]{:S(2)}, u32[]{:S(2)}) collective-permute-start(bf16[64,4224]{1,0:T(8,128)(2,1)S(1)} %get-tuple-element.50), channel_id=1, source_target_pairs={{0,1},{1,0},{2,3},{3,2},{4,5},{5,4},{6,7},{7,6},{8,9},{9,8},{10,11... | collective-permute-start | bytes 1622024 | tf_op jit(solution)/shard_map/ppermute | solution.py:96
  5.1 11.7 %collective-permute-start.8 = (bf16[128,1408]{1,0:T(8,128)(2,1)S(1)}, bf16[128,1408]{1,0:T(8,128)(2,1)S(1)}, u32[]{:S(2)}, u32[]{:S(2)}) collective-permute-start(bf16[128,1408]{1,0:T(8,128)(2,1)S(1)} %get-tuple-element.46), channel_id=1, source_target_pairs={{0,48},{1,49},{2,50},{3,51},{4,52},{5,53},{6,54},{7,55},{8,56},{9,... | collective-permute-start | bytes 1081352 | tf_op jit(solution)/shard_map/ppermute | solution.py:83
  8.0 12.5 %collective-permute-start.12 = (bf16[128,1408]{1,0:T(8,128)(2,1)S(1)}, bf16[128,1408]{1,0:T(8,128)(2,1)S(1)}, u32[]{:S(2)}, u32[]{:S(2)}) collective-permute-start(bf16[128,1408]{1,0:T(8,128)(2,1)S(1)} %get-tuple-element.47), channel_id=1, source_target_pairs={{0,12},{1,13},{2,14},{3,15},{4,8},{5,9},{6,10},{7,11},{8,4},{9,5},... | collective-permute-start | bytes 1081352 | tf_op jit(solution)/shard_map/ppermute | solution.py:83
  12.1 12.5 %collective-permute-start.9 = (bf16[128,1408]{1,0:T(8,128)(2,1)S(1)}, bf16[128,1408]{1,0:T(8,128)(2,1)S(1)}, u32[]{:S(2)}, u32[]{:S(2)}) collective-permute-start(bf16[128,1408]{1,0:T(8,128)(2,1)S(1)} %get-tuple-element.48), channel_id=1, source_target_pairs={{0,66},{1,67},{2,64},{3,65},{4,70},{5,71},{6,68},{7,69},{8,74},{9,... | collective-permute-start | bytes 1081352 | tf_op jit(solution)/shard_map/ppermute | solution.py:83
  15.1 13.2 %collective-permute-start.1 = (bf16[128,2048]{1,0:T(8,128)(2,1)S(1)}, bf16[128,2048]{1,0:T(8,128)(2,1)S(1)}, u32[]{:S(2)}, u32[]{:S(2)}) collective-permute-start(bf16[128,2048]{1,0:T(8,128)(2,1)S(1)} %pad_maximum_fusion.27), channel_id=1, source_target_pairs={{0,16},{1,17},{2,18},{3,19},{4,20},{5,21},{6,22},{7,23},{8,24},{9,... | collective-permute-start | bytes 1572872 | tf_op jit(solution)/shard_map/ppermute | solution.py:83
  15.5 13.7 %collective-permute-start.2 = (bf16[128,2176]{1,0:T(8,128)(2,1)S(1)}, bf16[128,2176]{1,0:T(8,128)(2,1)S(1)}, u32[]{:S(2)}, u32[]{:S(2)}) collective-permute-start(bf16[128,2176]{1,0:T(8,128)(2,1)S(1)} %pad_maximum_fusion.19), channel_id=1, source_target_pairs={{0,4},{1,5},{2,6},{3,7},{4,0},{5,1},{6,2},{7,3},{8,12},{9,13},{10,... | collective-permute-start | bytes 1671176 | tf_op jit(solution)/shard_map/ppermute | solution.py:83
  16.9 21.8 %collective-permute-start.14 = (bf16[256,1408]{1,0:T(8,128)(2,1)S(1)}, bf16[256,1408]{1,0:T(8,128)(2,1)S(1)}, u32[]{:S(2)}, u32[]{:S(2)}) collective-permute-start(bf16[256,1408]{1,0:T(8,128)(2,1)S(1)} %pad_maximum_fusion.18), channel_id=1, source_target_pairs={{0,66},{1,67},{2,64},{3,65},{4,70},{5,71},{6,68},{7,69},{8,74},{9,... | collective-permute-start | bytes 2162696 | tf_op jit(solution)/shard_map/ppermute | solution.py:83
  20.6 19.4 %collective-permute-start.13 = (bf16[256,1408]{1,0:T(8,128)(2,1)S(1)}, bf16[256,1408]{1,0:T(8,128)(2,1)S(1)}, u32[]{:S(2)}, u32[]{:S(2)}) collective-permute-start(bf16[256,1408]{1,0:T(8,128)(2,1)S(1)} %pad_maximum_fusion.17), channel_id=1, source_target_pairs={{0,48},{1,49},{2,50},{3,51},{4,52},{5,53},{6,54},{7,55},{8,56},{9,... | collective-permute-start | bytes 2162696 | tf_op jit(solution)/shard_map/ppermute | solution.py:83
  24.7 19.1 %collective-permute-start.10 = (bf16[256,1408]{1,0:T(8,128)(2,1)S(1)}, bf16[256,1408]{1,0:T(8,128)(2,1)S(1)}, u32[]{:S(2)}, u32[]{:S(2)}) collective-permute-start(bf16[256,1408]{1,0:T(8,128)(2,1)S(1)} %pad_maximum_fusion.16), channel_id=1, source_target_pairs={{0,12},{1,13},{2,14},{3,15},{4,8},{5,9},{6,10},{7,11},{8,4},{9,5},... | collective-permute-start | bytes 2162696 | tf_op jit(solution)/shard_map/ppermute | solution.py:83
  28.4 23.5 %collective-permute-start.4 = (bf16[256,2048]{1,0:T(8,128)(2,1)S(1)}, bf16[256,2048]{1,0:T(8,128)(2,1)S(1)}, u32[]{:S(2)}, u32[]{:S(2)}) collective-permute-start(bf16[256,2048]{1,0:T(8,128)(2,1)S(1)} %pad_maximum_fusion.15), channel_id=1, source_target_pairs={{0,64},{1,65},{2,66},{3,67},{4,68},{5,69},{6,70},{7,71},{8,72},{9,... | collective-permute-start | bytes 3145736 | tf_op jit(solution)/shard_map/ppermute | solution.py:83
  29.3 24.7 %collective-permute-start.3 = (bf16[256,2176]{1,0:T(8,128)(2,1)S(1)}, bf16[256,2176]{1,0:T(8,128)(2,1)S(1)}, u32[]{:S(2)}, u32[]{:S(2)}) collective-permute-start(bf16[256,2176]{1,0:T(8,128)(2,1)S(1)} %pad_maximum_fusion.5), channel_id=1, source_target_pairs={{0,16},{1,17},{2,18},{3,19},{4,20},{5,21},{6,22},{7,23},{8,24},{9,... | collective-permute-start | bytes 3342344 | tf_op jit(solution)/shard_map/ppermute | solution.py:83
  38.8 37.7 %collective-permute-start.16 = (bf16[512,1408]{1,0:T(8,128)(2,1)S(1)}, bf16[512,1408]{1,0:T(8,128)(2,1)S(1)}, u32[]{:S(2)}, u32[]{:S(2)}) collective-permute-start(bf16[512,1408]{1,0:T(8,128)(2,1)S(1)} %pad_maximum_fusion.4), channel_id=1, source_target_pairs={{0,12},{1,13},{2,14},{3,15},{4,8},{5,9},{6,10},{7,11},{8,4},{9,5},... | collective-permute-start | bytes 4325384 | tf_op jit(solution)/shard_map/ppermute | solution.py:83
  40.0 36.0 %collective-permute-start.15 = (bf16[512,1408]{1,0:T(8,128)(2,1)S(1)}, bf16[512,1408]{1,0:T(8,128)(2,1)S(1)}, u32[]{:S(2)}, u32[]{:S(2)}) collective-permute-start(bf16[512,1408]{1,0:T(8,128)(2,1)S(1)} %pad_maximum_fusion.3), channel_id=1, source_target_pairs={{0,66},{1,67},{2,64},{3,65},{4,70},{5,71},{6,68},{7,69},{8,74},{9,... | collective-permute-start | bytes 4325384 | tf_op jit(solution)/shard_map/ppermute | solution.py:83
  43.9 31.9 %collective-permute-start.11 = (bf16[512,1408]{1,0:T(8,128)(2,1)S(1)}, bf16[512,1408]{1,0:T(8,128)(2,1)S(1)}, u32[]{:S(2)}, u32[]{:S(2)}) collective-permute-start(bf16[512,1408]{1,0:T(8,128)(2,1)S(1)} %pad_maximum_fusion.2), channel_id=1, source_target_pairs={{0,48},{1,49},{2,50},{3,51},{4,52},{5,53},{6,54},{7,55},{8,56},{9,... | collective-permute-start | bytes 4325384 | tf_op jit(solution)/shard_map/ppermute | solution.py:83
  52.2 45.1 %collective-permute-start.6 = (bf16[512,2048]{1,0:T(8,128)(2,1)S(1)}, bf16[512,2048]{1,0:T(8,128)(2,1)S(1)}, u32[]{:S(2)}, u32[]{:S(2)}) collective-permute-start(bf16[512,2048]{1,0:T(8,128)(2,1)S(1)} %pad_maximum_fusion.1), channel_id=1, source_target_pairs={{0,4},{1,5},{2,6},{3,7},{4,0},{5,1},{6,2},{7,3},{8,12},{9,13},{10,... | collective-permute-start | bytes 6291464 | tf_op jit(solution)/shard_map/ppermute | solution.py:83
  54.1 47.9 %collective-permute-start.5 = (bf16[512,2176]{1,0:T(8,128)(2,1)S(1)}, bf16[512,2176]{1,0:T(8,128)(2,1)S(1)}, u32[]{:S(2)}, u32[]{:S(2)}) collective-permute-start(bf16[512,2176]{1,0:T(8,128)(2,1)S(1)} %pad_maximum_fusion), channel_id=1, source_target_pairs={{0,64},{1,65},{2,66},{3,67},{4,68},{5,69},{6,70},{7,71},{8,72},{9,... | collective-permute-start | bytes 6684680 | tf_op jit(solution)/shard_map/ppermute | solution.py:83
  77.6 24.6 %slice-start = ((s8[4325376]{0:T(1024)(128)(4,1)}), s8[4194304]{0:T(1024)(128)(4,1)S(1)}, s32[]{:S(2)}) async-start(s8[4325376]{0:T(1024)(128)(4,1)} %bitcast.6), calls=%async_computation | async-start | bytes 8388608
  77.7 24.5 %slice-start.1 = ((s8[4325376]{0:T(1024)(128)(4,1)}), s8[131072]{0:T(1024)(128)(4,1)S(1)}, s32[]{:S(2)}) async-start(s8[4325376]{0:T(1024)(128)(4,1)} %bitcast.6), calls=%async_computation.1 | async-start | bytes 262144
  107.9 4.2 %collective-permute-start.17 = (f32[512,1024]{1,0:T(8,128)S(1)}, f32[512,1024]{1,0:T(8,128)S(1)}, u32[]{:S(2)}, u32[]{:S(2)}) collective-permute-start(f32[512,1024]{1,0:T(8,128)S(1)} %fusion.50), channel_id=1, source_target_pairs={{0,1},{1,0},{2,3},{3,2},{4,5},{5,4},{6,7},{7,6},{8,9},{9,8},{10,11... | collective-permute-start | bytes 6291464 | tf_op jit(solution)/shard_map/ppermute | solution.py:143
  118.8 2.0 %collective-permute-start.21 = (f32[512]{0:T(512)S(1)}, f32[512]{0:T(512)S(1)}, u32[]{:S(2)}, u32[]{:S(2)}) collective-permute-start(f32[512]{0:T(512)S(1)} %slice.414), channel_id=1, source_target_pairs={{0,1},{1,0},{2,3},{3,2},{4,5},{5,4},{6,7},{7,6},{8,9},{9,8},{10,11... | collective-permute-start | bytes 6152 | tf_op jit(solution)/shard_map/ppermute | solution.py:158
  119.1 14.3 %collective-permute-start.18 = (f32[256,512]{1,0:T(8,128)S(1)}, f32[256,512]{1,0:T(8,128)S(1)}, u32[]{:S(2)}, u32[]{:S(2)}) collective-permute-start(f32[256,512]{1,0:T(8,128)S(1)} %pad_maximum_fusion.28), channel_id=1, source_target_pairs={{0,16},{1,17},{2,18},{3,19},{4,20},{5,21},{6,22},{7,23},{8,24},{9,... | collective-permute-start | bytes 1572872 | tf_op jit(solution)/shard_map/ppermute | solution.py:118
  120.9 4.8 %collective-permute-start.22 = (f32[256]{0:T(256)S(1)}, f32[256]{0:T(256)S(1)}, u32[]{:S(2)}, u32[]{:S(2)}) collective-permute-start(f32[256]{0:T(256)S(1)} %pad_maximum_fusion.31), channel_id=1, source_target_pairs={{0,48},{1,49},{2,50},{3,51},{4,52},{5,53},{6,54},{7,55},{8,56},{9,... | collective-permute-start | bytes 3080 | tf_op jit(solution)/shard_map/ppermute | solution.py:118
  133.4 7.8 %collective-permute-start.19 = (f32[128,512]{1,0:T(8,128)S(1)}, f32[128,512]{1,0:T(8,128)S(1)}, u32[]{:S(2)}, u32[]{:S(2)}) collective-permute-start(f32[128,512]{1,0:T(8,128)S(1)} %pad_maximum_fusion.30), channel_id=1, source_target_pairs={{0,64},{1,65},{2,66},{3,67},{4,68},{5,69},{6,70},{7,71},{8,72},{9,... | collective-permute-start | bytes 786440 | tf_op jit(solution)/shard_map/ppermute | solution.py:118
  134.8 4.8 %collective-permute-start.23 = (f32[128]{0:T(128)S(1)}, f32[128]{0:T(128)S(1)}, u32[]{:S(2)}, u32[]{:S(2)}) collective-permute-start(f32[128]{0:T(128)S(1)} %pad_maximum_fusion.32), channel_id=1, source_target_pairs={{0,66},{1,67},{2,64},{3,65},{4,70},{5,71},{6,68},{7,69},{8,74},{9,... | collective-permute-start | bytes 1544 | tf_op jit(solution)/shard_map/ppermute | solution.py:118
  139.6 4.8 %collective-permute-start.24 = (f32[64]{0:T(128)S(1)}, f32[64]{0:T(128)S(1)}, u32[]{:S(2)}, u32[]{:S(2)}) collective-permute-start(f32[64]{0:T(128)S(1)} %slice_add_fusion.7), channel_id=1, source_target_pairs={{0,12},{1,13},{2,14},{3,15},{4,8},{5,9},{6,10},{7,11},{8,4},{9,5},... | collective-permute-start | bytes 776 | tf_op jit(solution)/shard_map/ppermute | solution.py:118
  141.3 5.0 %collective-permute-start.20 = (f32[64,512]{1,0:T(8,128)S(1)}, f32[64,512]{1,0:T(8,128)S(1)}, u32[]{:S(2)}, u32[]{:S(2)}) collective-permute-start(f32[64,512]{1,0:T(8,128)S(1)} %slice_add_fusion), channel_id=1, source_target_pairs={{0,4},{1,5},{2,6},{3,7},{4,0},{5,1},{6,2},{7,3},{8,12},{9,13},{10,... | collective-permute-start | bytes 393224 | tf_op jit(solution)/shard_map/ppermute | solution.py:118

commit v12 on v11

--- a/solution.py
+++ b/solution.py
@@ -108,10 +108,10 @@
     )
 
 
-def cube_reduce(blocks, mate, n):
+def cube_reduce(blocks, mate, n, order=(0, 1, 2)):
     blocks = list(blocks)
     live = list(range(8))
-    for a in range(3):
+    for a in order:
         send = [o for o in live if o & (1 << a)]
         keep = [o for o in live if not o & (1 << a)]
         rows = blocks[0].shape[0]
@@ -122,6 +122,18 @@
             blocks[o ^ (1 << a)] = blocks[o ^ (1 << a)] + got[i * rows:(i + 1) * rows]
         live = keep
     return blocks[0]
+
+
+def cube_reduce_wide(blocks, mate, n):
+    cols = blocks[0].shape[1]
+    cut = [0, cols // 2, 3 * cols // 4, cols]
+    return jnp.concatenate(
+        [
+            cube_reduce([b[:, cut[p]:cut[p + 1]] for b in blocks], mate, n, THREE[p])
+            for p in range(3)
+        ],
+        axis=1,
+    )
 
 
 def local(train_grads, train_scale, train_class, test_grads, test_class):
@@ -152,7 +164,7 @@
         w, train_hot, (((0,), (0,)), ((), ())), preferred_element_type=jnp.float32
     )
     tp = jnp.sum(per_class * test_hot.astype(jnp.float32), axis=1)
-    train_attr = cube_reduce(
+    train_attr = cube_reduce_wide(
         [part[o * rows:(o + 1) * rows] for o in range(8)], train_mate, n
     )
     test_part = tp[:half] + lax.ppermute(tp[half:], AXES, core_pairs(n))

time: 147 us -> 148 us (level)
  starting transfers between devices: 34.5 us -> 37.9 us
  waiting for transfers between devices: 87.5 us -> 84.8 us
    ppermute x6 -> x12, waiting for transfers between devices: 20.6 us -> 16.9 us  [cube_reduce(): lax.ppermute(jnp.concatenate([blocks[o] for o in send]), AXES, mate_pairs...]
    ppermute x6 -> x12, starting transfers between devices: 5.64 us -> 9.03 us  [cube_reduce(): lax.ppermute(jnp.concatenate([blocks[o] for o in send]), AXES, mate_pairs...]
  transfers between devices with their start and end apart: 25 -> 31, of which waited for: 20 -> 22; matrix products, arithmetic and copies ran while one was open for 5% -> 5% of each run, Pallas kernels for 0% -> 0%
where the time goes in v12:
time: 148 us
  waiting for transfers between devices  84.8 us (57%)
  starting transfers between devices  37.9 us (26%)
  matrix products  11.2 us (8%)
  other arithmetic  6.94 us (5%)
  local copies, waits for them, and re-layouts  5.55 us (4%)
    ppermute x15, waiting for transfers between devices, chain(): got = lax.ppermute(buf, AXES, mate_pairs(n, a, mate))  63 us
    ppermute x15, starting transfers between devices, chain(): got = lax.ppermute(buf, AXES, mate_pairs(n, a, mate))  28.4 us
    ppermute x12, waiting for transfers between devices, cube_reduce(): lax.ppermute(jnp.concatenate([blocks[o] for o in send]), AXES, mate_pairs...  16.9 us
    dot_general x2, matrix products, partial(): lax.dot_general(t, te_all, (((1,), (1,)), ((), ())), preferred_element_ty...  9.58 us
    ppermute x12, starting transfers between devices, cube_reduce(): lax.ppermute(jnp.concatenate([blocks[o] for o in send]), AXES, mate_pairs...  9.03 us
    ppermute x1, waiting for transfers between devices, local(): got = lax.ppermute(partial(tr_all[half:]), AXES, core_pairs(n))  3.37 us
  transfers between devices with their start and end apart: 31, of which 22 were waited for; matrix products, arithmetic and copies ran while one was open for 5% of the time, Pallas kernels for 0%

profile of v12, /device:TPU:0, one launch (start us, length us, event | category | flops | bytes accessed | tf_op | source)
XLA Modules:
  0.0 147.8 jit_solution(4761573099561245547)
XLA Ops:
  0.7 1.3 fusion.46
  5.1 2.9 %collective-permute-start.8 = (bf16[128,1408]{1,0:T(8,128)(2,1)S(1)}, bf16[128,1408]{1,0:T(8,128)(2,1)S(1)}, u32[]{:S(2)}, u32[]{:S(2)}) collective-permute-start(bf16[128,1408]{1,0:T(8,128)(2,1)S(1)} %get-tuple-element.50), channel_id=1, source_target_pairs={{0,48},{1,49},{2,50},{3,51},{4,52},{5,53},{6,54},{7,55},{8,56},{9,... | collective-permute-start | bytes 1081352 | tf_op jit(solution)/shard_map/ppermute | solution.py:83
  8.0 4.0 %collective-permute-start.12 = (bf16[128,1408]{1,0:T(8,128)(2,1)S(1)}, bf16[128,1408]{1,0:T(8,128)(2,1)S(1)}, u32[]{:S(2)}, u32[]{:S(2)}) collective-permute-start(bf16[128,1408]{1,0:T(8,128)(2,1)S(1)} %get-tuple-element.51), channel_id=1, source_target_pairs={{0,12},{1,13},{2,14},{3,15},{4,8},{5,9},{6,10},{7,11},{8,4},{9,5},... | collective-permute-start | bytes 1081352 | tf_op jit(solution)/shard_map/ppermute | solution.py:83
  12.1 3.0 %collective-permute-start.9 = (bf16[128,1408]{1,0:T(8,128)(2,1)S(1)}, bf16[128,1408]{1,0:T(8,128)(2,1)S(1)}, u32[]{:S(2)}, u32[]{:S(2)}) collective-permute-start(bf16[128,1408]{1,0:T(8,128)(2,1)S(1)} %get-tuple-element.52), channel_id=1, source_target_pairs={{0,66},{1,67},{2,64},{3,65},{4,70},{5,71},{6,68},{7,69},{8,74},{9,... | collective-permute-start | bytes 1081352 | tf_op jit(solution)/shard_map/ppermute | solution.py:83
  16.9 3.2 %collective-permute-start.14 = (bf16[256,1408]{1,0:T(8,128)(2,1)S(1)}, bf16[256,1408]{1,0:T(8,128)(2,1)S(1)}, u32[]{:S(2)}, u32[]{:S(2)}) collective-permute-start(bf16[256,1408]{1,0:T(8,128)(2,1)S(1)} %pad_maximum_fusion.18), channel_id=1, source_target_pairs={{0,66},{1,67},{2,64},{3,65},{4,70},{5,71},{6,68},{7,69},{8,74},{9,... | collective-permute-start | bytes 2162696 | tf_op jit(solution)/shard_map/ppermute | solution.py:83
  20.6 2.4 %collective-permute-start.13 = (bf16[256,1408]{1,0:T(8,128)(2,1)S(1)}, bf16[256,1408]{1,0:T(8,128)(2,1)S(1)}, u32[]{:S(2)}, u32[]{:S(2)}) collective-permute-start(bf16[256,1408]{1,0:T(8,128)(2,1)S(1)} %pad_maximum_fusion.17), channel_id=1, source_target_pairs={{0,48},{1,49},{2,50},{3,51},{4,52},{5,53},{6,54},{7,55},{8,56},{9,... | collective-permute-start | bytes 2162696 | tf_op jit(solution)/shard_map/ppermute | solution.py:83
  23.0 1.6 %collective-permute-done.9 = bf16[128,1408]{1,0:T(8,128)(2,1)S(1)} collective-permute-done((bf16[128,1408]{1,0:T(8,128)(2,1)S(1)}, bf16[128,1408]{1,0:T(8,128)(2,1)S(1)}, u32[]{:S(2)}, u32[]{:S(2)}) %collective-permute-start.9) | collective-permute-done | bytes 360480 | tf_op jit(solution)/shard_map/ppermute | solution.py:83
  24.7 2.5 %collective-permute-start.10 = (bf16[256,1408]{1,0:T(8,128)(2,1)S(1)}, bf16[256,1408]{1,0:T(8,128)(2,1)S(1)}, u32[]{:S(2)}, u32[]{:S(2)}) collective-permute-start(bf16[256,1408]{1,0:T(8,128)(2,1)S(1)} %pad_maximum_fusion.16), channel_id=1, source_target_pairs={{0,12},{1,13},{2,14},{3,15},{4,8},{5,9},{6,10},{7,11},{8,4},{9,5},... | collective-permute-start | bytes 2162696 | tf_op jit(solution)/shard_map/ppermute | solution.py:83
  27.2 1.2 collective-permute-done.1
  29.3 1.8 %collective-permute-start.3 = (bf16[256,2176]{1,0:T(8,128)(2,1)S(1)}, bf16[256,2176]{1,0:T(8,128)(2,1)S(1)}, u32[]{:S(2)}, u32[]{:S(2)}) collective-permute-start(bf16[256,2176]{1,0:T(8,128)(2,1)S(1)} %pad_maximum_fusion.5), channel_id=1, source_target_pairs={{0,16},{1,17},{2,18},{3,19},{4,20},{5,21},{6,22},{7,23},{8,24},{9,... | collective-permute-start | bytes 3342344 | tf_op jit(solution)/shard_map/ppermute | solution.py:83
  31.1 7.6 %collective-permute-done.14 = bf16[256,1408]{1,0:T(8,128)(2,1)S(1)} collective-permute-done((bf16[256,1408]{1,0:T(8,128)(2,1)S(1)}, bf16[256,1408]{1,0:T(8,128)(2,1)S(1)}, u32[]{:S(2)}, u32[]{:S(2)}) %collective-permute-start.14) | collective-permute-done | bytes 720928 | tf_op jit(solution)/shard_map/ppermute | solution.py:83
  38.8 1.1 collective-permute-start.16
  40.0 3.0 %collective-permute-start.15 = (bf16[512,1408]{1,0:T(8,128)(2,1)S(1)}, bf16[512,1408]{1,0:T(8,128)(2,1)S(1)}, u32[]{:S(2)}, u32[]{:S(2)}) collective-permute-start(bf16[512,1408]{1,0:T(8,128)(2,1)S(1)} %pad_maximum_fusion.3), channel_id=1, source_target_pairs={{0,66},{1,67},{2,64},{3,65},{4,70},{5,71},{6,68},{7,69},{8,74},{9,... | collective-permute-start | bytes 4325384 | tf_op jit(solution)/shard_map/ppermute | solution.py:83
  43.9 2.2 %collective-permute-start.11 = (bf16[512,1408]{1,0:T(8,128)(2,1)S(1)}, bf16[512,1408]{1,0:T(8,128)(2,1)S(1)}, u32[]{:S(2)}, u32[]{:S(2)}) collective-permute-start(bf16[512,1408]{1,0:T(8,128)(2,1)S(1)} %pad_maximum_fusion.2), channel_id=1, source_target_pairs={{0,48},{1,49},{2,50},{3,51},{4,52},{5,53},{6,54},{7,55},{8,56},{9,... | collective-permute-start | bytes 4325384 | tf_op jit(solution)/shard_map/ppermute | solution.py:83
  46.2 5.7 %collective-permute-done.4 = bf16[256,2048]{1,0:T(8,128)(2,1)S(1)} collective-permute-done((bf16[256,2048]{1,0:T(8,128)(2,1)S(1)}, bf16[256,2048]{1,0:T(8,128)(2,1)S(1)}, u32[]{:S(2)}, u32[]{:S(2)}) %collective-permute-start.4) | collective-permute-done | bytes 1048608 | tf_op jit(solution)/shard_map/ppermute | solution.py:83
  52.4 1.6 %collective-permute-done.3 = bf16[256,2176]{1,0:T(8,128)(2,1)S(1)} collective-permute-done((bf16[256,2176]{1,0:T(8,128)(2,1)S(1)}, bf16[256,2176]{1,0:T(8,128)(2,1)S(1)}, u32[]{:S(2)}, u32[]{:S(2)}) %collective-permute-start.3) | collective-permute-done | bytes 1114144 | tf_op jit(solution)/shard_map/ppermute | solution.py:83
  54.1 1.5 %collective-permute-start.5 = (bf16[512,2176]{1,0:T(8,128)(2,1)S(1)}, bf16[512,2176]{1,0:T(8,128)(2,1)S(1)}, u32[]{:S(2)}, u32[]{:S(2)}) collective-permute-start(bf16[512,2176]{1,0:T(8,128)(2,1)S(1)} %pad_maximum_fusion), channel_id=1, source_target_pairs={{0,64},{1,65},{2,66},{3,67},{4,68},{5,69},{6,70},{7,71},{8,72},{9,... | collective-permute-start | bytes 6684680 | tf_op jit(solution)/shard_map/ppermute | solution.py:83
  56.6 19.2 %collective-permute-done.11 = bf16[512,1408]{1,0:T(8,128)(2,1)S(1)} collective-permute-done((bf16[512,1408]{1,0:T(8,128)(2,1)S(1)}, bf16[512,1408]{1,0:T(8,128)(2,1)S(1)}, u32[]{:S(2)}, u32[]{:S(2)}) %collective-permute-start.11) | collective-permute-done | bytes 1441824 | tf_op jit(solution)/shard_map/ppermute | solution.py:83
  77.7 19.6 %collective-permute-done.6 = bf16[512,2048]{1,0:T(8,128)(2,1)S(1)} collective-permute-done((bf16[512,2048]{1,0:T(8,128)(2,1)S(1)}, bf16[512,2048]{1,0:T(8,128)(2,1)S(1)}, u32[]{:S(2)}, u32[]{:S(2)}) %collective-permute-start.6) | collective-permute-done | bytes 2097184 | tf_op jit(solution)/shard_map/ppermute | solution.py:83
  97.5 4.5 %collective-permute-done.5 = bf16[512,2176]{1,0:T(8,128)(2,1)S(1)} collective-permute-done((bf16[512,2176]{1,0:T(8,128)(2,1)S(1)}, bf16[512,2176]{1,0:T(8,128)(2,1)S(1)}, u32[]{:S(2)}, u32[]{:S(2)}) %collective-permute-start.5) | collective-permute-done | bytes 2228256 | tf_op jit(solution)/shard_map/ppermute | solution.py:83
  103.1 4.8 %fusion.53 = f32[512,1024]{1,0:T(8,128)S(1)} fusion(bf16[512,4224]{1,0:T(8,128)(2,1)S(1)} %get-tuple-element.36, bf16[1024,4224]{1,0:T(8,128)(2,1)S(1)} %slice_dynamic-update-slice_fusion), kind=kOutput, calls=%fused_computation.177 | convolution fusion | flops 4429185024 | bytes 15073280 | tf_op jit(solution)/shard_map/dot_general | solution.py:151
  108.7 3.4 %collective-permute-done.17 = f32[512,1024]{1,0:T(8,128)S(1)} collective-permute-done((f32[512,1024]{1,0:T(8,128)S(1)}, f32[512,1024]{1,0:T(8,128)S(1)}, u32[]{:S(2)}, u32[]{:S(2)}) %collective-permute-start.17) | collective-permute-done | bytes 2097184 | tf_op jit(solution)/shard_map/ppermute | solution.py:155
  112.3 4.8 %fusion.2 = bf16[512,1024]{1,0:T(8,128)(2,1)S(1)} fusion(f32[512,512]{1,0:T(8,128)S(1)} %get-tuple-element.11, f32[512,512]{1,0:T(8,128)S(1)} %get-tuple-element.10, f32[512]{0:T(512)S(1)} %convert_reduce_fusion, bf16[512,4224]{1,0:T(8,128)(2,1)S(1)} %get-tuple-element.37, bf16[1024,4224]{1,0:T(8,128)(2,1)S(1)} %slice_dynamic-update-slice_fusion), kind=kOutput, calls=%fused_computation.5 | convolution fusion | flops 4431282176 | bytes 16123904 | tf_op jit(solution)/shard_map/dot_general | solution.py:151
  119.1 1.0 collective-permute-done.27
  120.2 0.9 collective-permute-start.28
  121.9 3.0 %collective-permute-done.28 = f32[256]{0:T(256)S(1)} collective-permute-done((f32[256]{0:T(256)S(1)}, f32[256]{0:T(256)S(1)}, u32[]{:S(2)}, u32[]{:S(2)}) %collective-permute-start.28) | collective-permute-done | bytes 1056 | tf_op jit(solution)/shard_map/ppermute | solution.py:118
  126.9 3.2 %collective-permute-done.29 = f32[128]{0:T(128)S(1)} collective-permute-done((f32[128]{0:T(128)S(1)}, f32[128]{0:T(128)S(1)}, u32[]{:S(2)}, u32[]{:S(2)}) %collective-permute-start.29) | collective-permute-done | bytes 544 | tf_op jit(solution)/shard_map/ppermute | solution.py:118
  131.8 3.2 %collective-permute-done.30 = f32[64]{0:T(128)S(1)} collective-permute-done((f32[64]{0:T(128)S(1)}, f32[64]{0:T(128)S(1)}, u32[]{:S(2)}, u32[]{:S(2)}) %collective-permute-start.30) | collective-permute-done | bytes 288 | tf_op jit(solution)/shard_map/ppermute | solution.py:118
  136.0 1.7 %collective-permute-start.23 = (f32[64,128]{1,0:T(8,128)S(1)}, f32[64,128]{1,0:T(8,128)S(1)}, u32[]{:S(2)}, u32[]{:S(2)}) collective-permute-start(f32[64,128]{1,0:T(8,128)S(1)} %get-tuple-element.61), channel_id=1, source_target_pairs={{0,16},{1,17},{2,18},{3,19},{4,20},{5,21},{6,22},{7,23},{8,24},{9,... | collective-permute-start | bytes 98312 | tf_op jit(solution)/shard_map/ppermute | solution.py:118
  138.3 1.9 %collective-permute-done.23 = f32[64,128]{1,0:T(8,128)S(1)} collective-permute-done((f32[64,128]{1,0:T(8,128)S(1)}, f32[64,128]{1,0:T(8,128)S(1)}, u32[]{:S(2)}, u32[]{:S(2)}) %collective-permute-start.23) | collective-permute-done | bytes 32800 | tf_op jit(solution)/shard_map/ppermute | solution.py:118
  140.8 1.9 %collective-permute-done.19 = f32[128,256]{1,0:T(8,128)S(1)} collective-permute-done((f32[128,256]{1,0:T(8,128)S(1)}, f32[128,256]{1,0:T(8,128)S(1)}, u32[]{:S(2)}, u32[]{:S(2)}) %collective-permute-start.19) | collective-permute-done | bytes 131104 | tf_op jit(solution)/shard_map/ppermute | solution.py:118
  144.2 2.8 %collective-permute-done.20 = f32[64,256]{1,0:T(8,128)S(1)} collective-permute-done((f32[64,256]{1,0:T(8,128)S(1)}, f32[64,256]{1,0:T(8,128)S(1)}, u32[]{:S(2)}, u32[]{:S(2)}) %collective-permute-start.20) | collective-permute-done | bytes 65568 | tf_op jit(solution)/shard_map/ppermute | solution.py:118
  (136 shorter events, 23.9 us)
Async XLA Ops:
  3.0 2.0 %collective-permute-start.7 = (bf16[64,4224]{1,0:T(8,128)(2,1)S(1)}, bf16[64,4224]{1,0:T(8,128)(2,1)S(1)}, u32[]{:S(2)}, u32[]{:S(2)}) collective-permute-start(bf16[64,4224]{1,0:T(8,128)(2,1)S(1)} %get-tuple-element.53), channel_id=1, source_target_pairs={{0,1},{1,0},{2,3},{3,2},{4,5},{5,4},{6,7},{7,6},{8,9},{9,8},{10,11... | collective-permute-start | bytes 1622024 | tf_op jit(solution)/shard_map/ppermute | solution.py:96
  4.4 10.7 %collective-permute-start = (bf16[64,4224]{1,0:T(8,128)(2,1)S(1)}, bf16[64,4224]{1,0:T(8,128)(2,1)S(1)}, u32[]{:S(2)}, u32[]{:S(2)}) collective-permute-start(bf16[64,4224]{1,0:T(8,128)(2,1)S(1)} %get-tuple-element.54), channel_id=1, source_target_pairs={{0,1},{1,0},{2,3},{3,2},{4,5},{5,4},{6,7},{7,6},{8,9},{9,8},{10,11... | collective-permute-start | bytes 1622024 | tf_op jit(solution)/shard_map/ppermute | solution.py:96
  5.1 11.7 %collective-permute-start.8 = (bf16[128,1408]{1,0:T(8,128)(2,1)S(1)}, bf16[128,1408]{1,0:T(8,128)(2,1)S(1)}, u32[]{:S(2)}, u32[]{:S(2)}) collective-permute-start(bf16[128,1408]{1,0:T(8,128)(2,1)S(1)} %get-tuple-element.50), channel_id=1, source_target_pairs={{0,48},{1,49},{2,50},{3,51},{4,52},{5,53},{6,54},{7,55},{8,56},{9,... | collective-permute-start | bytes 1081352 | tf_op jit(solution)/shard_map/ppermute | solution.py:83
  8.0 12.5 %collective-permute-start.12 = (bf16[128,1408]{1,0:T(8,128)(2,1)S(1)}, bf16[128,1408]{1,0:T(8,128)(2,1)S(1)}, u32[]{:S(2)}, u32[]{:S(2)}) collective-permute-start(bf16[128,1408]{1,0:T(8,128)(2,1)S(1)} %get-tuple-element.51), channel_id=1, source_target_pairs={{0,12},{1,13},{2,14},{3,15},{4,8},{5,9},{6,10},{7,11},{8,4},{9,5},... | collective-permute-start | bytes 1081352 | tf_op jit(solution)/shard_map/ppermute | solution.py:83
  12.1 12.5 %collective-permute-start.9 = (bf16[128,1408]{1,0:T(8,128)(2,1)S(1)}, bf16[128,1408]{1,0:T(8,128)(2,1)S(1)}, u32[]{:S(2)}, u32[]{:S(2)}) collective-permute-start(bf16[128,1408]{1,0:T(8,128)(2,1)S(1)} %get-tuple-element.52), channel_id=1, source_target_pairs={{0,66},{1,67},{2,64},{3,65},{4,70},{5,71},{6,68},{7,69},{8,74},{9,... | collective-permute-start | bytes 1081352 | tf_op jit(solution)/shard_map/ppermute | solution.py:83
  15.1 13.2 %collective-permute-start.1 = (bf16[128,2048]{1,0:T(8,128)(2,1)S(1)}, bf16[128,2048]{1,0:T(8,128)(2,1)S(1)}, u32[]{:S(2)}, u32[]{:S(2)}) collective-permute-start(bf16[128,2048]{1,0:T(8,128)(2,1)S(1)} %pad_maximum_fusion.27), channel_id=1, source_target_pairs={{0,16},{1,17},{2,18},{3,19},{4,20},{5,21},{6,22},{7,23},{8,24},{9,... | collective-permute-start | bytes 1572872 | tf_op jit(solution)/shard_map/ppermute | solution.py:83
  15.5 13.7 %collective-permute-start.2 = (bf16[128,2176]{1,0:T(8,128)(2,1)S(1)}, bf16[128,2176]{1,0:T(8,128)(2,1)S(1)}, u32[]{:S(2)}, u32[]{:S(2)}) collective-permute-start(bf16[128,2176]{1,0:T(8,128)(2,1)S(1)} %pad_maximum_fusion.19), channel_id=1, source_target_pairs={{0,4},{1,5},{2,6},{3,7},{4,0},{5,1},{6,2},{7,3},{8,12},{9,13},{10,... | collective-permute-start | bytes 1671176 | tf_op jit(solution)/shard_map/ppermute | solution.py:83
  16.9 21.8 %collective-permute-start.14 = (bf16[256,1408]{1,0:T(8,128)(2,1)S(1)}, bf16[256,1408]{1,0:T(8,128)(2,1)S(1)}, u32[]{:S(2)}, u32[]{:S(2)}) collective-permute-start(bf16[256,1408]{1,0:T(8,128)(2,1)S(1)} %pad_maximum_fusion.18), channel_id=1, source_target_pairs={{0,66},{1,67},{2,64},{3,65},{4,70},{5,71},{6,68},{7,69},{8,74},{9,... | collective-permute-start | bytes 2162696 | tf_op jit(solution)/shard_map/ppermute | solution.py:83
  20.6 19.4 %collective-permute-start.13 = (bf16[256,1408]{1,0:T(8,128)(2,1)S(1)}, bf16[256,1408]{1,0:T(8,128)(2,1)S(1)}, u32[]{:S(2)}, u32[]{:S(2)}) collective-permute-start(bf16[256,1408]{1,0:T(8,128)(2,1)S(1)} %pad_maximum_fusion.17), channel_id=1, source_target_pairs={{0,48},{1,49},{2,50},{3,51},{4,52},{5,53},{6,54},{7,55},{8,56},{9,... | collective-permute-start | bytes 2162696 | tf_op jit(solution)/shard_map/ppermute | solution.py:83
  24.7 19.1 %collective-permute-start.10 = (bf16[256,1408]{1,0:T(8,128)(2,1)S(1)}, bf16[256,1408]{1,0:T(8,128)(2,1)S(1)}, u32[]{:S(2)}, u32[]{:S(2)}) collective-permute-start(bf16[256,1408]{1,0:T(8,128)(2,1)S(1)} %pad_maximum_fusion.16), channel_id=1, source_target_pairs={{0,12},{1,13},{2,14},{3,15},{4,8},{5,9},{6,10},{7,11},{8,4},{9,5},... | collective-permute-start | bytes 2162696 | tf_op jit(solution)/shard_map/ppermute | solution.py:83
  28.4 23.5 %collective-permute-start.4 = (bf16[256,2048]{1,0:T(8,128)(2,1)S(1)}, bf16[256,2048]{1,0:T(8,128)(2,1)S(1)}, u32[]{:S(2)}, u32[]{:S(2)}) collective-permute-start(bf16[256,2048]{1,0:T(8,128)(2,1)S(1)} %pad_maximum_fusion.15), channel_id=1, source_target_pairs={{0,64},{1,65},{2,66},{3,67},{4,68},{5,69},{6,70},{7,71},{8,72},{9,... | collective-permute-start | bytes 3145736 | tf_op jit(solution)/shard_map/ppermute | solution.py:83
  29.3 24.7 %collective-permute-start.3 = (bf16[256,2176]{1,0:T(8,128)(2,1)S(1)}, bf16[256,2176]{1,0:T(8,128)(2,1)S(1)}, u32[]{:S(2)}, u32[]{:S(2)}) collective-permute-start(bf16[256,2176]{1,0:T(8,128)(2,1)S(1)} %pad_maximum_fusion.5), channel_id=1, source_target_pairs={{0,16},{1,17},{2,18},{3,19},{4,20},{5,21},{6,22},{7,23},{8,24},{9,... | collective-permute-start | bytes 3342344 | tf_op jit(solution)/shard_map/ppermute | solution.py:83
  38.8 37.7 %collective-permute-start.16 = (bf16[512,1408]{1,0:T(8,128)(2,1)S(1)}, bf16[512,1408]{1,0:T(8,128)(2,1)S(1)}, u32[]{:S(2)}, u32[]{:S(2)}) collective-permute-start(bf16[512,1408]{1,0:T(8,128)(2,1)S(1)} %pad_maximum_fusion.4), channel_id=1, source_target_pairs={{0,12},{1,13},{2,14},{3,15},{4,8},{5,9},{6,10},{7,11},{8,4},{9,5},... | collective-permute-start | bytes 4325384 | tf_op jit(solution)/shard_map/ppermute | solution.py:83
  40.0 36.0 %collective-permute-start.15 = (bf16[512,1408]{1,0:T(8,128)(2,1)S(1)}, bf16[512,1408]{1,0:T(8,128)(2,1)S(1)}, u32[]{:S(2)}, u32[]{:S(2)}) collective-permute-start(bf16[512,1408]{1,0:T(8,128)(2,1)S(1)} %pad_maximum_fusion.3), channel_id=1, source_target_pairs={{0,66},{1,67},{2,64},{3,65},{4,70},{5,71},{6,68},{7,69},{8,74},{9,... | collective-permute-start | bytes 4325384 | tf_op jit(solution)/shard_map/ppermute | solution.py:83
  43.9 31.9 %collective-permute-start.11 = (bf16[512,1408]{1,0:T(8,128)(2,1)S(1)}, bf16[512,1408]{1,0:T(8,128)(2,1)S(1)}, u32[]{:S(2)}, u32[]{:S(2)}) collective-permute-start(bf16[512,1408]{1,0:T(8,128)(2,1)S(1)} %pad_maximum_fusion.2), channel_id=1, source_target_pairs={{0,48},{1,49},{2,50},{3,51},{4,52},{5,53},{6,54},{7,55},{8,56},{9,... | collective-permute-start | bytes 4325384 | tf_op jit(solution)/shard_map/ppermute | solution.py:83
  52.2 45.1 %collective-permute-start.6 = (bf16[512,2048]{1,0:T(8,128)(2,1)S(1)}, bf16[512,2048]{1,0:T(8,128)(2,1)S(1)}, u32[]{:S(2)}, u32[]{:S(2)}) collective-permute-start(bf16[512,2048]{1,0:T(8,128)(2,1)S(1)} %pad_maximum_fusion.1), channel_id=1, source_target_pairs={{0,4},{1,5},{2,6},{3,7},{4,0},{5,1},{6,2},{7,3},{8,12},{9,13},{10,... | collective-permute-start | bytes 6291464 | tf_op jit(solution)/shard_map/ppermute | solution.py:83
  54.1 47.9 %collective-permute-start.5 = (bf16[512,2176]{1,0:T(8,128)(2,1)S(1)}, bf16[512,2176]{1,0:T(8,128)(2,1)S(1)}, u32[]{:S(2)}, u32[]{:S(2)}) collective-permute-start(bf16[512,2176]{1,0:T(8,128)(2,1)S(1)} %pad_maximum_fusion), channel_id=1, source_target_pairs={{0,64},{1,65},{2,66},{3,67},{4,68},{5,69},{6,70},{7,71},{8,72},{9,... | collective-permute-start | bytes 6684680 | tf_op jit(solution)/shard_map/ppermute | solution.py:83
  77.6 24.6 %slice-start = ((s8[4325376]{0:T(1024)(128)(4,1)}), s8[4194304]{0:T(1024)(128)(4,1)S(1)}, s32[]{:S(2)}) async-start(s8[4325376]{0:T(1024)(128)(4,1)} %bitcast.6), calls=%async_computation | async-start | bytes 8388608
  107.9 4.2 %collective-permute-start.17 = (f32[512,1024]{1,0:T(8,128)S(1)}, f32[512,1024]{1,0:T(8,128)S(1)}, u32[]{:S(2)}, u32[]{:S(2)}) collective-permute-start(f32[512,1024]{1,0:T(8,128)S(1)} %fusion.53), channel_id=1, source_target_pairs={{0,1},{1,0},{2,3},{3,2},{4,5},{5,4},{6,7},{7,6},{8,9},{9,8},{10,11... | collective-permute-start | bytes 6291464 | tf_op jit(solution)/shard_map/ppermute | solution.py:155
  118.8 1.2 collective-permute-start.27
  120.2 4.8 %collective-permute-start.28 = (f32[256]{0:T(256)S(1)}, f32[256]{0:T(256)S(1)}, u32[]{:S(2)}, u32[]{:S(2)}) collective-permute-start(f32[256]{0:T(256)S(1)} %pad_maximum_fusion.35), channel_id=1, source_target_pairs={{0,48},{1,49},{2,50},{3,51},{4,52},{5,53},{6,54},{7,55},{8,56},{9,... | collective-permute-start | bytes 3080 | tf_op jit(solution)/shard_map/ppermute | solution.py:118
  121.2 16.4 %collective-permute-start.18 = (f32[256,256]{1,0:T(8,128)S(1)}, f32[256,256]{1,0:T(8,128)S(1)}, u32[]{:S(2)}, u32[]{:S(2)}) collective-permute-start(f32[256,256]{1,0:T(8,128)S(1)} %pad_maximum_fusion.29), channel_id=1, source_target_pairs={{0,16},{1,17},{2,18},{3,19},{4,20},{5,21},{6,22},{7,23},{8,24},{9,... | collective-permute-start | bytes 786440 | tf_op jit(solution)/shard_map/ppermute | solution.py:118
  125.1 5.0 %collective-permute-start.29 = (f32[128]{0:T(128)S(1)}, f32[128]{0:T(128)S(1)}, u32[]{:S(2)}, u32[]{:S(2)}) collective-permute-start(f32[128]{0:T(128)S(1)} %pad_maximum_fusion.36), channel_id=1, source_target_pairs={{0,66},{1,67},{2,64},{3,65},{4,70},{5,71},{6,68},{7,69},{8,74},{9,... | collective-permute-start | bytes 1544 | tf_op jit(solution)/shard_map/ppermute | solution.py:118
  125.7 5.3 %collective-permute-start.21 = (f32[256,128]{1,0:T(8,128)S(1)}, f32[256,128]{1,0:T(8,128)S(1)}, u32[]{:S(2)}, u32[]{:S(2)}) collective-permute-start(f32[256,128]{1,0:T(8,128)S(1)} %pad_maximum_fusion.31), channel_id=1, source_target_pairs={{0,64},{1,65},{2,66},{3,67},{4,68},{5,69},{6,70},{7,71},{8,72},{9,... | collective-permute-start | bytes 393224 | tf_op jit(solution)/shard_map/ppermute | solution.py:118
  126.7 8.8 %collective-permute-start.24 = (f32[256,128]{1,0:T(8,128)S(1)}, f32[256,128]{1,0:T(8,128)S(1)}, u32[]{:S(2)}, u32[]{:S(2)}) collective-permute-start(f32[256,128]{1,0:T(8,128)S(1)} %slice.655), channel_id=1, source_target_pairs={{0,4},{1,5},{2,6},{3,7},{4,0},{5,1},{6,2},{7,3},{8,12},{9,13},{10,... | collective-permute-start | bytes 393224 | tf_op jit(solution)/shard_map/ppermute | solution.py:118
  130.2 4.8 %collective-permute-start.30 = (f32[64]{0:T(128)S(1)}, f32[64]{0:T(128)S(1)}, u32[]{:S(2)}, u32[]{:S(2)}) collective-permute-start(f32[64]{0:T(128)S(1)} %slice_add_fusion.19), channel_id=1, source_target_pairs={{0,12},{1,13},{2,14},{3,15},{4,8},{5,9},{6,10},{7,11},{8,4},{9,5},... | collective-permute-start | bytes 776 | tf_op jit(solution)/shard_map/ppermute | solution.py:118
  131.1 4.4 %collective-permute-start.22 = (f32[128,128]{1,0:T(8,128)S(1)}, f32[128,128]{1,0:T(8,128)S(1)}, u32[]{:S(2)}, u32[]{:S(2)}) collective-permute-start(f32[128,128]{1,0:T(8,128)S(1)} %pad_maximum_fusion.33), channel_id=1, source_target_pairs={{0,4},{1,5},{2,6},{3,7},{4,0},{5,1},{6,2},{7,3},{8,12},{9,13},{10,... | collective-permute-start | bytes 196616 | tf_op jit(solution)/shard_map/ppermute | solution.py:118
  135.5 4.7 %collective-permute-start.25 = (f32[128,128]{1,0:T(8,128)S(1)}, f32[128,128]{1,0:T(8,128)S(1)}, u32[]{:S(2)}, u32[]{:S(2)}) collective-permute-start(f32[128,128]{1,0:T(8,128)S(1)} %pad_maximum_fusion.34), channel_id=1, source_target_pairs={{0,16},{1,17},{2,18},{3,19},{4,20},{5,21},{6,22},{7,23},{8,24},{9,... | collective-permute-start | bytes 196616 | tf_op jit(solution)/shard_map/ppermute | solution.py:118
  136.0 4.2 %collective-permute-start.23 = (f32[64,128]{1,0:T(8,128)S(1)}, f32[64,128]{1,0:T(8,128)S(1)}, u32[]{:S(2)}, u32[]{:S(2)}) collective-permute-start(f32[64,128]{1,0:T(8,128)S(1)} %get-tuple-element.61), channel_id=1, source_target_pairs={{0,16},{1,17},{2,18},{3,19},{4,20},{5,21},{6,22},{7,23},{8,24},{9,... | collective-permute-start | bytes 98312 | tf_op jit(solution)/shard_map/ppermute | solution.py:118
  137.7 5.0 %collective-permute-start.19 = (f32[128,256]{1,0:T(8,128)S(1)}, f32[128,256]{1,0:T(8,128)S(1)}, u32[]{:S(2)}, u32[]{:S(2)}) collective-permute-start(f32[128,256]{1,0:T(8,128)S(1)} %pad_maximum_fusion.30), channel_id=1, source_target_pairs={{0,64},{1,65},{2,66},{3,67},{4,68},{5,69},{6,70},{7,71},{8,72},{9,... | collective-permute-start | bytes 393224 | tf_op jit(solution)/shard_map/ppermute | solution.py:118
  140.2 4.0 %collective-permute-start.26 = (f32[64,128]{1,0:T(8,128)S(1)}, f32[64,128]{1,0:T(8,128)S(1)}, u32[]{:S(2)}, u32[]{:S(2)}) collective-permute-start(f32[64,128]{1,0:T(8,128)S(1)} %get-tuple-element.60), channel_id=1, source_target_pairs={{0,64},{1,65},{2,66},{3,67},{4,68},{5,69},{6,70},{7,71},{8,72},{9,... | collective-permute-start | bytes 98312 | tf_op jit(solution)/shard_map/ppermute | solution.py:118
  142.7 4.3 %collective-permute-start.20 = (f32[64,256]{1,0:T(8,128)S(1)}, f32[64,256]{1,0:T(8,128)S(1)}, u32[]{:S(2)}, u32[]{:S(2)}) collective-permute-start(f32[64,256]{1,0:T(8,128)S(1)} %slice_add_fusion), channel_id=1, source_target_pairs={{0,4},{1,5},{2,6},{3,7},{4,0},{5,1},{6,2},{7,3},{8,12},{9,13},{10,... | collective-permute-start | bytes 196616 | tf_op jit(solution)/shard_map/ppermute | solution.py:118
  (3 other events, 27.0 us)

commit v13 on v11

--- a/solution.py
+++ b/solution.py
@@ -5,7 +5,8 @@
 
 NCLS = 512
 PAD = 128
-AXES = ("blk", "dp")
+AXES = ("y_lo", "x_hi", "x_lo", "z_hi", "z_lo", "y_hi", "core")
+CUBE = ("x_lo", "y_lo", "z_lo")
 THREE = ((0, 1, 2), (1, 2, 0), (2, 0, 1))
 TWO = ((0, 1, 2), (2, 0, 1))
 
@@ -87,25 +88,32 @@
     return [buf[at[o] * rows:(at[o] + 1) * rows] for o in range(8)]
 
 
-def half_gather(shard, mate, n, orders):
+def a2a_chain(part, order):
+    rows, cols = part.shape
+    buf = part[None]
+    for a in order:
+        buf = lax.all_to_all(jnp.stack([buf, buf]), CUBE[a], 0, 0, tiled=False)
+    for d, a in enumerate(reversed(order)):
+        buf = jnp.where(lax.axis_index(CUBE[a]) == 1, jnp.flip(buf, d), buf)
+    perm = [list(reversed(order)).index(a) for a in (2, 1, 0)]
+    buf = buf.reshape(2, 2, 2, rows, cols).transpose(perm + [3, 4])
+    return [buf.reshape(8, rows, cols)[o] for o in range(8)]
+
+
+def half_gather(shard, mate, n, orders, a2a=0):
     r, cols = shard.shape
     h = cols // 2
     c = lax.axis_index(AXES) % 2
     mine = lax.dynamic_slice_in_dim(shard, c * h, h, axis=1)
     give = lax.dynamic_slice_in_dim(shard, (1 - c) * h, h, axis=1)
     unit = jnp.concatenate([mine, lax.ppermute(give, AXES, core_pairs(n))])
-    cut = column_cuts(h, len(orders))
+    m = len(orders) + a2a
+    cut = column_cuts(h, m)
     parts = [chain(unit[:, cut[p]:cut[p + 1]], mate, n, order) for p, order in enumerate(orders)]
-    blocks = [jnp.concatenate([parts[p][o] for p in range(len(orders))], axis=1) for o in range(8)]
+    for p in range(len(orders), m):
+        parts.append(a2a_chain(unit[:, cut[p]:cut[p + 1]], THREE[p]))
+    blocks = [jnp.concatenate([parts[p][o] for p in range(m)], axis=1) for o in range(8)]
     return jnp.concatenate([b[:r] for b in blocks] + [b[r:] for b in blocks])
-
-
-def cube_gather(shard, mate, n, orders):
-    cut = column_cuts(shard.shape[1], len(orders))
-    return jnp.concatenate(
-        [chain(shard[:, cut[p]:cut[p + 1]], mate, n, order) for p, order in enumerate(orders)],
-        axis=1,
-    )
 
 
 def cube_reduce(blocks, mate, n):
@@ -132,7 +140,7 @@
     te = with_side(test_grads, split_class(test_class), 4)
     side = k // 2
     te_all = half_gather(te, test_mate, n, THREE)
-    tr_all = half_gather(tr, train_mate, n, TWO)
+    tr_all = half_gather(tr, train_mate, n, TWO, a2a=1)
     half = 8 * rows
 
     def partial(t):
@@ -163,6 +171,7 @@
 
 
 def solution(mesh):
+    fine = jax.sharding.Mesh(mesh.devices.reshape((2,) * 7), AXES)
     in_specs = (
         P(AXES, None),
         P(AXES),
@@ -171,4 +180,4 @@
         P(AXES),
     )
     out_specs = (P(AXES, None), P(AXES))
-    return jax.shard_map(local, mesh=mesh, in_specs=in_specs, out_specs=out_specs, check_vma=False)
+    return jax.shard_map(local, mesh=fine, in_specs=in_specs, out_specs=out_specs, check_vma=False)

time: 147 us -> 179 us (1.22)
  waiting for transfers between devices: 87.5 us -> 51.5 us
  local copies, waits for them, and re-layouts: 5.51 us -> 36 us
  other arithmetic: 6.94 us -> 36 us
  starting transfers between devices: 34.5 us -> 41.5 us
    ppermute x15, waiting for transfers between devices: 63 us -> 6.85 us  [chain(): got = lax.ppermute(buf, AXES, mate_pairs(n, a, mate))]
    all_to_all x0 -> x3, waiting for transfers between devices: none -> 22.5 us  [a2a_chain(): buf = lax.all_to_all(jnp.stack([buf, buf]), CUBE[a], 0, 0, tiled=False)]
    concatenate x10, other arithmetic: 1.03 us -> 20.3 us  [chain(): buf = jnp.concatenate([buf, got])]
    unnamed x25 -> x77, local copies, waits for them, and re-layouts: 2.74 us -> 18 us
    slice x10, local copies, waits for them, and re-layouts: 1.08 us -> 14.8 us  [chain(): return [buf[at[o] * rows:(at[o] + 1) * rows] for o in range(8)]]
    all_to_all x0 -> x3, starting transfers between devices: none -> 11.8 us  [a2a_chain(): buf = lax.all_to_all(jnp.stack([buf, buf]), CUBE[a], 0, 0, tiled=False)]
    ppermute x15, starting transfers between devices: 28.4 us -> 21.1 us  [chain(): got = lax.ppermute(buf, AXES, mate_pairs(n, a, mate))]
    another operation x0 -> x3, other arithmetic: none -> 5.39 us  [a2a_chain(): buf = lax.all_to_all(jnp.stack([buf, buf]), CUBE[a], 0, 0, tiled=False)]
  transfers between devices with their start and end apart: 25 -> 28, of which waited for: 20 -> 13; matrix products, arithmetic and copies ran while one was open for 5% -> 35% of each run, Pallas kernels for 0% -> 0%
where the time goes in v13:
time: 179 us; the launch traced here: 178 us
  waiting for transfers between devices  51.5 us (29%)
  starting transfers between devices  41.5 us (23%)
  local copies, waits for them, and re-layouts  36 us (20%)
  other arithmetic  36 us (20%)
  matrix products  11.3 us (6%)
    all_to_all x3, waiting for transfers between devices, a2a_chain(): buf = lax.all_to_all(jnp.stack([buf, buf]), CUBE[a], 0, 0, tiled=False)  22.5 us
    ppermute x15, starting transfers between devices, chain(): got = lax.ppermute(buf, AXES, mate_pairs(n, a, mate))  21.1 us
    concatenate x10, other arithmetic, chain(): buf = jnp.concatenate([buf, got])  20.3 us
    ppermute x6, waiting for transfers between devices, cube_reduce(): lax.ppermute(jnp.concatenate([blocks[o] for o in send]), AXES, mate_pairs...  18.6 us
    unnamed x77, local copies, waits for them, and re-layouts  18 us
    slice x10, local copies, waits for them, and re-layouts, chain(): return [buf[at[o] * rows:(at[o] + 1) * rows] for o in range(8)]  14.8 us
    all_to_all x3, starting transfers between devices, a2a_chain(): buf = lax.all_to_all(jnp.stack([buf, buf]), CUBE[a], 0, 0, tiled=False)  11.8 us
    dot_general x2, matrix products, partial(): lax.dot_general(t, te_all, (((1,), (1,)), ((), ())), preferred_element_ty...  9.6 us
  transfers between devices with their start and end apart: 28, of which 13 were waited for; matrix products, arithmetic and copies ran while one was open for 35% of the time, Pallas kernels for 0%

profile of v13, /device:TPU:0, one launch (start us, length us, event | category | flops | bytes accessed | tf_op | source)
XLA Modules:
  0.0 177.6 jit_solution(10454510584039875652)
XLA Ops:
  6.1 2.8 %collective-permute-start.8 = (bf16[128,1408]{1,0:T(8,128)(2,1)}, bf16[128,1408]{1,0:T(8,128)(2,1)S(1)}, u32[]{:S(2)}, u32[]{:S(2)}) collective-permute-start(bf16[128,1408]{1,0:T(8,128)(2,1)} %get-tuple-element.52), channel_id=1, source_target_pairs={{0,48},{1,49},{2,50},{3,51},{4,52},{5,53},{6,54},{7,55},{8,56},{9,... | collective-permute-start | bytes 1081352 | tf_op jit(solution)/shard_map/ppermute | solution.py:84
  8.9 4.0 %collective-permute-start.12 = (bf16[128,1408]{1,0:T(8,128)(2,1)S(1)}, bf16[128,1408]{1,0:T(8,128)(2,1)S(1)}, u32[]{:S(2)}, u32[]{:S(2)}) collective-permute-start(bf16[128,1408]{1,0:T(8,128)(2,1)S(1)} %get-tuple-element.53), channel_id=1, source_target_pairs={{0,12},{1,13},{2,14},{3,15},{4,8},{5,9},{6,10},{7,11},{8,4},{9,5},... | collective-permute-start | bytes 1081352 | tf_op jit(solution)/shard_map/ppermute | solution.py:84
  13.0 3.0 %collective-permute-start.9 = (bf16[128,1408]{1,0:T(8,128)(2,1)S(1)}, bf16[128,1408]{1,0:T(8,128)(2,1)S(1)}, u32[]{:S(2)}, u32[]{:S(2)}) collective-permute-start(bf16[128,1408]{1,0:T(8,128)(2,1)S(1)} %get-tuple-element.54), channel_id=1, source_target_pairs={{0,66},{1,67},{2,64},{3,65},{4,70},{5,71},{6,68},{7,69},{8,74},{9,... | collective-permute-start | bytes 1081352 | tf_op jit(solution)/shard_map/ppermute | solution.py:84
  16.0 2.1 %fusion.14 = (bf16[128,1408]{1,0:T(8,128)(2,1)}, bf16[1,1,128,1408]{3,2,1,0:T(8,128)(2,1)S(1)}, bf16[128,1408]{1,0:T(8,128)(2,1)}) fusion(bf16[64,4224]{1,0:T(8,128)(2,1)S(1)} %get-tuple-element.60, bf16[64,4224]{1,0:T(8,128)(2,1)} %collective-permute-done), kind=kLoop, calls=%fused_computation.93 | loop fusion | flops 2162688 | bytes 2162688 | tf_op jit(solution)/shard_map/concatenate | solution.py:109
  19.0 4.3 %all-to-all-start = ((bf16[2,1,128,1408]{3,2,1,0:T(8,128)(2,1)}), bf16[2,1,128,1408]{3,2,1,0:T(8,128)(2,1)}, u32[]{:S(2)}, u32[]{:S(2)}) async-start(bf16[2,1,128,1408]{3,2,1,0:T(8,128)(2,1)} %pad_maximum_fusion.23), calls=%async_computation | async-start | bytes 1441792 | tf_op jit(solution)/shard_map/all_to_all | solution.py:95
  23.5 1.9 %fusion.7 = bf16[128,2816]{1,0:T(8,128)(2,1)} fusion(bf16[64,4224]{1,0:T(8,128)(2,1)S(1)} %get-tuple-element.60, bf16[64,4224]{1,0:T(8,128)(2,1)} %collective-permute-done), kind=kLoop, calls=%fused_computation.49 | loop fusion | flops 1441792 | bytes 1802240 | tf_op jit(solution)/shard_map/concatenate | solution.py:109
  25.4 2.0 %pad_maximum_fusion.28 = bf16[256,1408]{1,0:T(8,128)(2,1)} fusion(bf16[128,1408]{1,0:T(8,128)(2,1)S(1)} %collective-permute-done.8, bf16[128,1408]{1,0:T(8,128)(2,1)} %get-tuple-element.52), kind=kLoop, calls=%fused_computation.55 | loop fusion | flops 1441792 | bytes 1441792 | tf_op jit(solution)/shard_map/concatenate | solution.py:85
  30.9 2.0 %collective-permute-start.10 = (bf16[256,1408]{1,0:T(8,128)(2,1)}, bf16[256,1408]{1,0:T(8,128)(2,1)}, u32[]{:S(2)}, u32[]{:S(2)}) collective-permute-start(bf16[256,1408]{1,0:T(8,128)(2,1)} %pad_maximum_fusion.26), channel_id=1, source_target_pairs={{0,12},{1,13},{2,14},{3,15},{4,8},{5,9},{6,10},{7,11},{8,4},{9,5},... | collective-permute-start | bytes 2162696 | tf_op jit(solution)/shard_map/ppermute | solution.py:84
  32.9 1.9 %pad_maximum_fusion.24 = bf16[256,1408]{1,0:T(8,128)(2,1)} fusion(bf16[128,1408]{1,0:T(8,128)(2,1)S(1)} %collective-permute-done.2, bf16[128,1408]{1,0:T(8,128)(2,1)} %get-tuple-element.58), kind=kLoop, calls=%fused_computation.51 | loop fusion | flops 1441792 | bytes 1441792 | tf_op jit(solution)/shard_map/concatenate | solution.py:85
  35.7 2.6 %pad_maximum_fusion.1 = bf16[2,2,1,128,1408]{4,3,1,2,0:T(8,128)(2,1)} fusion(bf16[1,2,1,128,1408]{4,3,1,2,0:T(8,128)(2,1)} %bitcast.1), kind=kLoop, calls=%fused_computation.13 | loop fusion | flops 720896 | bytes 2162688 | tf_op jit(solution)/shard_map/stack | solution.py:95
  38.3 3.6 %all-to-all-start.1 = ((bf16[2,2,1,128,1408]{4,3,1,2,0:T(8,128)(2,1)}), bf16[2,2,1,128,1408]{4,3,1,2,0:T(8,128)(2,1)S(1)}, u32[]{:S(2)}, u32[]{:S(2)}) async-start(bf16[2,2,1,128,1408]{4,3,1,2,0:T(8,128)(2,1)} %pad_maximum_fusion.1), calls=%async_computation.1 | async-start | bytes 2883584 | tf_op jit(solution)/shard_map/all_to_all | solution.py:95
  41.9 2.1 %pad_maximum_fusion.25 = bf16[256,1408]{1,0:T(8,128)(2,1)} fusion(bf16[128,1408]{1,0:T(8,128)(2,1)S(1)} %collective-permute-done.1, bf16[128,1408]{1,0:T(8,128)(2,1)} %get-tuple-element.56), kind=kLoop, calls=%fused_computation.52 | loop fusion | flops 1441792 | bytes 1441792 | tf_op jit(solution)/shard_map/concatenate | solution.py:85
  44.2 2.0 %collective-permute-done.14 = bf16[256,1408]{1,0:T(8,128)(2,1)} collective-permute-done((bf16[256,1408]{1,0:T(8,128)(2,1)}, bf16[256,1408]{1,0:T(8,128)(2,1)}, u32[]{:S(2)}, u32[]{:S(2)}) %collective-permute-start.14) | collective-permute-done | bytes 720928 | tf_op jit(solution)/shard_map/ppermute | solution.py:84
  46.1 2.4 %pad_maximum_fusion.6 = bf16[512,1408]{1,0:T(8,128)(2,1)} fusion(bf16[256,1408]{1,0:T(8,128)(2,1)} %collective-permute-done.14, bf16[128,1408]{1,0:T(8,128)(2,1)S(1)} %collective-permute-done.8, bf16[128,1408]{1,0:T(8,128)(2,1)} %get-tuple-element.52), kind=kLoop, calls=%fused_computation.18 | loop fusion | flops 4325376 | bytes 2883584 | tf_op jit(solution)/shard_map/concatenate | solution.py:85
  50.2 2.4 %pad_maximum_fusion.5 = bf16[512,1408]{1,0:T(8,128)(2,1)} fusion(bf16[256,1408]{1,0:T(8,128)(2,1)} %collective-permute-done.13, bf16[128,1408]{1,0:T(8,128)(2,1)S(1)} %collective-permute-done.12, bf16[128,1408]{1,0:T(8,128)(2,1)S(1)} %copy-done.13), kind=kLoop, calls=%fused_computation.17 | loop fusion | flops 4325376 | bytes 2883584 | tf_op jit(solution)/shard_map/concatenate | solution.py:85
  52.9 2.4 %pad_maximum_fusion.4 = bf16[512,1408]{1,0:T(8,128)(2,1)} fusion(bf16[256,1408]{1,0:T(8,128)(2,1)} %collective-permute-done.10, bf16[128,1408]{1,0:T(8,128)(2,1)S(1)} %collective-permute-done.9, bf16[128,1408]{1,0:T(8,128)(2,1)S(1)} %copy-done.11), kind=kLoop, calls=%fused_computation.16 | loop fusion | flops 4325376 | bytes 2883584 | tf_op jit(solution)/shard_map/concatenate | solution.py:85
  55.4 3.4 %collective-permute-start.11 = (bf16[512,1408]{1,0:T(8,128)(2,1)}, bf16[512,1408]{1,0:T(8,128)(2,1)}, u32[]{:S(2)}, u32[]{:S(2)}) collective-permute-start(bf16[512,1408]{1,0:T(8,128)(2,1)} %pad_maximum_fusion.4), channel_id=1, source_target_pairs={{0,48},{1,49},{2,50},{3,51},{4,52},{5,53},{6,54},{7,55},{8,56},{9,... | collective-permute-start | bytes 4325384 | tf_op jit(solution)/shard_map/ppermute | solution.py:84
  58.8 2.4 %pad_maximum_fusion.2 = bf16[512,1408]{1,0:T(8,128)(2,1)} fusion(bf16[256,1408]{1,0:T(8,128)(2,1)} %collective-permute-done.3, bf16[128,1408]{1,0:T(8,128)(2,1)S(1)} %collective-permute-done.2, bf16[128,1408]{1,0:T(8,128)(2,1)} %get-tuple-element.58), kind=kLoop, calls=%fused_computation.14 | loop fusion | flops 4325376 | bytes 2883584 | tf_op jit(solution)/shard_map/concatenate | solution.py:85
  62.6 4.6 %all-to-all-done.1 = bf16[2,2,1,128,1408]{4,3,1,2,0:T(8,128)(2,1)S(1)} async-done(((bf16[2,2,1,128,1408]{4,3,1,2,0:T(8,128)(2,1)}), bf16[2,2,1,128,1408]{4,3,1,2,0:T(8,128)(2,1)S(1)}, u32[]{:S(2)}, u32[]{:S(2)}) %all-to-all-start.1) | async-done | bytes 1441824 | tf_op jit(solution)/shard_map/all_to_all | solution.py:95
  69.1 3.9 %all-to-all-start.2 = ((bf16[2,2,2,1,128,1408]{5,4,2,1,3,0:T(8,128)(2,1)}), bf16[2,2,2,1,128,1408]{5,4,2,1,3,0:T(8,128)(2,1)S(1)}, u32[]{:S(2)}, u32[]{:S(2)}) async-start(bf16[2,2,2,1,128,1408]{5,4,2,1,3,0:T(8,128)(2,1)} %pad_maximum_fusion), calls=%async_computation.2 | async-start | bytes 5767168 | tf_op jit(solution)/shard_map/all_to_all | solution.py:95
  73.0 2.5 %pad_maximum_fusion.3 = bf16[512,1408]{1,0:T(8,128)(2,1)} fusion(bf16[256,1408]{1,0:T(8,128)(2,1)} %collective-permute-done.4, bf16[128,1408]{1,0:T(8,128)(2,1)} %copy-done.2, bf16[128,1408]{1,0:T(8,128)(2,1)} %get-tuple-element.56), kind=kLoop, calls=%fused_computation.15 | loop fusion | flops 4325376 | bytes 2883584 | tf_op jit(solution)/shard_map/concatenate | solution.py:85
  79.0 2.0 %fusion.35 = (bf16[128,1408]{1,0:T(8,128)(2,1)}, bf16[128,1408]{1,0:T(8,128)(2,1)}) fusion(bf16[256,1408]{1,0:T(8,128)(2,1)} %collective-permute-done.4), kind=kLoop, calls=%fused_computation.163 | loop fusion | bytes 1441792 | tf_op jit(solution)/shard_map/slice | solution.py:88
  81.1 2.1 %fusion.34 = (bf16[128,1408]{1,0:T(8,128)(2,1)}, bf16[128,1408]{1,0:T(8,128)(2,1)}) fusion(bf16[256,1408]{1,0:T(8,128)(2,1)} %collective-permute-done.3), kind=kLoop, calls=%fused_computation.162 | loop fusion | bytes 1441792 | tf_op jit(solution)/shard_map/slice | solution.py:88
  83.2 4.8 %collective-permute-done.11 = bf16[512,1408]{1,0:T(8,128)(2,1)} collective-permute-done((bf16[512,1408]{1,0:T(8,128)(2,1)}, bf16[512,1408]{1,0:T(8,128)(2,1)}, u32[]{:S(2)}, u32[]{:S(2)}) %collective-permute-start.11) | collective-permute-done | bytes 1441824 | tf_op jit(solution)/shard_map/ppermute | solution.py:84
  104.9 17.7 %all-to-all-done.2 = bf16[2,2,2,1,128,1408]{5,4,2,1,3,0:T(8,128)(2,1)S(1)} async-done(((bf16[2,2,2,1,128,1408]{5,4,2,1,3,0:T(8,128)(2,1)}), bf16[2,2,2,1,128,1408]{5,4,2,1,3,0:T(8,128)(2,1)S(1)}, u32[]{:S(2)}, u32[]{:S(2)}) %all-to-all-start.2) | async-done | bytes 2883616 | tf_op jit(solution)/shard_map/all_to_all | solution.py:95
  133.4 4.8 %fusion.37 = f32[512,1024]{1,0:T(8,128)S(1)} fusion(bf16[512,4224]{1,0:T(8,128)(2,1)S(1)} %get-tuple-element.36, bf16[1024,4224]{1,0:T(8,128)(2,1)S(1)} %slice_dynamic-update-slice_fusion.7), kind=kOutput, calls=%fused_computation.165 | convolution fusion | flops 4429185024 | bytes 15073280 | tf_op jit(solution)/shard_map/dot_general | solution.py:147
  139.3 3.4 %collective-permute-done.17 = f32[512,1024]{1,0:T(8,128)S(1)} collective-permute-done((f32[512,1024]{1,0:T(8,128)S(1)}, f32[512,1024]{1,0:T(8,128)S(1)}, u32[]{:S(2)}, u32[]{:S(2)}) %collective-permute-start.17) | collective-permute-done | bytes 2097184 | tf_op jit(solution)/shard_map/ppermute | solution.py:151
  142.8 4.8 %fusion.3 = bf16[512,1024]{1,0:T(8,128)(2,1)S(1)} fusion(f32[512,512]{1,0:T(8,128)S(1)} %get-tuple-element.13, f32[512,512]{1,0:T(8,128)S(1)} %get-tuple-element.12, f32[512]{0:T(512)S(1)} %convert_reduce_fusion, bf16[512,4224]{1,0:T(8,128)(2,1)S(1)} %get-tuple-element.37, bf16[1024,4224]{1,0:T(8,128)(2,1)S(1)} %slice_dynamic-update-slice_fusion.7), kind=kOutput, calls=%fused_computation.8 | convolution fusion | flops 4431282176 | bytes 16123904 | tf_op jit(solution)/shard_map/dot_general | solution.py:147
  152.8 3.3 %collective-permute-done.22 = f32[256]{0:T(256)S(1)} collective-permute-done((f32[256]{0:T(256)S(1)}, f32[256]{0:T(256)S(1)}, u32[]{:S(2)}, u32[]{:S(2)}) %collective-permute-start.22) | collective-permute-done | bytes 1056 | tf_op jit(solution)/shard_map/ppermute | solution.py:126
  156.2 7.7 %collective-permute-done.18 = f32[256,512]{1,0:T(8,128)S(1)} collective-permute-done((f32[256,512]{1,0:T(8,128)S(1)}, f32[256,512]{1,0:T(8,128)S(1)}, u32[]{:S(2)}, u32[]{:S(2)}) %collective-permute-start.18) | collective-permute-done | bytes 524320 | tf_op jit(solution)/shard_map/ppermute | solution.py:126
  166.5 3.5 %collective-permute-done.23 = f32[128]{0:T(128)S(1)} collective-permute-done((f32[128]{0:T(128)S(1)}, f32[128]{0:T(128)S(1)}, u32[]{:S(2)}, u32[]{:S(2)}) %collective-permute-start.23) | collective-permute-done | bytes 544 | tf_op jit(solution)/shard_map/ppermute | solution.py:126
  172.5 2.4 %collective-permute-done.24 = f32[64]{0:T(128)S(1)} collective-permute-done((f32[64]{0:T(128)S(1)}, f32[64]{0:T(128)S(1)}, u32[]{:S(2)}, u32[]{:S(2)}) %collective-permute-start.24) | collective-permute-done | bytes 288 | tf_op jit(solution)/shard_map/ppermute | solution.py:126
  (183 shorter events, 61.2 us)
Async XLA Ops:
  3.2 1.9 %collective-permute-start.7 = (bf16[64,4224]{1,0:T(8,128)(2,1)S(1)}, bf16[64,4224]{1,0:T(8,128)(2,1)S(1)}, u32[]{:S(2)}, u32[]{:S(2)}) collective-permute-start(bf16[64,4224]{1,0:T(8,128)(2,1)S(1)} %get-tuple-element.55), channel_id=1, source_target_pairs={{0,1},{1,0},{2,3},{3,2},{4,5},{5,4},{6,7},{7,6},{8,9},{9,8},{10,11... | collective-permute-start | bytes 1622024 | tf_op jit(solution)/shard_map/ppermute | solution.py:109
  4.6 11.4 %collective-permute-start = (bf16[64,4224]{1,0:T(8,128)(2,1)}, bf16[64,4224]{1,0:T(8,128)(2,1)}, u32[]{:S(2)}, u32[]{:S(2)}) collective-permute-start(bf16[64,4224]{1,0:T(8,128)(2,1)} %get-tuple-element.59), channel_id=1, source_target_pairs={{0,1},{1,0},{2,3},{3,2},{4,5},{5,4},{6,7},{7,6},{8,9},{9,8},{10,11... | collective-permute-start | bytes 1622024 | tf_op jit(solution)/shard_map/ppermute | solution.py:109
  6.1 21.6 %copy-start.12 = (bf16[128,1408]{1,0:T(8,128)(2,1)}, bf16[128,1408]{1,0:T(8,128)(2,1)S(1)}, u32[]{:S(2)}) copy-start(bf16[128,1408]{1,0:T(8,128)(2,1)S(1)} %get-tuple-element.53) | copy-start | bytes 1081348
  6.1 23.8 %copy-start.10 = (bf16[128,1408]{1,0:T(8,128)(2,1)}, bf16[128,1408]{1,0:T(8,128)(2,1)S(1)}, u32[]{:S(2)}) copy-start(bf16[128,1408]{1,0:T(8,128)(2,1)S(1)} %get-tuple-element.54) | copy-start | bytes 1081348
  6.1 19.4 %collective-permute-start.8 = (bf16[128,1408]{1,0:T(8,128)(2,1)}, bf16[128,1408]{1,0:T(8,128)(2,1)S(1)}, u32[]{:S(2)}, u32[]{:S(2)}) collective-permute-start(bf16[128,1408]{1,0:T(8,128)(2,1)} %get-tuple-element.52), channel_id=1, source_target_pairs={{0,48},{1,49},{2,50},{3,51},{4,52},{5,53},{6,54},{7,55},{8,56},{9,... | collective-permute-start | bytes 1081352 | tf_op jit(solution)/shard_map/ppermute | solution.py:84
  8.9 18.8 %collective-permute-start.12 = (bf16[128,1408]{1,0:T(8,128)(2,1)S(1)}, bf16[128,1408]{1,0:T(8,128)(2,1)S(1)}, u32[]{:S(2)}, u32[]{:S(2)}) collective-permute-start(bf16[128,1408]{1,0:T(8,128)(2,1)S(1)} %get-tuple-element.53), channel_id=1, source_target_pairs={{0,12},{1,13},{2,14},{3,15},{4,8},{5,9},{6,10},{7,11},{8,4},{9,5},... | collective-permute-start | bytes 1081352 | tf_op jit(solution)/shard_map/ppermute | solution.py:84
  13.0 16.9 %collective-permute-start.9 = (bf16[128,1408]{1,0:T(8,128)(2,1)S(1)}, bf16[128,1408]{1,0:T(8,128)(2,1)S(1)}, u32[]{:S(2)}, u32[]{:S(2)}) collective-permute-start(bf16[128,1408]{1,0:T(8,128)(2,1)S(1)} %get-tuple-element.54), channel_id=1, source_target_pairs={{0,66},{1,67},{2,64},{3,65},{4,70},{5,71},{6,68},{7,69},{8,74},{9,... | collective-permute-start | bytes 1081352 | tf_op jit(solution)/shard_map/ppermute | solution.py:84
  18.0 14.9 %collective-permute-start.2 = (bf16[128,1408]{1,0:T(8,128)(2,1)}, bf16[128,1408]{1,0:T(8,128)(2,1)S(1)}, u32[]{:S(2)}, u32[]{:S(2)}) collective-permute-start(bf16[128,1408]{1,0:T(8,128)(2,1)} %get-tuple-element.58), channel_id=1, source_target_pairs={{0,4},{1,5},{2,6},{3,7},{4,0},{5,1},{6,2},{7,3},{8,12},{9,13},{10,... | collective-permute-start | bytes 1081352 | tf_op jit(solution)/shard_map/ppermute | solution.py:84
  19.0 16.7 %all-to-all-start = ((bf16[2,1,128,1408]{3,2,1,0:T(8,128)(2,1)}), bf16[2,1,128,1408]{3,2,1,0:T(8,128)(2,1)}, u32[]{:S(2)}, u32[]{:S(2)}) async-start(bf16[2,1,128,1408]{3,2,1,0:T(8,128)(2,1)} %pad_maximum_fusion.23), calls=%async_computation | async-start | bytes 1441792 | tf_op jit(solution)/shard_map/all_to_all | solution.py:95
  23.2 18.7 %collective-permute-start.1 = (bf16[128,1408]{1,0:T(8,128)(2,1)}, bf16[128,1408]{1,0:T(8,128)(2,1)S(1)}, u32[]{:S(2)}, u32[]{:S(2)}) collective-permute-start(bf16[128,1408]{1,0:T(8,128)(2,1)} %get-tuple-element.56), channel_id=1, source_target_pairs={{0,16},{1,17},{2,18},{3,19},{4,20},{5,21},{6,22},{7,23},{8,24},{9,... | collective-permute-start | bytes 1081352 | tf_op jit(solution)/shard_map/ppermute | solution.py:84
  27.5 18.7 %collective-permute-start.14 = (bf16[256,1408]{1,0:T(8,128)(2,1)}, bf16[256,1408]{1,0:T(8,128)(2,1)}, u32[]{:S(2)}, u32[]{:S(2)}) collective-permute-start(bf16[256,1408]{1,0:T(8,128)(2,1)} %pad_maximum_fusion.28), channel_id=1, source_target_pairs={{0,66},{1,67},{2,64},{3,65},{4,70},{5,71},{6,68},{7,69},{8,74},{9,... | collective-permute-start | bytes 2162696 | tf_op jit(solution)/shard_map/ppermute | solution.py:84
  27.7 22.5 %copy-start.4 = (bf16[128,1408]{1,0:T(8,128)(2,1)}, bf16[128,1408]{1,0:T(8,128)(2,1)S(1)}, u32[]{:S(2)}) copy-start(bf16[128,1408]{1,0:T(8,128)(2,1)S(1)} %collective-permute-done.12) | copy-start | bytes 1081348
  28.8 21.5 %collective-permute-start.13 = (bf16[256,1408]{1,0:T(8,128)(2,1)}, bf16[256,1408]{1,0:T(8,128)(2,1)}, u32[]{:S(2)}, u32[]{:S(2)}) collective-permute-start(bf16[256,1408]{1,0:T(8,128)(2,1)} %pad_maximum_fusion.27), channel_id=1, source_target_pairs={{0,48},{1,49},{2,50},{3,51},{4,52},{5,53},{6,54},{7,55},{8,56},{9,... | collective-permute-start | bytes 2162696 | tf_op jit(solution)/shard_map/ppermute | solution.py:84
  29.9 23.0 %copy-start.6 = (bf16[128,1408]{1,0:T(8,128)(2,1)}, bf16[128,1408]{1,0:T(8,128)(2,1)S(1)}, u32[]{:S(2)}) copy-start(bf16[128,1408]{1,0:T(8,128)(2,1)S(1)} %collective-permute-done.9) | copy-start | bytes 1081348
  30.9 22.0 %collective-permute-start.10 = (bf16[256,1408]{1,0:T(8,128)(2,1)}, bf16[256,1408]{1,0:T(8,128)(2,1)}, u32[]{:S(2)}, u32[]{:S(2)}) collective-permute-start(bf16[256,1408]{1,0:T(8,128)(2,1)} %pad_maximum_fusion.26), channel_id=1, source_target_pairs={{0,12},{1,13},{2,14},{3,15},{4,8},{5,9},{6,10},{7,11},{8,4},{9,5},... | collective-permute-start | bytes 2162696 | tf_op jit(solution)/shard_map/ppermute | solution.py:84
  34.9 23.9 %collective-permute-start.3 = (bf16[256,1408]{1,0:T(8,128)(2,1)}, bf16[256,1408]{1,0:T(8,128)(2,1)}, u32[]{:S(2)}, u32[]{:S(2)}) collective-permute-start(bf16[256,1408]{1,0:T(8,128)(2,1)} %pad_maximum_fusion.24), channel_id=1, source_target_pairs={{0,16},{1,17},{2,18},{3,19},{4,20},{5,21},{6,22},{7,23},{8,24},{9,... | collective-permute-start | bytes 2162696 | tf_op jit(solution)/shard_map/ppermute | solution.py:84
  38.3 29.0 %all-to-all-start.1 = ((bf16[2,2,1,128,1408]{4,3,1,2,0:T(8,128)(2,1)}), bf16[2,2,1,128,1408]{4,3,1,2,0:T(8,128)(2,1)S(1)}, u32[]{:S(2)}, u32[]{:S(2)}) async-start(bf16[2,2,1,128,1408]{4,3,1,2,0:T(8,128)(2,1)} %pad_maximum_fusion.1), calls=%async_computation.1 | async-start | bytes 2883584 | tf_op jit(solution)/shard_map/all_to_all | solution.py:95
  44.0 29.0 %collective-permute-start.4 = (bf16[256,1408]{1,0:T(8,128)(2,1)}, bf16[256,1408]{1,0:T(8,128)(2,1)}, u32[]{:S(2)}, u32[]{:S(2)}) collective-permute-start(bf16[256,1408]{1,0:T(8,128)(2,1)} %pad_maximum_fusion.25), channel_id=1, source_target_pairs={{0,64},{1,65},{2,66},{3,67},{4,68},{5,69},{6,70},{7,71},{8,72},{9,... | collective-permute-start | bytes 2162696 | tf_op jit(solution)/shard_map/ppermute | solution.py:84
  48.6 45.1 %collective-permute-start.16 = (bf16[512,1408]{1,0:T(8,128)(2,1)}, bf16[512,1408]{1,0:T(8,128)(2,1)}, u32[]{:S(2)}, u32[]{:S(2)}) collective-permute-start(bf16[512,1408]{1,0:T(8,128)(2,1)} %pad_maximum_fusion.6), channel_id=1, source_target_pairs={{0,12},{1,13},{2,14},{3,15},{4,8},{5,9},{6,10},{7,11},{8,4},{9,5},... | collective-permute-start | bytes 4325384 | tf_op jit(solution)/shard_map/ppermute | solution.py:84
  52.6 37.8 %collective-permute-start.15 = (bf16[512,1408]{1,0:T(8,128)(2,1)}, bf16[512,1408]{1,0:T(8,128)(2,1)}, u32[]{:S(2)}, u32[]{:S(2)}) collective-permute-start(bf16[512,1408]{1,0:T(8,128)(2,1)} %pad_maximum_fusion.5), channel_id=1, source_target_pairs={{0,66},{1,67},{2,64},{3,65},{4,70},{5,71},{6,68},{7,69},{8,74},{9,... | collective-permute-start | bytes 4325384 | tf_op jit(solution)/shard_map/ppermute | solution.py:84
  55.4 32.6 %collective-permute-start.11 = (bf16[512,1408]{1,0:T(8,128)(2,1)}, bf16[512,1408]{1,0:T(8,128)(2,1)}, u32[]{:S(2)}, u32[]{:S(2)}) collective-permute-start(bf16[512,1408]{1,0:T(8,128)(2,1)} %pad_maximum_fusion.4), channel_id=1, source_target_pairs={{0,48},{1,49},{2,50},{3,51},{4,52},{5,53},{6,54},{7,55},{8,56},{9,... | collective-permute-start | bytes 4325384 | tf_op jit(solution)/shard_map/ppermute | solution.py:84
  61.2 66.2 %collective-permute-start.5 = (bf16[512,1408]{1,0:T(8,128)(2,1)}, bf16[512,1408]{1,0:T(8,128)(2,1)}, u32[]{:S(2)}, u32[]{:S(2)}) collective-permute-start(bf16[512,1408]{1,0:T(8,128)(2,1)} %pad_maximum_fusion.2), channel_id=1, source_target_pairs={{0,64},{1,65},{2,66},{3,67},{4,68},{5,69},{6,70},{7,71},{8,72},{9,... | collective-permute-start | bytes 4325384 | tf_op jit(solution)/shard_map/ppermute | solution.py:84
  69.1 53.6 %all-to-all-start.2 = ((bf16[2,2,2,1,128,1408]{5,4,2,1,3,0:T(8,128)(2,1)}), bf16[2,2,2,1,128,1408]{5,4,2,1,3,0:T(8,128)(2,1)S(1)}, u32[]{:S(2)}, u32[]{:S(2)}) async-start(bf16[2,2,2,1,128,1408]{5,4,2,1,3,0:T(8,128)(2,1)} %pad_maximum_fusion), calls=%async_computation.2 | async-start | bytes 5767168 | tf_op jit(solution)/shard_map/all_to_all | solution.py:95
  75.6 54.7 %collective-permute-start.6 = (bf16[512,1408]{1,0:T(8,128)(2,1)}, bf16[512,1408]{1,0:T(8,128)(2,1)}, u32[]{:S(2)}, u32[]{:S(2)}) collective-permute-start(bf16[512,1408]{1,0:T(8,128)(2,1)} %pad_maximum_fusion.3), channel_id=1, source_target_pairs={{0,4},{1,5},{2,6},{3,7},{4,0},{5,1},{6,2},{7,3},{8,12},{9,13},{10,... | collective-permute-start | bytes 4325384 | tf_op jit(solution)/shard_map/ppermute | solution.py:84
  138.2 4.5 %collective-permute-start.17 = (f32[512,1024]{1,0:T(8,128)S(1)}, f32[512,1024]{1,0:T(8,128)S(1)}, u32[]{:S(2)}, u32[]{:S(2)}) collective-permute-start(f32[512,1024]{1,0:T(8,128)S(1)} %fusion.37), channel_id=1, source_target_pairs={{0,1},{1,0},{2,3},{3,2},{4,5},{5,4},{6,7},{7,6},{8,9},{9,8},{10,11... | collective-permute-start | bytes 6291464 | tf_op jit(solution)/shard_map/ppermute | solution.py:151
  149.3 1.9 %collective-permute-start.21 = (f32[512]{0:T(512)S(1)}, f32[512]{0:T(512)S(1)}, u32[]{:S(2)}, u32[]{:S(2)}) collective-permute-start(f32[512]{0:T(512)S(1)} %slice.458), channel_id=1, source_target_pairs={{0,1},{1,0},{2,3},{3,2},{4,5},{5,4},{6,7},{7,6},{8,9},{9,8},{10,11... | collective-permute-start | bytes 6152 | tf_op jit(solution)/shard_map/ppermute | solution.py:166
  149.6 14.3 %collective-permute-start.18 = (f32[256,512]{1,0:T(8,128)S(1)}, f32[256,512]{1,0:T(8,128)S(1)}, u32[]{:S(2)}, u32[]{:S(2)}) collective-permute-start(f32[256,512]{1,0:T(8,128)S(1)} %pad_maximum_fusion.30), channel_id=1, source_target_pairs={{0,16},{1,17},{2,18},{3,19},{4,20},{5,21},{6,22},{7,23},{8,24},{9,... | collective-permute-start | bytes 1572872 | tf_op jit(solution)/shard_map/ppermute | solution.py:126
  151.3 4.8 %collective-permute-start.22 = (f32[256]{0:T(256)S(1)}, f32[256]{0:T(256)S(1)}, u32[]{:S(2)}, u32[]{:S(2)}) collective-permute-start(f32[256]{0:T(256)S(1)} %pad_maximum_fusion.34), channel_id=1, source_target_pairs={{0,48},{1,49},{2,50},{3,51},{4,52},{5,53},{6,54},{7,55},{8,56},{9,... | collective-permute-start | bytes 3080 | tf_op jit(solution)/shard_map/ppermute | solution.py:126
  164.0 7.9 %collective-permute-start.19 = (f32[128,512]{1,0:T(8,128)S(1)}, f32[128,512]{1,0:T(8,128)S(1)}, u32[]{:S(2)}, u32[]{:S(2)}) collective-permute-start(f32[128,512]{1,0:T(8,128)S(1)} %pad_maximum_fusion.33), channel_id=1, source_target_pairs={{0,64},{1,65},{2,66},{3,67},{4,68},{5,69},{6,70},{7,71},{8,72},{9,... | collective-permute-start | bytes 786440 | tf_op jit(solution)/shard_map/ppermute | solution.py:126
  165.3 4.8 %collective-permute-start.23 = (f32[128]{0:T(128)S(1)}, f32[128]{0:T(128)S(1)}, u32[]{:S(2)}, u32[]{:S(2)}) collective-permute-start(f32[128]{0:T(128)S(1)} %pad_maximum_fusion.35), channel_id=1, source_target_pairs={{0,66},{1,67},{2,64},{3,65},{4,70},{5,71},{6,68},{7,69},{8,74},{9,... | collective-permute-start | bytes 1544 | tf_op jit(solution)/shard_map/ppermute | solution.py:126
  170.1 4.8 %collective-permute-start.24 = (f32[64]{0:T(128)S(1)}, f32[64]{0:T(128)S(1)}, u32[]{:S(2)}, u32[]{:S(2)}) collective-permute-start(f32[64]{0:T(128)S(1)} %slice_add_fusion.7), channel_id=1, source_target_pairs={{0,12},{1,13},{2,14},{3,15},{4,8},{5,9},{6,10},{7,11},{8,4},{9,5},... | collective-permute-start | bytes 776 | tf_op jit(solution)/shard_map/ppermute | solution.py:126
  171.9 5.0 %collective-permute-start.20 = (f32[64,512]{1,0:T(8,128)S(1)}, f32[64,512]{1,0:T(8,128)S(1)}, u32[]{:S(2)}, u32[]{:S(2)}) collective-permute-start(f32[64,512]{1,0:T(8,128)S(1)} %slice_add_fusion), channel_id=1, source_target_pairs={{0,4},{1,5},{2,6},{3,7},{4,0},{5,1},{6,2},{7,3},{8,12},{9,13},{10,... | collective-permute-start | bytes 393224 | tf_op jit(solution)/shard_map/ppermute | solution.py:126
  (24 other events, 88.5 us)

commit v14 on v11

--- a/solution.py
+++ b/solution.py
@@ -87,25 +87,20 @@
     return [buf[at[o] * rows:(at[o] + 1) * rows] for o in range(8)]
 
 
-def half_gather(shard, mate, n, orders):
-    r, cols = shard.shape
-    h = cols // 2
+def half_unit(shard, n):
+    h = shard.shape[1] // 2
     c = lax.axis_index(AXES) % 2
     mine = lax.dynamic_slice_in_dim(shard, c * h, h, axis=1)
     give = lax.dynamic_slice_in_dim(shard, (1 - c) * h, h, axis=1)
-    unit = jnp.concatenate([mine, lax.ppermute(give, AXES, core_pairs(n))])
-    cut = column_cuts(h, len(orders))
+    return jnp.concatenate([mine, lax.ppermute(give, AXES, core_pairs(n))])
+
+
+def half_gather(unit, mate, n, orders):
+    r = unit.shape[0] // 2
+    cut = column_cuts(unit.shape[1], len(orders))
     parts = [chain(unit[:, cut[p]:cut[p + 1]], mate, n, order) for p, order in enumerate(orders)]
     blocks = [jnp.concatenate([parts[p][o] for p in range(len(orders))], axis=1) for o in range(8)]
     return jnp.concatenate([b[:r] for b in blocks] + [b[r:] for b in blocks])
-
-
-def cube_gather(shard, mate, n, orders):
-    cut = column_cuts(shard.shape[1], len(orders))
-    return jnp.concatenate(
-        [chain(shard[:, cut[p]:cut[p + 1]], mate, n, order) for p, order in enumerate(orders)],
-        axis=1,
-    )
 
 
 def cube_reduce(blocks, mate, n):
@@ -131,8 +126,9 @@
     tr = with_side(train_grads, (train_scale,) + split_class(train_class), 0)
     te = with_side(test_grads, split_class(test_class), 4)
     side = k // 2
-    te_all = half_gather(te, test_mate, n, THREE)
-    tr_all = half_gather(tr, train_mate, n, TWO)
+    tr_unit, te_unit = lax.optimization_barrier((half_unit(tr, n), half_unit(te, n)))
+    tr_all = half_gather(tr_unit, train_mate, n, TWO)
+    te_all = half_gather(te_unit, test_mate, n, THREE)
     half = 8 * rows
 
     def partial(t):

time: 147 us -> 150 us (1.020)
  waiting for transfers between devices: 87.5 us -> 89.1 us
    ppermute x15, starting transfers between devices: 28.4 us -> 31.4 us  [chain(): got = lax.ppermute(buf, AXES, mate_pairs(n, a, mate))]
    ppermute x6, starting transfers between devices: 5.64 us -> 3.53 us  [cube_reduce(): lax.ppermute(jnp.concatenate([blocks[o] for o in send]), AXES, mate_pairs...]
    ppermute x15, waiting for transfers between devices: 63 us -> 61.2 us  [chain(): got = lax.ppermute(buf, AXES, mate_pairs(n, a, mate))]
    ppermute x6, waiting for transfers between devices: 20.6 us -> 22.2 us  [cube_reduce(): lax.ppermute(jnp.concatenate([blocks[o] for o in send]), AXES, mate_pairs...]
  transfers between devices with their start and end apart: 25 -> 25, of which waited for: 20 -> 23; matrix products, arithmetic and copies ran while one was open for 5% -> 5% of each run, Pallas kernels for 0% -> 0%
where the time goes in v14:
time: 150 us
  waiting for transfers between devices  89.1 us (59%)
  starting transfers between devices  35.5 us (24%)
  matrix products  11.2 us (7%)
  other arithmetic  6.92 us (5%)
  local copies, waits for them, and re-layouts  5.73 us (4%)
    ppermute x15, waiting for transfers between devices, chain(): got = lax.ppermute(buf, AXES, mate_pairs(n, a, mate))  61.2 us
    ppermute x15, starting transfers between devices, chain(): got = lax.ppermute(buf, AXES, mate_pairs(n, a, mate))  31.4 us
    ppermute x6, waiting for transfers between devices, cube_reduce(): lax.ppermute(jnp.concatenate([blocks[o] for o in send]), AXES, mate_pairs...  22.2 us
    dot_general x2, matrix products, partial(): lax.dot_general(t, te_all, (((1,), (1,)), ((), ())), preferred_element_ty...  9.59 us
    ppermute x6, starting transfers between devices, cube_reduce(): lax.ppermute(jnp.concatenate([blocks[o] for o in send]), AXES, mate_pairs...  3.53 us
    ppermute x1, waiting for transfers between devices, local(): got = lax.ppermute(partial(tr_all[half:]), AXES, core_pairs(n))  3.37 us
  transfers between devices with their start and end apart: 25, of which 23 were waited for; matrix products, arithmetic and copies ran while one was open for 5% of the time, Pallas kernels for 0%

profile of v14, /device:TPU:0, one launch (start us, length us, event | category | flops | bytes accessed | tf_op | source)
XLA Modules:
  0.0 149.7 jit_solution(16190753509151091229)
XLA Ops:
  0.7 1.3 fusion.43
  5.1 1.3 collective-permute-done
  6.6 3.2 %collective-permute-start.9 = (bf16[128,1408]{1,0:T(8,128)(2,1)S(1)}, bf16[128,1408]{1,0:T(8,128)(2,1)S(1)}, u32[]{:S(2)}, u32[]{:S(2)}) collective-permute-start(bf16[128,1408]{1,0:T(8,128)(2,1)S(1)} %get-tuple-element.50), channel_id=1, source_target_pairs={{0,66},{1,67},{2,64},{3,65},{4,70},{5,71},{6,68},{7,69},{8,74},{9,... | collective-permute-start | bytes 1081352 | tf_op jit(solution)/shard_map/ppermute | solution.py:83
  9.7 4.0 %collective-permute-start.12 = (bf16[128,1408]{1,0:T(8,128)(2,1)S(1)}, bf16[128,1408]{1,0:T(8,128)(2,1)S(1)}, u32[]{:S(2)}, u32[]{:S(2)}) collective-permute-start(bf16[128,1408]{1,0:T(8,128)(2,1)S(1)} %get-tuple-element.49), channel_id=1, source_target_pairs={{0,12},{1,13},{2,14},{3,15},{4,8},{5,9},{6,10},{7,11},{8,4},{9,5},... | collective-permute-start | bytes 1081352 | tf_op jit(solution)/shard_map/ppermute | solution.py:83
  14.8 2.8 %collective-permute-start.8 = (bf16[128,1408]{1,0:T(8,128)(2,1)S(1)}, bf16[128,1408]{1,0:T(8,128)(2,1)S(1)}, u32[]{:S(2)}, u32[]{:S(2)}) collective-permute-start(bf16[128,1408]{1,0:T(8,128)(2,1)S(1)} %get-tuple-element.48), channel_id=1, source_target_pairs={{0,48},{1,49},{2,50},{3,51},{4,52},{5,53},{6,54},{7,55},{8,56},{9,... | collective-permute-start | bytes 1081352 | tf_op jit(solution)/shard_map/ppermute | solution.py:83
  18.5 4.1 %collective-permute-start.10 = (bf16[256,1408]{1,0:T(8,128)(2,1)S(1)}, bf16[256,1408]{1,0:T(8,128)(2,1)S(1)}, u32[]{:S(2)}, u32[]{:S(2)}) collective-permute-start(bf16[256,1408]{1,0:T(8,128)(2,1)S(1)} %pad_maximum_fusion.18), channel_id=1, source_target_pairs={{0,12},{1,13},{2,14},{3,15},{4,8},{5,9},{6,10},{7,11},{8,4},{9,5},... | collective-permute-start | bytes 2162696 | tf_op jit(solution)/shard_map/ppermute | solution.py:83
  22.7 2.8 %collective-permute-start.13 = (bf16[256,1408]{1,0:T(8,128)(2,1)S(1)}, bf16[256,1408]{1,0:T(8,128)(2,1)S(1)}, u32[]{:S(2)}, u32[]{:S(2)}) collective-permute-start(bf16[256,1408]{1,0:T(8,128)(2,1)S(1)} %pad_maximum_fusion.19), channel_id=1, source_target_pairs={{0,48},{1,49},{2,50},{3,51},{4,52},{5,53},{6,54},{7,55},{8,56},{9,... | collective-permute-start | bytes 2162696 | tf_op jit(solution)/shard_map/ppermute | solution.py:83
  26.3 2.3 %collective-permute-start.14 = (bf16[256,1408]{1,0:T(8,128)(2,1)S(1)}, bf16[256,1408]{1,0:T(8,128)(2,1)S(1)}, u32[]{:S(2)}, u32[]{:S(2)}) collective-permute-start(bf16[256,1408]{1,0:T(8,128)(2,1)S(1)} %pad_maximum_fusion.20), channel_id=1, source_target_pairs={{0,66},{1,67},{2,64},{3,65},{4,70},{5,71},{6,68},{7,69},{8,74},{9,... | collective-permute-start | bytes 2162696 | tf_op jit(solution)/shard_map/ppermute | solution.py:83
  28.6 2.1 %collective-permute-done.2 = bf16[128,2048]{1,0:T(8,128)(2,1)S(1)} collective-permute-done((bf16[128,2048]{1,0:T(8,128)(2,1)S(1)}, bf16[128,2048]{1,0:T(8,128)(2,1)S(1)}, u32[]{:S(2)}, u32[]{:S(2)}) %collective-permute-start.2) | collective-permute-done | bytes 524320 | tf_op jit(solution)/shard_map/ppermute | solution.py:83
  31.9 6.5 %collective-permute-done.10 = bf16[256,1408]{1,0:T(8,128)(2,1)S(1)} collective-permute-done((bf16[256,1408]{1,0:T(8,128)(2,1)S(1)}, bf16[256,1408]{1,0:T(8,128)(2,1)S(1)}, u32[]{:S(2)}, u32[]{:S(2)}) %collective-permute-start.10) | collective-permute-done | bytes 720928 | tf_op jit(solution)/shard_map/ppermute | solution.py:83
  38.4 2.8 %collective-permute-start.11 = (bf16[512,1408]{1,0:T(8,128)(2,1)S(1)}, bf16[512,1408]{1,0:T(8,128)(2,1)S(1)}, u32[]{:S(2)}, u32[]{:S(2)}) collective-permute-start(bf16[512,1408]{1,0:T(8,128)(2,1)S(1)} %pad_maximum_fusion.2), channel_id=1, source_target_pairs={{0,48},{1,49},{2,50},{3,51},{4,52},{5,53},{6,54},{7,55},{8,56},{9,... | collective-permute-start | bytes 4325384 | tf_op jit(solution)/shard_map/ppermute | solution.py:83
  41.9 2.5 %collective-permute-start.15 = (bf16[512,1408]{1,0:T(8,128)(2,1)S(1)}, bf16[512,1408]{1,0:T(8,128)(2,1)S(1)}, u32[]{:S(2)}, u32[]{:S(2)}) collective-permute-start(bf16[512,1408]{1,0:T(8,128)(2,1)S(1)} %pad_maximum_fusion.3), channel_id=1, source_target_pairs={{0,66},{1,67},{2,64},{3,65},{4,70},{5,71},{6,68},{7,69},{8,74},{9,... | collective-permute-start | bytes 4325384 | tf_op jit(solution)/shard_map/ppermute | solution.py:83
  44.5 3.0 %collective-permute-start.16 = (bf16[512,1408]{1,0:T(8,128)(2,1)S(1)}, bf16[512,1408]{1,0:T(8,128)(2,1)S(1)}, u32[]{:S(2)}, u32[]{:S(2)}) collective-permute-start(bf16[512,1408]{1,0:T(8,128)(2,1)S(1)} %pad_maximum_fusion.4), channel_id=1, source_target_pairs={{0,12},{1,13},{2,14},{3,15},{4,8},{5,9},{6,10},{7,11},{8,4},{9,5},... | collective-permute-start | bytes 4325384 | tf_op jit(solution)/shard_map/ppermute | solution.py:83
  47.7 6.7 %collective-permute-done.5 = bf16[256,2048]{1,0:T(8,128)(2,1)S(1)} collective-permute-done((bf16[256,2048]{1,0:T(8,128)(2,1)S(1)}, bf16[256,2048]{1,0:T(8,128)(2,1)S(1)}, u32[]{:S(2)}, u32[]{:S(2)}) %collective-permute-start.5) | collective-permute-done | bytes 1048608 | tf_op jit(solution)/shard_map/ppermute | solution.py:83
  54.6 1.5 %collective-permute-start.7 = (bf16[512,2048]{1,0:T(8,128)(2,1)S(1)}, bf16[512,2048]{1,0:T(8,128)(2,1)S(1)}, u32[]{:S(2)}, u32[]{:S(2)}) collective-permute-start(bf16[512,2048]{1,0:T(8,128)(2,1)S(1)} %pad_maximum_fusion.1), channel_id=1, source_target_pairs={{0,4},{1,5},{2,6},{3,7},{4,0},{5,1},{6,2},{7,3},{8,12},{9,13},{10,... | collective-permute-start | bytes 6291464 | tf_op jit(solution)/shard_map/ppermute | solution.py:83
  56.6 1.5 collective-permute-start.6
  58.2 0.9 fusion.26
  59.1 13.2 %collective-permute-done.11 = bf16[512,1408]{1,0:T(8,128)(2,1)S(1)} collective-permute-done((bf16[512,1408]{1,0:T(8,128)(2,1)S(1)}, bf16[512,1408]{1,0:T(8,128)(2,1)S(1)}, u32[]{:S(2)}, u32[]{:S(2)}) %collective-permute-start.11) | collective-permute-done | bytes 1441824 | tf_op jit(solution)/shard_map/ppermute | solution.py:83
  72.6 2.3 %collective-permute-done.15 = bf16[512,1408]{1,0:T(8,128)(2,1)S(1)} collective-permute-done((bf16[512,1408]{1,0:T(8,128)(2,1)S(1)}, bf16[512,1408]{1,0:T(8,128)(2,1)S(1)}, u32[]{:S(2)}, u32[]{:S(2)}) %collective-permute-start.15) | collective-permute-done | bytes 1441824 | tf_op jit(solution)/shard_map/ppermute | solution.py:83
  75.3 2.0 %collective-permute-done.16 = bf16[512,1408]{1,0:T(8,128)(2,1)S(1)} collective-permute-done((bf16[512,1408]{1,0:T(8,128)(2,1)S(1)}, bf16[512,1408]{1,0:T(8,128)(2,1)S(1)}, u32[]{:S(2)}, u32[]{:S(2)}) %collective-permute-start.16) | collective-permute-done | bytes 1441824 | tf_op jit(solution)/shard_map/ppermute | solution.py:83
  78.5 21.1 %collective-permute-done.7 = bf16[512,2048]{1,0:T(8,128)(2,1)S(1)} collective-permute-done((bf16[512,2048]{1,0:T(8,128)(2,1)S(1)}, bf16[512,2048]{1,0:T(8,128)(2,1)S(1)}, u32[]{:S(2)}, u32[]{:S(2)}) %collective-permute-start.7) | collective-permute-done | bytes 2097184 | tf_op jit(solution)/shard_map/ppermute | solution.py:83
  99.9 4.8 %collective-permute-done.6 = bf16[512,2176]{1,0:T(8,128)(2,1)S(1)} collective-permute-done((bf16[512,2176]{1,0:T(8,128)(2,1)S(1)}, bf16[512,2176]{1,0:T(8,128)(2,1)S(1)}, u32[]{:S(2)}, u32[]{:S(2)}) %collective-permute-start.6) | collective-permute-done | bytes 2228256 | tf_op jit(solution)/shard_map/ppermute | solution.py:83
  105.8 4.8 %fusion.49 = f32[512,1024]{1,0:T(8,128)S(1)} fusion(bf16[512,4224]{1,0:T(8,128)(2,1)S(1)} %get-tuple-element.32, bf16[1024,4224]{1,0:T(8,128)(2,1)S(1)} %slice_dynamic-update-slice_fusion), kind=kOutput, calls=%fused_computation.152 | convolution fusion | flops 4429185024 | bytes 15073280 | tf_op jit(solution)/shard_map/dot_general | solution.py:135
  111.4 3.4 %collective-permute-done.17 = f32[512,1024]{1,0:T(8,128)S(1)} collective-permute-done((f32[512,1024]{1,0:T(8,128)S(1)}, f32[512,1024]{1,0:T(8,128)S(1)}, u32[]{:S(2)}, u32[]{:S(2)}) %collective-permute-start.17) | collective-permute-done | bytes 2097184 | tf_op jit(solution)/shard_map/ppermute | solution.py:139
  115.0 4.8 %fusion.2 = bf16[512,1024]{1,0:T(8,128)(2,1)S(1)} fusion(f32[512,512]{1,0:T(8,128)S(1)} %get-tuple-element.11, f32[512,512]{1,0:T(8,128)S(1)} %get-tuple-element.10, f32[512]{0:T(512)S(1)} %convert_reduce_fusion, bf16[512,4224]{1,0:T(8,128)(2,1)S(1)} %get-tuple-element.33, bf16[1024,4224]{1,0:T(8,128)(2,1)S(1)} %slice_dynamic-update-slice_fusion), kind=kOutput, calls=%fused_computation.5 | convolution fusion | flops 4431282176 | bytes 16123904 | tf_op jit(solution)/shard_map/dot_general | solution.py:135
  123.4 4.3 %collective-permute-done.22 = f32[256]{0:T(256)S(1)} collective-permute-done((f32[256]{0:T(256)S(1)}, f32[256]{0:T(256)S(1)}, u32[]{:S(2)}, u32[]{:S(2)}) %collective-permute-start.22) | collective-permute-done | bytes 1056 | tf_op jit(solution)/shard_map/ppermute | solution.py:113
  127.7 8.3 %collective-permute-done.18 = f32[256,512]{1,0:T(8,128)S(1)} collective-permute-done((f32[256,512]{1,0:T(8,128)S(1)}, f32[256,512]{1,0:T(8,128)S(1)}, u32[]{:S(2)}, u32[]{:S(2)}) %collective-permute-start.18) | collective-permute-done | bytes 524320 | tf_op jit(solution)/shard_map/ppermute | solution.py:113
  136.1 1.0 collective-permute-start.19
  137.9 4.1 %collective-permute-done.23 = f32[128]{0:T(128)S(1)} collective-permute-done((f32[128]{0:T(128)S(1)}, f32[128]{0:T(128)S(1)}, u32[]{:S(2)}, u32[]{:S(2)}) %collective-permute-start.23) | collective-permute-done | bytes 544 | tf_op jit(solution)/shard_map/ppermute | solution.py:113
  142.3 1.7 %collective-permute-done.19 = f32[128,512]{1,0:T(8,128)S(1)} collective-permute-done((f32[128,512]{1,0:T(8,128)S(1)}, f32[128,512]{1,0:T(8,128)S(1)}, u32[]{:S(2)}, u32[]{:S(2)}) %collective-permute-start.19) | collective-permute-done | bytes 262176 | tf_op jit(solution)/shard_map/ppermute | solution.py:113
  144.6 2.2 %collective-permute-done.24 = f32[64]{0:T(128)S(1)} collective-permute-done((f32[64]{0:T(128)S(1)}, f32[64]{0:T(128)S(1)}, u32[]{:S(2)}, u32[]{:S(2)}) %collective-permute-start.24) | collective-permute-done | bytes 288 | tf_op jit(solution)/shard_map/ppermute | solution.py:113
  147.3 1.8 %collective-permute-done.20 = f32[64,512]{1,0:T(8,128)S(1)} collective-permute-done((f32[64,512]{1,0:T(8,128)S(1)}, f32[64,512]{1,0:T(8,128)S(1)}, u32[]{:S(2)}, u32[]{:S(2)}) %collective-permute-start.20) | collective-permute-done | bytes 131104 | tf_op jit(solution)/shard_map/ppermute | solution.py:113
  (117 shorter events, 19.3 us)
Async XLA Ops:
  2.7 1.2 copy-start
  2.8 1.2 copy-start.1
  3.0 2.0 %collective-permute-start.1 = (bf16[64,4224]{1,0:T(8,128)(2,1)S(1)}, bf16[64,4224]{1,0:T(8,128)(2,1)S(1)}, u32[]{:S(2)}, u32[]{:S(2)}) collective-permute-start(bf16[64,4224]{1,0:T(8,128)(2,1)S(1)} %get-tuple-element.52), channel_id=1, source_target_pairs={{0,1},{1,0},{2,3},{3,2},{4,5},{5,4},{6,7},{7,6},{8,9},{9,8},{10,11... | collective-permute-start | bytes 1622024 | tf_op jit(solution)/shard_map/ppermute | solution.py:95
  4.4 2.0 %collective-permute-start = (bf16[64,4224]{1,0:T(8,128)(2,1)S(1)}, bf16[64,4224]{1,0:T(8,128)(2,1)S(1)}, u32[]{:S(2)}, u32[]{:S(2)}) collective-permute-start(bf16[64,4224]{1,0:T(8,128)(2,1)S(1)} %get-tuple-element.54), channel_id=1, source_target_pairs={{0,1},{1,0},{2,3},{3,2},{4,5},{5,4},{6,7},{7,6},{8,9},{9,8},{10,11... | collective-permute-start | bytes 1622024 | tf_op jit(solution)/shard_map/ppermute | solution.py:95
  6.6 11.9 %collective-permute-start.9 = (bf16[128,1408]{1,0:T(8,128)(2,1)S(1)}, bf16[128,1408]{1,0:T(8,128)(2,1)S(1)}, u32[]{:S(2)}, u32[]{:S(2)}) collective-permute-start(bf16[128,1408]{1,0:T(8,128)(2,1)S(1)} %get-tuple-element.50), channel_id=1, source_target_pairs={{0,66},{1,67},{2,64},{3,65},{4,70},{5,71},{6,68},{7,69},{8,74},{9,... | collective-permute-start | bytes 1081352 | tf_op jit(solution)/shard_map/ppermute | solution.py:83
  9.7 12.9 %collective-permute-start.12 = (bf16[128,1408]{1,0:T(8,128)(2,1)S(1)}, bf16[128,1408]{1,0:T(8,128)(2,1)S(1)}, u32[]{:S(2)}, u32[]{:S(2)}) collective-permute-start(bf16[128,1408]{1,0:T(8,128)(2,1)S(1)} %get-tuple-element.49), channel_id=1, source_target_pairs={{0,12},{1,13},{2,14},{3,15},{4,8},{5,9},{6,10},{7,11},{8,4},{9,5},... | collective-permute-start | bytes 1081352 | tf_op jit(solution)/shard_map/ppermute | solution.py:83
  14.8 11.4 %collective-permute-start.8 = (bf16[128,1408]{1,0:T(8,128)(2,1)S(1)}, bf16[128,1408]{1,0:T(8,128)(2,1)S(1)}, u32[]{:S(2)}, u32[]{:S(2)}) collective-permute-start(bf16[128,1408]{1,0:T(8,128)(2,1)S(1)} %get-tuple-element.48), channel_id=1, source_target_pairs={{0,48},{1,49},{2,50},{3,51},{4,52},{5,53},{6,54},{7,55},{8,56},{9,... | collective-permute-start | bytes 1081352 | tf_op jit(solution)/shard_map/ppermute | solution.py:83
  17.6 13.8 %collective-permute-start.3 = (bf16[128,2176]{1,0:T(8,128)(2,1)S(1)}, bf16[128,2176]{1,0:T(8,128)(2,1)S(1)}, u32[]{:S(2)}, u32[]{:S(2)}) collective-permute-start(bf16[128,2176]{1,0:T(8,128)(2,1)S(1)} %slice.339), channel_id=1, source_target_pairs={{0,4},{1,5},{2,6},{3,7},{4,0},{5,1},{6,2},{7,3},{8,12},{9,13},{10,... | collective-permute-start | bytes 1671176 | tf_op jit(solution)/shard_map/ppermute | solution.py:83
  17.6 13.1 %collective-permute-start.2 = (bf16[128,2048]{1,0:T(8,128)(2,1)S(1)}, bf16[128,2048]{1,0:T(8,128)(2,1)S(1)}, u32[]{:S(2)}, u32[]{:S(2)}) collective-permute-start(bf16[128,2048]{1,0:T(8,128)(2,1)S(1)} %slice.338), channel_id=1, source_target_pairs={{0,16},{1,17},{2,18},{3,19},{4,20},{5,21},{6,22},{7,23},{8,24},{9,... | collective-permute-start | bytes 1572872 | tf_op jit(solution)/shard_map/ppermute | solution.py:83
  18.5 19.8 %collective-permute-start.10 = (bf16[256,1408]{1,0:T(8,128)(2,1)S(1)}, bf16[256,1408]{1,0:T(8,128)(2,1)S(1)}, u32[]{:S(2)}, u32[]{:S(2)}) collective-permute-start(bf16[256,1408]{1,0:T(8,128)(2,1)S(1)} %pad_maximum_fusion.18), channel_id=1, source_target_pairs={{0,12},{1,13},{2,14},{3,15},{4,8},{5,9},{6,10},{7,11},{8,4},{9,5},... | collective-permute-start | bytes 2162696 | tf_op jit(solution)/shard_map/ppermute | solution.py:83
  22.7 19.0 %collective-permute-start.13 = (bf16[256,1408]{1,0:T(8,128)(2,1)S(1)}, bf16[256,1408]{1,0:T(8,128)(2,1)S(1)}, u32[]{:S(2)}, u32[]{:S(2)}) collective-permute-start(bf16[256,1408]{1,0:T(8,128)(2,1)S(1)} %pad_maximum_fusion.19), channel_id=1, source_target_pairs={{0,48},{1,49},{2,50},{3,51},{4,52},{5,53},{6,54},{7,55},{8,56},{9,... | collective-permute-start | bytes 2162696 | tf_op jit(solution)/shard_map/ppermute | solution.py:83
  26.3 18.1 %collective-permute-start.14 = (bf16[256,1408]{1,0:T(8,128)(2,1)S(1)}, bf16[256,1408]{1,0:T(8,128)(2,1)S(1)}, u32[]{:S(2)}, u32[]{:S(2)}) collective-permute-start(bf16[256,1408]{1,0:T(8,128)(2,1)S(1)} %pad_maximum_fusion.20), channel_id=1, source_target_pairs={{0,66},{1,67},{2,64},{3,65},{4,70},{5,71},{6,68},{7,69},{8,74},{9,... | collective-permute-start | bytes 2162696 | tf_op jit(solution)/shard_map/ppermute | solution.py:83
  30.8 23.5 %collective-permute-start.5 = (bf16[256,2048]{1,0:T(8,128)(2,1)S(1)}, bf16[256,2048]{1,0:T(8,128)(2,1)S(1)}, u32[]{:S(2)}, u32[]{:S(2)}) collective-permute-start(bf16[256,2048]{1,0:T(8,128)(2,1)S(1)} %pad_maximum_fusion.17), channel_id=1, source_target_pairs={{0,64},{1,65},{2,66},{3,67},{4,68},{5,69},{6,70},{7,71},{8,72},{9,... | collective-permute-start | bytes 3145736 | tf_op jit(solution)/shard_map/ppermute | solution.py:83
  31.6 24.9 %collective-permute-start.4 = (bf16[256,2176]{1,0:T(8,128)(2,1)S(1)}, bf16[256,2176]{1,0:T(8,128)(2,1)S(1)}, u32[]{:S(2)}, u32[]{:S(2)}) collective-permute-start(bf16[256,2176]{1,0:T(8,128)(2,1)S(1)} %pad_maximum_fusion.5), channel_id=1, source_target_pairs={{0,16},{1,17},{2,18},{3,19},{4,20},{5,21},{6,22},{7,23},{8,24},{9,... | collective-permute-start | bytes 3342344 | tf_op jit(solution)/shard_map/ppermute | solution.py:83
  38.4 33.9 %collective-permute-start.11 = (bf16[512,1408]{1,0:T(8,128)(2,1)S(1)}, bf16[512,1408]{1,0:T(8,128)(2,1)S(1)}, u32[]{:S(2)}, u32[]{:S(2)}) collective-permute-start(bf16[512,1408]{1,0:T(8,128)(2,1)S(1)} %pad_maximum_fusion.2), channel_id=1, source_target_pairs={{0,48},{1,49},{2,50},{3,51},{4,52},{5,53},{6,54},{7,55},{8,56},{9,... | collective-permute-start | bytes 4325384 | tf_op jit(solution)/shard_map/ppermute | solution.py:83
  41.9 33.1 %collective-permute-start.15 = (bf16[512,1408]{1,0:T(8,128)(2,1)S(1)}, bf16[512,1408]{1,0:T(8,128)(2,1)S(1)}, u32[]{:S(2)}, u32[]{:S(2)}) collective-permute-start(bf16[512,1408]{1,0:T(8,128)(2,1)S(1)} %pad_maximum_fusion.3), channel_id=1, source_target_pairs={{0,66},{1,67},{2,64},{3,65},{4,70},{5,71},{6,68},{7,69},{8,74},{9,... | collective-permute-start | bytes 4325384 | tf_op jit(solution)/shard_map/ppermute | solution.py:83
  44.5 32.9 %collective-permute-start.16 = (bf16[512,1408]{1,0:T(8,128)(2,1)S(1)}, bf16[512,1408]{1,0:T(8,128)(2,1)S(1)}, u32[]{:S(2)}, u32[]{:S(2)}) collective-permute-start(bf16[512,1408]{1,0:T(8,128)(2,1)S(1)} %pad_maximum_fusion.4), channel_id=1, source_target_pairs={{0,12},{1,13},{2,14},{3,15},{4,8},{5,9},{6,10},{7,11},{8,4},{9,5},... | collective-permute-start | bytes 4325384 | tf_op jit(solution)/shard_map/ppermute | solution.py:83
  54.6 45.1 %collective-permute-start.7 = (bf16[512,2048]{1,0:T(8,128)(2,1)S(1)}, bf16[512,2048]{1,0:T(8,128)(2,1)S(1)}, u32[]{:S(2)}, u32[]{:S(2)}) collective-permute-start(bf16[512,2048]{1,0:T(8,128)(2,1)S(1)} %pad_maximum_fusion.1), channel_id=1, source_target_pairs={{0,4},{1,5},{2,6},{3,7},{4,0},{5,1},{6,2},{7,3},{8,12},{9,13},{10,... | collective-permute-start | bytes 6291464 | tf_op jit(solution)/shard_map/ppermute | solution.py:83
  56.6 48.1 %collective-permute-start.6 = (bf16[512,2176]{1,0:T(8,128)(2,1)S(1)}, bf16[512,2176]{1,0:T(8,128)(2,1)S(1)}, u32[]{:S(2)}, u32[]{:S(2)}) collective-permute-start(bf16[512,2176]{1,0:T(8,128)(2,1)S(1)} %pad_maximum_fusion), channel_id=1, source_target_pairs={{0,64},{1,65},{2,66},{3,67},{4,68},{5,69},{6,70},{7,71},{8,72},{9,... | collective-permute-start | bytes 6684680 | tf_op jit(solution)/shard_map/ppermute | solution.py:83
  78.5 26.4 %slice-start = ((s8[4325376]{0:T(1024)(128)(4,1)}), s8[4194304]{0:T(1024)(128)(4,1)S(1)}, s32[]{:S(2)}) async-start(s8[4325376]{0:T(1024)(128)(4,1)} %bitcast.6), calls=%async_computation | async-start | bytes 8388608
  78.5 26.3 %slice-start.1 = ((s8[4325376]{0:T(1024)(128)(4,1)}), s8[131072]{0:T(1024)(128)(4,1)S(1)}, s32[]{:S(2)}) async-start(s8[4325376]{0:T(1024)(128)(4,1)} %bitcast.6), calls=%async_computation.1 | async-start | bytes 262144
  110.6 4.2 %collective-permute-start.17 = (f32[512,1024]{1,0:T(8,128)S(1)}, f32[512,1024]{1,0:T(8,128)S(1)}, u32[]{:S(2)}, u32[]{:S(2)}) collective-permute-start(f32[512,1024]{1,0:T(8,128)S(1)} %fusion.49), channel_id=1, source_target_pairs={{0,1},{1,0},{2,3},{3,2},{4,5},{5,4},{6,7},{7,6},{8,9},{9,8},{10,11... | collective-permute-start | bytes 6291464 | tf_op jit(solution)/shard_map/ppermute | solution.py:139
  121.5 1.2 collective-permute-start.21
  121.8 14.3 %collective-permute-start.18 = (f32[256,512]{1,0:T(8,128)S(1)}, f32[256,512]{1,0:T(8,128)S(1)}, u32[]{:S(2)}, u32[]{:S(2)}) collective-permute-start(f32[256,512]{1,0:T(8,128)S(1)} %pad_maximum_fusion.28), channel_id=1, source_target_pairs={{0,16},{1,17},{2,18},{3,19},{4,20},{5,21},{6,22},{7,23},{8,24},{9,... | collective-permute-start | bytes 1572872 | tf_op jit(solution)/shard_map/ppermute | solution.py:113
  122.9 4.8 %collective-permute-start.22 = (f32[256]{0:T(256)S(1)}, f32[256]{0:T(256)S(1)}, u32[]{:S(2)}, u32[]{:S(2)}) collective-permute-start(f32[256]{0:T(256)S(1)} %pad_maximum_fusion.30), channel_id=1, source_target_pairs={{0,48},{1,49},{2,50},{3,51},{4,52},{5,53},{6,54},{7,55},{8,56},{9,... | collective-permute-start | bytes 3080 | tf_op jit(solution)/shard_map/ppermute | solution.py:113
  136.1 7.8 %collective-permute-start.19 = (f32[128,512]{1,0:T(8,128)S(1)}, f32[128,512]{1,0:T(8,128)S(1)}, u32[]{:S(2)}, u32[]{:S(2)}) collective-permute-start(f32[128,512]{1,0:T(8,128)S(1)} %pad_maximum_fusion.29), channel_id=1, source_target_pairs={{0,64},{1,65},{2,66},{3,67},{4,68},{5,69},{6,70},{7,71},{8,72},{9,... | collective-permute-start | bytes 786440 | tf_op jit(solution)/shard_map/ppermute | solution.py:113
  137.2 4.8 %collective-permute-start.23 = (f32[128]{0:T(128)S(1)}, f32[128]{0:T(128)S(1)}, u32[]{:S(2)}, u32[]{:S(2)}) collective-permute-start(f32[128]{0:T(128)S(1)} %pad_maximum_fusion.31), channel_id=1, source_target_pairs={{0,66},{1,67},{2,64},{3,65},{4,70},{5,71},{6,68},{7,69},{8,74},{9,... | collective-permute-start | bytes 1544 | tf_op jit(solution)/shard_map/ppermute | solution.py:113
  142.0 4.8 %collective-permute-start.24 = (f32[64]{0:T(128)S(1)}, f32[64]{0:T(128)S(1)}, u32[]{:S(2)}, u32[]{:S(2)}) collective-permute-start(f32[64]{0:T(128)S(1)} %slice_add_fusion.7), channel_id=1, source_target_pairs={{0,12},{1,13},{2,14},{3,15},{4,8},{5,9},{6,10},{7,11},{8,4},{9,5},... | collective-permute-start | bytes 776 | tf_op jit(solution)/shard_map/ppermute | solution.py:113
  144.0 5.0 %collective-permute-start.20 = (f32[64,512]{1,0:T(8,128)S(1)}, f32[64,512]{1,0:T(8,128)S(1)}, u32[]{:S(2)}, u32[]{:S(2)}) collective-permute-start(f32[64,512]{1,0:T(8,128)S(1)} %slice_add_fusion), channel_id=1, source_target_pairs={{0,4},{1,5},{2,6},{3,7},{4,0},{5,1},{6,2},{7,3},{8,12},{9,13},{10,... | collective-permute-start | bytes 393224 | tf_op jit(solution)/shard_map/ppermute | solution.py:113

commit v15 on v11

--- a/solution.py
+++ b/solution.py
@@ -141,7 +141,8 @@
         )
 
     got = lax.ppermute(partial(tr_all[half:]), AXES, core_pairs(n))
-    raw = partial(tr_all[:half]) + jnp.concatenate([got[:, half:], got[:, :half]], axis=1)
+    own = lax.optimization_barrier(partial(tr_all[:half]))
+    raw = own + jnp.concatenate([got[:, half:], got[:, :half]], axis=1)
     tr_mine = tr_all[:half]
     scale = tr_mine[:, side].astype(jnp.float32)
     train_hot = indicator(join_class(tr_mine, side + 1))

time: 147 us -> 144 us (0.980)
  waiting for transfers between devices: 87.5 us -> 83.5 us
    ppermute x1, waiting for transfers between devices: 3.37 us -> 0.01 us  [local(): got = lax.ppermute(partial(tr_all[half:]), AXES, core_pairs(n))]
  transfers between devices with their start and end apart: 25 -> 25, of which waited for: 20 -> 19; matrix products, arithmetic and copies ran while one was open for 5% -> 8% of each run, Pallas kernels for 0% -> 0%
where the time goes in v15:
time: 144 us
  waiting for transfers between devices  83.5 us (58%)
  starting transfers between devices  34.9 us (24%)
  matrix products  11.2 us (8%)
  other arithmetic  7.43 us (5%)
  local copies, waits for them, and re-layouts  5.49 us (4%)
    ppermute x15, waiting for transfers between devices, chain(): got = lax.ppermute(buf, AXES, mate_pairs(n, a, mate))  63.1 us
    ppermute x15, starting transfers between devices, chain(): got = lax.ppermute(buf, AXES, mate_pairs(n, a, mate))  28.4 us
    ppermute x6, waiting for transfers between devices, cube_reduce(): lax.ppermute(jnp.concatenate([blocks[o] for o in send]), AXES, mate_pairs...  19.9 us
    dot_general x2, matrix products, partial(): lax.dot_general(t, te_all, (((1,), (1,)), ((), ())), preferred_element_ty...  9.57 us
    ppermute x6, starting transfers between devices, cube_reduce(): lax.ppermute(jnp.concatenate([blocks[o] for o in send]), AXES, mate_pairs...  5.61 us
  transfers between devices with their start and end apart: 25, of which 19 were waited for; matrix products, arithmetic and copies ran while one was open for 8% of the time, Pallas kernels for 0%

profile of v15, /device:TPU:0, one launch (start us, length us, event | category | flops | bytes accessed | tf_op | source)
XLA Modules:
  0.0 143.8 jit_solution(17321501295094012411)
XLA Ops:
  0.7 1.3 fusion.43
  5.1 2.9 %collective-permute-start.8 = (bf16[128,1408]{1,0:T(8,128)(2,1)S(1)}, bf16[128,1408]{1,0:T(8,128)(2,1)S(1)}, u32[]{:S(2)}, u32[]{:S(2)}) collective-permute-start(bf16[128,1408]{1,0:T(8,128)(2,1)S(1)} %get-tuple-element.46), channel_id=1, source_target_pairs={{0,48},{1,49},{2,50},{3,51},{4,52},{5,53},{6,54},{7,55},{8,56},{9,... | collective-permute-start | bytes 1081352 | tf_op jit(solution)/shard_map/ppermute | solution.py:83
  8.0 4.0 %collective-permute-start.12 = (bf16[128,1408]{1,0:T(8,128)(2,1)S(1)}, bf16[128,1408]{1,0:T(8,128)(2,1)S(1)}, u32[]{:S(2)}, u32[]{:S(2)}) collective-permute-start(bf16[128,1408]{1,0:T(8,128)(2,1)S(1)} %get-tuple-element.47), channel_id=1, source_target_pairs={{0,12},{1,13},{2,14},{3,15},{4,8},{5,9},{6,10},{7,11},{8,4},{9,5},... | collective-permute-start | bytes 1081352 | tf_op jit(solution)/shard_map/ppermute | solution.py:83
  12.1 3.0 %collective-permute-start.9 = (bf16[128,1408]{1,0:T(8,128)(2,1)S(1)}, bf16[128,1408]{1,0:T(8,128)(2,1)S(1)}, u32[]{:S(2)}, u32[]{:S(2)}) collective-permute-start(bf16[128,1408]{1,0:T(8,128)(2,1)S(1)} %get-tuple-element.48), channel_id=1, source_target_pairs={{0,66},{1,67},{2,64},{3,65},{4,70},{5,71},{6,68},{7,69},{8,74},{9,... | collective-permute-start | bytes 1081352 | tf_op jit(solution)/shard_map/ppermute | solution.py:83
  16.9 3.2 %collective-permute-start.14 = (bf16[256,1408]{1,0:T(8,128)(2,1)S(1)}, bf16[256,1408]{1,0:T(8,128)(2,1)S(1)}, u32[]{:S(2)}, u32[]{:S(2)}) collective-permute-start(bf16[256,1408]{1,0:T(8,128)(2,1)S(1)} %pad_maximum_fusion.18), channel_id=1, source_target_pairs={{0,66},{1,67},{2,64},{3,65},{4,70},{5,71},{6,68},{7,69},{8,74},{9,... | collective-permute-start | bytes 2162696 | tf_op jit(solution)/shard_map/ppermute | solution.py:83
  20.6 2.4 %collective-permute-start.13 = (bf16[256,1408]{1,0:T(8,128)(2,1)S(1)}, bf16[256,1408]{1,0:T(8,128)(2,1)S(1)}, u32[]{:S(2)}, u32[]{:S(2)}) collective-permute-start(bf16[256,1408]{1,0:T(8,128)(2,1)S(1)} %pad_maximum_fusion.17), channel_id=1, source_target_pairs={{0,48},{1,49},{2,50},{3,51},{4,52},{5,53},{6,54},{7,55},{8,56},{9,... | collective-permute-start | bytes 2162696 | tf_op jit(solution)/shard_map/ppermute | solution.py:83
  23.0 1.6 %collective-permute-done.9 = bf16[128,1408]{1,0:T(8,128)(2,1)S(1)} collective-permute-done((bf16[128,1408]{1,0:T(8,128)(2,1)S(1)}, bf16[128,1408]{1,0:T(8,128)(2,1)S(1)}, u32[]{:S(2)}, u32[]{:S(2)}) %collective-permute-start.9) | collective-permute-done | bytes 360480 | tf_op jit(solution)/shard_map/ppermute | solution.py:83
  24.7 2.5 %collective-permute-start.10 = (bf16[256,1408]{1,0:T(8,128)(2,1)S(1)}, bf16[256,1408]{1,0:T(8,128)(2,1)S(1)}, u32[]{:S(2)}, u32[]{:S(2)}) collective-permute-start(bf16[256,1408]{1,0:T(8,128)(2,1)S(1)} %pad_maximum_fusion.16), channel_id=1, source_target_pairs={{0,12},{1,13},{2,14},{3,15},{4,8},{5,9},{6,10},{7,11},{8,4},{9,5},... | collective-permute-start | bytes 2162696 | tf_op jit(solution)/shard_map/ppermute | solution.py:83
  27.2 1.2 collective-permute-done.1
  29.3 1.8 %collective-permute-start.3 = (bf16[256,2176]{1,0:T(8,128)(2,1)S(1)}, bf16[256,2176]{1,0:T(8,128)(2,1)S(1)}, u32[]{:S(2)}, u32[]{:S(2)}) collective-permute-start(bf16[256,2176]{1,0:T(8,128)(2,1)S(1)} %pad_maximum_fusion.5), channel_id=1, source_target_pairs={{0,16},{1,17},{2,18},{3,19},{4,20},{5,21},{6,22},{7,23},{8,24},{9,... | collective-permute-start | bytes 3342344 | tf_op jit(solution)/shard_map/ppermute | solution.py:83
  31.1 7.6 %collective-permute-done.14 = bf16[256,1408]{1,0:T(8,128)(2,1)S(1)} collective-permute-done((bf16[256,1408]{1,0:T(8,128)(2,1)S(1)}, bf16[256,1408]{1,0:T(8,128)(2,1)S(1)}, u32[]{:S(2)}, u32[]{:S(2)}) %collective-permute-start.14) | collective-permute-done | bytes 720928 | tf_op jit(solution)/shard_map/ppermute | solution.py:83
  38.8 1.1 collective-permute-start.16
  40.1 3.0 %collective-permute-start.15 = (bf16[512,1408]{1,0:T(8,128)(2,1)S(1)}, bf16[512,1408]{1,0:T(8,128)(2,1)S(1)}, u32[]{:S(2)}, u32[]{:S(2)}) collective-permute-start(bf16[512,1408]{1,0:T(8,128)(2,1)S(1)} %pad_maximum_fusion.3), channel_id=1, source_target_pairs={{0,66},{1,67},{2,64},{3,65},{4,70},{5,71},{6,68},{7,69},{8,74},{9,... | collective-permute-start | bytes 4325384 | tf_op jit(solution)/shard_map/ppermute | solution.py:83
  43.9 2.2 %collective-permute-start.11 = (bf16[512,1408]{1,0:T(8,128)(2,1)S(1)}, bf16[512,1408]{1,0:T(8,128)(2,1)S(1)}, u32[]{:S(2)}, u32[]{:S(2)}) collective-permute-start(bf16[512,1408]{1,0:T(8,128)(2,1)S(1)} %pad_maximum_fusion.2), channel_id=1, source_target_pairs={{0,48},{1,49},{2,50},{3,51},{4,52},{5,53},{6,54},{7,55},{8,56},{9,... | collective-permute-start | bytes 4325384 | tf_op jit(solution)/shard_map/ppermute | solution.py:83
  46.2 5.7 %collective-permute-done.4 = bf16[256,2048]{1,0:T(8,128)(2,1)S(1)} collective-permute-done((bf16[256,2048]{1,0:T(8,128)(2,1)S(1)}, bf16[256,2048]{1,0:T(8,128)(2,1)S(1)}, u32[]{:S(2)}, u32[]{:S(2)}) %collective-permute-start.4) | collective-permute-done | bytes 1048608 | tf_op jit(solution)/shard_map/ppermute | solution.py:83
  52.3 1.6 %collective-permute-done.3 = bf16[256,2176]{1,0:T(8,128)(2,1)S(1)} collective-permute-done((bf16[256,2176]{1,0:T(8,128)(2,1)S(1)}, bf16[256,2176]{1,0:T(8,128)(2,1)S(1)}, u32[]{:S(2)}, u32[]{:S(2)}) %collective-permute-start.3) | collective-permute-done | bytes 1114144 | tf_op jit(solution)/shard_map/ppermute | solution.py:83
  54.1 1.5 %collective-permute-start.5 = (bf16[512,2176]{1,0:T(8,128)(2,1)S(1)}, bf16[512,2176]{1,0:T(8,128)(2,1)S(1)}, u32[]{:S(2)}, u32[]{:S(2)}) collective-permute-start(bf16[512,2176]{1,0:T(8,128)(2,1)S(1)} %pad_maximum_fusion), channel_id=1, source_target_pairs={{0,64},{1,65},{2,66},{3,67},{4,68},{5,69},{6,70},{7,71},{8,72},{9,... | collective-permute-start | bytes 6684680 | tf_op jit(solution)/shard_map/ppermute | solution.py:83
  55.8 0.9 fusion.26
  56.7 19.2 %collective-permute-done.11 = bf16[512,1408]{1,0:T(8,128)(2,1)S(1)} collective-permute-done((bf16[512,1408]{1,0:T(8,128)(2,1)S(1)}, bf16[512,1408]{1,0:T(8,128)(2,1)S(1)}, u32[]{:S(2)}, u32[]{:S(2)}) %collective-permute-start.11) | collective-permute-done | bytes 1441824 | tf_op jit(solution)/shard_map/ppermute | solution.py:83
  77.7 19.5 %collective-permute-done.6 = bf16[512,2048]{1,0:T(8,128)(2,1)S(1)} collective-permute-done((bf16[512,2048]{1,0:T(8,128)(2,1)S(1)}, bf16[512,2048]{1,0:T(8,128)(2,1)S(1)}, u32[]{:S(2)}, u32[]{:S(2)}) %collective-permute-start.6) | collective-permute-done | bytes 2097184 | tf_op jit(solution)/shard_map/ppermute | solution.py:83
  97.4 4.6 %collective-permute-done.5 = bf16[512,2176]{1,0:T(8,128)(2,1)S(1)} collective-permute-done((bf16[512,2176]{1,0:T(8,128)(2,1)S(1)}, bf16[512,2176]{1,0:T(8,128)(2,1)S(1)}, u32[]{:S(2)}, u32[]{:S(2)}) %collective-permute-start.5) | collective-permute-done | bytes 2228256 | tf_op jit(solution)/shard_map/ppermute | solution.py:83
  103.1 4.8 %fusion.51 = f32[512,1024]{1,0:T(8,128)S(1)} fusion(bf16[512,4224]{1,0:T(8,128)(2,1)S(1)} %get-tuple-element.32, bf16[1024,4224]{1,0:T(8,128)(2,1)S(1)} %slice_dynamic-update-slice_fusion), kind=kOutput, calls=%fused_computation.159 | convolution fusion | flops 4429185024 | bytes 15073280 | tf_op jit(solution)/shard_map/dot_general | solution.py:139
  108.4 4.8 %fusion.50 = f32[512,1024]{1,0:T(8,128)S(1)} fusion(bf16[512,4224]{1,0:T(8,128)(2,1)S(1)} %get-tuple-element.33, bf16[1024,4224]{1,0:T(8,128)(2,1)S(1)} %slice_dynamic-update-slice_fusion), kind=kOutput, calls=%fused_computation.158 | convolution fusion | flops 4429185024 | bytes 15073280 | tf_op jit(solution)/shard_map/dot_general | solution.py:139
  115.0 0.9 multiply_reduce_fusion
  116.6 1.6 %collective-permute-start.18 = (f32[256,512]{1,0:T(8,128)S(1)}, f32[256,512]{1,0:T(8,128)S(1)}, u32[]{:S(2)}, u32[]{:S(2)}) collective-permute-start(f32[256,512]{1,0:T(8,128)S(1)} %pad_maximum_fusion.28), channel_id=1, source_target_pairs={{0,16},{1,17},{2,18},{3,19},{4,20},{5,21},{6,22},{7,23},{8,24},{9,... | collective-permute-start | bytes 1572872 | tf_op jit(solution)/shard_map/ppermute | solution.py:118
  118.9 4.3 %collective-permute-done.22 = f32[256]{0:T(256)S(1)} collective-permute-done((f32[256]{0:T(256)S(1)}, f32[256]{0:T(256)S(1)}, u32[]{:S(2)}, u32[]{:S(2)}) %collective-permute-start.22) | collective-permute-done | bytes 1056 | tf_op jit(solution)/shard_map/ppermute | solution.py:118
  123.2 7.2 %collective-permute-done.18 = f32[256,512]{1,0:T(8,128)S(1)} collective-permute-done((f32[256,512]{1,0:T(8,128)S(1)}, f32[256,512]{1,0:T(8,128)S(1)}, u32[]{:S(2)}, u32[]{:S(2)}) %collective-permute-start.18) | collective-permute-done | bytes 524320 | tf_op jit(solution)/shard_map/ppermute | solution.py:118
  130.6 1.3 collective-permute-start.19
  132.3 4.3 %collective-permute-done.23 = f32[128]{0:T(128)S(1)} collective-permute-done((f32[128]{0:T(128)S(1)}, f32[128]{0:T(128)S(1)}, u32[]{:S(2)}, u32[]{:S(2)}) %collective-permute-start.23) | collective-permute-done | bytes 544 | tf_op jit(solution)/shard_map/ppermute | solution.py:118
  138.1 0.9 collective-permute-start.20
  139.0 2.5 %collective-permute-done.24 = f32[64]{0:T(128)S(1)} collective-permute-done((f32[64]{0:T(128)S(1)}, f32[64]{0:T(128)S(1)}, u32[]{:S(2)}, u32[]{:S(2)}) %collective-permute-start.24) | collective-permute-done | bytes 288 | tf_op jit(solution)/shard_map/ppermute | solution.py:118
  142.0 1.1 collective-permute-done.20
  (115 shorter events, 17.9 us)
Async XLA Ops:
  2.7 1.2 copy-start
  2.8 1.2 copy-start.1
  3.0 2.0 %collective-permute-start.7 = (bf16[64,4224]{1,0:T(8,128)(2,1)S(1)}, bf16[64,4224]{1,0:T(8,128)(2,1)S(1)}, u32[]{:S(2)}, u32[]{:S(2)}) collective-permute-start(bf16[64,4224]{1,0:T(8,128)(2,1)S(1)} %get-tuple-element.49), channel_id=1, source_target_pairs={{0,1},{1,0},{2,3},{3,2},{4,5},{5,4},{6,7},{7,6},{8,9},{9,8},{10,11... | collective-permute-start | bytes 1622024 | tf_op jit(solution)/shard_map/ppermute | solution.py:96
  4.4 10.7 %collective-permute-start = (bf16[64,4224]{1,0:T(8,128)(2,1)S(1)}, bf16[64,4224]{1,0:T(8,128)(2,1)S(1)}, u32[]{:S(2)}, u32[]{:S(2)}) collective-permute-start(bf16[64,4224]{1,0:T(8,128)(2,1)S(1)} %get-tuple-element.50), channel_id=1, source_target_pairs={{0,1},{1,0},{2,3},{3,2},{4,5},{5,4},{6,7},{7,6},{8,9},{9,8},{10,11... | collective-permute-start | bytes 1622024 | tf_op jit(solution)/shard_map/ppermute | solution.py:96
  5.1 11.7 %collective-permute-start.8 = (bf16[128,1408]{1,0:T(8,128)(2,1)S(1)}, bf16[128,1408]{1,0:T(8,128)(2,1)S(1)}, u32[]{:S(2)}, u32[]{:S(2)}) collective-permute-start(bf16[128,1408]{1,0:T(8,128)(2,1)S(1)} %get-tuple-element.46), channel_id=1, source_target_pairs={{0,48},{1,49},{2,50},{3,51},{4,52},{5,53},{6,54},{7,55},{8,56},{9,... | collective-permute-start | bytes 1081352 | tf_op jit(solution)/shard_map/ppermute | solution.py:83
  8.0 12.5 %collective-permute-start.12 = (bf16[128,1408]{1,0:T(8,128)(2,1)S(1)}, bf16[128,1408]{1,0:T(8,128)(2,1)S(1)}, u32[]{:S(2)}, u32[]{:S(2)}) collective-permute-start(bf16[128,1408]{1,0:T(8,128)(2,1)S(1)} %get-tuple-element.47), channel_id=1, source_target_pairs={{0,12},{1,13},{2,14},{3,15},{4,8},{5,9},{6,10},{7,11},{8,4},{9,5},... | collective-permute-start | bytes 1081352 | tf_op jit(solution)/shard_map/ppermute | solution.py:83
  12.1 12.5 %collective-permute-start.9 = (bf16[128,1408]{1,0:T(8,128)(2,1)S(1)}, bf16[128,1408]{1,0:T(8,128)(2,1)S(1)}, u32[]{:S(2)}, u32[]{:S(2)}) collective-permute-start(bf16[128,1408]{1,0:T(8,128)(2,1)S(1)} %get-tuple-element.48), channel_id=1, source_target_pairs={{0,66},{1,67},{2,64},{3,65},{4,70},{5,71},{6,68},{7,69},{8,74},{9,... | collective-permute-start | bytes 1081352 | tf_op jit(solution)/shard_map/ppermute | solution.py:83
  15.1 13.2 %collective-permute-start.1 = (bf16[128,2048]{1,0:T(8,128)(2,1)S(1)}, bf16[128,2048]{1,0:T(8,128)(2,1)S(1)}, u32[]{:S(2)}, u32[]{:S(2)}) collective-permute-start(bf16[128,2048]{1,0:T(8,128)(2,1)S(1)} %pad_maximum_fusion.27), channel_id=1, source_target_pairs={{0,16},{1,17},{2,18},{3,19},{4,20},{5,21},{6,22},{7,23},{8,24},{9,... | collective-permute-start | bytes 1572872 | tf_op jit(solution)/shard_map/ppermute | solution.py:83
  15.5 13.7 %collective-permute-start.2 = (bf16[128,2176]{1,0:T(8,128)(2,1)S(1)}, bf16[128,2176]{1,0:T(8,128)(2,1)S(1)}, u32[]{:S(2)}, u32[]{:S(2)}) collective-permute-start(bf16[128,2176]{1,0:T(8,128)(2,1)S(1)} %pad_maximum_fusion.19), channel_id=1, source_target_pairs={{0,4},{1,5},{2,6},{3,7},{4,0},{5,1},{6,2},{7,3},{8,12},{9,13},{10,... | collective-permute-start | bytes 1671176 | tf_op jit(solution)/shard_map/ppermute | solution.py:83
  16.9 21.8 %collective-permute-start.14 = (bf16[256,1408]{1,0:T(8,128)(2,1)S(1)}, bf16[256,1408]{1,0:T(8,128)(2,1)S(1)}, u32[]{:S(2)}, u32[]{:S(2)}) collective-permute-start(bf16[256,1408]{1,0:T(8,128)(2,1)S(1)} %pad_maximum_fusion.18), channel_id=1, source_target_pairs={{0,66},{1,67},{2,64},{3,65},{4,70},{5,71},{6,68},{7,69},{8,74},{9,... | collective-permute-start | bytes 2162696 | tf_op jit(solution)/shard_map/ppermute | solution.py:83
  20.6 19.4 %collective-permute-start.13 = (bf16[256,1408]{1,0:T(8,128)(2,1)S(1)}, bf16[256,1408]{1,0:T(8,128)(2,1)S(1)}, u32[]{:S(2)}, u32[]{:S(2)}) collective-permute-start(bf16[256,1408]{1,0:T(8,128)(2,1)S(1)} %pad_maximum_fusion.17), channel_id=1, source_target_pairs={{0,48},{1,49},{2,50},{3,51},{4,52},{5,53},{6,54},{7,55},{8,56},{9,... | collective-permute-start | bytes 2162696 | tf_op jit(solution)/shard_map/ppermute | solution.py:83
  24.7 19.1 %collective-permute-start.10 = (bf16[256,1408]{1,0:T(8,128)(2,1)S(1)}, bf16[256,1408]{1,0:T(8,128)(2,1)S(1)}, u32[]{:S(2)}, u32[]{:S(2)}) collective-permute-start(bf16[256,1408]{1,0:T(8,128)(2,1)S(1)} %pad_maximum_fusion.16), channel_id=1, source_target_pairs={{0,12},{1,13},{2,14},{3,15},{4,8},{5,9},{6,10},{7,11},{8,4},{9,5},... | collective-permute-start | bytes 2162696 | tf_op jit(solution)/shard_map/ppermute | solution.py:83
  28.4 23.5 %collective-permute-start.4 = (bf16[256,2048]{1,0:T(8,128)(2,1)S(1)}, bf16[256,2048]{1,0:T(8,128)(2,1)S(1)}, u32[]{:S(2)}, u32[]{:S(2)}) collective-permute-start(bf16[256,2048]{1,0:T(8,128)(2,1)S(1)} %pad_maximum_fusion.15), channel_id=1, source_target_pairs={{0,64},{1,65},{2,66},{3,67},{4,68},{5,69},{6,70},{7,71},{8,72},{9,... | collective-permute-start | bytes 3145736 | tf_op jit(solution)/shard_map/ppermute | solution.py:83
  29.3 24.7 %collective-permute-start.3 = (bf16[256,2176]{1,0:T(8,128)(2,1)S(1)}, bf16[256,2176]{1,0:T(8,128)(2,1)S(1)}, u32[]{:S(2)}, u32[]{:S(2)}) collective-permute-start(bf16[256,2176]{1,0:T(8,128)(2,1)S(1)} %pad_maximum_fusion.5), channel_id=1, source_target_pairs={{0,16},{1,17},{2,18},{3,19},{4,20},{5,21},{6,22},{7,23},{8,24},{9,... | collective-permute-start | bytes 3342344 | tf_op jit(solution)/shard_map/ppermute | solution.py:83
  38.8 37.7 %collective-permute-start.16 = (bf16[512,1408]{1,0:T(8,128)(2,1)S(1)}, bf16[512,1408]{1,0:T(8,128)(2,1)S(1)}, u32[]{:S(2)}, u32[]{:S(2)}) collective-permute-start(bf16[512,1408]{1,0:T(8,128)(2,1)S(1)} %pad_maximum_fusion.4), channel_id=1, source_target_pairs={{0,12},{1,13},{2,14},{3,15},{4,8},{5,9},{6,10},{7,11},{8,4},{9,5},... | collective-permute-start | bytes 4325384 | tf_op jit(solution)/shard_map/ppermute | solution.py:83
  40.1 36.0 %collective-permute-start.15 = (bf16[512,1408]{1,0:T(8,128)(2,1)S(1)}, bf16[512,1408]{1,0:T(8,128)(2,1)S(1)}, u32[]{:S(2)}, u32[]{:S(2)}) collective-permute-start(bf16[512,1408]{1,0:T(8,128)(2,1)S(1)} %pad_maximum_fusion.3), channel_id=1, source_target_pairs={{0,66},{1,67},{2,64},{3,65},{4,70},{5,71},{6,68},{7,69},{8,74},{9,... | collective-permute-start | bytes 4325384 | tf_op jit(solution)/shard_map/ppermute | solution.py:83
  43.9 31.9 %collective-permute-start.11 = (bf16[512,1408]{1,0:T(8,128)(2,1)S(1)}, bf16[512,1408]{1,0:T(8,128)(2,1)S(1)}, u32[]{:S(2)}, u32[]{:S(2)}) collective-permute-start(bf16[512,1408]{1,0:T(8,128)(2,1)S(1)} %pad_maximum_fusion.2), channel_id=1, source_target_pairs={{0,48},{1,49},{2,50},{3,51},{4,52},{5,53},{6,54},{7,55},{8,56},{9,... | collective-permute-start | bytes 4325384 | tf_op jit(solution)/shard_map/ppermute | solution.py:83
  52.1 45.1 %collective-permute-start.6 = (bf16[512,2048]{1,0:T(8,128)(2,1)S(1)}, bf16[512,2048]{1,0:T(8,128)(2,1)S(1)}, u32[]{:S(2)}, u32[]{:S(2)}) collective-permute-start(bf16[512,2048]{1,0:T(8,128)(2,1)S(1)} %pad_maximum_fusion.1), channel_id=1, source_target_pairs={{0,4},{1,5},{2,6},{3,7},{4,0},{5,1},{6,2},{7,3},{8,12},{9,13},{10,... | collective-permute-start | bytes 6291464 | tf_op jit(solution)/shard_map/ppermute | solution.py:83
  54.1 47.9 %collective-permute-start.5 = (bf16[512,2176]{1,0:T(8,128)(2,1)S(1)}, bf16[512,2176]{1,0:T(8,128)(2,1)S(1)}, u32[]{:S(2)}, u32[]{:S(2)}) collective-permute-start(bf16[512,2176]{1,0:T(8,128)(2,1)S(1)} %pad_maximum_fusion), channel_id=1, source_target_pairs={{0,64},{1,65},{2,66},{3,67},{4,68},{5,69},{6,70},{7,71},{8,72},{9,... | collective-permute-start | bytes 6684680 | tf_op jit(solution)/shard_map/ppermute | solution.py:83
  77.6 24.6 %slice-start = ((s8[4325376]{0:T(1024)(128)(4,1)}), s8[4194304]{0:T(1024)(128)(4,1)S(1)}, s32[]{:S(2)}) async-start(s8[4325376]{0:T(1024)(128)(4,1)} %bitcast.6), calls=%async_computation | async-start | bytes 8388608
  77.7 24.5 %slice-start.1 = ((s8[4325376]{0:T(1024)(128)(4,1)}), s8[131072]{0:T(1024)(128)(4,1)S(1)}, s32[]{:S(2)}) async-start(s8[4325376]{0:T(1024)(128)(4,1)} %bitcast.6), calls=%async_computation.1 | async-start | bytes 262144
  107.9 5.7 %collective-permute-start.17 = (f32[512,1024]{1,0:T(8,128)S(1)}, f32[512,1024]{1,0:T(8,128)S(1)}, u32[]{:S(2)}, u32[]{:S(2)}) collective-permute-start(f32[512,1024]{1,0:T(8,128)S(1)} %fusion.51), channel_id=1, source_target_pairs={{0,1},{1,0},{2,3},{3,2},{4,5},{5,4},{6,7},{7,6},{8,9},{9,8},{10,11... | collective-permute-start | bytes 6291464 | tf_op jit(solution)/shard_map/ppermute | solution.py:143
  115.9 2.3 %collective-permute-start.21 = (f32[512]{0:T(512)S(1)}, f32[512]{0:T(512)S(1)}, u32[]{:S(2)}, u32[]{:S(2)}) collective-permute-start(f32[512]{0:T(512)S(1)} %slice.414), channel_id=1, source_target_pairs={{0,1},{1,0},{2,3},{3,2},{4,5},{5,4},{6,7},{7,6},{8,9},{9,8},{10,11... | collective-permute-start | bytes 6152 | tf_op jit(solution)/shard_map/ppermute | solution.py:159
  116.6 13.9 %collective-permute-start.18 = (f32[256,512]{1,0:T(8,128)S(1)}, f32[256,512]{1,0:T(8,128)S(1)}, u32[]{:S(2)}, u32[]{:S(2)}) collective-permute-start(f32[256,512]{1,0:T(8,128)S(1)} %pad_maximum_fusion.28), channel_id=1, source_target_pairs={{0,16},{1,17},{2,18},{3,19},{4,20},{5,21},{6,22},{7,23},{8,24},{9,... | collective-permute-start | bytes 1572872 | tf_op jit(solution)/shard_map/ppermute | solution.py:118
  118.4 4.8 %collective-permute-start.22 = (f32[256]{0:T(256)S(1)}, f32[256]{0:T(256)S(1)}, u32[]{:S(2)}, u32[]{:S(2)}) collective-permute-start(f32[256]{0:T(256)S(1)} %pad_maximum_fusion.31), channel_id=1, source_target_pairs={{0,48},{1,49},{2,50},{3,51},{4,52},{5,53},{6,54},{7,55},{8,56},{9,... | collective-permute-start | bytes 3080 | tf_op jit(solution)/shard_map/ppermute | solution.py:118
  130.6 7.5 %collective-permute-start.19 = (f32[128,512]{1,0:T(8,128)S(1)}, f32[128,512]{1,0:T(8,128)S(1)}, u32[]{:S(2)}, u32[]{:S(2)}) collective-permute-start(f32[128,512]{1,0:T(8,128)S(1)} %pad_maximum_fusion.30), channel_id=1, source_target_pairs={{0,64},{1,65},{2,66},{3,67},{4,68},{5,69},{6,70},{7,71},{8,72},{9,... | collective-permute-start | bytes 786440 | tf_op jit(solution)/shard_map/ppermute | solution.py:118
  131.9 4.8 %collective-permute-start.23 = (f32[128]{0:T(128)S(1)}, f32[128]{0:T(128)S(1)}, u32[]{:S(2)}, u32[]{:S(2)}) collective-permute-start(f32[128]{0:T(128)S(1)} %pad_maximum_fusion.32), channel_id=1, source_target_pairs={{0,66},{1,67},{2,64},{3,65},{4,70},{5,71},{6,68},{7,69},{8,74},{9,... | collective-permute-start | bytes 1544 | tf_op jit(solution)/shard_map/ppermute | solution.py:118
  136.7 4.8 %collective-permute-start.24 = (f32[64]{0:T(128)S(1)}, f32[64]{0:T(128)S(1)}, u32[]{:S(2)}, u32[]{:S(2)}) collective-permute-start(f32[64]{0:T(128)S(1)} %slice_add_fusion.7), channel_id=1, source_target_pairs={{0,12},{1,13},{2,14},{3,15},{4,8},{5,9},{6,10},{7,11},{8,4},{9,5},... | collective-permute-start | bytes 776 | tf_op jit(solution)/shard_map/ppermute | solution.py:118
  138.1 5.0 %collective-permute-start.20 = (f32[64,512]{1,0:T(8,128)S(1)}, f32[64,512]{1,0:T(8,128)S(1)}, u32[]{:S(2)}, u32[]{:S(2)}) collective-permute-start(f32[64,512]{1,0:T(8,128)S(1)} %slice_add_fusion), channel_id=1, source_target_pairs={{0,4},{1,5},{2,6},{3,7},{4,0},{5,1},{6,2},{7,3},{8,12},{9,13},{10,... | collective-permute-start | bytes 393224 | tf_op jit(solution)/shard_map/ppermute | solution.py:118

commit v16 on v15

--- a/solution.py
+++ b/solution.py
@@ -108,18 +108,38 @@
     )
 
 
+HALVE = ((0, 1, 2), (1, 2, 0))
+
+
+def halve_pairs(n, step, mate):
+    out = []
+    for L in range(n):
+        v, c = coords(L)
+        a = HALVE[c][step]
+        w = list(v)
+        w[a] = mate(v[a])
+        out.append((L, lin(w, c)))
+    return out
+
+
 def cube_reduce(blocks, mate, n):
-    blocks = list(blocks)
+    def phys(q, order):
+        return sum(((q >> s) & 1) << order[s] for s in range(3))
+
+    stacked = jnp.stack(blocks)
+    c = lax.axis_index(AXES) % 2
+    stacked = jnp.where(c == 0, stacked, stacked[jnp.array([phys(q, HALVE[1]) for q in range(8)])])
+    blocks = [stacked[q] for q in range(8)]
     live = list(range(8))
-    for a in range(3):
-        send = [o for o in live if o & (1 << a)]
-        keep = [o for o in live if not o & (1 << a)]
+    for step in range(3):
+        send = [q for q in live if q & (1 << step)]
+        keep = [q for q in live if not q & (1 << step)]
         rows = blocks[0].shape[0]
         got = lax.ppermute(
-            jnp.concatenate([blocks[o] for o in send]), AXES, mate_pairs(n, a, mate)
+            jnp.concatenate([blocks[q] for q in send]), AXES, halve_pairs(n, step, mate)
         )
-        for i, o in enumerate(send):
-            blocks[o ^ (1 << a)] = blocks[o ^ (1 << a)] + got[i * rows:(i + 1) * rows]
+        for i, q in enumerate(send):
+            blocks[q ^ (1 << step)] = blocks[q ^ (1 << step)] + got[i * rows:(i + 1) * rows]
         live = keep
     return blocks[0]
 

time: 144 us -> 148 us (1.028)
  matrix products: 11.2 us -> 16.3 us
  waiting for transfers between devices: 83.5 us -> 78.4 us
  other arithmetic: 7.43 us -> 10.5 us
    ppermute x6, waiting for transfers between devices: 19.9 us -> 14.8 us  [cube_reduce(): lax.ppermute(jnp.concatenate([blocks[q] for q in send]), AXES, halve_pair...]
    dot_general x2, matrix products: 9.57 us -> 14.7 us  [partial(): lax.dot_general(t, te_all, (((1,), (1,)), ((), ())), preferred_element_ty...]
    add x2, other arithmetic: 0.65 us -> 2.66 us  [join_class(): return hi * 32 + lo]
  transfers between devices with their start and end apart: 25 -> 25, of which waited for: 19 -> 18; matrix products, arithmetic and copies ran while one was open for 8% -> 14% of each run, Pallas kernels for 0% -> 0%
where the time goes in v16:
time: 148 us
  waiting for transfers between devices  78.4 us (53%)
  starting transfers between devices  34.2 us (23%)
  matrix products  16.3 us (11%)
  other arithmetic  10.5 us (7%)
  local copies, waits for them, and re-layouts  6.83 us (5%)
    ppermute x15, waiting for transfers between devices, chain(): got = lax.ppermute(buf, AXES, mate_pairs(n, a, mate))  63.1 us
    ppermute x15, starting transfers between devices, chain(): got = lax.ppermute(buf, AXES, mate_pairs(n, a, mate))  28.4 us
    ppermute x6, waiting for transfers between devices, cube_reduce(): lax.ppermute(jnp.concatenate([blocks[q] for q in send]), AXES, halve_pair...  14.8 us
    dot_general x2, matrix products, partial(): lax.dot_general(t, te_all, (((1,), (1,)), ((), ())), preferred_element_ty...  14.7 us
    ppermute x6, starting transfers between devices, cube_reduce(): lax.ppermute(jnp.concatenate([blocks[q] for q in send]), AXES, halve_pair...  5.05 us
  transfers between devices with their start and end apart: 25, of which 18 were waited for; matrix products, arithmetic and copies ran while one was open for 14% of the time, Pallas kernels for 0%

profile of v16, /device:TPU:0, one launch (start us, length us, event | category | flops | bytes accessed | tf_op | source)
XLA Modules:
  0.0 147.6 jit_solution(2403636835293191879)
XLA Ops:
  0.7 1.3 fusion.53
  5.1 2.9 %collective-permute-start.8 = (bf16[128,1408]{1,0:T(8,128)(2,1)S(1)}, bf16[128,1408]{1,0:T(8,128)(2,1)S(1)}, u32[]{:S(2)}, u32[]{:S(2)}) collective-permute-start(bf16[128,1408]{1,0:T(8,128)(2,1)S(1)} %get-tuple-element.46), channel_id=1, source_target_pairs={{0,48},{1,49},{2,50},{3,51},{4,52},{5,53},{6,54},{7,55},{8,56},{9,... | collective-permute-start | bytes 1081352 | tf_op jit(solution)/shard_map/ppermute | solution.py:83
  8.0 4.0 %collective-permute-start.12 = (bf16[128,1408]{1,0:T(8,128)(2,1)S(1)}, bf16[128,1408]{1,0:T(8,128)(2,1)S(1)}, u32[]{:S(2)}, u32[]{:S(2)}) collective-permute-start(bf16[128,1408]{1,0:T(8,128)(2,1)S(1)} %get-tuple-element.47), channel_id=1, source_target_pairs={{0,12},{1,13},{2,14},{3,15},{4,8},{5,9},{6,10},{7,11},{8,4},{9,5},... | collective-permute-start | bytes 1081352 | tf_op jit(solution)/shard_map/ppermute | solution.py:83
  12.1 3.0 %collective-permute-start.9 = (bf16[128,1408]{1,0:T(8,128)(2,1)S(1)}, bf16[128,1408]{1,0:T(8,128)(2,1)S(1)}, u32[]{:S(2)}, u32[]{:S(2)}) collective-permute-start(bf16[128,1408]{1,0:T(8,128)(2,1)S(1)} %get-tuple-element.48), channel_id=1, source_target_pairs={{0,66},{1,67},{2,64},{3,65},{4,70},{5,71},{6,68},{7,69},{8,74},{9,... | collective-permute-start | bytes 1081352 | tf_op jit(solution)/shard_map/ppermute | solution.py:83
  16.9 3.2 %collective-permute-start.14 = (bf16[256,1408]{1,0:T(8,128)(2,1)S(1)}, bf16[256,1408]{1,0:T(8,128)(2,1)S(1)}, u32[]{:S(2)}, u32[]{:S(2)}) collective-permute-start(bf16[256,1408]{1,0:T(8,128)(2,1)S(1)} %pad_maximum_fusion.18), channel_id=1, source_target_pairs={{0,66},{1,67},{2,64},{3,65},{4,70},{5,71},{6,68},{7,69},{8,74},{9,... | collective-permute-start | bytes 2162696 | tf_op jit(solution)/shard_map/ppermute | solution.py:83
  20.6 2.4 %collective-permute-start.13 = (bf16[256,1408]{1,0:T(8,128)(2,1)S(1)}, bf16[256,1408]{1,0:T(8,128)(2,1)S(1)}, u32[]{:S(2)}, u32[]{:S(2)}) collective-permute-start(bf16[256,1408]{1,0:T(8,128)(2,1)S(1)} %pad_maximum_fusion.17), channel_id=1, source_target_pairs={{0,48},{1,49},{2,50},{3,51},{4,52},{5,53},{6,54},{7,55},{8,56},{9,... | collective-permute-start | bytes 2162696 | tf_op jit(solution)/shard_map/ppermute | solution.py:83
  23.0 1.6 %collective-permute-done.9 = bf16[128,1408]{1,0:T(8,128)(2,1)S(1)} collective-permute-done((bf16[128,1408]{1,0:T(8,128)(2,1)S(1)}, bf16[128,1408]{1,0:T(8,128)(2,1)S(1)}, u32[]{:S(2)}, u32[]{:S(2)}) %collective-permute-start.9) | collective-permute-done | bytes 360480 | tf_op jit(solution)/shard_map/ppermute | solution.py:83
  24.7 2.5 %collective-permute-start.10 = (bf16[256,1408]{1,0:T(8,128)(2,1)S(1)}, bf16[256,1408]{1,0:T(8,128)(2,1)S(1)}, u32[]{:S(2)}, u32[]{:S(2)}) collective-permute-start(bf16[256,1408]{1,0:T(8,128)(2,1)S(1)} %pad_maximum_fusion.16), channel_id=1, source_target_pairs={{0,12},{1,13},{2,14},{3,15},{4,8},{5,9},{6,10},{7,11},{8,4},{9,5},... | collective-permute-start | bytes 2162696 | tf_op jit(solution)/shard_map/ppermute | solution.py:83
  27.2 1.2 collective-permute-done.1
  29.3 1.8 %collective-permute-start.3 = (bf16[256,2176]{1,0:T(8,128)(2,1)S(1)}, bf16[256,2176]{1,0:T(8,128)(2,1)S(1)}, u32[]{:S(2)}, u32[]{:S(2)}) collective-permute-start(bf16[256,2176]{1,0:T(8,128)(2,1)S(1)} %pad_maximum_fusion.5), channel_id=1, source_target_pairs={{0,16},{1,17},{2,18},{3,19},{4,20},{5,21},{6,22},{7,23},{8,24},{9,... | collective-permute-start | bytes 3342344 | tf_op jit(solution)/shard_map/ppermute | solution.py:83
  31.1 7.6 %collective-permute-done.14 = bf16[256,1408]{1,0:T(8,128)(2,1)S(1)} collective-permute-done((bf16[256,1408]{1,0:T(8,128)(2,1)S(1)}, bf16[256,1408]{1,0:T(8,128)(2,1)S(1)}, u32[]{:S(2)}, u32[]{:S(2)}) %collective-permute-start.14) | collective-permute-done | bytes 720928 | tf_op jit(solution)/shard_map/ppermute | solution.py:83
  38.8 1.1 collective-permute-start.16
  40.0 3.0 %collective-permute-start.15 = (bf16[512,1408]{1,0:T(8,128)(2,1)S(1)}, bf16[512,1408]{1,0:T(8,128)(2,1)S(1)}, u32[]{:S(2)}, u32[]{:S(2)}) collective-permute-start(bf16[512,1408]{1,0:T(8,128)(2,1)S(1)} %pad_maximum_fusion.3), channel_id=1, source_target_pairs={{0,66},{1,67},{2,64},{3,65},{4,70},{5,71},{6,68},{7,69},{8,74},{9,... | collective-permute-start | bytes 4325384 | tf_op jit(solution)/shard_map/ppermute | solution.py:83
  43.9 2.2 %collective-permute-start.11 = (bf16[512,1408]{1,0:T(8,128)(2,1)S(1)}, bf16[512,1408]{1,0:T(8,128)(2,1)S(1)}, u32[]{:S(2)}, u32[]{:S(2)}) collective-permute-start(bf16[512,1408]{1,0:T(8,128)(2,1)S(1)} %pad_maximum_fusion.2), channel_id=1, source_target_pairs={{0,48},{1,49},{2,50},{3,51},{4,52},{5,53},{6,54},{7,55},{8,56},{9,... | collective-permute-start | bytes 4325384 | tf_op jit(solution)/shard_map/ppermute | solution.py:83
  46.2 5.7 %collective-permute-done.4 = bf16[256,2048]{1,0:T(8,128)(2,1)S(1)} collective-permute-done((bf16[256,2048]{1,0:T(8,128)(2,1)S(1)}, bf16[256,2048]{1,0:T(8,128)(2,1)S(1)}, u32[]{:S(2)}, u32[]{:S(2)}) %collective-permute-start.4) | collective-permute-done | bytes 1048608 | tf_op jit(solution)/shard_map/ppermute | solution.py:83
  52.4 1.6 %collective-permute-done.3 = bf16[256,2176]{1,0:T(8,128)(2,1)S(1)} collective-permute-done((bf16[256,2176]{1,0:T(8,128)(2,1)S(1)}, bf16[256,2176]{1,0:T(8,128)(2,1)S(1)}, u32[]{:S(2)}, u32[]{:S(2)}) %collective-permute-start.3) | collective-permute-done | bytes 1114144 | tf_op jit(solution)/shard_map/ppermute | solution.py:83
  54.2 1.5 %collective-permute-start.5 = (bf16[512,2176]{1,0:T(8,128)(2,1)S(1)}, bf16[512,2176]{1,0:T(8,128)(2,1)S(1)}, u32[]{:S(2)}, u32[]{:S(2)}) collective-permute-start(bf16[512,2176]{1,0:T(8,128)(2,1)S(1)} %pad_maximum_fusion), channel_id=1, source_target_pairs={{0,64},{1,65},{2,66},{3,67},{4,68},{5,69},{6,70},{7,71},{8,72},{9,... | collective-permute-start | bytes 6684680 | tf_op jit(solution)/shard_map/ppermute | solution.py:83
  56.6 19.2 %collective-permute-done.11 = bf16[512,1408]{1,0:T(8,128)(2,1)S(1)} collective-permute-done((bf16[512,1408]{1,0:T(8,128)(2,1)S(1)}, bf16[512,1408]{1,0:T(8,128)(2,1)S(1)}, u32[]{:S(2)}, u32[]{:S(2)}) %collective-permute-start.11) | collective-permute-done | bytes 1441824 | tf_op jit(solution)/shard_map/ppermute | solution.py:83
  77.7 19.6 %collective-permute-done.6 = bf16[512,2048]{1,0:T(8,128)(2,1)S(1)} collective-permute-done((bf16[512,2048]{1,0:T(8,128)(2,1)S(1)}, bf16[512,2048]{1,0:T(8,128)(2,1)S(1)}, u32[]{:S(2)}, u32[]{:S(2)}) %collective-permute-start.6) | collective-permute-done | bytes 2097184 | tf_op jit(solution)/shard_map/ppermute | solution.py:83
  97.5 4.5 %collective-permute-done.5 = bf16[512,2176]{1,0:T(8,128)(2,1)S(1)} collective-permute-done((bf16[512,2176]{1,0:T(8,128)(2,1)S(1)}, bf16[512,2176]{1,0:T(8,128)(2,1)S(1)}, u32[]{:S(2)}, u32[]{:S(2)}) %collective-permute-start.5) | collective-permute-done | bytes 2228256 | tf_op jit(solution)/shard_map/ppermute | solution.py:83
  103.1 6.1 %fusion.60 = f32[512,1024]{1,0:T(8,128)} fusion(bf16[512,4224]{1,0:T(8,128)(2,1)S(1)} %get-tuple-element.32, bf16[1024,4224]{1,0:T(8,128)(2,1)S(1)} %slice_dynamic-update-slice_fusion), kind=kOutput, calls=%fused_computation.201 | convolution fusion | flops 4429185024 | bytes 15073280 | tf_op jit(solution)/shard_map/dot_general | solution.py:159
  109.2 1.4 add_reduce_fusion
  110.7 8.6 %fusion.59 = f32[512,1024]{1,0:T(8,128)S(1)} fusion(bf16[512,4224]{1,0:T(8,128)(2,1)} %copy-done.1, bf16[1024,4224]{1,0:T(8,128)(2,1)} %copy-done.2), kind=kOutput, calls=%fused_computation.200 | convolution fusion | flops 4429185024 | bytes 15073280 | tf_op jit(solution)/shard_map/dot_general | solution.py:159
  119.2 1.0 convert_reduce_fusion
  120.3 1.2 add_reduce_fusion.1
  122.9 0.9 multiply_reduce_fusion
  125.5 1.7 %collective-permute-start.18 = (f32[256,512]{1,0:T(8,128)S(1)}, f32[256,512]{1,0:T(8,128)S(1)}, u32[]{:S(2)}, u32[]{:S(2)}) collective-permute-start(f32[256,512]{1,0:T(8,128)S(1)} %pad_maximum_fusion.28), channel_id=1, source_target_pairs={{0,16},{1,65},{2,18},{3,67},{4,20},{5,69},{6,22},{7,71},{8,24},{9,... | collective-permute-start | bytes 1572872 | tf_op jit(solution)/shard_map/ppermute | solution.py:138
  128.4 4.3 %collective-permute-done.22 = f32[256]{0:T(256)S(1)} collective-permute-done((f32[256]{0:T(256)S(1)}, f32[256]{0:T(256)S(1)}, u32[]{:S(2)}, u32[]{:S(2)}) %collective-permute-start.22) | collective-permute-done | bytes 1056 | tf_op jit(solution)/shard_map/ppermute | solution.py:138
  132.8 2.0 %collective-permute-done.18 = f32[256,512]{1,0:T(8,128)S(1)} collective-permute-done((f32[256,512]{1,0:T(8,128)S(1)}, f32[256,512]{1,0:T(8,128)S(1)}, u32[]{:S(2)}, u32[]{:S(2)}) %collective-permute-start.18) | collective-permute-done | bytes 524320 | tf_op jit(solution)/shard_map/ppermute | solution.py:138
  134.8 1.3 collective-permute-start.19
  136.6 4.3 %collective-permute-done.23 = f32[128]{0:T(128)S(1)} collective-permute-done((f32[128]{0:T(128)S(1)}, f32[128]{0:T(128)S(1)}, u32[]{:S(2)}, u32[]{:S(2)}) %collective-permute-start.23) | collective-permute-done | bytes 544 | tf_op jit(solution)/shard_map/ppermute | solution.py:138
  142.2 3.5 %collective-permute-done.24 = f32[64]{0:T(128)S(1)} collective-permute-done((f32[64]{0:T(128)S(1)}, f32[64]{0:T(128)S(1)}, u32[]{:S(2)}, u32[]{:S(2)}) %collective-permute-start.24) | collective-permute-done | bytes 288 | tf_op jit(solution)/shard_map/ppermute | solution.py:138
  (136 shorter events, 20.0 us)
Async XLA Ops:
  2.7 1.2 copy-start
  2.8 1.2 copy-start.3
  3.0 2.0 %collective-permute-start.7 = (bf16[64,4224]{1,0:T(8,128)(2,1)S(1)}, bf16[64,4224]{1,0:T(8,128)(2,1)S(1)}, u32[]{:S(2)}, u32[]{:S(2)}) collective-permute-start(bf16[64,4224]{1,0:T(8,128)(2,1)S(1)} %get-tuple-element.49), channel_id=1, source_target_pairs={{0,1},{1,0},{2,3},{3,2},{4,5},{5,4},{6,7},{7,6},{8,9},{9,8},{10,11... | collective-permute-start | bytes 1622024 | tf_op jit(solution)/shard_map/ppermute | solution.py:96
  4.4 10.7 %collective-permute-start = (bf16[64,4224]{1,0:T(8,128)(2,1)S(1)}, bf16[64,4224]{1,0:T(8,128)(2,1)S(1)}, u32[]{:S(2)}, u32[]{:S(2)}) collective-permute-start(bf16[64,4224]{1,0:T(8,128)(2,1)S(1)} %get-tuple-element.50), channel_id=1, source_target_pairs={{0,1},{1,0},{2,3},{3,2},{4,5},{5,4},{6,7},{7,6},{8,9},{9,8},{10,11... | collective-permute-start | bytes 1622024 | tf_op jit(solution)/shard_map/ppermute | solution.py:96
  5.1 11.7 %collective-permute-start.8 = (bf16[128,1408]{1,0:T(8,128)(2,1)S(1)}, bf16[128,1408]{1,0:T(8,128)(2,1)S(1)}, u32[]{:S(2)}, u32[]{:S(2)}) collective-permute-start(bf16[128,1408]{1,0:T(8,128)(2,1)S(1)} %get-tuple-element.46), channel_id=1, source_target_pairs={{0,48},{1,49},{2,50},{3,51},{4,52},{5,53},{6,54},{7,55},{8,56},{9,... | collective-permute-start | bytes 1081352 | tf_op jit(solution)/shard_map/ppermute | solution.py:83
  8.0 12.5 %collective-permute-start.12 = (bf16[128,1408]{1,0:T(8,128)(2,1)S(1)}, bf16[128,1408]{1,0:T(8,128)(2,1)S(1)}, u32[]{:S(2)}, u32[]{:S(2)}) collective-permute-start(bf16[128,1408]{1,0:T(8,128)(2,1)S(1)} %get-tuple-element.47), channel_id=1, source_target_pairs={{0,12},{1,13},{2,14},{3,15},{4,8},{5,9},{6,10},{7,11},{8,4},{9,5},... | collective-permute-start | bytes 1081352 | tf_op jit(solution)/shard_map/ppermute | solution.py:83
  12.1 12.5 %collective-permute-start.9 = (bf16[128,1408]{1,0:T(8,128)(2,1)S(1)}, bf16[128,1408]{1,0:T(8,128)(2,1)S(1)}, u32[]{:S(2)}, u32[]{:S(2)}) collective-permute-start(bf16[128,1408]{1,0:T(8,128)(2,1)S(1)} %get-tuple-element.48), channel_id=1, source_target_pairs={{0,66},{1,67},{2,64},{3,65},{4,70},{5,71},{6,68},{7,69},{8,74},{9,... | collective-permute-start | bytes 1081352 | tf_op jit(solution)/shard_map/ppermute | solution.py:83
  15.1 13.2 %collective-permute-start.1 = (bf16[128,2048]{1,0:T(8,128)(2,1)S(1)}, bf16[128,2048]{1,0:T(8,128)(2,1)S(1)}, u32[]{:S(2)}, u32[]{:S(2)}) collective-permute-start(bf16[128,2048]{1,0:T(8,128)(2,1)S(1)} %pad_maximum_fusion.27), channel_id=1, source_target_pairs={{0,16},{1,17},{2,18},{3,19},{4,20},{5,21},{6,22},{7,23},{8,24},{9,... | collective-permute-start | bytes 1572872 | tf_op jit(solution)/shard_map/ppermute | solution.py:83
  15.5 13.7 %collective-permute-start.2 = (bf16[128,2176]{1,0:T(8,128)(2,1)S(1)}, bf16[128,2176]{1,0:T(8,128)(2,1)S(1)}, u32[]{:S(2)}, u32[]{:S(2)}) collective-permute-start(bf16[128,2176]{1,0:T(8,128)(2,1)S(1)} %pad_maximum_fusion.19), channel_id=1, source_target_pairs={{0,4},{1,5},{2,6},{3,7},{4,0},{5,1},{6,2},{7,3},{8,12},{9,13},{10,... | collective-permute-start | bytes 1671176 | tf_op jit(solution)/shard_map/ppermute | solution.py:83
  16.9 21.8 %collective-permute-start.14 = (bf16[256,1408]{1,0:T(8,128)(2,1)S(1)}, bf16[256,1408]{1,0:T(8,128)(2,1)S(1)}, u32[]{:S(2)}, u32[]{:S(2)}) collective-permute-start(bf16[256,1408]{1,0:T(8,128)(2,1)S(1)} %pad_maximum_fusion.18), channel_id=1, source_target_pairs={{0,66},{1,67},{2,64},{3,65},{4,70},{5,71},{6,68},{7,69},{8,74},{9,... | collective-permute-start | bytes 2162696 | tf_op jit(solution)/shard_map/ppermute | solution.py:83
  20.6 19.4 %collective-permute-start.13 = (bf16[256,1408]{1,0:T(8,128)(2,1)S(1)}, bf16[256,1408]{1,0:T(8,128)(2,1)S(1)}, u32[]{:S(2)}, u32[]{:S(2)}) collective-permute-start(bf16[256,1408]{1,0:T(8,128)(2,1)S(1)} %pad_maximum_fusion.17), channel_id=1, source_target_pairs={{0,48},{1,49},{2,50},{3,51},{4,52},{5,53},{6,54},{7,55},{8,56},{9,... | collective-permute-start | bytes 2162696 | tf_op jit(solution)/shard_map/ppermute | solution.py:83
  24.7 19.1 %collective-permute-start.10 = (bf16[256,1408]{1,0:T(8,128)(2,1)S(1)}, bf16[256,1408]{1,0:T(8,128)(2,1)S(1)}, u32[]{:S(2)}, u32[]{:S(2)}) collective-permute-start(bf16[256,1408]{1,0:T(8,128)(2,1)S(1)} %pad_maximum_fusion.16), channel_id=1, source_target_pairs={{0,12},{1,13},{2,14},{3,15},{4,8},{5,9},{6,10},{7,11},{8,4},{9,5},... | collective-permute-start | bytes 2162696 | tf_op jit(solution)/shard_map/ppermute | solution.py:83
  28.4 23.5 %collective-permute-start.4 = (bf16[256,2048]{1,0:T(8,128)(2,1)S(1)}, bf16[256,2048]{1,0:T(8,128)(2,1)S(1)}, u32[]{:S(2)}, u32[]{:S(2)}) collective-permute-start(bf16[256,2048]{1,0:T(8,128)(2,1)S(1)} %pad_maximum_fusion.15), channel_id=1, source_target_pairs={{0,64},{1,65},{2,66},{3,67},{4,68},{5,69},{6,70},{7,71},{8,72},{9,... | collective-permute-start | bytes 3145736 | tf_op jit(solution)/shard_map/ppermute | solution.py:83
  29.3 24.7 %collective-permute-start.3 = (bf16[256,2176]{1,0:T(8,128)(2,1)S(1)}, bf16[256,2176]{1,0:T(8,128)(2,1)S(1)}, u32[]{:S(2)}, u32[]{:S(2)}) collective-permute-start(bf16[256,2176]{1,0:T(8,128)(2,1)S(1)} %pad_maximum_fusion.5), channel_id=1, source_target_pairs={{0,16},{1,17},{2,18},{3,19},{4,20},{5,21},{6,22},{7,23},{8,24},{9,... | collective-permute-start | bytes 3342344 | tf_op jit(solution)/shard_map/ppermute | solution.py:83
  38.8 37.7 %collective-permute-start.16 = (bf16[512,1408]{1,0:T(8,128)(2,1)S(1)}, bf16[512,1408]{1,0:T(8,128)(2,1)S(1)}, u32[]{:S(2)}, u32[]{:S(2)}) collective-permute-start(bf16[512,1408]{1,0:T(8,128)(2,1)S(1)} %pad_maximum_fusion.4), channel_id=1, source_target_pairs={{0,12},{1,13},{2,14},{3,15},{4,8},{5,9},{6,10},{7,11},{8,4},{9,5},... | collective-permute-start | bytes 4325384 | tf_op jit(solution)/shard_map/ppermute | solution.py:83
  40.0 36.0 %collective-permute-start.15 = (bf16[512,1408]{1,0:T(8,128)(2,1)S(1)}, bf16[512,1408]{1,0:T(8,128)(2,1)S(1)}, u32[]{:S(2)}, u32[]{:S(2)}) collective-permute-start(bf16[512,1408]{1,0:T(8,128)(2,1)S(1)} %pad_maximum_fusion.3), channel_id=1, source_target_pairs={{0,66},{1,67},{2,64},{3,65},{4,70},{5,71},{6,68},{7,69},{8,74},{9,... | collective-permute-start | bytes 4325384 | tf_op jit(solution)/shard_map/ppermute | solution.py:83
  43.9 31.9 %collective-permute-start.11 = (bf16[512,1408]{1,0:T(8,128)(2,1)S(1)}, bf16[512,1408]{1,0:T(8,128)(2,1)S(1)}, u32[]{:S(2)}, u32[]{:S(2)}) collective-permute-start(bf16[512,1408]{1,0:T(8,128)(2,1)S(1)} %pad_maximum_fusion.2), channel_id=1, source_target_pairs={{0,48},{1,49},{2,50},{3,51},{4,52},{5,53},{6,54},{7,55},{8,56},{9,... | collective-permute-start | bytes 4325384 | tf_op jit(solution)/shard_map/ppermute | solution.py:83
  52.2 45.1 %collective-permute-start.6 = (bf16[512,2048]{1,0:T(8,128)(2,1)S(1)}, bf16[512,2048]{1,0:T(8,128)(2,1)S(1)}, u32[]{:S(2)}, u32[]{:S(2)}) collective-permute-start(bf16[512,2048]{1,0:T(8,128)(2,1)S(1)} %pad_maximum_fusion.1), channel_id=1, source_target_pairs={{0,4},{1,5},{2,6},{3,7},{4,0},{5,1},{6,2},{7,3},{8,12},{9,13},{10,... | collective-permute-start | bytes 6291464 | tf_op jit(solution)/shard_map/ppermute | solution.py:83
  54.2 47.9 %collective-permute-start.5 = (bf16[512,2176]{1,0:T(8,128)(2,1)S(1)}, bf16[512,2176]{1,0:T(8,128)(2,1)S(1)}, u32[]{:S(2)}, u32[]{:S(2)}) collective-permute-start(bf16[512,2176]{1,0:T(8,128)(2,1)S(1)} %pad_maximum_fusion), channel_id=1, source_target_pairs={{0,64},{1,65},{2,66},{3,67},{4,68},{5,69},{6,70},{7,71},{8,72},{9,... | collective-permute-start | bytes 6684680 | tf_op jit(solution)/shard_map/ppermute | solution.py:83
  77.6 24.6 %slice-start = ((s8[4325376]{0:T(1024)(128)(4,1)}), s8[4194304]{0:T(1024)(128)(4,1)S(1)}, s32[]{:S(2)}) async-start(s8[4325376]{0:T(1024)(128)(4,1)} %bitcast.100), calls=%async_computation | async-start | bytes 8388608
  77.7 25.4 %copy-start.2 = (bf16[1024,4224]{1,0:T(8,128)(2,1)}, bf16[1024,4224]{1,0:T(8,128)(2,1)S(1)}, u32[]{:S(2)}) copy-start(bf16[1024,4224]{1,0:T(8,128)(2,1)S(1)} %slice_dynamic-update-slice_fusion) | copy-start | bytes 25952260
  77.7 24.5 %slice-start.1 = ((s8[4325376]{0:T(1024)(128)(4,1)}), s8[131072]{0:T(1024)(128)(4,1)S(1)}, s32[]{:S(2)}) async-start(s8[4325376]{0:T(1024)(128)(4,1)} %bitcast.100), calls=%async_computation.1 | async-start | bytes 262144
  103.1 6.1 %copy-start.1 = (bf16[512,4224]{1,0:T(8,128)(2,1)}, bf16[512,4224]{1,0:T(8,128)(2,1)S(1)}, u32[]{:S(2)}) copy-start(bf16[512,4224]{1,0:T(8,128)(2,1)S(1)} %get-tuple-element.33) | copy-start | bytes 12976132
  103.1 6.1 %copy-start.4 = (s32[8]{0:T(128)S(1)}, s32[8]{0:T(128)}, u32[]{:S(2)}) copy-start(s32[8]{0:T(128)} %constant.101) | copy-start | bytes 100
  109.2 12.3 %collective-permute-start.17 = (f32[512,1024]{1,0:T(8,128)}, f32[512,1024]{1,0:T(8,128)S(1)}, u32[]{:S(2)}, u32[]{:S(2)}) collective-permute-start(f32[512,1024]{1,0:T(8,128)} %fusion.60), channel_id=1, source_target_pairs={{0,1},{1,0},{2,3},{3,2},{4,5},{5,4},{6,7},{7,6},{8,9},{9,8},{10,11... | collective-permute-start | bytes 6291464 | tf_op jit(solution)/shard_map/ppermute | solution.py:163
  123.8 3.3 %collective-permute-start.21 = (f32[512]{0:T(512)S(1)}, f32[512]{0:T(512)S(1)}, u32[]{:S(2)}, u32[]{:S(2)}) collective-permute-start(f32[512]{0:T(512)S(1)} %slice.470), channel_id=1, source_target_pairs={{0,1},{1,0},{2,3},{3,2},{4,5},{5,4},{6,7},{7,6},{8,9},{9,8},{10,11... | collective-permute-start | bytes 6152 | tf_op jit(solution)/shard_map/ppermute | solution.py:179
  125.5 9.3 %collective-permute-start.18 = (f32[256,512]{1,0:T(8,128)S(1)}, f32[256,512]{1,0:T(8,128)S(1)}, u32[]{:S(2)}, u32[]{:S(2)}) collective-permute-start(f32[256,512]{1,0:T(8,128)S(1)} %pad_maximum_fusion.28), channel_id=1, source_target_pairs={{0,16},{1,65},{2,18},{3,67},{4,20},{5,69},{6,22},{7,71},{8,24},{9,... | collective-permute-start | bytes 1572872 | tf_op jit(solution)/shard_map/ppermute | solution.py:138
  127.9 4.8 %collective-permute-start.22 = (f32[256]{0:T(256)S(1)}, f32[256]{0:T(256)S(1)}, u32[]{:S(2)}, u32[]{:S(2)}) collective-permute-start(f32[256]{0:T(256)S(1)} %pad_maximum_fusion.31), channel_id=1, source_target_pairs={{0,48},{1,67},{2,50},{3,65},{4,52},{5,71},{6,54},{7,69},{8,56},{9,... | collective-permute-start | bytes 3080 | tf_op jit(solution)/shard_map/ppermute | solution.py:138
  134.8 7.0 %collective-permute-start.19 = (f32[128,512]{1,0:T(8,128)S(1)}, f32[128,512]{1,0:T(8,128)S(1)}, u32[]{:S(2)}, u32[]{:S(2)}) collective-permute-start(f32[128,512]{1,0:T(8,128)S(1)} %pad_maximum_fusion.30), channel_id=1, source_target_pairs={{0,64},{1,5},{2,66},{3,7},{4,68},{5,1},{6,70},{7,3},{8,72},{9,13},... | collective-permute-start | bytes 786440 | tf_op jit(solution)/shard_map/ppermute | solution.py:138
  136.2 4.8 %collective-permute-start.23 = (f32[128]{0:T(128)S(1)}, f32[128]{0:T(128)S(1)}, u32[]{:S(2)}, u32[]{:S(2)}) collective-permute-start(f32[128]{0:T(128)S(1)} %pad_maximum_fusion.32), channel_id=1, source_target_pairs={{0,66},{1,13},{2,64},{3,15},{4,70},{5,9},{6,68},{7,11},{8,74},{9,5... | collective-permute-start | bytes 1544 | tf_op jit(solution)/shard_map/ppermute | solution.py:138
  141.0 4.8 %collective-permute-start.24 = (f32[64]{0:T(128)S(1)}, f32[64]{0:T(128)S(1)}, u32[]{:S(2)}, u32[]{:S(2)}) collective-permute-start(f32[64]{0:T(128)S(1)} %fusion.41), channel_id=1, source_target_pairs={{0,12},{1,49},{2,14},{3,51},{4,8},{5,53},{6,10},{7,55},{8,4},{9,57... | collective-permute-start | bytes 776 | tf_op jit(solution)/shard_map/ppermute | solution.py:138
  141.9 5.0 %collective-permute-start.20 = (f32[64,512]{1,0:T(8,128)S(1)}, f32[64,512]{1,0:T(8,128)S(1)}, u32[]{:S(2)}, u32[]{:S(2)}) collective-permute-start(f32[64,512]{1,0:T(8,128)S(1)} %slice_add_fusion), channel_id=1, source_target_pairs={{0,4},{1,17},{2,6},{3,19},{4,0},{5,21},{6,2},{7,23},{8,12},{9,25},... | collective-permute-start | bytes 393224 | tf_op jit(solution)/shard_map/ppermute | solution.py:138

commit v17 on v16

--- a/solution.py
+++ b/solution.py
@@ -108,6 +108,22 @@
     )
 
 
+def cube_reduce(blocks, mate, n):
+    blocks = list(blocks)
+    live = list(range(8))
+    for a in range(3):
+        send = [o for o in live if o & (1 << a)]
+        keep = [o for o in live if not o & (1 << a)]
+        rows = blocks[0].shape[0]
+        got = lax.ppermute(
+            jnp.concatenate([blocks[o] for o in send]), AXES, mate_pairs(n, a, mate)
+        )
+        for i, o in enumerate(send):
+            blocks[o ^ (1 << a)] = blocks[o ^ (1 << a)] + got[i * rows:(i + 1) * rows]
+        live = keep
+    return blocks[0]
+
+
 HALVE = ((0, 1, 2), (1, 2, 0))
 
 
@@ -122,14 +138,12 @@
     return out
 
 
-def cube_reduce(blocks, mate, n):
+def cube_reduce_split(blocks, mate, n):
     def phys(q, order):
         return sum(((q >> s) & 1) << order[s] for s in range(3))
 
-    stacked = jnp.stack(blocks)
     c = lax.axis_index(AXES) % 2
-    stacked = jnp.where(c == 0, stacked, stacked[jnp.array([phys(q, HALVE[1]) for q in range(8)])])
-    blocks = [stacked[q] for q in range(8)]
+    blocks = [jnp.where(c == 0, blocks[phys(q, HALVE[0])], blocks[phys(q, HALVE[1])]) for q in range(8)]
     live = list(range(8))
     for step in range(3):
         send = [q for q in live if q & (1 << step)]
@@ -173,7 +187,7 @@
         w, train_hot, (((0,), (0,)), ((), ())), preferred_element_type=jnp.float32
     )
     tp = jnp.sum(per_class * test_hot.astype(jnp.float32), axis=1)
-    train_attr = cube_reduce(
+    train_attr = cube_reduce_split(
         [part[o * rows:(o + 1) * rows] for o in range(8)], train_mate, n
     )
     test_part = tp[:half] + lax.ppermute(tp[half:], AXES, core_pairs(n))

time: 148 us -> 147 us (level)
  transfers between devices with their start and end apart: 25 -> 25, of which waited for: 18 -> 18; matrix products, arithmetic and copies ran while one was open for 14% -> 13% of each run, Pallas kernels for 0% -> 0%
where the time goes in v17:
time: 147 us
  waiting for transfers between devices  79 us (54%)
  starting transfers between devices  34.2 us (23%)
  matrix products  16.3 us (11%)
  other arithmetic  10.3 us (7%)
  local copies, waits for them, and re-layouts  5.49 us (4%)
    ppermute x15, waiting for transfers between devices, chain(): got = lax.ppermute(buf, AXES, mate_pairs(n, a, mate))  63.1 us
    ppermute x15, starting transfers between devices, chain(): got = lax.ppermute(buf, AXES, mate_pairs(n, a, mate))  28.4 us
    dot_general x2, matrix products, partial(): lax.dot_general(t, te_all, (((1,), (1,)), ((), ())), preferred_element_ty...  14.6 us
    ppermute x3, waiting for transfers between devices, cube_reduce(): lax.ppermute(jnp.concatenate([blocks[o] for o in send]), AXES, mate_pairs...  12.1 us
    ppermute x3, waiting for transfers between devices, cube_reduce_split(): lax.ppermute(jnp.concatenate([blocks[q] for q in send]), AXES, halve_pair...  3.27 us
    ppermute x3, starting transfers between devices, cube_reduce_split(): lax.ppermute(jnp.concatenate([blocks[q] for q in send]), AXES, halve_pair...  3.26 us
  transfers between devices with their start and end apart: 25, of which 18 were waited for; matrix products, arithmetic and copies ran while one was open for 13% of the time, Pallas kernels for 0%

profile of v17, /device:TPU:0, one launch (start us, length us, event | category | flops | bytes accessed | tf_op | source)
XLA Modules:
  0.0 146.7 jit_solution(7951021404039392499)
XLA Ops:
  0.7 1.3 fusion.42
  5.1 2.9 %collective-permute-start.8 = (bf16[128,1408]{1,0:T(8,128)(2,1)S(1)}, bf16[128,1408]{1,0:T(8,128)(2,1)S(1)}, u32[]{:S(2)}, u32[]{:S(2)}) collective-permute-start(bf16[128,1408]{1,0:T(8,128)(2,1)S(1)} %get-tuple-element.46), channel_id=1, source_target_pairs={{0,48},{1,49},{2,50},{3,51},{4,52},{5,53},{6,54},{7,55},{8,56},{9,... | collective-permute-start | bytes 1081352 | tf_op jit(solution)/shard_map/ppermute | solution.py:83
  8.0 4.0 %collective-permute-start.12 = (bf16[128,1408]{1,0:T(8,128)(2,1)S(1)}, bf16[128,1408]{1,0:T(8,128)(2,1)S(1)}, u32[]{:S(2)}, u32[]{:S(2)}) collective-permute-start(bf16[128,1408]{1,0:T(8,128)(2,1)S(1)} %get-tuple-element.47), channel_id=1, source_target_pairs={{0,12},{1,13},{2,14},{3,15},{4,8},{5,9},{6,10},{7,11},{8,4},{9,5},... | collective-permute-start | bytes 1081352 | tf_op jit(solution)/shard_map/ppermute | solution.py:83
  12.1 3.0 %collective-permute-start.9 = (bf16[128,1408]{1,0:T(8,128)(2,1)S(1)}, bf16[128,1408]{1,0:T(8,128)(2,1)S(1)}, u32[]{:S(2)}, u32[]{:S(2)}) collective-permute-start(bf16[128,1408]{1,0:T(8,128)(2,1)S(1)} %get-tuple-element.48), channel_id=1, source_target_pairs={{0,66},{1,67},{2,64},{3,65},{4,70},{5,71},{6,68},{7,69},{8,74},{9,... | collective-permute-start | bytes 1081352 | tf_op jit(solution)/shard_map/ppermute | solution.py:83
  16.9 3.2 %collective-permute-start.14 = (bf16[256,1408]{1,0:T(8,128)(2,1)S(1)}, bf16[256,1408]{1,0:T(8,128)(2,1)S(1)}, u32[]{:S(2)}, u32[]{:S(2)}) collective-permute-start(bf16[256,1408]{1,0:T(8,128)(2,1)S(1)} %pad_maximum_fusion.18), channel_id=1, source_target_pairs={{0,66},{1,67},{2,64},{3,65},{4,70},{5,71},{6,68},{7,69},{8,74},{9,... | collective-permute-start | bytes 2162696 | tf_op jit(solution)/shard_map/ppermute | solution.py:83
  20.6 2.4 %collective-permute-start.13 = (bf16[256,1408]{1,0:T(8,128)(2,1)S(1)}, bf16[256,1408]{1,0:T(8,128)(2,1)S(1)}, u32[]{:S(2)}, u32[]{:S(2)}) collective-permute-start(bf16[256,1408]{1,0:T(8,128)(2,1)S(1)} %pad_maximum_fusion.17), channel_id=1, source_target_pairs={{0,48},{1,49},{2,50},{3,51},{4,52},{5,53},{6,54},{7,55},{8,56},{9,... | collective-permute-start | bytes 2162696 | tf_op jit(solution)/shard_map/ppermute | solution.py:83
  23.0 1.6 %collective-permute-done.9 = bf16[128,1408]{1,0:T(8,128)(2,1)S(1)} collective-permute-done((bf16[128,1408]{1,0:T(8,128)(2,1)S(1)}, bf16[128,1408]{1,0:T(8,128)(2,1)S(1)}, u32[]{:S(2)}, u32[]{:S(2)}) %collective-permute-start.9) | collective-permute-done | bytes 360480 | tf_op jit(solution)/shard_map/ppermute | solution.py:83
  24.7 2.5 %collective-permute-start.10 = (bf16[256,1408]{1,0:T(8,128)(2,1)S(1)}, bf16[256,1408]{1,0:T(8,128)(2,1)S(1)}, u32[]{:S(2)}, u32[]{:S(2)}) collective-permute-start(bf16[256,1408]{1,0:T(8,128)(2,1)S(1)} %pad_maximum_fusion.16), channel_id=1, source_target_pairs={{0,12},{1,13},{2,14},{3,15},{4,8},{5,9},{6,10},{7,11},{8,4},{9,5},... | collective-permute-start | bytes 2162696 | tf_op jit(solution)/shard_map/ppermute | solution.py:83
  27.2 1.2 collective-permute-done.1
  29.3 1.8 %collective-permute-start.3 = (bf16[256,2176]{1,0:T(8,128)(2,1)S(1)}, bf16[256,2176]{1,0:T(8,128)(2,1)S(1)}, u32[]{:S(2)}, u32[]{:S(2)}) collective-permute-start(bf16[256,2176]{1,0:T(8,128)(2,1)S(1)} %pad_maximum_fusion.5), channel_id=1, source_target_pairs={{0,16},{1,17},{2,18},{3,19},{4,20},{5,21},{6,22},{7,23},{8,24},{9,... | collective-permute-start | bytes 3342344 | tf_op jit(solution)/shard_map/ppermute | solution.py:83
  31.1 7.6 %collective-permute-done.14 = bf16[256,1408]{1,0:T(8,128)(2,1)S(1)} collective-permute-done((bf16[256,1408]{1,0:T(8,128)(2,1)S(1)}, bf16[256,1408]{1,0:T(8,128)(2,1)S(1)}, u32[]{:S(2)}, u32[]{:S(2)}) %collective-permute-start.14) | collective-permute-done | bytes 720928 | tf_op jit(solution)/shard_map/ppermute | solution.py:83
  38.8 1.1 collective-permute-start.16
  40.0 3.0 %collective-permute-start.15 = (bf16[512,1408]{1,0:T(8,128)(2,1)S(1)}, bf16[512,1408]{1,0:T(8,128)(2,1)S(1)}, u32[]{:S(2)}, u32[]{:S(2)}) collective-permute-start(bf16[512,1408]{1,0:T(8,128)(2,1)S(1)} %pad_maximum_fusion.3), channel_id=1, source_target_pairs={{0,66},{1,67},{2,64},{3,65},{4,70},{5,71},{6,68},{7,69},{8,74},{9,... | collective-permute-start | bytes 4325384 | tf_op jit(solution)/shard_map/ppermute | solution.py:83
  43.9 2.2 %collective-permute-start.11 = (bf16[512,1408]{1,0:T(8,128)(2,1)S(1)}, bf16[512,1408]{1,0:T(8,128)(2,1)S(1)}, u32[]{:S(2)}, u32[]{:S(2)}) collective-permute-start(bf16[512,1408]{1,0:T(8,128)(2,1)S(1)} %pad_maximum_fusion.2), channel_id=1, source_target_pairs={{0,48},{1,49},{2,50},{3,51},{4,52},{5,53},{6,54},{7,55},{8,56},{9,... | collective-permute-start | bytes 4325384 | tf_op jit(solution)/shard_map/ppermute | solution.py:83
  46.2 5.7 %collective-permute-done.4 = bf16[256,2048]{1,0:T(8,128)(2,1)S(1)} collective-permute-done((bf16[256,2048]{1,0:T(8,128)(2,1)S(1)}, bf16[256,2048]{1,0:T(8,128)(2,1)S(1)}, u32[]{:S(2)}, u32[]{:S(2)}) %collective-permute-start.4) | collective-permute-done | bytes 1048608 | tf_op jit(solution)/shard_map/ppermute | solution.py:83
  52.4 1.6 %collective-permute-done.3 = bf16[256,2176]{1,0:T(8,128)(2,1)S(1)} collective-permute-done((bf16[256,2176]{1,0:T(8,128)(2,1)S(1)}, bf16[256,2176]{1,0:T(8,128)(2,1)S(1)}, u32[]{:S(2)}, u32[]{:S(2)}) %collective-permute-start.3) | collective-permute-done | bytes 1114144 | tf_op jit(solution)/shard_map/ppermute | solution.py:83
  54.1 1.5 %collective-permute-start.5 = (bf16[512,2176]{1,0:T(8,128)(2,1)S(1)}, bf16[512,2176]{1,0:T(8,128)(2,1)S(1)}, u32[]{:S(2)}, u32[]{:S(2)}) collective-permute-start(bf16[512,2176]{1,0:T(8,128)(2,1)S(1)} %pad_maximum_fusion), channel_id=1, source_target_pairs={{0,64},{1,65},{2,66},{3,67},{4,68},{5,69},{6,70},{7,71},{8,72},{9,... | collective-permute-start | bytes 6684680 | tf_op jit(solution)/shard_map/ppermute | solution.py:83
  56.6 19.2 %collective-permute-done.11 = bf16[512,1408]{1,0:T(8,128)(2,1)S(1)} collective-permute-done((bf16[512,1408]{1,0:T(8,128)(2,1)S(1)}, bf16[512,1408]{1,0:T(8,128)(2,1)S(1)}, u32[]{:S(2)}, u32[]{:S(2)}) %collective-permute-start.11) | collective-permute-done | bytes 1441824 | tf_op jit(solution)/shard_map/ppermute | solution.py:83
  77.7 19.6 %collective-permute-done.6 = bf16[512,2048]{1,0:T(8,128)(2,1)S(1)} collective-permute-done((bf16[512,2048]{1,0:T(8,128)(2,1)S(1)}, bf16[512,2048]{1,0:T(8,128)(2,1)S(1)}, u32[]{:S(2)}, u32[]{:S(2)}) %collective-permute-start.6) | collective-permute-done | bytes 2097184 | tf_op jit(solution)/shard_map/ppermute | solution.py:83
  97.5 4.5 %collective-permute-done.5 = bf16[512,2176]{1,0:T(8,128)(2,1)S(1)} collective-permute-done((bf16[512,2176]{1,0:T(8,128)(2,1)S(1)}, bf16[512,2176]{1,0:T(8,128)(2,1)S(1)}, u32[]{:S(2)}, u32[]{:S(2)}) %collective-permute-start.5) | collective-permute-done | bytes 2228256 | tf_op jit(solution)/shard_map/ppermute | solution.py:83
  103.1 6.1 %fusion.50 = f32[512,1024]{1,0:T(8,128)} fusion(bf16[512,4224]{1,0:T(8,128)(2,1)S(1)} %get-tuple-element.32, bf16[1024,4224]{1,0:T(8,128)(2,1)S(1)} %slice_dynamic-update-slice_fusion), kind=kOutput, calls=%fused_computation.161 | convolution fusion | flops 4429185024 | bytes 15073280 | tf_op jit(solution)/shard_map/dot_general | solution.py:173
  109.2 1.4 add_reduce_fusion
  110.6 8.6 %fusion.49 = f32[512,1024]{1,0:T(8,128)S(1)} fusion(bf16[512,4224]{1,0:T(8,128)(2,1)} %copy-done.1, bf16[1024,4224]{1,0:T(8,128)(2,1)} %copy-done.2), kind=kOutput, calls=%fused_computation.160 | convolution fusion | flops 4429185024 | bytes 15073280 | tf_op jit(solution)/shard_map/dot_general | solution.py:173
  119.2 1.0 convert_reduce_fusion
  120.2 1.2 add_reduce_fusion.1
  122.9 0.9 multiply_reduce_fusion
  124.5 1.7 %collective-permute-start.18 = (f32[256,512]{1,0:T(8,128)S(1)}, f32[256,512]{1,0:T(8,128)S(1)}, u32[]{:S(2)}, u32[]{:S(2)}) collective-permute-start(f32[256,512]{1,0:T(8,128)S(1)} %pad_maximum_fusion.28), channel_id=1, source_target_pairs={{0,16},{1,65},{2,18},{3,67},{4,20},{5,69},{6,22},{7,71},{8,24},{9,... | collective-permute-start | bytes 1572872 | tf_op jit(solution)/shard_map/ppermute | solution.py:152
  126.8 4.3 %collective-permute-done.22 = f32[256]{0:T(256)S(1)} collective-permute-done((f32[256]{0:T(256)S(1)}, f32[256]{0:T(256)S(1)}, u32[]{:S(2)}, u32[]{:S(2)}) %collective-permute-start.22) | collective-permute-done | bytes 1056 | tf_op jit(solution)/shard_map/ppermute | solution.py:118
  131.2 2.6 %collective-permute-done.18 = f32[256,512]{1,0:T(8,128)S(1)} collective-permute-done((f32[256,512]{1,0:T(8,128)S(1)}, f32[256,512]{1,0:T(8,128)S(1)}, u32[]{:S(2)}, u32[]{:S(2)}) %collective-permute-start.18) | collective-permute-done | bytes 524320 | tf_op jit(solution)/shard_map/ppermute | solution.py:152
  133.8 1.3 collective-permute-start.19
  135.6 4.3 %collective-permute-done.23 = f32[128]{0:T(128)S(1)} collective-permute-done((f32[128]{0:T(128)S(1)}, f32[128]{0:T(128)S(1)}, u32[]{:S(2)}, u32[]{:S(2)}) %collective-permute-start.23) | collective-permute-done | bytes 544 | tf_op jit(solution)/shard_map/ppermute | solution.py:118
  141.2 3.5 %collective-permute-done.24 = f32[64]{0:T(128)S(1)} collective-permute-done((f32[64]{0:T(128)S(1)}, f32[64]{0:T(128)S(1)}, u32[]{:S(2)}, u32[]{:S(2)}) %collective-permute-start.24) | collective-permute-done | bytes 288 | tf_op jit(solution)/shard_map/ppermute | solution.py:118
  (119 shorter events, 18.5 us)
Async XLA Ops:
  2.7 1.2 copy-start
  2.8 1.2 copy-start.3
  3.0 2.0 %collective-permute-start.7 = (bf16[64,4224]{1,0:T(8,128)(2,1)S(1)}, bf16[64,4224]{1,0:T(8,128)(2,1)S(1)}, u32[]{:S(2)}, u32[]{:S(2)}) collective-permute-start(bf16[64,4224]{1,0:T(8,128)(2,1)S(1)} %get-tuple-element.49), channel_id=1, source_target_pairs={{0,1},{1,0},{2,3},{3,2},{4,5},{5,4},{6,7},{7,6},{8,9},{9,8},{10,11... | collective-permute-start | bytes 1622024 | tf_op jit(solution)/shard_map/ppermute | solution.py:96
  4.4 10.7 %collective-permute-start = (bf16[64,4224]{1,0:T(8,128)(2,1)S(1)}, bf16[64,4224]{1,0:T(8,128)(2,1)S(1)}, u32[]{:S(2)}, u32[]{:S(2)}) collective-permute-start(bf16[64,4224]{1,0:T(8,128)(2,1)S(1)} %get-tuple-element.50), channel_id=1, source_target_pairs={{0,1},{1,0},{2,3},{3,2},{4,5},{5,4},{6,7},{7,6},{8,9},{9,8},{10,11... | collective-permute-start | bytes 1622024 | tf_op jit(solution)/shard_map/ppermute | solution.py:96
  5.1 11.7 %collective-permute-start.8 = (bf16[128,1408]{1,0:T(8,128)(2,1)S(1)}, bf16[128,1408]{1,0:T(8,128)(2,1)S(1)}, u32[]{:S(2)}, u32[]{:S(2)}) collective-permute-start(bf16[128,1408]{1,0:T(8,128)(2,1)S(1)} %get-tuple-element.46), channel_id=1, source_target_pairs={{0,48},{1,49},{2,50},{3,51},{4,52},{5,53},{6,54},{7,55},{8,56},{9,... | collective-permute-start | bytes 1081352 | tf_op jit(solution)/shard_map/ppermute | solution.py:83
  8.0 12.5 %collective-permute-start.12 = (bf16[128,1408]{1,0:T(8,128)(2,1)S(1)}, bf16[128,1408]{1,0:T(8,128)(2,1)S(1)}, u32[]{:S(2)}, u32[]{:S(2)}) collective-permute-start(bf16[128,1408]{1,0:T(8,128)(2,1)S(1)} %get-tuple-element.47), channel_id=1, source_target_pairs={{0,12},{1,13},{2,14},{3,15},{4,8},{5,9},{6,10},{7,11},{8,4},{9,5},... | collective-permute-start | bytes 1081352 | tf_op jit(solution)/shard_map/ppermute | solution.py:83
  12.1 12.5 %collective-permute-start.9 = (bf16[128,1408]{1,0:T(8,128)(2,1)S(1)}, bf16[128,1408]{1,0:T(8,128)(2,1)S(1)}, u32[]{:S(2)}, u32[]{:S(2)}) collective-permute-start(bf16[128,1408]{1,0:T(8,128)(2,1)S(1)} %get-tuple-element.48), channel_id=1, source_target_pairs={{0,66},{1,67},{2,64},{3,65},{4,70},{5,71},{6,68},{7,69},{8,74},{9,... | collective-permute-start | bytes 1081352 | tf_op jit(solution)/shard_map/ppermute | solution.py:83
  15.1 13.2 %collective-permute-start.1 = (bf16[128,2048]{1,0:T(8,128)(2,1)S(1)}, bf16[128,2048]{1,0:T(8,128)(2,1)S(1)}, u32[]{:S(2)}, u32[]{:S(2)}) collective-permute-start(bf16[128,2048]{1,0:T(8,128)(2,1)S(1)} %pad_maximum_fusion.27), channel_id=1, source_target_pairs={{0,16},{1,17},{2,18},{3,19},{4,20},{5,21},{6,22},{7,23},{8,24},{9,... | collective-permute-start | bytes 1572872 | tf_op jit(solution)/shard_map/ppermute | solution.py:83
  15.5 13.7 %collective-permute-start.2 = (bf16[128,2176]{1,0:T(8,128)(2,1)S(1)}, bf16[128,2176]{1,0:T(8,128)(2,1)S(1)}, u32[]{:S(2)}, u32[]{:S(2)}) collective-permute-start(bf16[128,2176]{1,0:T(8,128)(2,1)S(1)} %pad_maximum_fusion.19), channel_id=1, source_target_pairs={{0,4},{1,5},{2,6},{3,7},{4,0},{5,1},{6,2},{7,3},{8,12},{9,13},{10,... | collective-permute-start | bytes 1671176 | tf_op jit(solution)/shard_map/ppermute | solution.py:83
  16.9 21.8 %collective-permute-start.14 = (bf16[256,1408]{1,0:T(8,128)(2,1)S(1)}, bf16[256,1408]{1,0:T(8,128)(2,1)S(1)}, u32[]{:S(2)}, u32[]{:S(2)}) collective-permute-start(bf16[256,1408]{1,0:T(8,128)(2,1)S(1)} %pad_maximum_fusion.18), channel_id=1, source_target_pairs={{0,66},{1,67},{2,64},{3,65},{4,70},{5,71},{6,68},{7,69},{8,74},{9,... | collective-permute-start | bytes 2162696 | tf_op jit(solution)/shard_map/ppermute | solution.py:83
  20.6 19.4 %collective-permute-start.13 = (bf16[256,1408]{1,0:T(8,128)(2,1)S(1)}, bf16[256,1408]{1,0:T(8,128)(2,1)S(1)}, u32[]{:S(2)}, u32[]{:S(2)}) collective-permute-start(bf16[256,1408]{1,0:T(8,128)(2,1)S(1)} %pad_maximum_fusion.17), channel_id=1, source_target_pairs={{0,48},{1,49},{2,50},{3,51},{4,52},{5,53},{6,54},{7,55},{8,56},{9,... | collective-permute-start | bytes 2162696 | tf_op jit(solution)/shard_map/ppermute | solution.py:83
  24.7 19.1 %collective-permute-start.10 = (bf16[256,1408]{1,0:T(8,128)(2,1)S(1)}, bf16[256,1408]{1,0:T(8,128)(2,1)S(1)}, u32[]{:S(2)}, u32[]{:S(2)}) collective-permute-start(bf16[256,1408]{1,0:T(8,128)(2,1)S(1)} %pad_maximum_fusion.16), channel_id=1, source_target_pairs={{0,12},{1,13},{2,14},{3,15},{4,8},{5,9},{6,10},{7,11},{8,4},{9,5},... | collective-permute-start | bytes 2162696 | tf_op jit(solution)/shard_map/ppermute | solution.py:83
  28.4 23.5 %collective-permute-start.4 = (bf16[256,2048]{1,0:T(8,128)(2,1)S(1)}, bf16[256,2048]{1,0:T(8,128)(2,1)S(1)}, u32[]{:S(2)}, u32[]{:S(2)}) collective-permute-start(bf16[256,2048]{1,0:T(8,128)(2,1)S(1)} %pad_maximum_fusion.15), channel_id=1, source_target_pairs={{0,64},{1,65},{2,66},{3,67},{4,68},{5,69},{6,70},{7,71},{8,72},{9,... | collective-permute-start | bytes 3145736 | tf_op jit(solution)/shard_map/ppermute | solution.py:83
  29.3 24.7 %collective-permute-start.3 = (bf16[256,2176]{1,0:T(8,128)(2,1)S(1)}, bf16[256,2176]{1,0:T(8,128)(2,1)S(1)}, u32[]{:S(2)}, u32[]{:S(2)}) collective-permute-start(bf16[256,2176]{1,0:T(8,128)(2,1)S(1)} %pad_maximum_fusion.5), channel_id=1, source_target_pairs={{0,16},{1,17},{2,18},{3,19},{4,20},{5,21},{6,22},{7,23},{8,24},{9,... | collective-permute-start | bytes 3342344 | tf_op jit(solution)/shard_map/ppermute | solution.py:83
  38.8 37.7 %collective-permute-start.16 = (bf16[512,1408]{1,0:T(8,128)(2,1)S(1)}, bf16[512,1408]{1,0:T(8,128)(2,1)S(1)}, u32[]{:S(2)}, u32[]{:S(2)}) collective-permute-start(bf16[512,1408]{1,0:T(8,128)(2,1)S(1)} %pad_maximum_fusion.4), channel_id=1, source_target_pairs={{0,12},{1,13},{2,14},{3,15},{4,8},{5,9},{6,10},{7,11},{8,4},{9,5},... | collective-permute-start | bytes 4325384 | tf_op jit(solution)/shard_map/ppermute | solution.py:83
  40.0 36.0 %collective-permute-start.15 = (bf16[512,1408]{1,0:T(8,128)(2,1)S(1)}, bf16[512,1408]{1,0:T(8,128)(2,1)S(1)}, u32[]{:S(2)}, u32[]{:S(2)}) collective-permute-start(bf16[512,1408]{1,0:T(8,128)(2,1)S(1)} %pad_maximum_fusion.3), channel_id=1, source_target_pairs={{0,66},{1,67},{2,64},{3,65},{4,70},{5,71},{6,68},{7,69},{8,74},{9,... | collective-permute-start | bytes 4325384 | tf_op jit(solution)/shard_map/ppermute | solution.py:83
  43.9 31.9 %collective-permute-start.11 = (bf16[512,1408]{1,0:T(8,128)(2,1)S(1)}, bf16[512,1408]{1,0:T(8,128)(2,1)S(1)}, u32[]{:S(2)}, u32[]{:S(2)}) collective-permute-start(bf16[512,1408]{1,0:T(8,128)(2,1)S(1)} %pad_maximum_fusion.2), channel_id=1, source_target_pairs={{0,48},{1,49},{2,50},{3,51},{4,52},{5,53},{6,54},{7,55},{8,56},{9,... | collective-permute-start | bytes 4325384 | tf_op jit(solution)/shard_map/ppermute | solution.py:83
  52.2 45.1 %collective-permute-start.6 = (bf16[512,2048]{1,0:T(8,128)(2,1)S(1)}, bf16[512,2048]{1,0:T(8,128)(2,1)S(1)}, u32[]{:S(2)}, u32[]{:S(2)}) collective-permute-start(bf16[512,2048]{1,0:T(8,128)(2,1)S(1)} %pad_maximum_fusion.1), channel_id=1, source_target_pairs={{0,4},{1,5},{2,6},{3,7},{4,0},{5,1},{6,2},{7,3},{8,12},{9,13},{10,... | collective-permute-start | bytes 6291464 | tf_op jit(solution)/shard_map/ppermute | solution.py:83
  54.1 47.9 %collective-permute-start.5 = (bf16[512,2176]{1,0:T(8,128)(2,1)S(1)}, bf16[512,2176]{1,0:T(8,128)(2,1)S(1)}, u32[]{:S(2)}, u32[]{:S(2)}) collective-permute-start(bf16[512,2176]{1,0:T(8,128)(2,1)S(1)} %pad_maximum_fusion), channel_id=1, source_target_pairs={{0,64},{1,65},{2,66},{3,67},{4,68},{5,69},{6,70},{7,71},{8,72},{9,... | collective-permute-start | bytes 6684680 | tf_op jit(solution)/shard_map/ppermute | solution.py:83
  77.6 24.6 %slice-start = ((s8[4325376]{0:T(1024)(128)(4,1)}), s8[4194304]{0:T(1024)(128)(4,1)S(1)}, s32[]{:S(2)}) async-start(s8[4325376]{0:T(1024)(128)(4,1)} %bitcast.6), calls=%async_computation | async-start | bytes 8388608
  77.7 25.4 %copy-start.2 = (bf16[1024,4224]{1,0:T(8,128)(2,1)}, bf16[1024,4224]{1,0:T(8,128)(2,1)S(1)}, u32[]{:S(2)}) copy-start(bf16[1024,4224]{1,0:T(8,128)(2,1)S(1)} %slice_dynamic-update-slice_fusion) | copy-start | bytes 25952260
  77.7 24.5 %slice-start.1 = ((s8[4325376]{0:T(1024)(128)(4,1)}), s8[131072]{0:T(1024)(128)(4,1)S(1)}, s32[]{:S(2)}) async-start(s8[4325376]{0:T(1024)(128)(4,1)} %bitcast.6), calls=%async_computation.1 | async-start | bytes 262144
  103.1 6.1 %copy-start.1 = (bf16[512,4224]{1,0:T(8,128)(2,1)}, bf16[512,4224]{1,0:T(8,128)(2,1)S(1)}, u32[]{:S(2)}) copy-start(bf16[512,4224]{1,0:T(8,128)(2,1)S(1)} %get-tuple-element.33) | copy-start | bytes 12976132
  109.2 12.3 %collective-permute-start.17 = (f32[512,1024]{1,0:T(8,128)}, f32[512,1024]{1,0:T(8,128)S(1)}, u32[]{:S(2)}, u32[]{:S(2)}) collective-permute-start(f32[512,1024]{1,0:T(8,128)} %fusion.50), channel_id=1, source_target_pairs={{0,1},{1,0},{2,3},{3,2},{4,5},{5,4},{6,7},{7,6},{8,9},{9,8},{10,11... | collective-permute-start | bytes 6291464 | tf_op jit(solution)/shard_map/ppermute | solution.py:177
  123.8 2.4 %collective-permute-start.21 = (f32[512]{0:T(512)S(1)}, f32[512]{0:T(512)S(1)}, u32[]{:S(2)}, u32[]{:S(2)}) collective-permute-start(f32[512]{0:T(512)S(1)} %slice.414), channel_id=1, source_target_pairs={{0,1},{1,0},{2,3},{3,2},{4,5},{5,4},{6,7},{7,6},{8,9},{9,8},{10,11... | collective-permute-start | bytes 6152 | tf_op jit(solution)/shard_map/ppermute | solution.py:193
  124.5 9.3 %collective-permute-start.18 = (f32[256,512]{1,0:T(8,128)S(1)}, f32[256,512]{1,0:T(8,128)S(1)}, u32[]{:S(2)}, u32[]{:S(2)}) collective-permute-start(f32[256,512]{1,0:T(8,128)S(1)} %pad_maximum_fusion.28), channel_id=1, source_target_pairs={{0,16},{1,65},{2,18},{3,67},{4,20},{5,69},{6,22},{7,71},{8,24},{9,... | collective-permute-start | bytes 1572872 | tf_op jit(solution)/shard_map/ppermute | solution.py:152
  126.3 4.8 %collective-permute-start.22 = (f32[256]{0:T(256)S(1)}, f32[256]{0:T(256)S(1)}, u32[]{:S(2)}, u32[]{:S(2)}) collective-permute-start(f32[256]{0:T(256)S(1)} %pad_maximum_fusion.31), channel_id=1, source_target_pairs={{0,48},{1,49},{2,50},{3,51},{4,52},{5,53},{6,54},{7,55},{8,56},{9,... | collective-permute-start | bytes 3080 | tf_op jit(solution)/shard_map/ppermute | solution.py:118
  133.8 7.0 %collective-permute-start.19 = (f32[128,512]{1,0:T(8,128)S(1)}, f32[128,512]{1,0:T(8,128)S(1)}, u32[]{:S(2)}, u32[]{:S(2)}) collective-permute-start(f32[128,512]{1,0:T(8,128)S(1)} %pad_maximum_fusion.30), channel_id=1, source_target_pairs={{0,64},{1,5},{2,66},{3,7},{4,68},{5,1},{6,70},{7,3},{8,72},{9,13},... | collective-permute-start | bytes 786440 | tf_op jit(solution)/shard_map/ppermute | solution.py:152
  135.2 4.8 %collective-permute-start.23 = (f32[128]{0:T(128)S(1)}, f32[128]{0:T(128)S(1)}, u32[]{:S(2)}, u32[]{:S(2)}) collective-permute-start(f32[128]{0:T(128)S(1)} %pad_maximum_fusion.32), channel_id=1, source_target_pairs={{0,66},{1,67},{2,64},{3,65},{4,70},{5,71},{6,68},{7,69},{8,74},{9,... | collective-permute-start | bytes 1544 | tf_op jit(solution)/shard_map/ppermute | solution.py:118
  140.0 4.8 %collective-permute-start.24 = (f32[64]{0:T(128)S(1)}, f32[64]{0:T(128)S(1)}, u32[]{:S(2)}, u32[]{:S(2)}) collective-permute-start(f32[64]{0:T(128)S(1)} %slice_add_fusion.7), channel_id=1, source_target_pairs={{0,12},{1,13},{2,14},{3,15},{4,8},{5,9},{6,10},{7,11},{8,4},{9,5},... | collective-permute-start | bytes 776 | tf_op jit(solution)/shard_map/ppermute | solution.py:118
  140.9 5.0 %collective-permute-start.20 = (f32[64,512]{1,0:T(8,128)S(1)}, f32[64,512]{1,0:T(8,128)S(1)}, u32[]{:S(2)}, u32[]{:S(2)}) collective-permute-start(f32[64,512]{1,0:T(8,128)S(1)} %slice_add_fusion), channel_id=1, source_target_pairs={{0,4},{1,17},{2,6},{3,19},{4,0},{5,21},{6,2},{7,23},{8,12},{9,25},... | collective-permute-start | bytes 393224 | tf_op jit(solution)/shard_map/ppermute | solution.py:152

commit v18 on v15

--- a/solution.py
+++ b/solution.py
@@ -87,7 +87,7 @@
     return [buf[at[o] * rows:(at[o] + 1) * rows] for o in range(8)]
 
 
-def half_gather(shard, mate, n, orders):
+def half_gather(shard, mate, n, orders, split=False):
     r, cols = shard.shape
     h = cols // 2
     c = lax.axis_index(AXES) % 2
@@ -96,6 +96,8 @@
     unit = jnp.concatenate([mine, lax.ppermute(give, AXES, core_pairs(n))])
     cut = column_cuts(h, len(orders))
     parts = [chain(unit[:, cut[p]:cut[p + 1]], mate, n, order) for p, order in enumerate(orders)]
+    if split:
+        return [jnp.concatenate([b[:r] for b in q] + [b[r:] for b in q]) for q in parts], cut
     blocks = [jnp.concatenate([parts[p][o] for p in range(len(orders))], axis=1) for o in range(8)]
     return jnp.concatenate([b[:r] for b in blocks] + [b[r:] for b in blocks])
 
@@ -132,20 +134,26 @@
     te = with_side(test_grads, split_class(test_class), 4)
     side = k // 2
     te_all = half_gather(te, test_mate, n, THREE)
-    tr_all = half_gather(tr, train_mate, n, TWO)
+    tr_cols, cut = half_gather(tr, train_mate, n, TWO, split=True)
     half = 8 * rows
 
-    def partial(t):
-        return lax.dot_general(
-            t, te_all, (((1,), (1,)), ((), ())), preferred_element_type=jnp.float32
+    def partial(lo, hi):
+        return sum(
+            lax.dot_general(
+                t[lo:hi], te_all[:, cut[p]:cut[p + 1]], (((1,), (1,)), ((), ())),
+                preferred_element_type=jnp.float32,
+            )
+            for p, t in enumerate(tr_cols)
         )
 
-    got = lax.ppermute(partial(tr_all[half:]), AXES, core_pairs(n))
-    own = lax.optimization_barrier(partial(tr_all[:half]))
+    got = lax.ppermute(partial(half, 2 * half), AXES, core_pairs(n))
+    own = lax.optimization_barrier(partial(0, half))
     raw = own + jnp.concatenate([got[:, half:], got[:, :half]], axis=1)
+    tr_all = tr_cols[-1]
     tr_mine = tr_all[:half]
-    scale = tr_mine[:, side].astype(jnp.float32)
-    train_hot = indicator(join_class(tr_mine, side + 1))
+    tr_side = side - cut[-2]
+    scale = tr_mine[:, tr_side].astype(jnp.float32)
+    train_hot = indicator(join_class(tr_mine, tr_side + 1))
     test_hot = indicator(join_class(te_all, side + 4))
     w = jnp.tanh(scale[:, None] * raw).astype(jnp.bfloat16)
     part = jnp.dot(w, test_hot, preferred_element_type=jnp.float32)

time: 144 us -> 146 us (1.014)
  local copies, waits for them, and re-layouts: 5.49 us -> 8.45 us
  other arithmetic: 7.43 us -> 5.68 us
  waiting for transfers between devices: 83.5 us -> 85.1 us
    unnamed x25 -> x47, local copies, waits for them, and re-layouts: 2.74 us -> 5.29 us
    unnamed x7 -> x1, other arithmetic: 1.6 us -> 0.01 us
    ppermute x6, starting transfers between devices: 5.61 us -> 4.02 us  [cube_reduce(): lax.ppermute(jnp.concatenate([blocks[o] for o in send]), AXES, mate_pairs...]
    dot_general x2 -> x4, matrix products: 9.57 us -> 9.98 us  [partial(): lax.dot_general(t[lo:hi], te_all[:, cut[p]:cut[p + 1]], (((1,), (1,)), ((...]
  transfers between devices with their start and end apart: 25 -> 25, of which waited for: 19 -> 18; matrix products, arithmetic and copies ran while one was open for 8% -> 9% of each run, Pallas kernels for 0% -> 0%
where the time goes in v18:
time: 146 us
  waiting for transfers between devices  85.1 us (58%)
  starting transfers between devices  33.5 us (23%)
  matrix products  11.6 us (8%)
  local copies, waits for them, and re-layouts  8.45 us (6%)
  other arithmetic  5.68 us (4%)
    ppermute x15, waiting for transfers between devices, chain(): got = lax.ppermute(buf, AXES, mate_pairs(n, a, mate))  63.2 us
    ppermute x15, starting transfers between devices, chain(): got = lax.ppermute(buf, AXES, mate_pairs(n, a, mate))  28.1 us
    ppermute x6, waiting for transfers between devices, cube_reduce(): lax.ppermute(jnp.concatenate([blocks[o] for o in send]), AXES, mate_pairs...  21.3 us
    dot_general x4, matrix products, partial(): lax.dot_general(t[lo:hi], te_all[:, cut[p]:cut[p + 1]], (((1,), (1,)), ((...  9.98 us
    unnamed x47, local copies, waits for them, and re-layouts  5.29 us
    ppermute x6, starting transfers between devices, cube_reduce(): lax.ppermute(jnp.concatenate([blocks[o] for o in send]), AXES, mate_pairs...  4.02 us
  transfers between devices with their start and end apart: 25, of which 18 were waited for; matrix products, arithmetic and copies ran while one was open for 9% of the time, Pallas kernels for 0%

profile of v18, /device:TPU:0, one launch (start us, length us, event | category | flops | bytes accessed | tf_op | source)
XLA Modules:
  0.0 145.7 jit_solution(1334123684293624193)
XLA Ops:
  0.7 1.3 fusion.34
  2.8 1.1 constant_dynamic-update-slice_fusion.1
  6.2 2.9 %collective-permute-start.8 = (bf16[128,1408]{1,0:T(8,128)(2,1)S(1)}, bf16[128,1408]{1,0:T(8,128)(2,1)S(1)}, u32[]{:S(2)}, u32[]{:S(2)}) collective-permute-start(bf16[128,1408]{1,0:T(8,128)(2,1)S(1)} %get-tuple-element.40), channel_id=1, source_target_pairs={{0,48},{1,49},{2,50},{3,51},{4,52},{5,53},{6,54},{7,55},{8,56},{9,... | collective-permute-start | bytes 1081352 | tf_op jit(solution)/shard_map/ppermute | solution.py:83
  9.1 4.0 %collective-permute-start.12 = (bf16[128,1408]{1,0:T(8,128)(2,1)S(1)}, bf16[128,1408]{1,0:T(8,128)(2,1)S(1)}, u32[]{:S(2)}, u32[]{:S(2)}) collective-permute-start(bf16[128,1408]{1,0:T(8,128)(2,1)S(1)} %get-tuple-element.41), channel_id=1, source_target_pairs={{0,12},{1,13},{2,14},{3,15},{4,8},{5,9},{6,10},{7,11},{8,4},{9,5},... | collective-permute-start | bytes 1081352 | tf_op jit(solution)/shard_map/ppermute | solution.py:83
  13.2 3.0 %collective-permute-start.9 = (bf16[128,1408]{1,0:T(8,128)(2,1)S(1)}, bf16[128,1408]{1,0:T(8,128)(2,1)S(1)}, u32[]{:S(2)}, u32[]{:S(2)}) collective-permute-start(bf16[128,1408]{1,0:T(8,128)(2,1)S(1)} %get-tuple-element.42), channel_id=1, source_target_pairs={{0,66},{1,67},{2,64},{3,65},{4,70},{5,71},{6,68},{7,69},{8,74},{9,... | collective-permute-start | bytes 1081352 | tf_op jit(solution)/shard_map/ppermute | solution.py:83
  18.0 3.2 %collective-permute-start.14 = (bf16[256,1408]{1,0:T(8,128)(2,1)S(1)}, bf16[256,1408]{1,0:T(8,128)(2,1)S(1)}, u32[]{:S(2)}, u32[]{:S(2)}) collective-permute-start(bf16[256,1408]{1,0:T(8,128)(2,1)S(1)} %pad_maximum_fusion.18), channel_id=1, source_target_pairs={{0,66},{1,67},{2,64},{3,65},{4,70},{5,71},{6,68},{7,69},{8,74},{9,... | collective-permute-start | bytes 2162696 | tf_op jit(solution)/shard_map/ppermute | solution.py:83
  21.7 2.4 %collective-permute-start.13 = (bf16[256,1408]{1,0:T(8,128)(2,1)S(1)}, bf16[256,1408]{1,0:T(8,128)(2,1)S(1)}, u32[]{:S(2)}, u32[]{:S(2)}) collective-permute-start(bf16[256,1408]{1,0:T(8,128)(2,1)S(1)} %pad_maximum_fusion.17), channel_id=1, source_target_pairs={{0,48},{1,49},{2,50},{3,51},{4,52},{5,53},{6,54},{7,55},{8,56},{9,... | collective-permute-start | bytes 2162696 | tf_op jit(solution)/shard_map/ppermute | solution.py:83
  24.1 1.6 %collective-permute-done.9 = bf16[128,1408]{1,0:T(8,128)(2,1)S(1)} collective-permute-done((bf16[128,1408]{1,0:T(8,128)(2,1)S(1)}, bf16[128,1408]{1,0:T(8,128)(2,1)S(1)}, u32[]{:S(2)}, u32[]{:S(2)}) %collective-permute-start.9) | collective-permute-done | bytes 360480 | tf_op jit(solution)/shard_map/ppermute | solution.py:83
  25.8 2.5 %collective-permute-start.10 = (bf16[256,1408]{1,0:T(8,128)(2,1)S(1)}, bf16[256,1408]{1,0:T(8,128)(2,1)S(1)}, u32[]{:S(2)}, u32[]{:S(2)}) collective-permute-start(bf16[256,1408]{1,0:T(8,128)(2,1)S(1)} %pad_maximum_fusion.16), channel_id=1, source_target_pairs={{0,12},{1,13},{2,14},{3,15},{4,8},{5,9},{6,10},{7,11},{8,4},{9,5},... | collective-permute-start | bytes 2162696 | tf_op jit(solution)/shard_map/ppermute | solution.py:83
  28.3 1.3 collective-permute-done.4
  31.1 8.7 %collective-permute-done.14 = bf16[256,1408]{1,0:T(8,128)(2,1)S(1)} collective-permute-done((bf16[256,1408]{1,0:T(8,128)(2,1)S(1)}, bf16[256,1408]{1,0:T(8,128)(2,1)S(1)}, u32[]{:S(2)}, u32[]{:S(2)}) %collective-permute-start.14) | collective-permute-done | bytes 720928 | tf_op jit(solution)/shard_map/ppermute | solution.py:83
  39.9 1.1 collective-permute-start.16
  41.1 3.0 %collective-permute-start.15 = (bf16[512,1408]{1,0:T(8,128)(2,1)S(1)}, bf16[512,1408]{1,0:T(8,128)(2,1)S(1)}, u32[]{:S(2)}, u32[]{:S(2)}) collective-permute-start(bf16[512,1408]{1,0:T(8,128)(2,1)S(1)} %pad_maximum_fusion.3), channel_id=1, source_target_pairs={{0,66},{1,67},{2,64},{3,65},{4,70},{5,71},{6,68},{7,69},{8,74},{9,... | collective-permute-start | bytes 4325384 | tf_op jit(solution)/shard_map/ppermute | solution.py:83
  45.0 2.2 %collective-permute-start.11 = (bf16[512,1408]{1,0:T(8,128)(2,1)S(1)}, bf16[512,1408]{1,0:T(8,128)(2,1)S(1)}, u32[]{:S(2)}, u32[]{:S(2)}) collective-permute-start(bf16[512,1408]{1,0:T(8,128)(2,1)S(1)} %pad_maximum_fusion.2), channel_id=1, source_target_pairs={{0,48},{1,49},{2,50},{3,51},{4,52},{5,53},{6,54},{7,55},{8,56},{9,... | collective-permute-start | bytes 4325384 | tf_op jit(solution)/shard_map/ppermute | solution.py:83
  47.4 5.8 %collective-permute-done.5 = bf16[256,2048]{1,0:T(8,128)(2,1)S(1)} collective-permute-done((bf16[256,2048]{1,0:T(8,128)(2,1)S(1)}, bf16[256,2048]{1,0:T(8,128)(2,1)S(1)}, u32[]{:S(2)}, u32[]{:S(2)}) %collective-permute-start.5) | collective-permute-done | bytes 1048608 | tf_op jit(solution)/shard_map/ppermute | solution.py:83
  53.4 1.5 %collective-permute-start.6 = (bf16[512,2048]{1,0:T(8,128)(2,1)S(1)}, bf16[512,2048]{1,0:T(8,128)(2,1)S(1)}, u32[]{:S(2)}, u32[]{:S(2)}) collective-permute-start(bf16[512,2048]{1,0:T(8,128)(2,1)S(1)} %pad_maximum_fusion.1), channel_id=1, source_target_pairs={{0,4},{1,5},{2,6},{3,7},{4,0},{5,1},{6,2},{7,3},{8,12},{9,13},{10,... | collective-permute-start | bytes 6291464 | tf_op jit(solution)/shard_map/ppermute | solution.py:83
  55.0 1.3 copy-done.1
  56.5 1.2 collective-permute-start.3
  57.7 19.2 %collective-permute-done.11 = bf16[512,1408]{1,0:T(8,128)(2,1)S(1)} collective-permute-done((bf16[512,1408]{1,0:T(8,128)(2,1)S(1)}, bf16[512,1408]{1,0:T(8,128)(2,1)S(1)}, u32[]{:S(2)}, u32[]{:S(2)}) %collective-permute-start.11) | collective-permute-done | bytes 1441824 | tf_op jit(solution)/shard_map/ppermute | solution.py:83
  78.8 19.6 %collective-permute-done.6 = bf16[512,2048]{1,0:T(8,128)(2,1)S(1)} collective-permute-done((bf16[512,2048]{1,0:T(8,128)(2,1)S(1)}, bf16[512,2048]{1,0:T(8,128)(2,1)S(1)}, u32[]{:S(2)}, u32[]{:S(2)}) %collective-permute-start.6) | collective-permute-done | bytes 2097184 | tf_op jit(solution)/shard_map/ppermute | solution.py:83
  98.6 5.3 %collective-permute-done.3 = bf16[512,2176]{1,0:T(8,128)(2,1)S(1)} collective-permute-done((bf16[512,2176]{1,0:T(8,128)(2,1)S(1)}, bf16[512,2176]{1,0:T(8,128)(2,1)S(1)}, u32[]{:S(2)}, u32[]{:S(2)}) %collective-permute-start.3) | collective-permute-done | bytes 2228256 | tf_op jit(solution)/shard_map/ppermute | solution.py:83
  104.3 2.6 %fusion = f32[512,1024]{1,0:T(8,128)S(1)} fusion(bf16[512,2176]{1,0:T(8,128)(2,1)S(1)} %get-tuple-element.4, bf16[1024,4224]{1,0:T(8,128)(2,1)S(1)} %slice_dynamic-update-slice_fusion), kind=kOutput, calls=%fused_computation | convolution fusion | flops 2281701376 | bytes 8781824 | tf_op jit(solution)/shard_map/dot_general | solution.py:142
  107.0 2.4 %fusion.16 = f32[512,1024]{1,0:T(8,128)S(1)} fusion(f32[512,1024]{1,0:T(8,128)S(1)} %fusion, bf16[512,2048]{1,0:T(8,128)(2,1)S(1)} %get-tuple-element.14, bf16[1024,4224]{1,0:T(8,128)(2,1)S(1)} %slice_dynamic-update-slice_fusion), kind=kOutput, calls=%fused_computation.19 | convolution fusion | flops 2148007936 | bytes 10485760 | tf_op jit(solution)/shard_map/dot_general | solution.py:142
  110.1 2.6 %fusion.2 = f32[512,1024]{1,0:T(8,128)S(1)} fusion(bf16[512,2176]{1,0:T(8,128)(2,1)S(1)} %get-tuple-element.5, bf16[1024,4224]{1,0:T(8,128)(2,1)S(1)} %slice_dynamic-update-slice_fusion), kind=kOutput, calls=%fused_computation.2 | convolution fusion | flops 2281701376 | bytes 8781824 | tf_op jit(solution)/shard_map/dot_general | solution.py:142
  112.7 2.4 %fusion.13 = f32[512,1024]{1,0:T(8,128)S(1)} fusion(f32[512,1024]{1,0:T(8,128)S(1)} %fusion.2, bf16[512,2048]{1,0:T(8,128)(2,1)S(1)} %get-tuple-element.15, bf16[1024,4224]{1,0:T(8,128)(2,1)S(1)} %slice_dynamic-update-slice_fusion), kind=kOutput, calls=%fused_computation.18 | convolution fusion | flops 2148007936 | bytes 10485760 | tf_op jit(solution)/shard_map/dot_general | solution.py:142
  120.1 4.1 %collective-permute-done.22 = f32[256]{0:T(256)S(1)} collective-permute-done((f32[256]{0:T(256)S(1)}, f32[256]{0:T(256)S(1)}, u32[]{:S(2)}, u32[]{:S(2)}) %collective-permute-start.22) | collective-permute-done | bytes 1056 | tf_op jit(solution)/shard_map/ppermute | solution.py:120
  124.2 8.2 %collective-permute-done.18 = f32[256,512]{1,0:T(8,128)S(1)} collective-permute-done((f32[256,512]{1,0:T(8,128)S(1)}, f32[256,512]{1,0:T(8,128)S(1)}, u32[]{:S(2)}, u32[]{:S(2)}) %collective-permute-start.18) | collective-permute-done | bytes 524320 | tf_op jit(solution)/shard_map/ppermute | solution.py:120
  132.5 1.3 collective-permute-start.19
  134.2 4.3 %collective-permute-done.23 = f32[128]{0:T(128)S(1)} collective-permute-done((f32[128]{0:T(128)S(1)}, f32[128]{0:T(128)S(1)}, u32[]{:S(2)}, u32[]{:S(2)}) %collective-permute-start.23) | collective-permute-done | bytes 544 | tf_op jit(solution)/shard_map/ppermute | solution.py:120
  138.8 1.1 collective-permute-done.19
  140.9 2.5 %collective-permute-done.24 = f32[64]{0:T(128)S(1)} collective-permute-done((f32[64]{0:T(128)S(1)}, f32[64]{0:T(128)S(1)}, u32[]{:S(2)}, u32[]{:S(2)}) %collective-permute-start.24) | collective-permute-done | bytes 288 | tf_op jit(solution)/shard_map/ppermute | solution.py:120
  143.9 1.1 collective-permute-done.20
  (131 shorter events, 19.4 us)
Async XLA Ops:
  2.7 1.3 copy-start
  4.0 2.1 %collective-permute-start.7 = (bf16[64,4224]{1,0:T(8,128)(2,1)}, bf16[64,4224]{1,0:T(8,128)(2,1)S(1)}, u32[]{:S(2)}, u32[]{:S(2)}) collective-permute-start(bf16[64,4224]{1,0:T(8,128)(2,1)} %get-tuple-element.43), channel_id=1, source_target_pairs={{0,1},{1,0},{2,3},{3,2},{4,5},{5,4},{6,7},{7,6},{8,9},{9,8},{10,11... | collective-permute-start | bytes 1622024 | tf_op jit(solution)/shard_map/ppermute | solution.py:96
  5.2 11.0 %collective-permute-start = (bf16[64,4224]{1,0:T(8,128)(2,1)}, bf16[64,4224]{1,0:T(8,128)(2,1)S(1)}, u32[]{:S(2)}, u32[]{:S(2)}) collective-permute-start(bf16[64,4224]{1,0:T(8,128)(2,1)} %get-tuple-element.44), channel_id=1, source_target_pairs={{0,1},{1,0},{2,3},{3,2},{4,5},{5,4},{6,7},{7,6},{8,9},{9,8},{10,11... | collective-permute-start | bytes 1622024 | tf_op jit(solution)/shard_map/ppermute | solution.py:96
  6.2 11.7 %collective-permute-start.8 = (bf16[128,1408]{1,0:T(8,128)(2,1)S(1)}, bf16[128,1408]{1,0:T(8,128)(2,1)S(1)}, u32[]{:S(2)}, u32[]{:S(2)}) collective-permute-start(bf16[128,1408]{1,0:T(8,128)(2,1)S(1)} %get-tuple-element.40), channel_id=1, source_target_pairs={{0,48},{1,49},{2,50},{3,51},{4,52},{5,53},{6,54},{7,55},{8,56},{9,... | collective-permute-start | bytes 1081352 | tf_op jit(solution)/shard_map/ppermute | solution.py:83
  9.1 12.5 %collective-permute-start.12 = (bf16[128,1408]{1,0:T(8,128)(2,1)S(1)}, bf16[128,1408]{1,0:T(8,128)(2,1)S(1)}, u32[]{:S(2)}, u32[]{:S(2)}) collective-permute-start(bf16[128,1408]{1,0:T(8,128)(2,1)S(1)} %get-tuple-element.41), channel_id=1, source_target_pairs={{0,12},{1,13},{2,14},{3,15},{4,8},{5,9},{6,10},{7,11},{8,4},{9,5},... | collective-permute-start | bytes 1081352 | tf_op jit(solution)/shard_map/ppermute | solution.py:83
  13.2 12.5 %collective-permute-start.9 = (bf16[128,1408]{1,0:T(8,128)(2,1)S(1)}, bf16[128,1408]{1,0:T(8,128)(2,1)S(1)}, u32[]{:S(2)}, u32[]{:S(2)}) collective-permute-start(bf16[128,1408]{1,0:T(8,128)(2,1)S(1)} %get-tuple-element.42), channel_id=1, source_target_pairs={{0,66},{1,67},{2,64},{3,65},{4,70},{5,71},{6,68},{7,69},{8,74},{9,... | collective-permute-start | bytes 1081352 | tf_op jit(solution)/shard_map/ppermute | solution.py:83
  16.2 14.4 %collective-permute-start.1 = (bf16[128,2176]{1,0:T(8,128)(2,1)S(1)}, bf16[128,2176]{1,0:T(8,128)(2,1)S(1)}, u32[]{:S(2)}, u32[]{:S(2)}) collective-permute-start(bf16[128,2176]{1,0:T(8,128)(2,1)S(1)} %fusion.20), channel_id=1, source_target_pairs={{0,4},{1,5},{2,6},{3,7},{4,0},{5,1},{6,2},{7,3},{8,12},{9,13},{10,... | collective-permute-start | bytes 1671176 | tf_op jit(solution)/shard_map/ppermute | solution.py:83
  16.4 13.2 %collective-permute-start.4 = (bf16[128,2048]{1,0:T(8,128)(2,1)S(1)}, bf16[128,2048]{1,0:T(8,128)(2,1)S(1)}, u32[]{:S(2)}, u32[]{:S(2)}) collective-permute-start(bf16[128,2048]{1,0:T(8,128)(2,1)S(1)} %pad_maximum_fusion.19), channel_id=1, source_target_pairs={{0,16},{1,17},{2,18},{3,19},{4,20},{5,21},{6,22},{7,23},{8,24},{9,... | collective-permute-start | bytes 1572872 | tf_op jit(solution)/shard_map/ppermute | solution.py:83
  18.0 21.8 %collective-permute-start.14 = (bf16[256,1408]{1,0:T(8,128)(2,1)S(1)}, bf16[256,1408]{1,0:T(8,128)(2,1)S(1)}, u32[]{:S(2)}, u32[]{:S(2)}) collective-permute-start(bf16[256,1408]{1,0:T(8,128)(2,1)S(1)} %pad_maximum_fusion.18), channel_id=1, source_target_pairs={{0,66},{1,67},{2,64},{3,65},{4,70},{5,71},{6,68},{7,69},{8,74},{9,... | collective-permute-start | bytes 2162696 | tf_op jit(solution)/shard_map/ppermute | solution.py:83
  21.7 19.4 %collective-permute-start.13 = (bf16[256,1408]{1,0:T(8,128)(2,1)S(1)}, bf16[256,1408]{1,0:T(8,128)(2,1)S(1)}, u32[]{:S(2)}, u32[]{:S(2)}) collective-permute-start(bf16[256,1408]{1,0:T(8,128)(2,1)S(1)} %pad_maximum_fusion.17), channel_id=1, source_target_pairs={{0,48},{1,49},{2,50},{3,51},{4,52},{5,53},{6,54},{7,55},{8,56},{9,... | collective-permute-start | bytes 2162696 | tf_op jit(solution)/shard_map/ppermute | solution.py:83
  25.8 19.1 %collective-permute-start.10 = (bf16[256,1408]{1,0:T(8,128)(2,1)S(1)}, bf16[256,1408]{1,0:T(8,128)(2,1)S(1)}, u32[]{:S(2)}, u32[]{:S(2)}) collective-permute-start(bf16[256,1408]{1,0:T(8,128)(2,1)S(1)} %pad_maximum_fusion.16), channel_id=1, source_target_pairs={{0,12},{1,13},{2,14},{3,15},{4,8},{5,9},{6,10},{7,11},{8,4},{9,5},... | collective-permute-start | bytes 2162696 | tf_op jit(solution)/shard_map/ppermute | solution.py:83
  29.6 23.5 %collective-permute-start.5 = (bf16[256,2048]{1,0:T(8,128)(2,1)S(1)}, bf16[256,2048]{1,0:T(8,128)(2,1)S(1)}, u32[]{:S(2)}, u32[]{:S(2)}) collective-permute-start(bf16[256,2048]{1,0:T(8,128)(2,1)S(1)} %pad_maximum_fusion.15), channel_id=1, source_target_pairs={{0,64},{1,65},{2,66},{3,67},{4,68},{5,69},{6,70},{7,71},{8,72},{9,... | collective-permute-start | bytes 3145736 | tf_op jit(solution)/shard_map/ppermute | solution.py:83
  30.7 25.6 %collective-permute-start.2 = (bf16[256,2176]{1,0:T(8,128)(2,1)S(1)}, bf16[256,2176]{1,0:T(8,128)(2,1)S(1)}, u32[]{:S(2)}, u32[]{:S(2)}) collective-permute-start(bf16[256,2176]{1,0:T(8,128)(2,1)S(1)} %pad_maximum_fusion.5), channel_id=1, source_target_pairs={{0,16},{1,17},{2,18},{3,19},{4,20},{5,21},{6,22},{7,23},{8,24},{9,... | collective-permute-start | bytes 3342344 | tf_op jit(solution)/shard_map/ppermute | solution.py:83
  39.9 37.7 %collective-permute-start.16 = (bf16[512,1408]{1,0:T(8,128)(2,1)S(1)}, bf16[512,1408]{1,0:T(8,128)(2,1)S(1)}, u32[]{:S(2)}, u32[]{:S(2)}) collective-permute-start(bf16[512,1408]{1,0:T(8,128)(2,1)S(1)} %pad_maximum_fusion.4), channel_id=1, source_target_pairs={{0,12},{1,13},{2,14},{3,15},{4,8},{5,9},{6,10},{7,11},{8,4},{9,5},... | collective-permute-start | bytes 4325384 | tf_op jit(solution)/shard_map/ppermute | solution.py:83
  41.1 36.1 %collective-permute-start.15 = (bf16[512,1408]{1,0:T(8,128)(2,1)S(1)}, bf16[512,1408]{1,0:T(8,128)(2,1)S(1)}, u32[]{:S(2)}, u32[]{:S(2)}) collective-permute-start(bf16[512,1408]{1,0:T(8,128)(2,1)S(1)} %pad_maximum_fusion.3), channel_id=1, source_target_pairs={{0,66},{1,67},{2,64},{3,65},{4,70},{5,71},{6,68},{7,69},{8,74},{9,... | collective-permute-start | bytes 4325384 | tf_op jit(solution)/shard_map/ppermute | solution.py:83
  45.0 31.9 %collective-permute-start.11 = (bf16[512,1408]{1,0:T(8,128)(2,1)S(1)}, bf16[512,1408]{1,0:T(8,128)(2,1)S(1)}, u32[]{:S(2)}, u32[]{:S(2)}) collective-permute-start(bf16[512,1408]{1,0:T(8,128)(2,1)S(1)} %pad_maximum_fusion.2), channel_id=1, source_target_pairs={{0,48},{1,49},{2,50},{3,51},{4,52},{5,53},{6,54},{7,55},{8,56},{9,... | collective-permute-start | bytes 4325384 | tf_op jit(solution)/shard_map/ppermute | solution.py:83
  47.2 29.9 %slice-start = ((s8[8650752]{0:T(1024)(128)(4,1)}), s8[4194304]{0:T(1024)(128)(4,1)S(1)}, s32[]{:S(2)}) async-start(s8[8650752]{0:T(1024)(128)(4,1)} %bitcast.6), calls=%async_computation | async-start | bytes 8388608
  47.3 7.6 %copy-start.3 = (bf16[512,2048]{1,0:T(8,128)(2,1)S(1)}, bf16[512,2048]{1,0:T(8,128)(2,1)}, u32[]{:S(2)}) copy-start(bf16[512,2048]{1,0:T(8,128)(2,1)} %get-tuple-element.66) | copy-start | bytes 6291460
  47.3 29.8 %slice-start.1 = ((s8[8650752]{0:T(1024)(128)(4,1)}), s8[4194304]{0:T(1024)(128)(4,1)S(1)}, s32[]{:S(2)}) async-start(s8[8650752]{0:T(1024)(128)(4,1)} %bitcast.6), calls=%async_computation.1 | async-start | bytes 8388608
  53.4 45.1 %collective-permute-start.6 = (bf16[512,2048]{1,0:T(8,128)(2,1)S(1)}, bf16[512,2048]{1,0:T(8,128)(2,1)S(1)}, u32[]{:S(2)}, u32[]{:S(2)}) collective-permute-start(bf16[512,2048]{1,0:T(8,128)(2,1)S(1)} %pad_maximum_fusion.1), channel_id=1, source_target_pairs={{0,4},{1,5},{2,6},{3,7},{4,0},{5,1},{6,2},{7,3},{8,12},{9,13},{10,... | collective-permute-start | bytes 6291464 | tf_op jit(solution)/shard_map/ppermute | solution.py:83
  55.0 1.3 copy-start.1
  56.3 20.8 %slice-start.2 = ((s8[8650752]{0:T(1024)(128)(4,1)}), s8[262144]{0:T(1024)(128)(4,1)S(1)}, s32[]{:S(2)}) async-start(s8[8650752]{0:T(1024)(128)(4,1)} %bitcast.6), calls=%async_computation.2 | async-start | bytes 524288
  56.5 47.5 %collective-permute-start.3 = (bf16[512,2176]{1,0:T(8,128)(2,1)S(1)}, bf16[512,2176]{1,0:T(8,128)(2,1)S(1)}, u32[]{:S(2)}, u32[]{:S(2)}) collective-permute-start(bf16[512,2176]{1,0:T(8,128)(2,1)S(1)} %pad_maximum_fusion), channel_id=1, source_target_pairs={{0,64},{1,65},{2,66},{3,67},{4,68},{5,69},{6,70},{7,71},{8,72},{9,... | collective-permute-start | bytes 6684680 | tf_op jit(solution)/shard_map/ppermute | solution.py:83
  78.6 19.9 %copy-start.2 = (bf16[512,2048]{1,0:T(8,128)(2,1)S(1)}, bf16[512,2048]{1,0:T(8,128)(2,1)}, u32[]{:S(2)}) copy-start(bf16[512,2048]{1,0:T(8,128)(2,1)} %copy-done.1) | copy-start | bytes 6291460
  109.3 6.1 %collective-permute-start.17 = (f32[512,1024]{1,0:T(8,128)S(1)}, f32[512,1024]{1,0:T(8,128)S(1)}, u32[]{:S(2)}, u32[]{:S(2)}) collective-permute-start(f32[512,1024]{1,0:T(8,128)S(1)} %fusion.16), channel_id=1, source_target_pairs={{0,1},{1,0},{2,3},{3,2},{4,5},{5,4},{6,7},{7,6},{8,9},{9,8},{10,11... | collective-permute-start | bytes 6291464 | tf_op jit(solution)/shard_map/ppermute | solution.py:149
  117.8 1.4 collective-permute-start.21
  118.5 13.9 %collective-permute-start.18 = (f32[256,512]{1,0:T(8,128)S(1)}, f32[256,512]{1,0:T(8,128)S(1)}, u32[]{:S(2)}, u32[]{:S(2)}) collective-permute-start(f32[256,512]{1,0:T(8,128)S(1)} %pad_maximum_fusion.20), channel_id=1, source_target_pairs={{0,16},{1,17},{2,18},{3,19},{4,20},{5,21},{6,22},{7,23},{8,24},{9,... | collective-permute-start | bytes 1572872 | tf_op jit(solution)/shard_map/ppermute | solution.py:120
  119.4 4.8 %collective-permute-start.22 = (f32[256]{0:T(256)S(1)}, f32[256]{0:T(256)S(1)}, u32[]{:S(2)}, u32[]{:S(2)}) collective-permute-start(f32[256]{0:T(256)S(1)} %pad_maximum_fusion.23), channel_id=1, source_target_pairs={{0,48},{1,49},{2,50},{3,51},{4,52},{5,53},{6,54},{7,55},{8,56},{9,... | collective-permute-start | bytes 3080 | tf_op jit(solution)/shard_map/ppermute | solution.py:120
  132.5 7.5 %collective-permute-start.19 = (f32[128,512]{1,0:T(8,128)S(1)}, f32[128,512]{1,0:T(8,128)S(1)}, u32[]{:S(2)}, u32[]{:S(2)}) collective-permute-start(f32[128,512]{1,0:T(8,128)S(1)} %pad_maximum_fusion.22), channel_id=1, source_target_pairs={{0,64},{1,65},{2,66},{3,67},{4,68},{5,69},{6,70},{7,71},{8,72},{9,... | collective-permute-start | bytes 786440 | tf_op jit(solution)/shard_map/ppermute | solution.py:120
  133.8 4.8 %collective-permute-start.23 = (f32[128]{0:T(128)S(1)}, f32[128]{0:T(128)S(1)}, u32[]{:S(2)}, u32[]{:S(2)}) collective-permute-start(f32[128]{0:T(128)S(1)} %pad_maximum_fusion.24), channel_id=1, source_target_pairs={{0,66},{1,67},{2,64},{3,65},{4,70},{5,71},{6,68},{7,69},{8,74},{9,... | collective-permute-start | bytes 1544 | tf_op jit(solution)/shard_map/ppermute | solution.py:120
  138.7 4.8 %collective-permute-start.24 = (f32[64]{0:T(128)S(1)}, f32[64]{0:T(128)S(1)}, u32[]{:S(2)}, u32[]{:S(2)}) collective-permute-start(f32[64]{0:T(128)S(1)} %slice_add_fusion.7), channel_id=1, source_target_pairs={{0,12},{1,13},{2,14},{3,15},{4,8},{5,9},{6,10},{7,11},{8,4},{9,5},... | collective-permute-start | bytes 776 | tf_op jit(solution)/shard_map/ppermute | solution.py:120
  140.0 5.0 %collective-permute-start.20 = (f32[64,512]{1,0:T(8,128)S(1)}, f32[64,512]{1,0:T(8,128)S(1)}, u32[]{:S(2)}, u32[]{:S(2)}) collective-permute-start(f32[64,512]{1,0:T(8,128)S(1)} %slice_add_fusion), channel_id=1, source_target_pairs={{0,4},{1,5},{2,6},{3,7},{4,0},{5,1},{6,2},{7,3},{8,12},{9,13},{10,... | collective-permute-start | bytes 393224 | tf_op jit(solution)/shard_map/ppermute | solution.py:120
  (1 other events, 1.3 us)

commit v19 on v14

--- a/solution.py
+++ b/solution.py
@@ -75,10 +75,14 @@
     return [(tiles * p // m) * 128 for p in range(m)] + [cols]
 
 
-def chain(part, mate, n, order):
+def chain(part, mate, n, order, first=None):
     rows = part.shape[0]
     buf = part
     labs = [0]
+    if first is not None:
+        buf = jnp.concatenate([buf, first])
+        labs = [0, 1 << order[0]]
+        order = order[1:]
     for a in order:
         got = lax.ppermute(buf, AXES, mate_pairs(n, a, mate))
         buf = jnp.concatenate([buf, got])
@@ -95,12 +99,17 @@
     return jnp.concatenate([mine, lax.ppermute(give, AXES, core_pairs(n))])
 
 
-def half_gather(unit, mate, n, orders):
-    r = unit.shape[0] // 2
-    cut = column_cuts(unit.shape[1], len(orders))
-    parts = [chain(unit[:, cut[p]:cut[p + 1]], mate, n, order) for p, order in enumerate(orders)]
+def half_gather(pieces, mate, n, orders, firsts=None):
+    r = pieces[0].shape[0] // 2
+    firsts = firsts or [None] * len(orders)
+    parts = [chain(q, mate, n, order, f) for q, order, f in zip(pieces, orders, firsts)]
     blocks = [jnp.concatenate([parts[p][o] for p in range(len(orders))], axis=1) for o in range(8)]
     return jnp.concatenate([b[:r] for b in blocks] + [b[r:] for b in blocks])
+
+
+def column_pieces(unit, m):
+    cut = column_cuts(unit.shape[1], m)
+    return [unit[:, cut[p]:cut[p + 1]] for p in range(m)]
 
 
 def cube_reduce(blocks, mate, n):
@@ -126,9 +135,14 @@
     tr = with_side(train_grads, (train_scale,) + split_class(train_class), 0)
     te = with_side(test_grads, split_class(test_class), 4)
     side = k // 2
-    tr_unit, te_unit = lax.optimization_barrier((half_unit(tr, n), half_unit(te, n)))
-    tr_all = half_gather(tr_unit, train_mate, n, TWO)
-    te_all = half_gather(te_unit, test_mate, n, THREE)
+    tr_pieces = column_pieces(half_unit(tr, n), len(TWO))
+    tr_first = [
+        lax.ppermute(q, AXES, mate_pairs(n, order[0], train_mate))
+        for q, order in zip(tr_pieces, TWO)
+    ]
+    te_unit, tr_first = lax.optimization_barrier((half_unit(te, n), tr_first))
+    tr_all = half_gather(tr_pieces, train_mate, n, TWO, tr_first)
+    te_all = half_gather(column_pieces(te_unit, len(THREE)), test_mate, n, THREE)
     half = 8 * rows
 
     def partial(t):
@@ -137,7 +151,8 @@
         )
 
     got = lax.ppermute(partial(tr_all[half:]), AXES, core_pairs(n))
-    raw = partial(tr_all[:half]) + jnp.concatenate([got[:, half:], got[:, :half]], axis=1)
+    own = lax.optimization_barrier(partial(tr_all[:half]))
+    raw = own + jnp.concatenate([got[:, half:], got[:, :half]], axis=1)
     tr_mine = tr_all[:half]
     scale = tr_mine[:, side].astype(jnp.float32)
     train_hot = indicator(join_class(tr_mine, side + 1))

time: 150 us -> 149 us (level)
  starting transfers between devices: 35.5 us -> 30.3 us
  waiting for transfers between devices: 89.1 us -> 92.7 us
    ppermute x0 -> x2, waiting for transfers between devices: none -> 11.3 us  [local(): lax.ppermute(q, AXES, mate_pairs(n, order[0], train_mate))]
    ppermute x15 -> x13, starting transfers between devices: 31.4 us -> 23.8 us  [chain(): got = lax.ppermute(buf, AXES, mate_pairs(n, a, mate))]
    ppermute x15 -> x13, waiting for transfers between devices: 61.2 us -> 57.4 us  [chain(): got = lax.ppermute(buf, AXES, mate_pairs(n, a, mate))]
    ppermute x0 -> x2, starting transfers between devices: none -> 3.65 us  [local(): lax.ppermute(q, AXES, mate_pairs(n, order[0], train_mate))]
    ppermute x1, waiting for transfers between devices: 3.37 us -> 0.01 us  [local(): got = lax.ppermute(partial(tr_all[half:]), AXES, core_pairs(n))]
    ppermute x6, starting transfers between devices: 3.53 us -> 1.99 us  [cube_reduce(): lax.ppermute(jnp.concatenate([blocks[o] for o in send]), AXES, mate_pairs...]
  transfers between devices with their start and end apart: 25 -> 25, of which waited for: 23 -> 15; matrix products, arithmetic and copies ran while one was open for 5% -> 8% of each run, Pallas kernels for 0% -> 0%
where the time goes in v19:
time: 149 us
  waiting for transfers between devices  92.7 us (62%)
  starting transfers between devices  30.3 us (20%)
  matrix products  11.2 us (8%)
  other arithmetic  7.36 us (5%)
  local copies, waits for them, and re-layouts  5.6 us (4%)
    ppermute x13, waiting for transfers between devices, chain(): got = lax.ppermute(buf, AXES, mate_pairs(n, a, mate))  57.4 us
    ppermute x13, starting transfers between devices, chain(): got = lax.ppermute(buf, AXES, mate_pairs(n, a, mate))  23.8 us
    ppermute x6, waiting for transfers between devices, cube_reduce(): lax.ppermute(jnp.concatenate([blocks[o] for o in send]), AXES, mate_pairs...  22.9 us
    ppermute x2, waiting for transfers between devices, local(): lax.ppermute(q, AXES, mate_pairs(n, order[0], train_mate))  11.3 us
    dot_general x2, matrix products, partial(): lax.dot_general(t, te_all, (((1,), (1,)), ((), ())), preferred_element_ty...  9.56 us
    ppermute x2, starting transfers between devices, local(): lax.ppermute(q, AXES, mate_pairs(n, order[0], train_mate))  3.65 us
  transfers between devices with their start and end apart: 25, of which 15 were waited for; matrix products, arithmetic and copies ran while one was open for 8% of the time, Pallas kernels for 0%

profile of v19, /device:TPU:0, one launch (start us, length us, event | category | flops | bytes accessed | tf_op | source)
XLA Modules:
  0.0 148.5 jit_solution(8894398393903096369)
XLA Ops:
  0.7 1.3 fusion.44
  3.1 0.9 copy-done
  5.1 2.1 %collective-permute-start.3 = (bf16[128,2176]{1,0:T(8,128)(2,1)S(1)}, bf16[128,2176]{1,0:T(8,128)(2,1)S(1)}, u32[]{:S(2)}, u32[]{:S(2)}) collective-permute-start(bf16[128,2176]{1,0:T(8,128)(2,1)S(1)} %pad_maximum_fusion.20), channel_id=1, source_target_pairs={{0,4},{1,5},{2,6},{3,7},{4,0},{5,1},{6,2},{7,3},{8,12},{9,13},{10,... | collective-permute-start | bytes 1671176 | tf_op jit(solution)/shard_map/ppermute | solution.py:140
  7.2 1.6 %collective-permute-start.2 = (bf16[128,2048]{1,0:T(8,128)(2,1)S(1)}, bf16[128,2048]{1,0:T(8,128)(2,1)S(1)}, u32[]{:S(2)}, u32[]{:S(2)}) collective-permute-start(bf16[128,2048]{1,0:T(8,128)(2,1)S(1)} %pad_maximum_fusion.28), channel_id=1, source_target_pairs={{0,16},{1,17},{2,18},{3,19},{4,20},{5,21},{6,22},{7,23},{8,24},{9,... | collective-permute-start | bytes 1572872 | tf_op jit(solution)/shard_map/ppermute | solution.py:140
  8.9 0.8 constant_dynamic-update-slice_fusion.1
  9.7 11.3 %collective-permute-done.2 = bf16[128,2048]{1,0:T(8,128)(2,1)S(1)} collective-permute-done((bf16[128,2048]{1,0:T(8,128)(2,1)S(1)}, bf16[128,2048]{1,0:T(8,128)(2,1)S(1)}, u32[]{:S(2)}, u32[]{:S(2)}) %collective-permute-start.2) | collective-permute-done | bytes 524320 | tf_op jit(solution)/shard_map/ppermute | solution.py:140
  21.1 2.8 %collective-permute-start.8 = (bf16[128,1408]{1,0:T(8,128)(2,1)S(1)}, bf16[128,1408]{1,0:T(8,128)(2,1)S(1)}, u32[]{:S(2)}, u32[]{:S(2)}) collective-permute-start(bf16[128,1408]{1,0:T(8,128)(2,1)S(1)} %get-tuple-element.50), channel_id=1, source_target_pairs={{0,48},{1,49},{2,50},{3,51},{4,52},{5,53},{6,54},{7,55},{8,56},{9,... | collective-permute-start | bytes 1081352 | tf_op jit(solution)/shard_map/ppermute | solution.py:87
  24.0 3.0 %collective-permute-start.9 = (bf16[128,1408]{1,0:T(8,128)(2,1)S(1)}, bf16[128,1408]{1,0:T(8,128)(2,1)S(1)}, u32[]{:S(2)}, u32[]{:S(2)}) collective-permute-start(bf16[128,1408]{1,0:T(8,128)(2,1)S(1)} %get-tuple-element.52), channel_id=1, source_target_pairs={{0,66},{1,67},{2,64},{3,65},{4,70},{5,71},{6,68},{7,69},{8,74},{9,... | collective-permute-start | bytes 1081352 | tf_op jit(solution)/shard_map/ppermute | solution.py:87
  27.0 3.0 %collective-permute-start.12 = (bf16[128,1408]{1,0:T(8,128)(2,1)S(1)}, bf16[128,1408]{1,0:T(8,128)(2,1)S(1)}, u32[]{:S(2)}, u32[]{:S(2)}) collective-permute-start(bf16[128,1408]{1,0:T(8,128)(2,1)S(1)} %get-tuple-element.51), channel_id=1, source_target_pairs={{0,12},{1,13},{2,14},{3,15},{4,8},{5,9},{6,10},{7,11},{8,4},{9,5},... | collective-permute-start | bytes 1081352 | tf_op jit(solution)/shard_map/ppermute | solution.py:87
  30.6 1.1 collective-permute-done.8
  31.8 3.1 %collective-permute-start.14 = (bf16[256,1408]{1,0:T(8,128)(2,1)S(1)}, bf16[256,1408]{1,0:T(8,128)(2,1)S(1)}, u32[]{:S(2)}, u32[]{:S(2)}) collective-permute-start(bf16[256,1408]{1,0:T(8,128)(2,1)S(1)} %pad_maximum_fusion.19), channel_id=1, source_target_pairs={{0,66},{1,67},{2,64},{3,65},{4,70},{5,71},{6,68},{7,69},{8,74},{9,... | collective-permute-start | bytes 2162696 | tf_op jit(solution)/shard_map/ppermute | solution.py:87
  34.9 3.4 %collective-permute-start.10 = (bf16[256,1408]{1,0:T(8,128)(2,1)S(1)}, bf16[256,1408]{1,0:T(8,128)(2,1)S(1)}, u32[]{:S(2)}, u32[]{:S(2)}) collective-permute-start(bf16[256,1408]{1,0:T(8,128)(2,1)S(1)} %pad_maximum_fusion.17), channel_id=1, source_target_pairs={{0,12},{1,13},{2,14},{3,15},{4,8},{5,9},{6,10},{7,11},{8,4},{9,5},... | collective-permute-start | bytes 2162696 | tf_op jit(solution)/shard_map/ppermute | solution.py:87
  38.4 2.8 %collective-permute-start.13 = (bf16[256,1408]{1,0:T(8,128)(2,1)S(1)}, bf16[256,1408]{1,0:T(8,128)(2,1)S(1)}, u32[]{:S(2)}, u32[]{:S(2)}) collective-permute-start(bf16[256,1408]{1,0:T(8,128)(2,1)S(1)} %pad_maximum_fusion.18), channel_id=1, source_target_pairs={{0,48},{1,49},{2,50},{3,51},{4,52},{5,53},{6,54},{7,55},{8,56},{9,... | collective-permute-start | bytes 2162696 | tf_op jit(solution)/shard_map/ppermute | solution.py:87
  41.2 12.4 %collective-permute-done.5 = bf16[256,2048]{1,0:T(8,128)(2,1)S(1)} collective-permute-done((bf16[256,2048]{1,0:T(8,128)(2,1)S(1)}, bf16[256,2048]{1,0:T(8,128)(2,1)S(1)}, u32[]{:S(2)}, u32[]{:S(2)}) %collective-permute-start.5) | collective-permute-done | bytes 1048608 | tf_op jit(solution)/shard_map/ppermute | solution.py:87
  54.3 1.0 collective-permute-start.16
  55.4 0.7 collective-permute-start.11
  56.3 2.9 %collective-permute-start.15 = (bf16[512,1408]{1,0:T(8,128)(2,1)S(1)}, bf16[512,1408]{1,0:T(8,128)(2,1)S(1)}, u32[]{:S(2)}, u32[]{:S(2)}) collective-permute-start(bf16[512,1408]{1,0:T(8,128)(2,1)S(1)} %pad_maximum_fusion.3), channel_id=1, source_target_pairs={{0,66},{1,67},{2,64},{3,65},{4,70},{5,71},{6,68},{7,69},{8,74},{9,... | collective-permute-start | bytes 4325384 | tf_op jit(solution)/shard_map/ppermute | solution.py:87
  59.9 0.9 fusion.26
  60.8 26.4 %collective-permute-done.11 = bf16[512,1408]{1,0:T(8,128)(2,1)S(1)} collective-permute-done((bf16[512,1408]{1,0:T(8,128)(2,1)S(1)}, bf16[512,1408]{1,0:T(8,128)(2,1)S(1)}, u32[]{:S(2)}, u32[]{:S(2)}) %collective-permute-start.11) | collective-permute-done | bytes 1441824 | tf_op jit(solution)/shard_map/ppermute | solution.py:87
  89.5 9.5 %collective-permute-done.7 = bf16[512,2048]{1,0:T(8,128)(2,1)S(1)} collective-permute-done((bf16[512,2048]{1,0:T(8,128)(2,1)S(1)}, bf16[512,2048]{1,0:T(8,128)(2,1)S(1)}, u32[]{:S(2)}, u32[]{:S(2)}) %collective-permute-start.7) | collective-permute-done | bytes 2097184 | tf_op jit(solution)/shard_map/ppermute | solution.py:87
  99.2 7.5 %collective-permute-done.6 = bf16[512,2176]{1,0:T(8,128)(2,1)S(1)} collective-permute-done((bf16[512,2176]{1,0:T(8,128)(2,1)S(1)}, bf16[512,2176]{1,0:T(8,128)(2,1)S(1)}, u32[]{:S(2)}, u32[]{:S(2)}) %collective-permute-start.6) | collective-permute-done | bytes 2228256 | tf_op jit(solution)/shard_map/ppermute | solution.py:87
  107.8 4.8 %fusion.50 = f32[512,1024]{1,0:T(8,128)S(1)} fusion(bf16[512,4224]{1,0:T(8,128)(2,1)S(1)} %get-tuple-element.36, bf16[1024,4224]{1,0:T(8,128)(2,1)S(1)} %slice_dynamic-update-slice_fusion), kind=kOutput, calls=%fused_computation.154 | convolution fusion | flops 4429185024 | bytes 15073280 | tf_op jit(solution)/shard_map/dot_general | solution.py:149
  113.1 4.8 %fusion.49 = f32[512,1024]{1,0:T(8,128)S(1)} fusion(bf16[512,4224]{1,0:T(8,128)(2,1)S(1)} %get-tuple-element.37, bf16[1024,4224]{1,0:T(8,128)(2,1)S(1)} %slice_dynamic-update-slice_fusion), kind=kOutput, calls=%fused_computation.153 | convolution fusion | flops 4429185024 | bytes 15073280 | tf_op jit(solution)/shard_map/dot_general | solution.py:149
  119.0 0.8 fusion.4
  119.7 0.9 multiply_reduce_fusion
  122.2 0.8 collective-permute-start.22
  123.0 4.0 %collective-permute-done.22 = f32[256]{0:T(256)S(1)} collective-permute-done((f32[256]{0:T(256)S(1)}, f32[256]{0:T(256)S(1)}, u32[]{:S(2)}, u32[]{:S(2)}) %collective-permute-start.22) | collective-permute-done | bytes 1056 | tf_op jit(solution)/shard_map/ppermute | solution.py:122
  127.1 8.2 %collective-permute-done.18 = f32[256,512]{1,0:T(8,128)S(1)} collective-permute-done((f32[256,512]{1,0:T(8,128)S(1)}, f32[256,512]{1,0:T(8,128)S(1)}, u32[]{:S(2)}, u32[]{:S(2)}) %collective-permute-start.18) | collective-permute-done | bytes 524320 | tf_op jit(solution)/shard_map/ppermute | solution.py:122
  136.1 4.4 %collective-permute-done.23 = f32[128]{0:T(128)S(1)} collective-permute-done((f32[128]{0:T(128)S(1)}, f32[128]{0:T(128)S(1)}, u32[]{:S(2)}, u32[]{:S(2)}) %collective-permute-start.23) | collective-permute-done | bytes 544 | tf_op jit(solution)/shard_map/ppermute | solution.py:122
  140.9 1.9 %collective-permute-done.19 = f32[128,512]{1,0:T(8,128)S(1)} collective-permute-done((f32[128,512]{1,0:T(8,128)S(1)}, f32[128,512]{1,0:T(8,128)S(1)}, u32[]{:S(2)}, u32[]{:S(2)}) %collective-permute-start.19) | collective-permute-done | bytes 262176 | tf_op jit(solution)/shard_map/ppermute | solution.py:122
  142.9 2.4 %collective-permute-done.24 = f32[64]{0:T(128)S(1)} collective-permute-done((f32[64]{0:T(128)S(1)}, f32[64]{0:T(128)S(1)}, u32[]{:S(2)}, u32[]{:S(2)}) %collective-permute-start.24) | collective-permute-done | bytes 288 | tf_op jit(solution)/shard_map/ppermute | solution.py:122
  145.8 2.0 %collective-permute-done.20 = f32[64,512]{1,0:T(8,128)S(1)} collective-permute-done((f32[64,512]{1,0:T(8,128)S(1)}, f32[64,512]{1,0:T(8,128)S(1)}, u32[]{:S(2)}, u32[]{:S(2)}) %collective-permute-start.20) | collective-permute-done | bytes 131104 | tf_op jit(solution)/shard_map/ppermute | solution.py:122
  (117 shorter events, 13.9 us)
Async XLA Ops:
  0.6 2.0 %copy-start.1 = (bf16[64]{0:T(256)(128)(2,1)S(1)}, bf16[64]{0:T(256)(128)(2,1)}, u32[]{:S(2)}) copy-start(bf16[64]{0:T(256)(128)(2,1)} %param.6) | copy-start | bytes 388
  2.8 1.2 copy-start
  3.0 2.0 %collective-permute-start.1 = (bf16[64,4224]{1,0:T(8,128)(2,1)S(1)}, bf16[64,4224]{1,0:T(8,128)(2,1)S(1)}, u32[]{:S(2)}, u32[]{:S(2)}) collective-permute-start(bf16[64,4224]{1,0:T(8,128)(2,1)S(1)} %get-tuple-element.53), channel_id=1, source_target_pairs={{0,1},{1,0},{2,3},{3,2},{4,5},{5,4},{6,7},{7,6},{8,9},{9,8},{10,11... | collective-permute-start | bytes 1622024 | tf_op jit(solution)/shard_map/ppermute | solution.py:99
  4.4 4.4 %collective-permute-start = (bf16[64,4224]{1,0:T(8,128)(2,1)S(1)}, bf16[64,4224]{1,0:T(8,128)(2,1)S(1)}, u32[]{:S(2)}, u32[]{:S(2)}) collective-permute-start(bf16[64,4224]{1,0:T(8,128)(2,1)S(1)} %get-tuple-element.55), channel_id=1, source_target_pairs={{0,1},{1,0},{2,3},{3,2},{4,5},{5,4},{6,7},{7,6},{8,9},{9,8},{10,11... | collective-permute-start | bytes 1622024 | tf_op jit(solution)/shard_map/ppermute | solution.py:99
  5.1 15.9 %collective-permute-start.3 = (bf16[128,2176]{1,0:T(8,128)(2,1)S(1)}, bf16[128,2176]{1,0:T(8,128)(2,1)S(1)}, u32[]{:S(2)}, u32[]{:S(2)}) collective-permute-start(bf16[128,2176]{1,0:T(8,128)(2,1)S(1)} %pad_maximum_fusion.20), channel_id=1, source_target_pairs={{0,4},{1,5},{2,6},{3,7},{4,0},{5,1},{6,2},{7,3},{8,12},{9,13},{10,... | collective-permute-start | bytes 1671176 | tf_op jit(solution)/shard_map/ppermute | solution.py:140
  7.2 13.8 %collective-permute-start.2 = (bf16[128,2048]{1,0:T(8,128)(2,1)S(1)}, bf16[128,2048]{1,0:T(8,128)(2,1)S(1)}, u32[]{:S(2)}, u32[]{:S(2)}) collective-permute-start(bf16[128,2048]{1,0:T(8,128)(2,1)S(1)} %pad_maximum_fusion.28), channel_id=1, source_target_pairs={{0,16},{1,17},{2,18},{3,19},{4,20},{5,21},{6,22},{7,23},{8,24},{9,... | collective-permute-start | bytes 1572872 | tf_op jit(solution)/shard_map/ppermute | solution.py:140
  21.1 10.6 %collective-permute-start.8 = (bf16[128,1408]{1,0:T(8,128)(2,1)S(1)}, bf16[128,1408]{1,0:T(8,128)(2,1)S(1)}, u32[]{:S(2)}, u32[]{:S(2)}) collective-permute-start(bf16[128,1408]{1,0:T(8,128)(2,1)S(1)} %get-tuple-element.50), channel_id=1, source_target_pairs={{0,48},{1,49},{2,50},{3,51},{4,52},{5,53},{6,54},{7,55},{8,56},{9,... | collective-permute-start | bytes 1081352 | tf_op jit(solution)/shard_map/ppermute | solution.py:87
  24.0 10.9 %collective-permute-start.9 = (bf16[128,1408]{1,0:T(8,128)(2,1)S(1)}, bf16[128,1408]{1,0:T(8,128)(2,1)S(1)}, u32[]{:S(2)}, u32[]{:S(2)}) collective-permute-start(bf16[128,1408]{1,0:T(8,128)(2,1)S(1)} %get-tuple-element.52), channel_id=1, source_target_pairs={{0,66},{1,67},{2,64},{3,65},{4,70},{5,71},{6,68},{7,69},{8,74},{9,... | collective-permute-start | bytes 1081352 | tf_op jit(solution)/shard_map/ppermute | solution.py:87
  27.0 11.3 %collective-permute-start.12 = (bf16[128,1408]{1,0:T(8,128)(2,1)S(1)}, bf16[128,1408]{1,0:T(8,128)(2,1)S(1)}, u32[]{:S(2)}, u32[]{:S(2)}) collective-permute-start(bf16[128,1408]{1,0:T(8,128)(2,1)S(1)} %get-tuple-element.51), channel_id=1, source_target_pairs={{0,12},{1,13},{2,14},{3,15},{4,8},{5,9},{6,10},{7,11},{8,4},{9,5},... | collective-permute-start | bytes 1081352 | tf_op jit(solution)/shard_map/ppermute | solution.py:87
  30.0 23.6 %collective-permute-start.5 = (bf16[256,2048]{1,0:T(8,128)(2,1)S(1)}, bf16[256,2048]{1,0:T(8,128)(2,1)S(1)}, u32[]{:S(2)}, u32[]{:S(2)}) collective-permute-start(bf16[256,2048]{1,0:T(8,128)(2,1)S(1)} %pad_maximum_fusion.16), channel_id=1, source_target_pairs={{0,64},{1,65},{2,66},{3,67},{4,68},{5,69},{6,70},{7,71},{8,72},{9,... | collective-permute-start | bytes 3145736 | tf_op jit(solution)/shard_map/ppermute | solution.py:87
  30.3 29.0 %collective-permute-start.4 = (bf16[256,2176]{1,0:T(8,128)(2,1)S(1)}, bf16[256,2176]{1,0:T(8,128)(2,1)S(1)}, u32[]{:S(2)}, u32[]{:S(2)}) collective-permute-start(bf16[256,2176]{1,0:T(8,128)(2,1)S(1)} %pad_maximum_fusion.5), channel_id=1, source_target_pairs={{0,16},{1,17},{2,18},{3,19},{4,20},{5,21},{6,22},{7,23},{8,24},{9,... | collective-permute-start | bytes 3342344 | tf_op jit(solution)/shard_map/ppermute | solution.py:87
  31.8 22.4 %collective-permute-start.14 = (bf16[256,1408]{1,0:T(8,128)(2,1)S(1)}, bf16[256,1408]{1,0:T(8,128)(2,1)S(1)}, u32[]{:S(2)}, u32[]{:S(2)}) collective-permute-start(bf16[256,1408]{1,0:T(8,128)(2,1)S(1)} %pad_maximum_fusion.19), channel_id=1, source_target_pairs={{0,66},{1,67},{2,64},{3,65},{4,70},{5,71},{6,68},{7,69},{8,74},{9,... | collective-permute-start | bytes 2162696 | tf_op jit(solution)/shard_map/ppermute | solution.py:87
  34.9 20.4 %collective-permute-start.10 = (bf16[256,1408]{1,0:T(8,128)(2,1)S(1)}, bf16[256,1408]{1,0:T(8,128)(2,1)S(1)}, u32[]{:S(2)}, u32[]{:S(2)}) collective-permute-start(bf16[256,1408]{1,0:T(8,128)(2,1)S(1)} %pad_maximum_fusion.17), channel_id=1, source_target_pairs={{0,12},{1,13},{2,14},{3,15},{4,8},{5,9},{6,10},{7,11},{8,4},{9,5},... | collective-permute-start | bytes 2162696 | tf_op jit(solution)/shard_map/ppermute | solution.py:87
  38.4 17.8 %collective-permute-start.13 = (bf16[256,1408]{1,0:T(8,128)(2,1)S(1)}, bf16[256,1408]{1,0:T(8,128)(2,1)S(1)}, u32[]{:S(2)}, u32[]{:S(2)}) collective-permute-start(bf16[256,1408]{1,0:T(8,128)(2,1)S(1)} %pad_maximum_fusion.18), channel_id=1, source_target_pairs={{0,48},{1,49},{2,50},{3,51},{4,52},{5,53},{6,54},{7,55},{8,56},{9,... | collective-permute-start | bytes 2162696 | tf_op jit(solution)/shard_map/ppermute | solution.py:87
  53.8 45.2 %collective-permute-start.7 = (bf16[512,2048]{1,0:T(8,128)(2,1)S(1)}, bf16[512,2048]{1,0:T(8,128)(2,1)S(1)}, u32[]{:S(2)}, u32[]{:S(2)}) collective-permute-start(bf16[512,2048]{1,0:T(8,128)(2,1)S(1)} %pad_maximum_fusion.1), channel_id=1, source_target_pairs={{0,4},{1,5},{2,6},{3,7},{4,0},{5,1},{6,2},{7,3},{8,12},{9,13},{10,... | collective-permute-start | bytes 6291464 | tf_op jit(solution)/shard_map/ppermute | solution.py:87
  54.3 33.9 %collective-permute-start.16 = (bf16[512,1408]{1,0:T(8,128)(2,1)S(1)}, bf16[512,1408]{1,0:T(8,128)(2,1)S(1)}, u32[]{:S(2)}, u32[]{:S(2)}) collective-permute-start(bf16[512,1408]{1,0:T(8,128)(2,1)S(1)} %pad_maximum_fusion.4), channel_id=1, source_target_pairs={{0,12},{1,13},{2,14},{3,15},{4,8},{5,9},{6,10},{7,11},{8,4},{9,5},... | collective-permute-start | bytes 4325384 | tf_op jit(solution)/shard_map/ppermute | solution.py:87
  55.4 31.7 %collective-permute-start.11 = (bf16[512,1408]{1,0:T(8,128)(2,1)S(1)}, bf16[512,1408]{1,0:T(8,128)(2,1)S(1)}, u32[]{:S(2)}, u32[]{:S(2)}) collective-permute-start(bf16[512,1408]{1,0:T(8,128)(2,1)S(1)} %pad_maximum_fusion.2), channel_id=1, source_target_pairs={{0,48},{1,49},{2,50},{3,51},{4,52},{5,53},{6,54},{7,55},{8,56},{9,... | collective-permute-start | bytes 4325384 | tf_op jit(solution)/shard_map/ppermute | solution.py:87
  56.3 31.6 %collective-permute-start.15 = (bf16[512,1408]{1,0:T(8,128)(2,1)S(1)}, bf16[512,1408]{1,0:T(8,128)(2,1)S(1)}, u32[]{:S(2)}, u32[]{:S(2)}) collective-permute-start(bf16[512,1408]{1,0:T(8,128)(2,1)S(1)} %pad_maximum_fusion.3), channel_id=1, source_target_pairs={{0,66},{1,67},{2,64},{3,65},{4,70},{5,71},{6,68},{7,69},{8,74},{9,... | collective-permute-start | bytes 4325384 | tf_op jit(solution)/shard_map/ppermute | solution.py:87
  59.5 47.2 %collective-permute-start.6 = (bf16[512,2176]{1,0:T(8,128)(2,1)S(1)}, bf16[512,2176]{1,0:T(8,128)(2,1)S(1)}, u32[]{:S(2)}, u32[]{:S(2)}) collective-permute-start(bf16[512,2176]{1,0:T(8,128)(2,1)S(1)} %pad_maximum_fusion), channel_id=1, source_target_pairs={{0,64},{1,65},{2,66},{3,67},{4,68},{5,69},{6,70},{7,71},{8,72},{9,... | collective-permute-start | bytes 6684680 | tf_op jit(solution)/shard_map/ppermute | solution.py:87
  89.4 17.5 %slice-start = ((s8[4325376]{0:T(1024)(128)(4,1)}), s8[4194304]{0:T(1024)(128)(4,1)S(1)}, s32[]{:S(2)}) async-start(s8[4325376]{0:T(1024)(128)(4,1)} %bitcast.6), calls=%async_computation | async-start | bytes 8388608
  89.4 17.5 %slice-start.1 = ((s8[4325376]{0:T(1024)(128)(4,1)}), s8[131072]{0:T(1024)(128)(4,1)S(1)}, s32[]{:S(2)}) async-start(s8[4325376]{0:T(1024)(128)(4,1)} %bitcast.6), calls=%async_computation.1 | async-start | bytes 262144
  112.6 5.7 %collective-permute-start.17 = (f32[512,1024]{1,0:T(8,128)S(1)}, f32[512,1024]{1,0:T(8,128)S(1)}, u32[]{:S(2)}, u32[]{:S(2)}) collective-permute-start(f32[512,1024]{1,0:T(8,128)S(1)} %fusion.50), channel_id=1, source_target_pairs={{0,1},{1,0},{2,3},{3,2},{4,5},{5,4},{6,7},{7,6},{8,9},{9,8},{10,11... | collective-permute-start | bytes 6291464 | tf_op jit(solution)/shard_map/ppermute | solution.py:153
  120.6 1.4 collective-permute-start.21
  121.3 13.9 %collective-permute-start.18 = (f32[256,512]{1,0:T(8,128)S(1)}, f32[256,512]{1,0:T(8,128)S(1)}, u32[]{:S(2)}, u32[]{:S(2)}) collective-permute-start(f32[256,512]{1,0:T(8,128)S(1)} %pad_maximum_fusion.29), channel_id=1, source_target_pairs={{0,16},{1,17},{2,18},{3,19},{4,20},{5,21},{6,22},{7,23},{8,24},{9,... | collective-permute-start | bytes 1572872 | tf_op jit(solution)/shard_map/ppermute | solution.py:122
  122.2 4.8 %collective-permute-start.22 = (f32[256]{0:T(256)S(1)}, f32[256]{0:T(256)S(1)}, u32[]{:S(2)}, u32[]{:S(2)}) collective-permute-start(f32[256]{0:T(256)S(1)} %pad_maximum_fusion.31), channel_id=1, source_target_pairs={{0,48},{1,49},{2,50},{3,51},{4,52},{5,53},{6,54},{7,55},{8,56},{9,... | collective-permute-start | bytes 3080 | tf_op jit(solution)/shard_map/ppermute | solution.py:122
  135.3 7.5 %collective-permute-start.19 = (f32[128,512]{1,0:T(8,128)S(1)}, f32[128,512]{1,0:T(8,128)S(1)}, u32[]{:S(2)}, u32[]{:S(2)}) collective-permute-start(f32[128,512]{1,0:T(8,128)S(1)} %pad_maximum_fusion.30), channel_id=1, source_target_pairs={{0,64},{1,65},{2,66},{3,67},{4,68},{5,69},{6,70},{7,71},{8,72},{9,... | collective-permute-start | bytes 786440 | tf_op jit(solution)/shard_map/ppermute | solution.py:122
  135.7 4.8 %collective-permute-start.23 = (f32[128]{0:T(128)S(1)}, f32[128]{0:T(128)S(1)}, u32[]{:S(2)}, u32[]{:S(2)}) collective-permute-start(f32[128]{0:T(128)S(1)} %pad_maximum_fusion.32), channel_id=1, source_target_pairs={{0,66},{1,67},{2,64},{3,65},{4,70},{5,71},{6,68},{7,69},{8,74},{9,... | collective-permute-start | bytes 1544 | tf_op jit(solution)/shard_map/ppermute | solution.py:122
  140.6 4.8 %collective-permute-start.24 = (f32[64]{0:T(128)S(1)}, f32[64]{0:T(128)S(1)}, u32[]{:S(2)}, u32[]{:S(2)}) collective-permute-start(f32[64]{0:T(128)S(1)} %slice_add_fusion.7), channel_id=1, source_target_pairs={{0,12},{1,13},{2,14},{3,15},{4,8},{5,9},{6,10},{7,11},{8,4},{9,5},... | collective-permute-start | bytes 776 | tf_op jit(solution)/shard_map/ppermute | solution.py:122
  142.8 5.0 %collective-permute-start.20 = (f32[64,512]{1,0:T(8,128)S(1)}, f32[64,512]{1,0:T(8,128)S(1)}, u32[]{:S(2)}, u32[]{:S(2)}) collective-permute-start(f32[64,512]{1,0:T(8,128)S(1)} %slice_add_fusion), channel_id=1, source_target_pairs={{0,4},{1,5},{2,6},{3,7},{4,0},{5,1},{6,2},{7,3},{8,12},{9,13},{10,... | collective-permute-start | bytes 393224 | tf_op jit(solution)/shard_map/ppermute | solution.py:122

commit v20 on v15

--- a/solution.py
+++ b/solution.py
@@ -124,6 +124,27 @@
     return blocks[0]
 
 
+def offset_pairs(n, o, mate):
+    out = []
+    for L in range(n):
+        v, c = coords(L)
+        w = [mate(v[a]) if o & (1 << a) else v[a] for a in range(3)]
+        out.append((L, lin(w, c)))
+    return out
+
+
+def cube_reduce_square(blocks, mate, n):
+    blocks = list(blocks)
+    rows = blocks[0].shape[0]
+    for m in (1, 2, 3):
+        send = [o for o in range(8) if o & 3 == m]
+        got = lax.ppermute(jnp.concatenate([blocks[o] for o in send]), AXES, offset_pairs(n, m, mate))
+        for i, o in enumerate(send):
+            blocks[o ^ m] = blocks[o ^ m] + got[i * rows:(i + 1) * rows]
+    got = lax.ppermute(blocks[4], AXES, offset_pairs(n, 4, mate))
+    return blocks[0] + got
+
+
 def local(train_grads, train_scale, train_class, test_grads, test_class):
     n = 128
     k = train_grads.shape[1]
@@ -153,7 +174,7 @@
         w, train_hot, (((0,), (0,)), ((), ())), preferred_element_type=jnp.float32
     )
     tp = jnp.sum(per_class * test_hot.astype(jnp.float32), axis=1)
-    train_attr = cube_reduce(
+    train_attr = cube_reduce_square(
         [part[o * rows:(o + 1) * rows] for o in range(8)], train_mate, n
     )
     test_part = tp[:half] + lax.ppermute(tp[half:], AXES, core_pairs(n))

time: 144 us -> 138 us (0.958)
  waiting for transfers between devices: 83.5 us -> 76.3 us
    ppermute x6 -> x3, waiting for transfers between devices: 19.9 us -> 7.04 us  [cube_reduce(): lax.ppermute(jnp.concatenate([blocks[o] for o in send]), AXES, mate_pairs...]
    ppermute x0 -> x4, waiting for transfers between devices: none -> 5.65 us  [the longest x1 3.16 us: cube_reduce_square(): got = lax.ppermute(blocks[4], AXES, offset_pairs(n, 4, mate))]
    ppermute x0 -> x4, starting transfers between devices: none -> 4.27 us  [the longest x3 3.35 us: cube_reduce_square(): lax.ppermute(jnp.concatenate([blocks[o] for o in send]), AXES, offset_pai...]
    ppermute x6 -> x3, starting transfers between devices: 5.61 us -> 2.46 us  [cube_reduce(): lax.ppermute(jnp.concatenate([blocks[o] for o in send]), AXES, mate_pairs...]
  transfers between devices with their start and end apart: 25 -> 26, of which waited for: 19 -> 18; matrix products, arithmetic and copies ran while one was open for 8% -> 9% of each run, Pallas kernels for 0% -> 0%
where the time goes in v20:
time: 138 us
  waiting for transfers between devices  76.3 us (55%)
  starting transfers between devices  36 us (26%)
  matrix products  11.2 us (8%)
  other arithmetic  7.41 us (5%)
  local copies, waits for them, and re-layouts  5.52 us (4%)
    ppermute x15, waiting for transfers between devices, chain(): got = lax.ppermute(buf, AXES, mate_pairs(n, a, mate))  63.1 us
    ppermute x15, starting transfers between devices, chain(): got = lax.ppermute(buf, AXES, mate_pairs(n, a, mate))  28.4 us
    dot_general x2, matrix products, partial(): lax.dot_general(t, te_all, (((1,), (1,)), ((), ())), preferred_element_ty...  9.57 us
    ppermute x3, waiting for transfers between devices, cube_reduce(): lax.ppermute(jnp.concatenate([blocks[o] for o in send]), AXES, mate_pairs...  7.04 us
    ppermute x3, starting transfers between devices, cube_reduce_square(): lax.ppermute(jnp.concatenate([blocks[o] for o in send]), AXES, offset_pai...  3.35 us
    ppermute x1, waiting for transfers between devices, cube_reduce_square(): got = lax.ppermute(blocks[4], AXES, offset_pairs(n, 4, mate))  3.16 us
  transfers between devices with their start and end apart: 26, of which 18 were waited for; matrix products, arithmetic and copies ran while one was open for 9% of the time, Pallas kernels for 0%

profile of v20, /device:TPU:0, one launch (start us, length us, event | category | flops | bytes accessed | tf_op | source)
XLA Modules:
  0.0 137.7 jit_solution(6854891396118548081)
XLA Ops:
  0.7 1.3 fusion.43
  5.1 2.9 %collective-permute-start.8 = (bf16[128,1408]{1,0:T(8,128)(2,1)S(1)}, bf16[128,1408]{1,0:T(8,128)(2,1)S(1)}, u32[]{:S(2)}, u32[]{:S(2)}) collective-permute-start(bf16[128,1408]{1,0:T(8,128)(2,1)S(1)} %get-tuple-element.44), channel_id=1, source_target_pairs={{0,48},{1,49},{2,50},{3,51},{4,52},{5,53},{6,54},{7,55},{8,56},{9,... | collective-permute-start | bytes 1081352 | tf_op jit(solution)/shard_map/ppermute | solution.py:83
  8.0 4.0 %collective-permute-start.12 = (bf16[128,1408]{1,0:T(8,128)(2,1)S(1)}, bf16[128,1408]{1,0:T(8,128)(2,1)S(1)}, u32[]{:S(2)}, u32[]{:S(2)}) collective-permute-start(bf16[128,1408]{1,0:T(8,128)(2,1)S(1)} %get-tuple-element.45), channel_id=1, source_target_pairs={{0,12},{1,13},{2,14},{3,15},{4,8},{5,9},{6,10},{7,11},{8,4},{9,5},... | collective-permute-start | bytes 1081352 | tf_op jit(solution)/shard_map/ppermute | solution.py:83
  12.1 3.0 %collective-permute-start.9 = (bf16[128,1408]{1,0:T(8,128)(2,1)S(1)}, bf16[128,1408]{1,0:T(8,128)(2,1)S(1)}, u32[]{:S(2)}, u32[]{:S(2)}) collective-permute-start(bf16[128,1408]{1,0:T(8,128)(2,1)S(1)} %get-tuple-element.46), channel_id=1, source_target_pairs={{0,66},{1,67},{2,64},{3,65},{4,70},{5,71},{6,68},{7,69},{8,74},{9,... | collective-permute-start | bytes 1081352 | tf_op jit(solution)/shard_map/ppermute | solution.py:83
  16.9 3.2 %collective-permute-start.14 = (bf16[256,1408]{1,0:T(8,128)(2,1)S(1)}, bf16[256,1408]{1,0:T(8,128)(2,1)S(1)}, u32[]{:S(2)}, u32[]{:S(2)}) collective-permute-start(bf16[256,1408]{1,0:T(8,128)(2,1)S(1)} %pad_maximum_fusion.18), channel_id=1, source_target_pairs={{0,66},{1,67},{2,64},{3,65},{4,70},{5,71},{6,68},{7,69},{8,74},{9,... | collective-permute-start | bytes 2162696 | tf_op jit(solution)/shard_map/ppermute | solution.py:83
  20.6 2.4 %collective-permute-start.13 = (bf16[256,1408]{1,0:T(8,128)(2,1)S(1)}, bf16[256,1408]{1,0:T(8,128)(2,1)S(1)}, u32[]{:S(2)}, u32[]{:S(2)}) collective-permute-start(bf16[256,1408]{1,0:T(8,128)(2,1)S(1)} %pad_maximum_fusion.17), channel_id=1, source_target_pairs={{0,48},{1,49},{2,50},{3,51},{4,52},{5,53},{6,54},{7,55},{8,56},{9,... | collective-permute-start | bytes 2162696 | tf_op jit(solution)/shard_map/ppermute | solution.py:83
  23.0 1.6 %collective-permute-done.9 = bf16[128,1408]{1,0:T(8,128)(2,1)S(1)} collective-permute-done((bf16[128,1408]{1,0:T(8,128)(2,1)S(1)}, bf16[128,1408]{1,0:T(8,128)(2,1)S(1)}, u32[]{:S(2)}, u32[]{:S(2)}) %collective-permute-start.9) | collective-permute-done | bytes 360480 | tf_op jit(solution)/shard_map/ppermute | solution.py:83
  24.7 2.5 %collective-permute-start.10 = (bf16[256,1408]{1,0:T(8,128)(2,1)S(1)}, bf16[256,1408]{1,0:T(8,128)(2,1)S(1)}, u32[]{:S(2)}, u32[]{:S(2)}) collective-permute-start(bf16[256,1408]{1,0:T(8,128)(2,1)S(1)} %pad_maximum_fusion.16), channel_id=1, source_target_pairs={{0,12},{1,13},{2,14},{3,15},{4,8},{5,9},{6,10},{7,11},{8,4},{9,5},... | collective-permute-start | bytes 2162696 | tf_op jit(solution)/shard_map/ppermute | solution.py:83
  27.2 1.2 collective-permute-done.1
  29.3 1.8 %collective-permute-start.3 = (bf16[256,2176]{1,0:T(8,128)(2,1)S(1)}, bf16[256,2176]{1,0:T(8,128)(2,1)S(1)}, u32[]{:S(2)}, u32[]{:S(2)}) collective-permute-start(bf16[256,2176]{1,0:T(8,128)(2,1)S(1)} %pad_maximum_fusion.5), channel_id=1, source_target_pairs={{0,16},{1,17},{2,18},{3,19},{4,20},{5,21},{6,22},{7,23},{8,24},{9,... | collective-permute-start | bytes 3342344 | tf_op jit(solution)/shard_map/ppermute | solution.py:83
  31.1 7.6 %collective-permute-done.14 = bf16[256,1408]{1,0:T(8,128)(2,1)S(1)} collective-permute-done((bf16[256,1408]{1,0:T(8,128)(2,1)S(1)}, bf16[256,1408]{1,0:T(8,128)(2,1)S(1)}, u32[]{:S(2)}, u32[]{:S(2)}) %collective-permute-start.14) | collective-permute-done | bytes 720928 | tf_op jit(solution)/shard_map/ppermute | solution.py:83
  38.8 1.1 collective-permute-start.16
  40.1 3.0 %collective-permute-start.15 = (bf16[512,1408]{1,0:T(8,128)(2,1)S(1)}, bf16[512,1408]{1,0:T(8,128)(2,1)S(1)}, u32[]{:S(2)}, u32[]{:S(2)}) collective-permute-start(bf16[512,1408]{1,0:T(8,128)(2,1)S(1)} %pad_maximum_fusion.3), channel_id=1, source_target_pairs={{0,66},{1,67},{2,64},{3,65},{4,70},{5,71},{6,68},{7,69},{8,74},{9,... | collective-permute-start | bytes 4325384 | tf_op jit(solution)/shard_map/ppermute | solution.py:83
  43.9 2.2 %collective-permute-start.11 = (bf16[512,1408]{1,0:T(8,128)(2,1)S(1)}, bf16[512,1408]{1,0:T(8,128)(2,1)S(1)}, u32[]{:S(2)}, u32[]{:S(2)}) collective-permute-start(bf16[512,1408]{1,0:T(8,128)(2,1)S(1)} %pad_maximum_fusion.2), channel_id=1, source_target_pairs={{0,48},{1,49},{2,50},{3,51},{4,52},{5,53},{6,54},{7,55},{8,56},{9,... | collective-permute-start | bytes 4325384 | tf_op jit(solution)/shard_map/ppermute | solution.py:83
  46.2 5.7 %collective-permute-done.4 = bf16[256,2048]{1,0:T(8,128)(2,1)S(1)} collective-permute-done((bf16[256,2048]{1,0:T(8,128)(2,1)S(1)}, bf16[256,2048]{1,0:T(8,128)(2,1)S(1)}, u32[]{:S(2)}, u32[]{:S(2)}) %collective-permute-start.4) | collective-permute-done | bytes 1048608 | tf_op jit(solution)/shard_map/ppermute | solution.py:83
  52.3 1.6 %collective-permute-done.3 = bf16[256,2176]{1,0:T(8,128)(2,1)S(1)} collective-permute-done((bf16[256,2176]{1,0:T(8,128)(2,1)S(1)}, bf16[256,2176]{1,0:T(8,128)(2,1)S(1)}, u32[]{:S(2)}, u32[]{:S(2)}) %collective-permute-start.3) | collective-permute-done | bytes 1114144 | tf_op jit(solution)/shard_map/ppermute | solution.py:83
  54.1 1.5 %collective-permute-start.5 = (bf16[512,2176]{1,0:T(8,128)(2,1)S(1)}, bf16[512,2176]{1,0:T(8,128)(2,1)S(1)}, u32[]{:S(2)}, u32[]{:S(2)}) collective-permute-start(bf16[512,2176]{1,0:T(8,128)(2,1)S(1)} %pad_maximum_fusion), channel_id=1, source_target_pairs={{0,64},{1,65},{2,66},{3,67},{4,68},{5,69},{6,70},{7,71},{8,72},{9,... | collective-permute-start | bytes 6684680 | tf_op jit(solution)/shard_map/ppermute | solution.py:83
  55.8 0.9 fusion.26
  56.7 19.2 %collective-permute-done.11 = bf16[512,1408]{1,0:T(8,128)(2,1)S(1)} collective-permute-done((bf16[512,1408]{1,0:T(8,128)(2,1)S(1)}, bf16[512,1408]{1,0:T(8,128)(2,1)S(1)}, u32[]{:S(2)}, u32[]{:S(2)}) %collective-permute-start.11) | collective-permute-done | bytes 1441824 | tf_op jit(solution)/shard_map/ppermute | solution.py:83
  77.7 19.5 %collective-permute-done.6 = bf16[512,2048]{1,0:T(8,128)(2,1)S(1)} collective-permute-done((bf16[512,2048]{1,0:T(8,128)(2,1)S(1)}, bf16[512,2048]{1,0:T(8,128)(2,1)S(1)}, u32[]{:S(2)}, u32[]{:S(2)}) %collective-permute-start.6) | collective-permute-done | bytes 2097184 | tf_op jit(solution)/shard_map/ppermute | solution.py:83
  97.4 4.6 %collective-permute-done.5 = bf16[512,2176]{1,0:T(8,128)(2,1)S(1)} collective-permute-done((bf16[512,2176]{1,0:T(8,128)(2,1)S(1)}, bf16[512,2176]{1,0:T(8,128)(2,1)S(1)}, u32[]{:S(2)}, u32[]{:S(2)}) %collective-permute-start.5) | collective-permute-done | bytes 2228256 | tf_op jit(solution)/shard_map/ppermute | solution.py:83
  103.1 4.8 %fusion.51 = f32[512,1024]{1,0:T(8,128)S(1)} fusion(bf16[512,4224]{1,0:T(8,128)(2,1)S(1)} %get-tuple-element.30, bf16[1024,4224]{1,0:T(8,128)(2,1)S(1)} %slice_dynamic-update-slice_fusion), kind=kOutput, calls=%fused_computation.160 | convolution fusion | flops 4429185024 | bytes 15073280 | tf_op jit(solution)/shard_map/dot_general | solution.py:160
  108.4 4.8 %fusion.50 = f32[512,1024]{1,0:T(8,128)S(1)} fusion(bf16[512,4224]{1,0:T(8,128)(2,1)S(1)} %get-tuple-element.31, bf16[1024,4224]{1,0:T(8,128)(2,1)S(1)} %slice_dynamic-update-slice_fusion), kind=kOutput, calls=%fused_computation.159 | convolution fusion | flops 4429185024 | bytes 15073280 | tf_op jit(solution)/shard_map/dot_general | solution.py:160
  115.0 0.9 multiply_reduce_fusion
  116.6 1.6 %collective-permute-start.18 = (f32[128,512]{1,0:T(8,128)S(1)}, f32[128,512]{1,0:T(8,128)S(1)}, u32[]{:S(2)}, u32[]{:S(2)}) collective-permute-start(f32[128,512]{1,0:T(8,128)S(1)} %pad_maximum_fusion.29), channel_id=1, source_target_pairs={{0,16},{1,17},{2,18},{3,19},{4,20},{5,21},{6,22},{7,23},{8,24},{9,... | collective-permute-start | bytes 786440 | tf_op jit(solution)/shard_map/ppermute | solution.py:141
  119.5 1.3 collective-permute-start.20
  120.8 2.7 %collective-permute-done.23 = f32[256]{0:T(256)S(1)} collective-permute-done((f32[256]{0:T(256)S(1)}, f32[256]{0:T(256)S(1)}, u32[]{:S(2)}, u32[]{:S(2)}) %collective-permute-start.23) | collective-permute-done | bytes 1056 | tf_op jit(solution)/shard_map/ppermute | solution.py:118
  123.7 0.9 collective-permute-start.24
  124.7 3.8 %collective-permute-done.24 = f32[128]{0:T(128)S(1)} collective-permute-done((f32[128]{0:T(128)S(1)}, f32[128]{0:T(128)S(1)}, u32[]{:S(2)}, u32[]{:S(2)}) %collective-permute-start.24) | collective-permute-done | bytes 544 | tf_op jit(solution)/shard_map/ppermute | solution.py:118
  129.4 2.5 %collective-permute-done.19 = f32[128,512]{1,0:T(8,128)S(1)} collective-permute-done((f32[128,512]{1,0:T(8,128)S(1)}, f32[128,512]{1,0:T(8,128)S(1)}, u32[]{:S(2)}, u32[]{:S(2)}) %collective-permute-start.19) | collective-permute-done | bytes 262176 | tf_op jit(solution)/shard_map/ppermute | solution.py:141
  132.0 0.9 collective-permute-start.21
  133.8 3.2 %collective-permute-done.21 = f32[64,512]{1,0:T(8,128)S(1)} collective-permute-done((f32[64,512]{1,0:T(8,128)S(1)}, f32[64,512]{1,0:T(8,128)S(1)}, u32[]{:S(2)}, u32[]{:S(2)}) %collective-permute-start.21) | collective-permute-done | bytes 131104 | tf_op jit(solution)/shard_map/ppermute | solution.py:144
  (117 shorter events, 18.0 us)
Async XLA Ops:
  2.7 1.2 copy-start
  2.8 1.2 copy-start.1
  3.0 2.0 %collective-permute-start.7 = (bf16[64,4224]{1,0:T(8,128)(2,1)S(1)}, bf16[64,4224]{1,0:T(8,128)(2,1)S(1)}, u32[]{:S(2)}, u32[]{:S(2)}) collective-permute-start(bf16[64,4224]{1,0:T(8,128)(2,1)S(1)} %get-tuple-element.47), channel_id=1, source_target_pairs={{0,1},{1,0},{2,3},{3,2},{4,5},{5,4},{6,7},{7,6},{8,9},{9,8},{10,11... | collective-permute-start | bytes 1622024 | tf_op jit(solution)/shard_map/ppermute | solution.py:96
  4.4 10.7 %collective-permute-start = (bf16[64,4224]{1,0:T(8,128)(2,1)S(1)}, bf16[64,4224]{1,0:T(8,128)(2,1)S(1)}, u32[]{:S(2)}, u32[]{:S(2)}) collective-permute-start(bf16[64,4224]{1,0:T(8,128)(2,1)S(1)} %get-tuple-element.48), channel_id=1, source_target_pairs={{0,1},{1,0},{2,3},{3,2},{4,5},{5,4},{6,7},{7,6},{8,9},{9,8},{10,11... | collective-permute-start | bytes 1622024 | tf_op jit(solution)/shard_map/ppermute | solution.py:96
  5.1 11.7 %collective-permute-start.8 = (bf16[128,1408]{1,0:T(8,128)(2,1)S(1)}, bf16[128,1408]{1,0:T(8,128)(2,1)S(1)}, u32[]{:S(2)}, u32[]{:S(2)}) collective-permute-start(bf16[128,1408]{1,0:T(8,128)(2,1)S(1)} %get-tuple-element.44), channel_id=1, source_target_pairs={{0,48},{1,49},{2,50},{3,51},{4,52},{5,53},{6,54},{7,55},{8,56},{9,... | collective-permute-start | bytes 1081352 | tf_op jit(solution)/shard_map/ppermute | solution.py:83
  8.0 12.5 %collective-permute-start.12 = (bf16[128,1408]{1,0:T(8,128)(2,1)S(1)}, bf16[128,1408]{1,0:T(8,128)(2,1)S(1)}, u32[]{:S(2)}, u32[]{:S(2)}) collective-permute-start(bf16[128,1408]{1,0:T(8,128)(2,1)S(1)} %get-tuple-element.45), channel_id=1, source_target_pairs={{0,12},{1,13},{2,14},{3,15},{4,8},{5,9},{6,10},{7,11},{8,4},{9,5},... | collective-permute-start | bytes 1081352 | tf_op jit(solution)/shard_map/ppermute | solution.py:83
  12.1 12.5 %collective-permute-start.9 = (bf16[128,1408]{1,0:T(8,128)(2,1)S(1)}, bf16[128,1408]{1,0:T(8,128)(2,1)S(1)}, u32[]{:S(2)}, u32[]{:S(2)}) collective-permute-start(bf16[128,1408]{1,0:T(8,128)(2,1)S(1)} %get-tuple-element.46), channel_id=1, source_target_pairs={{0,66},{1,67},{2,64},{3,65},{4,70},{5,71},{6,68},{7,69},{8,74},{9,... | collective-permute-start | bytes 1081352 | tf_op jit(solution)/shard_map/ppermute | solution.py:83
  15.1 13.2 %collective-permute-start.1 = (bf16[128,2048]{1,0:T(8,128)(2,1)S(1)}, bf16[128,2048]{1,0:T(8,128)(2,1)S(1)}, u32[]{:S(2)}, u32[]{:S(2)}) collective-permute-start(bf16[128,2048]{1,0:T(8,128)(2,1)S(1)} %pad_maximum_fusion.27), channel_id=1, source_target_pairs={{0,16},{1,17},{2,18},{3,19},{4,20},{5,21},{6,22},{7,23},{8,24},{9,... | collective-permute-start | bytes 1572872 | tf_op jit(solution)/shard_map/ppermute | solution.py:83
  15.5 13.7 %collective-permute-start.2 = (bf16[128,2176]{1,0:T(8,128)(2,1)S(1)}, bf16[128,2176]{1,0:T(8,128)(2,1)S(1)}, u32[]{:S(2)}, u32[]{:S(2)}) collective-permute-start(bf16[128,2176]{1,0:T(8,128)(2,1)S(1)} %pad_maximum_fusion.19), channel_id=1, source_target_pairs={{0,4},{1,5},{2,6},{3,7},{4,0},{5,1},{6,2},{7,3},{8,12},{9,13},{10,... | collective-permute-start | bytes 1671176 | tf_op jit(solution)/shard_map/ppermute | solution.py:83
  16.9 21.8 %collective-permute-start.14 = (bf16[256,1408]{1,0:T(8,128)(2,1)S(1)}, bf16[256,1408]{1,0:T(8,128)(2,1)S(1)}, u32[]{:S(2)}, u32[]{:S(2)}) collective-permute-start(bf16[256,1408]{1,0:T(8,128)(2,1)S(1)} %pad_maximum_fusion.18), channel_id=1, source_target_pairs={{0,66},{1,67},{2,64},{3,65},{4,70},{5,71},{6,68},{7,69},{8,74},{9,... | collective-permute-start | bytes 2162696 | tf_op jit(solution)/shard_map/ppermute | solution.py:83
  20.6 19.4 %collective-permute-start.13 = (bf16[256,1408]{1,0:T(8,128)(2,1)S(1)}, bf16[256,1408]{1,0:T(8,128)(2,1)S(1)}, u32[]{:S(2)}, u32[]{:S(2)}) collective-permute-start(bf16[256,1408]{1,0:T(8,128)(2,1)S(1)} %pad_maximum_fusion.17), channel_id=1, source_target_pairs={{0,48},{1,49},{2,50},{3,51},{4,52},{5,53},{6,54},{7,55},{8,56},{9,... | collective-permute-start | bytes 2162696 | tf_op jit(solution)/shard_map/ppermute | solution.py:83
  24.7 19.1 %collective-permute-start.10 = (bf16[256,1408]{1,0:T(8,128)(2,1)S(1)}, bf16[256,1408]{1,0:T(8,128)(2,1)S(1)}, u32[]{:S(2)}, u32[]{:S(2)}) collective-permute-start(bf16[256,1408]{1,0:T(8,128)(2,1)S(1)} %pad_maximum_fusion.16), channel_id=1, source_target_pairs={{0,12},{1,13},{2,14},{3,15},{4,8},{5,9},{6,10},{7,11},{8,4},{9,5},... | collective-permute-start | bytes 2162696 | tf_op jit(solution)/shard_map/ppermute | solution.py:83
  28.4 23.5 %collective-permute-start.4 = (bf16[256,2048]{1,0:T(8,128)(2,1)S(1)}, bf16[256,2048]{1,0:T(8,128)(2,1)S(1)}, u32[]{:S(2)}, u32[]{:S(2)}) collective-permute-start(bf16[256,2048]{1,0:T(8,128)(2,1)S(1)} %pad_maximum_fusion.15), channel_id=1, source_target_pairs={{0,64},{1,65},{2,66},{3,67},{4,68},{5,69},{6,70},{7,71},{8,72},{9,... | collective-permute-start | bytes 3145736 | tf_op jit(solution)/shard_map/ppermute | solution.py:83
  29.3 24.7 %collective-permute-start.3 = (bf16[256,2176]{1,0:T(8,128)(2,1)S(1)}, bf16[256,2176]{1,0:T(8,128)(2,1)S(1)}, u32[]{:S(2)}, u32[]{:S(2)}) collective-permute-start(bf16[256,2176]{1,0:T(8,128)(2,1)S(1)} %pad_maximum_fusion.5), channel_id=1, source_target_pairs={{0,16},{1,17},{2,18},{3,19},{4,20},{5,21},{6,22},{7,23},{8,24},{9,... | collective-permute-start | bytes 3342344 | tf_op jit(solution)/shard_map/ppermute | solution.py:83
  38.8 37.7 %collective-permute-start.16 = (bf16[512,1408]{1,0:T(8,128)(2,1)S(1)}, bf16[512,1408]{1,0:T(8,128)(2,1)S(1)}, u32[]{:S(2)}, u32[]{:S(2)}) collective-permute-start(bf16[512,1408]{1,0:T(8,128)(2,1)S(1)} %pad_maximum_fusion.4), channel_id=1, source_target_pairs={{0,12},{1,13},{2,14},{3,15},{4,8},{5,9},{6,10},{7,11},{8,4},{9,5},... | collective-permute-start | bytes 4325384 | tf_op jit(solution)/shard_map/ppermute | solution.py:83
  40.1 36.0 %collective-permute-start.15 = (bf16[512,1408]{1,0:T(8,128)(2,1)S(1)}, bf16[512,1408]{1,0:T(8,128)(2,1)S(1)}, u32[]{:S(2)}, u32[]{:S(2)}) collective-permute-start(bf16[512,1408]{1,0:T(8,128)(2,1)S(1)} %pad_maximum_fusion.3), channel_id=1, source_target_pairs={{0,66},{1,67},{2,64},{3,65},{4,70},{5,71},{6,68},{7,69},{8,74},{9,... | collective-permute-start | bytes 4325384 | tf_op jit(solution)/shard_map/ppermute | solution.py:83
  43.9 31.9 %collective-permute-start.11 = (bf16[512,1408]{1,0:T(8,128)(2,1)S(1)}, bf16[512,1408]{1,0:T(8,128)(2,1)S(1)}, u32[]{:S(2)}, u32[]{:S(2)}) collective-permute-start(bf16[512,1408]{1,0:T(8,128)(2,1)S(1)} %pad_maximum_fusion.2), channel_id=1, source_target_pairs={{0,48},{1,49},{2,50},{3,51},{4,52},{5,53},{6,54},{7,55},{8,56},{9,... | collective-permute-start | bytes 4325384 | tf_op jit(solution)/shard_map/ppermute | solution.py:83
  52.1 45.1 %collective-permute-start.6 = (bf16[512,2048]{1,0:T(8,128)(2,1)S(1)}, bf16[512,2048]{1,0:T(8,128)(2,1)S(1)}, u32[]{:S(2)}, u32[]{:S(2)}) collective-permute-start(bf16[512,2048]{1,0:T(8,128)(2,1)S(1)} %pad_maximum_fusion.1), channel_id=1, source_target_pairs={{0,4},{1,5},{2,6},{3,7},{4,0},{5,1},{6,2},{7,3},{8,12},{9,13},{10,... | collective-permute-start | bytes 6291464 | tf_op jit(solution)/shard_map/ppermute | solution.py:83
  54.1 47.9 %collective-permute-start.5 = (bf16[512,2176]{1,0:T(8,128)(2,1)S(1)}, bf16[512,2176]{1,0:T(8,128)(2,1)S(1)}, u32[]{:S(2)}, u32[]{:S(2)}) collective-permute-start(bf16[512,2176]{1,0:T(8,128)(2,1)S(1)} %pad_maximum_fusion), channel_id=1, source_target_pairs={{0,64},{1,65},{2,66},{3,67},{4,68},{5,69},{6,70},{7,71},{8,72},{9,... | collective-permute-start | bytes 6684680 | tf_op jit(solution)/shard_map/ppermute | solution.py:83
  77.6 24.6 %slice-start = ((s8[4325376]{0:T(1024)(128)(4,1)}), s8[4194304]{0:T(1024)(128)(4,1)S(1)}, s32[]{:S(2)}) async-start(s8[4325376]{0:T(1024)(128)(4,1)} %bitcast.6), calls=%async_computation | async-start | bytes 8388608
  77.7 24.5 %slice-start.1 = ((s8[4325376]{0:T(1024)(128)(4,1)}), s8[131072]{0:T(1024)(128)(4,1)S(1)}, s32[]{:S(2)}) async-start(s8[4325376]{0:T(1024)(128)(4,1)} %bitcast.6), calls=%async_computation.1 | async-start | bytes 262144
  107.9 5.7 %collective-permute-start.17 = (f32[512,1024]{1,0:T(8,128)S(1)}, f32[512,1024]{1,0:T(8,128)S(1)}, u32[]{:S(2)}, u32[]{:S(2)}) collective-permute-start(f32[512,1024]{1,0:T(8,128)S(1)} %fusion.51), channel_id=1, source_target_pairs={{0,1},{1,0},{2,3},{3,2},{4,5},{5,4},{6,7},{7,6},{8,9},{9,8},{10,11... | collective-permute-start | bytes 6291464 | tf_op jit(solution)/shard_map/ppermute | solution.py:164
  115.9 2.7 %collective-permute-start.22 = (f32[512]{0:T(512)S(1)}, f32[512]{0:T(512)S(1)}, u32[]{:S(2)}, u32[]{:S(2)}) collective-permute-start(f32[512]{0:T(512)S(1)} %slice.414), channel_id=1, source_target_pairs={{0,1},{1,0},{2,3},{3,2},{4,5},{5,4},{6,7},{7,6},{8,9},{9,8},{10,11... | collective-permute-start | bytes 6152 | tf_op jit(solution)/shard_map/ppermute | solution.py:180
  116.6 12.8 %collective-permute-start.18 = (f32[128,512]{1,0:T(8,128)S(1)}, f32[128,512]{1,0:T(8,128)S(1)}, u32[]{:S(2)}, u32[]{:S(2)}) collective-permute-start(f32[128,512]{1,0:T(8,128)S(1)} %pad_maximum_fusion.29), channel_id=1, source_target_pairs={{0,16},{1,17},{2,18},{3,19},{4,20},{5,21},{6,22},{7,23},{8,24},{9,... | collective-permute-start | bytes 786440 | tf_op jit(solution)/shard_map/ppermute | solution.py:141
  118.3 13.6 %collective-permute-start.19 = (f32[128,512]{1,0:T(8,128)S(1)}, f32[128,512]{1,0:T(8,128)S(1)}, u32[]{:S(2)}, u32[]{:S(2)}) collective-permute-start(f32[128,512]{1,0:T(8,128)S(1)} %pad_maximum_fusion.30), channel_id=1, source_target_pairs={{0,64},{1,65},{2,66},{3,67},{4,68},{5,69},{6,70},{7,71},{8,72},{9,... | collective-permute-start | bytes 786440 | tf_op jit(solution)/shard_map/ppermute | solution.py:141
  118.8 4.8 %collective-permute-start.23 = (f32[256]{0:T(256)S(1)}, f32[256]{0:T(256)S(1)}, u32[]{:S(2)}, u32[]{:S(2)}) collective-permute-start(f32[256]{0:T(256)S(1)} %pad_maximum_fusion.32), channel_id=1, source_target_pairs={{0,48},{1,49},{2,50},{3,51},{4,52},{5,53},{6,54},{7,55},{8,56},{9,... | collective-permute-start | bytes 3080 | tf_op jit(solution)/shard_map/ppermute | solution.py:118
  119.5 12.4 %collective-permute-start.20 = (f32[128,512]{1,0:T(8,128)S(1)}, f32[128,512]{1,0:T(8,128)S(1)}, u32[]{:S(2)}, u32[]{:S(2)}) collective-permute-start(f32[128,512]{1,0:T(8,128)S(1)} %pad_maximum_fusion.31), channel_id=1, source_target_pairs={{0,80},{1,81},{2,82},{3,83},{4,84},{5,85},{6,86},{7,87},{8,88},{9,... | collective-permute-start | bytes 786440 | tf_op jit(solution)/shard_map/ppermute | solution.py:141
  123.7 4.8 %collective-permute-start.24 = (f32[128]{0:T(128)S(1)}, f32[128]{0:T(128)S(1)}, u32[]{:S(2)}, u32[]{:S(2)}) collective-permute-start(f32[128]{0:T(128)S(1)} %pad_maximum_fusion.33), channel_id=1, source_target_pairs={{0,66},{1,67},{2,64},{3,65},{4,70},{5,71},{6,68},{7,69},{8,74},{9,... | collective-permute-start | bytes 1544 | tf_op jit(solution)/shard_map/ppermute | solution.py:118
  128.6 4.8 %collective-permute-start.25 = (f32[64]{0:T(128)S(1)}, f32[64]{0:T(128)S(1)}, u32[]{:S(2)}, u32[]{:S(2)}) collective-permute-start(f32[64]{0:T(128)S(1)} %slice_add_fusion.7), channel_id=1, source_target_pairs={{0,12},{1,13},{2,14},{3,15},{4,8},{5,9},{6,10},{7,11},{8,4},{9,5},... | collective-permute-start | bytes 776 | tf_op jit(solution)/shard_map/ppermute | solution.py:118
  132.0 5.0 %collective-permute-start.21 = (f32[64,512]{1,0:T(8,128)S(1)}, f32[64,512]{1,0:T(8,128)S(1)}, u32[]{:S(2)}, u32[]{:S(2)}) collective-permute-start(f32[64,512]{1,0:T(8,128)S(1)} %slice_add_fusion), channel_id=1, source_target_pairs={{0,4},{1,5},{2,6},{3,7},{4,0},{5,1},{6,2},{7,3},{8,12},{9,13},{10,... | collective-permute-start | bytes 393224 | tf_op jit(solution)/shard_map/ppermute | solution.py:144

commit v21 on v20

--- a/solution.py
+++ b/solution.py
@@ -178,7 +178,7 @@
         [part[o * rows:(o + 1) * rows] for o in range(8)], train_mate, n
     )
     test_part = tp[:half] + lax.ppermute(tp[half:], AXES, core_pairs(n))
-    test_attr = cube_reduce(
+    test_attr = cube_reduce_square(
         [test_part[o * rows:(o + 1) * rows] for o in range(8)], test_mate, n
     )
     return (train_attr, test_attr)

time: 138 us -> 139 us (level)
    ppermute x3 -> x0, waiting for transfers between devices: 7.04 us -> none  [cube_reduce(): lax.ppermute(jnp.concatenate([blocks[o] for o in send]), AXES, mate_pairs...]
    ppermute x3 -> x6, waiting for transfers between devices: 2.49 us -> 8.46 us  [cube_reduce_square(): lax.ppermute(jnp.concatenate([blocks[o] for o in send]), AXES, offset_pai...]
    ppermute x3 -> x6, starting transfers between devices: 3.35 us -> 6.74 us  [cube_reduce_square(): lax.ppermute(jnp.concatenate([blocks[o] for o in send]), AXES, offset_pai...]
    ppermute x3 -> x0, starting transfers between devices: 2.46 us -> none  [cube_reduce(): lax.ppermute(jnp.concatenate([blocks[o] for o in send]), AXES, mate_pairs...]
    ppermute x1 -> x2, waiting for transfers between devices: 3.16 us -> 4.42 us  [cube_reduce_square(): got = lax.ppermute(blocks[4], AXES, offset_pairs(n, 4, mate))]
  transfers between devices with their start and end apart: 26 -> 27, of which waited for: 18 -> 17; matrix products, arithmetic and copies ran while one was open for 9% -> 9% of each run, Pallas kernels for 0% -> 0%
where the time goes in v21:
time: 139 us
  waiting for transfers between devices  76.5 us (55%)
  starting transfers between devices  37.2 us (27%)
  matrix products  11.2 us (8%)
  other arithmetic  7.41 us (5%)
  local copies, waits for them, and re-layouts  5.52 us (4%)
    ppermute x15, waiting for transfers between devices, chain(): got = lax.ppermute(buf, AXES, mate_pairs(n, a, mate))  63.1 us
    ppermute x15, starting transfers between devices, chain(): got = lax.ppermute(buf, AXES, mate_pairs(n, a, mate))  28.4 us
    dot_general x2, matrix products, partial(): lax.dot_general(t, te_all, (((1,), (1,)), ((), ())), preferred_element_ty...  9.57 us
    ppermute x6, waiting for transfers between devices, cube_reduce_square(): lax.ppermute(jnp.concatenate([blocks[o] for o in send]), AXES, offset_pai...  8.46 us
    ppermute x6, starting transfers between devices, cube_reduce_square(): lax.ppermute(jnp.concatenate([blocks[o] for o in send]), AXES, offset_pai...  6.74 us
    ppermute x2, waiting for transfers between devices, cube_reduce_square(): got = lax.ppermute(blocks[4], AXES, offset_pairs(n, 4, mate))  4.42 us
  transfers between devices with their start and end apart: 27, of which 17 were waited for; matrix products, arithmetic and copies ran while one was open for 9% of the time, Pallas kernels for 0%

profile of v21, /device:TPU:0, one launch (start us, length us, event | category | flops | bytes accessed | tf_op | source)
XLA Modules:
  0.0 139.1 jit_solution(17768780518587221078)
XLA Ops:
  0.7 1.3 fusion.43
  5.1 2.9 %collective-permute-start.8 = (bf16[128,1408]{1,0:T(8,128)(2,1)S(1)}, bf16[128,1408]{1,0:T(8,128)(2,1)S(1)}, u32[]{:S(2)}, u32[]{:S(2)}) collective-permute-start(bf16[128,1408]{1,0:T(8,128)(2,1)S(1)} %get-tuple-element.44), channel_id=1, source_target_pairs={{0,48},{1,49},{2,50},{3,51},{4,52},{5,53},{6,54},{7,55},{8,56},{9,... | collective-permute-start | bytes 1081352 | tf_op jit(solution)/shard_map/ppermute | solution.py:83
  8.0 4.0 %collective-permute-start.12 = (bf16[128,1408]{1,0:T(8,128)(2,1)S(1)}, bf16[128,1408]{1,0:T(8,128)(2,1)S(1)}, u32[]{:S(2)}, u32[]{:S(2)}) collective-permute-start(bf16[128,1408]{1,0:T(8,128)(2,1)S(1)} %get-tuple-element.45), channel_id=1, source_target_pairs={{0,12},{1,13},{2,14},{3,15},{4,8},{5,9},{6,10},{7,11},{8,4},{9,5},... | collective-permute-start | bytes 1081352 | tf_op jit(solution)/shard_map/ppermute | solution.py:83
  12.1 3.0 %collective-permute-start.9 = (bf16[128,1408]{1,0:T(8,128)(2,1)S(1)}, bf16[128,1408]{1,0:T(8,128)(2,1)S(1)}, u32[]{:S(2)}, u32[]{:S(2)}) collective-permute-start(bf16[128,1408]{1,0:T(8,128)(2,1)S(1)} %get-tuple-element.46), channel_id=1, source_target_pairs={{0,66},{1,67},{2,64},{3,65},{4,70},{5,71},{6,68},{7,69},{8,74},{9,... | collective-permute-start | bytes 1081352 | tf_op jit(solution)/shard_map/ppermute | solution.py:83
  16.9 3.2 %collective-permute-start.14 = (bf16[256,1408]{1,0:T(8,128)(2,1)S(1)}, bf16[256,1408]{1,0:T(8,128)(2,1)S(1)}, u32[]{:S(2)}, u32[]{:S(2)}) collective-permute-start(bf16[256,1408]{1,0:T(8,128)(2,1)S(1)} %pad_maximum_fusion.18), channel_id=1, source_target_pairs={{0,66},{1,67},{2,64},{3,65},{4,70},{5,71},{6,68},{7,69},{8,74},{9,... | collective-permute-start | bytes 2162696 | tf_op jit(solution)/shard_map/ppermute | solution.py:83
  20.6 2.4 %collective-permute-start.13 = (bf16[256,1408]{1,0:T(8,128)(2,1)S(1)}, bf16[256,1408]{1,0:T(8,128)(2,1)S(1)}, u32[]{:S(2)}, u32[]{:S(2)}) collective-permute-start(bf16[256,1408]{1,0:T(8,128)(2,1)S(1)} %pad_maximum_fusion.17), channel_id=1, source_target_pairs={{0,48},{1,49},{2,50},{3,51},{4,52},{5,53},{6,54},{7,55},{8,56},{9,... | collective-permute-start | bytes 2162696 | tf_op jit(solution)/shard_map/ppermute | solution.py:83
  23.0 1.6 %collective-permute-done.9 = bf16[128,1408]{1,0:T(8,128)(2,1)S(1)} collective-permute-done((bf16[128,1408]{1,0:T(8,128)(2,1)S(1)}, bf16[128,1408]{1,0:T(8,128)(2,1)S(1)}, u32[]{:S(2)}, u32[]{:S(2)}) %collective-permute-start.9) | collective-permute-done | bytes 360480 | tf_op jit(solution)/shard_map/ppermute | solution.py:83
  24.7 2.5 %collective-permute-start.10 = (bf16[256,1408]{1,0:T(8,128)(2,1)S(1)}, bf16[256,1408]{1,0:T(8,128)(2,1)S(1)}, u32[]{:S(2)}, u32[]{:S(2)}) collective-permute-start(bf16[256,1408]{1,0:T(8,128)(2,1)S(1)} %pad_maximum_fusion.16), channel_id=1, source_target_pairs={{0,12},{1,13},{2,14},{3,15},{4,8},{5,9},{6,10},{7,11},{8,4},{9,5},... | collective-permute-start | bytes 2162696 | tf_op jit(solution)/shard_map/ppermute | solution.py:83
  27.2 1.2 collective-permute-done.1
  29.3 1.8 %collective-permute-start.3 = (bf16[256,2176]{1,0:T(8,128)(2,1)S(1)}, bf16[256,2176]{1,0:T(8,128)(2,1)S(1)}, u32[]{:S(2)}, u32[]{:S(2)}) collective-permute-start(bf16[256,2176]{1,0:T(8,128)(2,1)S(1)} %pad_maximum_fusion.5), channel_id=1, source_target_pairs={{0,16},{1,17},{2,18},{3,19},{4,20},{5,21},{6,22},{7,23},{8,24},{9,... | collective-permute-start | bytes 3342344 | tf_op jit(solution)/shard_map/ppermute | solution.py:83
  31.1 7.6 %collective-permute-done.14 = bf16[256,1408]{1,0:T(8,128)(2,1)S(1)} collective-permute-done((bf16[256,1408]{1,0:T(8,128)(2,1)S(1)}, bf16[256,1408]{1,0:T(8,128)(2,1)S(1)}, u32[]{:S(2)}, u32[]{:S(2)}) %collective-permute-start.14) | collective-permute-done | bytes 720928 | tf_op jit(solution)/shard_map/ppermute | solution.py:83
  38.8 1.1 collective-permute-start.16
  40.1 3.0 %collective-permute-start.15 = (bf16[512,1408]{1,0:T(8,128)(2,1)S(1)}, bf16[512,1408]{1,0:T(8,128)(2,1)S(1)}, u32[]{:S(2)}, u32[]{:S(2)}) collective-permute-start(bf16[512,1408]{1,0:T(8,128)(2,1)S(1)} %pad_maximum_fusion.3), channel_id=1, source_target_pairs={{0,66},{1,67},{2,64},{3,65},{4,70},{5,71},{6,68},{7,69},{8,74},{9,... | collective-permute-start | bytes 4325384 | tf_op jit(solution)/shard_map/ppermute | solution.py:83
  43.9 2.2 %collective-permute-start.11 = (bf16[512,1408]{1,0:T(8,128)(2,1)S(1)}, bf16[512,1408]{1,0:T(8,128)(2,1)S(1)}, u32[]{:S(2)}, u32[]{:S(2)}) collective-permute-start(bf16[512,1408]{1,0:T(8,128)(2,1)S(1)} %pad_maximum_fusion.2), channel_id=1, source_target_pairs={{0,48},{1,49},{2,50},{3,51},{4,52},{5,53},{6,54},{7,55},{8,56},{9,... | collective-permute-start | bytes 4325384 | tf_op jit(solution)/shard_map/ppermute | solution.py:83
  46.2 5.7 %collective-permute-done.4 = bf16[256,2048]{1,0:T(8,128)(2,1)S(1)} collective-permute-done((bf16[256,2048]{1,0:T(8,128)(2,1)S(1)}, bf16[256,2048]{1,0:T(8,128)(2,1)S(1)}, u32[]{:S(2)}, u32[]{:S(2)}) %collective-permute-start.4) | collective-permute-done | bytes 1048608 | tf_op jit(solution)/shard_map/ppermute | solution.py:83
  52.3 1.6 %collective-permute-done.3 = bf16[256,2176]{1,0:T(8,128)(2,1)S(1)} collective-permute-done((bf16[256,2176]{1,0:T(8,128)(2,1)S(1)}, bf16[256,2176]{1,0:T(8,128)(2,1)S(1)}, u32[]{:S(2)}, u32[]{:S(2)}) %collective-permute-start.3) | collective-permute-done | bytes 1114144 | tf_op jit(solution)/shard_map/ppermute | solution.py:83
  54.1 1.5 %collective-permute-start.5 = (bf16[512,2176]{1,0:T(8,128)(2,1)S(1)}, bf16[512,2176]{1,0:T(8,128)(2,1)S(1)}, u32[]{:S(2)}, u32[]{:S(2)}) collective-permute-start(bf16[512,2176]{1,0:T(8,128)(2,1)S(1)} %pad_maximum_fusion), channel_id=1, source_target_pairs={{0,64},{1,65},{2,66},{3,67},{4,68},{5,69},{6,70},{7,71},{8,72},{9,... | collective-permute-start | bytes 6684680 | tf_op jit(solution)/shard_map/ppermute | solution.py:83
  55.8 0.9 fusion.26
  56.7 19.2 %collective-permute-done.11 = bf16[512,1408]{1,0:T(8,128)(2,1)S(1)} collective-permute-done((bf16[512,1408]{1,0:T(8,128)(2,1)S(1)}, bf16[512,1408]{1,0:T(8,128)(2,1)S(1)}, u32[]{:S(2)}, u32[]{:S(2)}) %collective-permute-start.11) | collective-permute-done | bytes 1441824 | tf_op jit(solution)/shard_map/ppermute | solution.py:83
  77.7 19.5 %collective-permute-done.6 = bf16[512,2048]{1,0:T(8,128)(2,1)S(1)} collective-permute-done((bf16[512,2048]{1,0:T(8,128)(2,1)S(1)}, bf16[512,2048]{1,0:T(8,128)(2,1)S(1)}, u32[]{:S(2)}, u32[]{:S(2)}) %collective-permute-start.6) | collective-permute-done | bytes 2097184 | tf_op jit(solution)/shard_map/ppermute | solution.py:83
  97.4 4.6 %collective-permute-done.5 = bf16[512,2176]{1,0:T(8,128)(2,1)S(1)} collective-permute-done((bf16[512,2176]{1,0:T(8,128)(2,1)S(1)}, bf16[512,2176]{1,0:T(8,128)(2,1)S(1)}, u32[]{:S(2)}, u32[]{:S(2)}) %collective-permute-start.5) | collective-permute-done | bytes 2228256 | tf_op jit(solution)/shard_map/ppermute | solution.py:83
  103.1 4.8 %fusion.51 = f32[512,1024]{1,0:T(8,128)S(1)} fusion(bf16[512,4224]{1,0:T(8,128)(2,1)S(1)} %get-tuple-element.30, bf16[1024,4224]{1,0:T(8,128)(2,1)S(1)} %slice_dynamic-update-slice_fusion), kind=kOutput, calls=%fused_computation.159 | convolution fusion | flops 4429185024 | bytes 15073280 | tf_op jit(solution)/shard_map/dot_general | solution.py:160
  108.4 4.8 %fusion.50 = f32[512,1024]{1,0:T(8,128)S(1)} fusion(bf16[512,4224]{1,0:T(8,128)(2,1)S(1)} %get-tuple-element.31, bf16[1024,4224]{1,0:T(8,128)(2,1)S(1)} %slice_dynamic-update-slice_fusion), kind=kOutput, calls=%fused_computation.158 | convolution fusion | flops 4429185024 | bytes 15073280 | tf_op jit(solution)/shard_map/dot_general | solution.py:160
  115.0 0.9 multiply_reduce_fusion
  116.8 1.6 %collective-permute-start.18 = (f32[128,512]{1,0:T(8,128)S(1)}, f32[128,512]{1,0:T(8,128)S(1)}, u32[]{:S(2)}, u32[]{:S(2)}) collective-permute-start(f32[128,512]{1,0:T(8,128)S(1)} %pad_maximum_fusion.29), channel_id=1, source_target_pairs={{0,16},{1,17},{2,18},{3,19},{4,20},{5,21},{6,22},{7,23},{8,24},{9,... | collective-permute-start | bytes 786440 | tf_op jit(solution)/shard_map/ppermute | solution.py:141
  118.9 1.7 %collective-permute-start.20 = (f32[128,512]{1,0:T(8,128)S(1)}, f32[128,512]{1,0:T(8,128)S(1)}, u32[]{:S(2)}, u32[]{:S(2)}) collective-permute-start(f32[128,512]{1,0:T(8,128)S(1)} %pad_maximum_fusion.31), channel_id=1, source_target_pairs={{0,80},{1,81},{2,82},{3,83},{4,84},{5,85},{6,86},{7,87},{8,88},{9,... | collective-permute-start | bytes 786440 | tf_op jit(solution)/shard_map/ppermute | solution.py:141
  120.7 0.9 collective-permute-start.23
  122.6 2.9 %collective-permute-done.23 = f32[128]{0:T(128)S(1)} collective-permute-done((f32[128]{0:T(128)S(1)}, f32[128]{0:T(128)S(1)}, u32[]{:S(2)}, u32[]{:S(2)}) %collective-permute-start.23) | collective-permute-done | bytes 544 | tf_op jit(solution)/shard_map/ppermute | solution.py:141
  125.5 1.3 collective-permute-start.25
  126.8 5.5 %collective-permute-done.25 = f32[128]{0:T(128)S(1)} collective-permute-done((f32[128]{0:T(128)S(1)}, f32[128]{0:T(128)S(1)}, u32[]{:S(2)}, u32[]{:S(2)}) %collective-permute-start.25) | collective-permute-done | bytes 544 | tf_op jit(solution)/shard_map/ppermute | solution.py:141
  132.4 0.9 collective-permute-start.26
  133.5 3.7 %collective-permute-done.26 = f32[64]{0:T(128)S(1)} collective-permute-done((f32[64]{0:T(128)S(1)}, f32[64]{0:T(128)S(1)}, u32[]{:S(2)}, u32[]{:S(2)}) %collective-permute-start.26) | collective-permute-done | bytes 288 | tf_op jit(solution)/shard_map/ppermute | solution.py:144
  (119 shorter events, 17.8 us)
Async XLA Ops:
  2.7 1.2 copy-start
  2.8 1.2 copy-start.1
  3.0 2.0 %collective-permute-start.7 = (bf16[64,4224]{1,0:T(8,128)(2,1)S(1)}, bf16[64,4224]{1,0:T(8,128)(2,1)S(1)}, u32[]{:S(2)}, u32[]{:S(2)}) collective-permute-start(bf16[64,4224]{1,0:T(8,128)(2,1)S(1)} %get-tuple-element.47), channel_id=1, source_target_pairs={{0,1},{1,0},{2,3},{3,2},{4,5},{5,4},{6,7},{7,6},{8,9},{9,8},{10,11... | collective-permute-start | bytes 1622024 | tf_op jit(solution)/shard_map/ppermute | solution.py:96
  4.4 10.7 %collective-permute-start = (bf16[64,4224]{1,0:T(8,128)(2,1)S(1)}, bf16[64,4224]{1,0:T(8,128)(2,1)S(1)}, u32[]{:S(2)}, u32[]{:S(2)}) collective-permute-start(bf16[64,4224]{1,0:T(8,128)(2,1)S(1)} %get-tuple-element.48), channel_id=1, source_target_pairs={{0,1},{1,0},{2,3},{3,2},{4,5},{5,4},{6,7},{7,6},{8,9},{9,8},{10,11... | collective-permute-start | bytes 1622024 | tf_op jit(solution)/shard_map/ppermute | solution.py:96
  5.1 11.7 %collective-permute-start.8 = (bf16[128,1408]{1,0:T(8,128)(2,1)S(1)}, bf16[128,1408]{1,0:T(8,128)(2,1)S(1)}, u32[]{:S(2)}, u32[]{:S(2)}) collective-permute-start(bf16[128,1408]{1,0:T(8,128)(2,1)S(1)} %get-tuple-element.44), channel_id=1, source_target_pairs={{0,48},{1,49},{2,50},{3,51},{4,52},{5,53},{6,54},{7,55},{8,56},{9,... | collective-permute-start | bytes 1081352 | tf_op jit(solution)/shard_map/ppermute | solution.py:83
  8.0 12.5 %collective-permute-start.12 = (bf16[128,1408]{1,0:T(8,128)(2,1)S(1)}, bf16[128,1408]{1,0:T(8,128)(2,1)S(1)}, u32[]{:S(2)}, u32[]{:S(2)}) collective-permute-start(bf16[128,1408]{1,0:T(8,128)(2,1)S(1)} %get-tuple-element.45), channel_id=1, source_target_pairs={{0,12},{1,13},{2,14},{3,15},{4,8},{5,9},{6,10},{7,11},{8,4},{9,5},... | collective-permute-start | bytes 1081352 | tf_op jit(solution)/shard_map/ppermute | solution.py:83
  12.1 12.5 %collective-permute-start.9 = (bf16[128,1408]{1,0:T(8,128)(2,1)S(1)}, bf16[128,1408]{1,0:T(8,128)(2,1)S(1)}, u32[]{:S(2)}, u32[]{:S(2)}) collective-permute-start(bf16[128,1408]{1,0:T(8,128)(2,1)S(1)} %get-tuple-element.46), channel_id=1, source_target_pairs={{0,66},{1,67},{2,64},{3,65},{4,70},{5,71},{6,68},{7,69},{8,74},{9,... | collective-permute-start | bytes 1081352 | tf_op jit(solution)/shard_map/ppermute | solution.py:83
  15.1 13.2 %collective-permute-start.1 = (bf16[128,2048]{1,0:T(8,128)(2,1)S(1)}, bf16[128,2048]{1,0:T(8,128)(2,1)S(1)}, u32[]{:S(2)}, u32[]{:S(2)}) collective-permute-start(bf16[128,2048]{1,0:T(8,128)(2,1)S(1)} %pad_maximum_fusion.27), channel_id=1, source_target_pairs={{0,16},{1,17},{2,18},{3,19},{4,20},{5,21},{6,22},{7,23},{8,24},{9,... | collective-permute-start | bytes 1572872 | tf_op jit(solution)/shard_map/ppermute | solution.py:83
  15.5 13.7 %collective-permute-start.2 = (bf16[128,2176]{1,0:T(8,128)(2,1)S(1)}, bf16[128,2176]{1,0:T(8,128)(2,1)S(1)}, u32[]{:S(2)}, u32[]{:S(2)}) collective-permute-start(bf16[128,2176]{1,0:T(8,128)(2,1)S(1)} %pad_maximum_fusion.19), channel_id=1, source_target_pairs={{0,4},{1,5},{2,6},{3,7},{4,0},{5,1},{6,2},{7,3},{8,12},{9,13},{10,... | collective-permute-start | bytes 1671176 | tf_op jit(solution)/shard_map/ppermute | solution.py:83
  16.9 21.8 %collective-permute-start.14 = (bf16[256,1408]{1,0:T(8,128)(2,1)S(1)}, bf16[256,1408]{1,0:T(8,128)(2,1)S(1)}, u32[]{:S(2)}, u32[]{:S(2)}) collective-permute-start(bf16[256,1408]{1,0:T(8,128)(2,1)S(1)} %pad_maximum_fusion.18), channel_id=1, source_target_pairs={{0,66},{1,67},{2,64},{3,65},{4,70},{5,71},{6,68},{7,69},{8,74},{9,... | collective-permute-start | bytes 2162696 | tf_op jit(solution)/shard_map/ppermute | solution.py:83
  20.6 19.4 %collective-permute-start.13 = (bf16[256,1408]{1,0:T(8,128)(2,1)S(1)}, bf16[256,1408]{1,0:T(8,128)(2,1)S(1)}, u32[]{:S(2)}, u32[]{:S(2)}) collective-permute-start(bf16[256,1408]{1,0:T(8,128)(2,1)S(1)} %pad_maximum_fusion.17), channel_id=1, source_target_pairs={{0,48},{1,49},{2,50},{3,51},{4,52},{5,53},{6,54},{7,55},{8,56},{9,... | collective-permute-start | bytes 2162696 | tf_op jit(solution)/shard_map/ppermute | solution.py:83
  24.7 19.1 %collective-permute-start.10 = (bf16[256,1408]{1,0:T(8,128)(2,1)S(1)}, bf16[256,1408]{1,0:T(8,128)(2,1)S(1)}, u32[]{:S(2)}, u32[]{:S(2)}) collective-permute-start(bf16[256,1408]{1,0:T(8,128)(2,1)S(1)} %pad_maximum_fusion.16), channel_id=1, source_target_pairs={{0,12},{1,13},{2,14},{3,15},{4,8},{5,9},{6,10},{7,11},{8,4},{9,5},... | collective-permute-start | bytes 2162696 | tf_op jit(solution)/shard_map/ppermute | solution.py:83
  28.4 23.5 %collective-permute-start.4 = (bf16[256,2048]{1,0:T(8,128)(2,1)S(1)}, bf16[256,2048]{1,0:T(8,128)(2,1)S(1)}, u32[]{:S(2)}, u32[]{:S(2)}) collective-permute-start(bf16[256,2048]{1,0:T(8,128)(2,1)S(1)} %pad_maximum_fusion.15), channel_id=1, source_target_pairs={{0,64},{1,65},{2,66},{3,67},{4,68},{5,69},{6,70},{7,71},{8,72},{9,... | collective-permute-start | bytes 3145736 | tf_op jit(solution)/shard_map/ppermute | solution.py:83
  29.3 24.7 %collective-permute-start.3 = (bf16[256,2176]{1,0:T(8,128)(2,1)S(1)}, bf16[256,2176]{1,0:T(8,128)(2,1)S(1)}, u32[]{:S(2)}, u32[]{:S(2)}) collective-permute-start(bf16[256,2176]{1,0:T(8,128)(2,1)S(1)} %pad_maximum_fusion.5), channel_id=1, source_target_pairs={{0,16},{1,17},{2,18},{3,19},{4,20},{5,21},{6,22},{7,23},{8,24},{9,... | collective-permute-start | bytes 3342344 | tf_op jit(solution)/shard_map/ppermute | solution.py:83
  38.8 37.7 %collective-permute-start.16 = (bf16[512,1408]{1,0:T(8,128)(2,1)S(1)}, bf16[512,1408]{1,0:T(8,128)(2,1)S(1)}, u32[]{:S(2)}, u32[]{:S(2)}) collective-permute-start(bf16[512,1408]{1,0:T(8,128)(2,1)S(1)} %pad_maximum_fusion.4), channel_id=1, source_target_pairs={{0,12},{1,13},{2,14},{3,15},{4,8},{5,9},{6,10},{7,11},{8,4},{9,5},... | collective-permute-start | bytes 4325384 | tf_op jit(solution)/shard_map/ppermute | solution.py:83
  40.1 36.0 %collective-permute-start.15 = (bf16[512,1408]{1,0:T(8,128)(2,1)S(1)}, bf16[512,1408]{1,0:T(8,128)(2,1)S(1)}, u32[]{:S(2)}, u32[]{:S(2)}) collective-permute-start(bf16[512,1408]{1,0:T(8,128)(2,1)S(1)} %pad_maximum_fusion.3), channel_id=1, source_target_pairs={{0,66},{1,67},{2,64},{3,65},{4,70},{5,71},{6,68},{7,69},{8,74},{9,... | collective-permute-start | bytes 4325384 | tf_op jit(solution)/shard_map/ppermute | solution.py:83
  43.9 31.9 %collective-permute-start.11 = (bf16[512,1408]{1,0:T(8,128)(2,1)S(1)}, bf16[512,1408]{1,0:T(8,128)(2,1)S(1)}, u32[]{:S(2)}, u32[]{:S(2)}) collective-permute-start(bf16[512,1408]{1,0:T(8,128)(2,1)S(1)} %pad_maximum_fusion.2), channel_id=1, source_target_pairs={{0,48},{1,49},{2,50},{3,51},{4,52},{5,53},{6,54},{7,55},{8,56},{9,... | collective-permute-start | bytes 4325384 | tf_op jit(solution)/shard_map/ppermute | solution.py:83
  52.1 45.1 %collective-permute-start.6 = (bf16[512,2048]{1,0:T(8,128)(2,1)S(1)}, bf16[512,2048]{1,0:T(8,128)(2,1)S(1)}, u32[]{:S(2)}, u32[]{:S(2)}) collective-permute-start(bf16[512,2048]{1,0:T(8,128)(2,1)S(1)} %pad_maximum_fusion.1), channel_id=1, source_target_pairs={{0,4},{1,5},{2,6},{3,7},{4,0},{5,1},{6,2},{7,3},{8,12},{9,13},{10,... | collective-permute-start | bytes 6291464 | tf_op jit(solution)/shard_map/ppermute | solution.py:83
  54.1 47.9 %collective-permute-start.5 = (bf16[512,2176]{1,0:T(8,128)(2,1)S(1)}, bf16[512,2176]{1,0:T(8,128)(2,1)S(1)}, u32[]{:S(2)}, u32[]{:S(2)}) collective-permute-start(bf16[512,2176]{1,0:T(8,128)(2,1)S(1)} %pad_maximum_fusion), channel_id=1, source_target_pairs={{0,64},{1,65},{2,66},{3,67},{4,68},{5,69},{6,70},{7,71},{8,72},{9,... | collective-permute-start | bytes 6684680 | tf_op jit(solution)/shard_map/ppermute | solution.py:83
  77.6 24.6 %slice-start = ((s8[4325376]{0:T(1024)(128)(4,1)}), s8[4194304]{0:T(1024)(128)(4,1)S(1)}, s32[]{:S(2)}) async-start(s8[4325376]{0:T(1024)(128)(4,1)} %bitcast.6), calls=%async_computation | async-start | bytes 8388608
  77.7 24.5 %slice-start.1 = ((s8[4325376]{0:T(1024)(128)(4,1)}), s8[131072]{0:T(1024)(128)(4,1)S(1)}, s32[]{:S(2)}) async-start(s8[4325376]{0:T(1024)(128)(4,1)} %bitcast.6), calls=%async_computation.1 | async-start | bytes 262144
  107.9 5.7 %collective-permute-start.17 = (f32[512,1024]{1,0:T(8,128)S(1)}, f32[512,1024]{1,0:T(8,128)S(1)}, u32[]{:S(2)}, u32[]{:S(2)}) collective-permute-start(f32[512,1024]{1,0:T(8,128)S(1)} %fusion.51), channel_id=1, source_target_pairs={{0,1},{1,0},{2,3},{3,2},{4,5},{5,4},{6,7},{7,6},{8,9},{9,8},{10,11... | collective-permute-start | bytes 6291464 | tf_op jit(solution)/shard_map/ppermute | solution.py:164
  115.9 4.7 %collective-permute-start.22 = (f32[512]{0:T(512)S(1)}, f32[512]{0:T(512)S(1)}, u32[]{:S(2)}, u32[]{:S(2)}) collective-permute-start(f32[512]{0:T(512)S(1)} %slice.414), channel_id=1, source_target_pairs={{0,1},{1,0},{2,3},{3,2},{4,5},{5,4},{6,7},{7,6},{8,9},{9,8},{10,11... | collective-permute-start | bytes 6152 | tf_op jit(solution)/shard_map/ppermute | solution.py:180
  116.8 16.5 %collective-permute-start.18 = (f32[128,512]{1,0:T(8,128)S(1)}, f32[128,512]{1,0:T(8,128)S(1)}, u32[]{:S(2)}, u32[]{:S(2)}) collective-permute-start(f32[128,512]{1,0:T(8,128)S(1)} %pad_maximum_fusion.29), channel_id=1, source_target_pairs={{0,16},{1,17},{2,18},{3,19},{4,20},{5,21},{6,22},{7,23},{8,24},{9,... | collective-permute-start | bytes 786440 | tf_op jit(solution)/shard_map/ppermute | solution.py:141
  118.5 14.8 %collective-permute-start.19 = (f32[128,512]{1,0:T(8,128)S(1)}, f32[128,512]{1,0:T(8,128)S(1)}, u32[]{:S(2)}, u32[]{:S(2)}) collective-permute-start(f32[128,512]{1,0:T(8,128)S(1)} %pad_maximum_fusion.30), channel_id=1, source_target_pairs={{0,64},{1,65},{2,66},{3,67},{4,68},{5,69},{6,70},{7,71},{8,72},{9,... | collective-permute-start | bytes 786440 | tf_op jit(solution)/shard_map/ppermute | solution.py:141
  118.9 14.4 %collective-permute-start.20 = (f32[128,512]{1,0:T(8,128)S(1)}, f32[128,512]{1,0:T(8,128)S(1)}, u32[]{:S(2)}, u32[]{:S(2)}) collective-permute-start(f32[128,512]{1,0:T(8,128)S(1)} %pad_maximum_fusion.31), channel_id=1, source_target_pairs={{0,80},{1,81},{2,82},{3,83},{4,84},{5,85},{6,86},{7,87},{8,88},{9,... | collective-permute-start | bytes 786440 | tf_op jit(solution)/shard_map/ppermute | solution.py:141
  120.7 4.8 %collective-permute-start.23 = (f32[128]{0:T(128)S(1)}, f32[128]{0:T(128)S(1)}, u32[]{:S(2)}, u32[]{:S(2)}) collective-permute-start(f32[128]{0:T(128)S(1)} %pad_maximum_fusion.32), channel_id=1, source_target_pairs={{0,48},{1,49},{2,50},{3,51},{4,52},{5,53},{6,54},{7,55},{8,56},{9,... | collective-permute-start | bytes 1544 | tf_op jit(solution)/shard_map/ppermute | solution.py:141
  121.7 5.1 %collective-permute-start.24 = (f32[128]{0:T(128)S(1)}, f32[128]{0:T(128)S(1)}, u32[]{:S(2)}, u32[]{:S(2)}) collective-permute-start(f32[128]{0:T(128)S(1)} %pad_maximum_fusion.33), channel_id=1, source_target_pairs={{0,66},{1,67},{2,64},{3,65},{4,70},{5,71},{6,68},{7,69},{8,74},{9,... | collective-permute-start | bytes 1544 | tf_op jit(solution)/shard_map/ppermute | solution.py:141
  125.5 6.9 %collective-permute-start.25 = (f32[128]{0:T(128)S(1)}, f32[128]{0:T(128)S(1)}, u32[]{:S(2)}, u32[]{:S(2)}) collective-permute-start(f32[128]{0:T(128)S(1)} %pad_maximum_fusion.34), channel_id=1, source_target_pairs={{0,114},{1,115},{2,112},{3,113},{4,118},{5,119},{6,116},{7,117},{8... | collective-permute-start | bytes 1544 | tf_op jit(solution)/shard_map/ppermute | solution.py:141
  132.4 4.8 %collective-permute-start.26 = (f32[64]{0:T(128)S(1)}, f32[64]{0:T(128)S(1)}, u32[]{:S(2)}, u32[]{:S(2)}) collective-permute-start(f32[64]{0:T(128)S(1)} %slice_add_fusion.7), channel_id=1, source_target_pairs={{0,12},{1,13},{2,14},{3,15},{4,8},{5,9},{6,10},{7,11},{8,4},{9,5},... | collective-permute-start | bytes 776 | tf_op jit(solution)/shard_map/ppermute | solution.py:144
  133.4 5.0 %collective-permute-start.21 = (f32[64,512]{1,0:T(8,128)S(1)}, f32[64,512]{1,0:T(8,128)S(1)}, u32[]{:S(2)}, u32[]{:S(2)}) collective-permute-start(f32[64,512]{1,0:T(8,128)S(1)} %slice_add_fusion), channel_id=1, source_target_pairs={{0,4},{1,5},{2,6},{3,7},{4,0},{5,1},{6,2},{7,3},{8,12},{9,13},{10,... | collective-permute-start | bytes 393224 | tf_op jit(solution)/shard_map/ppermute | solution.py:144

commit v22 on v20

--- a/solution.py
+++ b/solution.py
@@ -161,22 +161,33 @@
             t, te_all, (((1,), (1,)), ((), ())), preferred_element_type=jnp.float32
         )
 
-    got = lax.ppermute(partial(tr_all[half:]), AXES, core_pairs(n))
-    own = lax.optimization_barrier(partial(tr_all[:half]))
-    raw = own + jnp.concatenate([got[:, half:], got[:, :half]], axis=1)
     tr_mine = tr_all[:half]
     scale = tr_mine[:, side].astype(jnp.float32)
     train_hot = indicator(join_class(tr_mine, side + 1))
     test_hot = indicator(join_class(te_all, side + 4))
-    w = jnp.tanh(scale[:, None] * raw).astype(jnp.bfloat16)
-    part = jnp.dot(w, test_hot, preferred_element_type=jnp.float32)
+    q = half // 2
+
+    def weights(lo, hi):
+        got = lax.ppermute(partial(tr_all[half + lo:half + hi]), AXES, core_pairs(n))
+        own = lax.optimization_barrier(partial(tr_all[lo:hi]))
+        raw = own + jnp.concatenate([got[:, half:], got[:, :half]], axis=1)
+        return jnp.tanh(scale[lo:hi, None] * raw).astype(jnp.bfloat16)
+
+    w_hi = weights(q, half)
+    part_hi = jnp.dot(w_hi, test_hot, preferred_element_type=jnp.float32)
+    from_z = lax.ppermute(part_hi, AXES, offset_pairs(n, 4, train_mate))
+    w_lo = weights(0, q)
+    part_lo = jnp.dot(w_lo, test_hot, preferred_element_type=jnp.float32) + from_z
+    blocks = [part_lo[o * rows:(o + 1) * rows] for o in range(4)]
+    for m in (1, 2, 3):
+        blocks[0] = blocks[0] + lax.ppermute(blocks[m], AXES, offset_pairs(n, m, train_mate))
+    train_attr = blocks[0]
     per_class = lax.dot_general(
-        w, train_hot, (((0,), (0,)), ((), ())), preferred_element_type=jnp.float32
+        w_lo, train_hot[:q], (((0,), (0,)), ((), ())), preferred_element_type=jnp.float32
+    ) + lax.dot_general(
+        w_hi, train_hot[q:], (((0,), (0,)), ((), ())), preferred_element_type=jnp.float32
     )
     tp = jnp.sum(per_class * test_hot.astype(jnp.float32), axis=1)
-    train_attr = cube_reduce_square(
-        [part[o * rows:(o + 1) * rows] for o in range(8)], train_mate, n
-    )
     test_part = tp[:half] + lax.ppermute(tp[half:], AXES, core_pairs(n))
     test_attr = cube_reduce(
         [test_part[o * rows:(o + 1) * rows] for o in range(8)], test_mate, n

time: 138 us -> 158 us (1.14)
  matrix products: 11.2 us -> 26.1 us
  local copies, waits for them, and re-layouts: 5.52 us -> 16.9 us
  waiting for transfers between devices: 76.3 us -> 69.1 us
    dot_general x2 -> x4, matrix products: 9.57 us -> 23.9 us  [partial(): lax.dot_general(t, te_all, (((1,), (1,)), ((), ())), preferred_element_ty...]
    ppermute x15, waiting for transfers between devices: 63.1 us -> 51.6 us  [chain(): got = lax.ppermute(buf, AXES, mate_pairs(n, a, mate))]
    unnamed x25 -> x20, local copies, waits for them, and re-layouts: 2.74 us -> 13.2 us
    ppermute x5 -> x6, waiting for transfers between devices: 5.65 us -> 7.98 us  [the longest x1 4.22 us: local(): from_z = lax.ppermute(part_hi, AXES, offset_pairs(n, 4, train_mate))]
    ppermute x5 -> x6, starting transfers between devices: 4.36 us -> 5.18 us  [the longest x3 3.57 us: local(): lax.ppermute(blocks[m], AXES, offset_pairs(n, m, train_mate))]
  transfers between devices with their start and end apart: 26 -> 27, of which waited for: 18 -> 20; matrix products, arithmetic and copies ran while one was open for 9% -> 25% of each run, Pallas kernels for 0% -> 0%
where the time goes in v22:
time: 158 us; the launch traced here: 156 us
  waiting for transfers between devices  69.1 us (44%)
  starting transfers between devices  35.6 us (23%)
  matrix products  26.1 us (17%)
  local copies, waits for them, and re-layouts  16.9 us (11%)
  other arithmetic  7.46 us (5%)
    ppermute x15, waiting for transfers between devices, chain(): got = lax.ppermute(buf, AXES, mate_pairs(n, a, mate))  51.6 us
    ppermute x15, starting transfers between devices, chain(): got = lax.ppermute(buf, AXES, mate_pairs(n, a, mate))  28.3 us
    dot_general x4, matrix products, partial(): lax.dot_general(t, te_all, (((1,), (1,)), ((), ())), preferred_element_ty...  23.9 us
    unnamed x20, local copies, waits for them, and re-layouts  13.2 us
    ppermute x3, waiting for transfers between devices, cube_reduce(): lax.ppermute(jnp.concatenate([blocks[o] for o in send]), AXES, mate_pairs...  7.46 us
    ppermute x1, waiting for transfers between devices, local(): from_z = lax.ppermute(part_hi, AXES, offset_pairs(n, 4, train_mate))  4.22 us
    ppermute x3, waiting for transfers between devices, local(): lax.ppermute(blocks[m], AXES, offset_pairs(n, m, train_mate))  3.76 us
    ppermute x3, starting transfers between devices, local(): lax.ppermute(blocks[m], AXES, offset_pairs(n, m, train_mate))  3.57 us
  transfers between devices with their start and end apart: 27, of which 20 were waited for; matrix products, arithmetic and copies ran while one was open for 25% of the time, Pallas kernels for 0%

profile of v22, /device:TPU:0, one launch (start us, length us, event | category | flops | bytes accessed | tf_op | source)
XLA Modules:
  0.0 156.3 jit_solution(14459027313742397417)
XLA Ops:
  0.7 1.3 fusion.131
  5.8 2.9 %collective-permute-start.8 = (bf16[128,1408]{1,0:T(8,128)(2,1)S(1)}, bf16[128,1408]{1,0:T(8,128)(2,1)S(1)}, u32[]{:S(2)}, u32[]{:S(2)}) collective-permute-start(bf16[128,1408]{1,0:T(8,128)(2,1)S(1)} %get-tuple-element.45), channel_id=1, source_target_pairs={{0,48},{1,49},{2,50},{3,51},{4,52},{5,53},{6,54},{7,55},{8,56},{9,... | collective-permute-start | bytes 1081352 | tf_op jit(solution)/shard_map/ppermute | solution.py:83
  8.8 4.0 %collective-permute-start.12 = (bf16[128,1408]{1,0:T(8,128)(2,1)S(1)}, bf16[128,1408]{1,0:T(8,128)(2,1)S(1)}, u32[]{:S(2)}, u32[]{:S(2)}) collective-permute-start(bf16[128,1408]{1,0:T(8,128)(2,1)S(1)} %get-tuple-element.46), channel_id=1, source_target_pairs={{0,12},{1,13},{2,14},{3,15},{4,8},{5,9},{6,10},{7,11},{8,4},{9,5},... | collective-permute-start | bytes 1081352 | tf_op jit(solution)/shard_map/ppermute | solution.py:83
  12.8 3.0 %collective-permute-start.9 = (bf16[128,1408]{1,0:T(8,128)(2,1)S(1)}, bf16[128,1408]{1,0:T(8,128)(2,1)S(1)}, u32[]{:S(2)}, u32[]{:S(2)}) collective-permute-start(bf16[128,1408]{1,0:T(8,128)(2,1)S(1)} %get-tuple-element.47), channel_id=1, source_target_pairs={{0,66},{1,67},{2,64},{3,65},{4,70},{5,71},{6,68},{7,69},{8,74},{9,... | collective-permute-start | bytes 1081352 | tf_op jit(solution)/shard_map/ppermute | solution.py:83
  16.3 1.3 collective-permute-done.8
  17.6 3.2 %collective-permute-start.14 = (bf16[256,1408]{1,0:T(8,128)(2,1)S(1)}, bf16[256,1408]{1,0:T(8,128)(2,1)S(1)}, u32[]{:S(2)}, u32[]{:S(2)}) collective-permute-start(bf16[256,1408]{1,0:T(8,128)(2,1)S(1)} %pad_maximum_fusion.20), channel_id=1, source_target_pairs={{0,66},{1,67},{2,64},{3,65},{4,70},{5,71},{6,68},{7,69},{8,74},{9,... | collective-permute-start | bytes 2162696 | tf_op jit(solution)/shard_map/ppermute | solution.py:83
  21.3 2.4 %collective-permute-start.13 = (bf16[256,1408]{1,0:T(8,128)(2,1)S(1)}, bf16[256,1408]{1,0:T(8,128)(2,1)S(1)}, u32[]{:S(2)}, u32[]{:S(2)}) collective-permute-start(bf16[256,1408]{1,0:T(8,128)(2,1)S(1)} %pad_maximum_fusion.19), channel_id=1, source_target_pairs={{0,48},{1,49},{2,50},{3,51},{4,52},{5,53},{6,54},{7,55},{8,56},{9,... | collective-permute-start | bytes 2162696 | tf_op jit(solution)/shard_map/ppermute | solution.py:83
  23.7 1.6 %collective-permute-done.9 = bf16[128,1408]{1,0:T(8,128)(2,1)S(1)} collective-permute-done((bf16[128,1408]{1,0:T(8,128)(2,1)S(1)}, bf16[128,1408]{1,0:T(8,128)(2,1)S(1)}, u32[]{:S(2)}, u32[]{:S(2)}) %collective-permute-start.9) | collective-permute-done | bytes 360480 | tf_op jit(solution)/shard_map/ppermute | solution.py:83
  25.4 2.5 %collective-permute-start.10 = (bf16[256,1408]{1,0:T(8,128)(2,1)S(1)}, bf16[256,1408]{1,0:T(8,128)(2,1)S(1)}, u32[]{:S(2)}, u32[]{:S(2)}) collective-permute-start(bf16[256,1408]{1,0:T(8,128)(2,1)S(1)} %pad_maximum_fusion.18), channel_id=1, source_target_pairs={{0,12},{1,13},{2,14},{3,15},{4,8},{5,9},{6,10},{7,11},{8,4},{9,5},... | collective-permute-start | bytes 2162696 | tf_op jit(solution)/shard_map/ppermute | solution.py:83
  27.9 1.3 collective-permute-done.1
  30.2 9.3 %collective-permute-done.14 = bf16[256,1408]{1,0:T(8,128)(2,1)S(1)} collective-permute-done((bf16[256,1408]{1,0:T(8,128)(2,1)S(1)}, bf16[256,1408]{1,0:T(8,128)(2,1)S(1)}, u32[]{:S(2)}, u32[]{:S(2)}) %collective-permute-start.14) | collective-permute-done | bytes 720928 | tf_op jit(solution)/shard_map/ppermute | solution.py:83
  39.5 1.1 collective-permute-start.16
  40.8 3.0 %collective-permute-start.15 = (bf16[512,1408]{1,0:T(8,128)(2,1)S(1)}, bf16[512,1408]{1,0:T(8,128)(2,1)S(1)}, u32[]{:S(2)}, u32[]{:S(2)}) collective-permute-start(bf16[512,1408]{1,0:T(8,128)(2,1)S(1)} %pad_maximum_fusion.5), channel_id=1, source_target_pairs={{0,66},{1,67},{2,64},{3,65},{4,70},{5,71},{6,68},{7,69},{8,74},{9,... | collective-permute-start | bytes 4325384 | tf_op jit(solution)/shard_map/ppermute | solution.py:83
  44.6 2.2 %collective-permute-start.11 = (bf16[512,1408]{1,0:T(8,128)(2,1)S(1)}, bf16[512,1408]{1,0:T(8,128)(2,1)S(1)}, u32[]{:S(2)}, u32[]{:S(2)}) collective-permute-start(bf16[512,1408]{1,0:T(8,128)(2,1)S(1)} %pad_maximum_fusion.4), channel_id=1, source_target_pairs={{0,48},{1,49},{2,50},{3,51},{4,52},{5,53},{6,54},{7,55},{8,56},{9,... | collective-permute-start | bytes 4325384 | tf_op jit(solution)/shard_map/ppermute | solution.py:83
  47.0 5.9 %collective-permute-done.4 = bf16[256,2048]{1,0:T(8,128)(2,1)S(1)} collective-permute-done((bf16[256,2048]{1,0:T(8,128)(2,1)S(1)}, bf16[256,2048]{1,0:T(8,128)(2,1)S(1)}, u32[]{:S(2)}, u32[]{:S(2)}) %collective-permute-start.4) | collective-permute-done | bytes 1048608 | tf_op jit(solution)/shard_map/ppermute | solution.py:83
  53.0 1.5 collective-permute-start.6
  54.9 1.4 collective-permute-start.5
  56.6 20.0 %collective-permute-done.11 = bf16[512,1408]{1,0:T(8,128)(2,1)S(1)} collective-permute-done((bf16[512,1408]{1,0:T(8,128)(2,1)S(1)}, bf16[512,1408]{1,0:T(8,128)(2,1)S(1)}, u32[]{:S(2)}, u32[]{:S(2)}) %collective-permute-start.11) | collective-permute-done | bytes 1441824 | tf_op jit(solution)/shard_map/ppermute | solution.py:83
  90.3 1.5 add_reduce_fusion
  91.8 6.2 %collective-permute-done.6 = bf16[512,2048]{1,0:T(8,128)(2,1)S(1)} collective-permute-done((bf16[512,2048]{1,0:T(8,128)(2,1)S(1)}, bf16[512,2048]{1,0:T(8,128)(2,1)S(1)}, u32[]{:S(2)}, u32[]{:S(2)}) %collective-permute-start.6) | collective-permute-done | bytes 2097184 | tf_op jit(solution)/shard_map/ppermute | solution.py:83
  98.2 4.6 %collective-permute-done.5 = bf16[512,2176]{1,0:T(8,128)(2,1)S(1)} collective-permute-done((bf16[512,2176]{1,0:T(8,128)(2,1)S(1)}, bf16[512,2176]{1,0:T(8,128)(2,1)S(1)}, u32[]{:S(2)}, u32[]{:S(2)}) %collective-permute-start.5) | collective-permute-done | bytes 2228256 | tf_op jit(solution)/shard_map/ppermute | solution.py:83
  103.0 6.0 %fusion.8 = f32[256,1024]{1,0:T(8,128)S(1)} fusion(bf16[1024,4224]{1,0:T(8,128)(2,1)} %slice_dynamic-update-slice_fusion, bf16[128,2176]{1,0:T(8,128)(2,1)S(1)} %get-tuple-element.24, bf16[128,2048]{1,0:T(8,128)(2,1)S(1)} %get-tuple-element.53, bf16[128,2176]{1,0:T(8,128)(2,1)S(1)} %get-tuple-element.25, bf16[128,2048]{1,0:T(8,128)(2,1)S(1)} %get-tuple-element.54, ...), kind=kOutput, calls=%fused_computation.14 | convolution fusion | flops 2243788800 | bytes 13484032 | tf_op jit(solution)/shard_map/dot_general | solution.py:160
  109.4 6.0 %fusion.55 = f32[256,1024]{1,0:T(8,128)S(1)} fusion(bf16[1024,4224]{1,0:T(8,128)(2,1)} %slice_dynamic-update-slice_fusion, bf16[64,4224]{1,0:T(8,128)(2,1)S(1)} %get-tuple-element.13, bf16[64,4224]{1,0:T(8,128)(2,1)S(1)} %get-tuple-element.15, bf16[64,4224]{1,0:T(8,128)(2,1)S(1)} %get-tuple-element.17, bf16[64,4224]{1,0:T(8,128)(2,1)S(1)} %get-tuple-element.19), kind=kOutput, calls=%fused_computation.52 | convolution fusion | flops 2223243264 | bytes 11862016 | tf_op jit(solution)/shard_map/dot_general | solution.py:160
  115.8 6.0 %fusion.13 = f32[256,1024]{1,0:T(8,128)S(1)} fusion(bf16[1024,4224]{1,0:T(8,128)(2,1)} %slice_dynamic-update-slice_fusion, bf16[128,2176]{1,0:T(8,128)(2,1)S(1)} %get-tuple-element.22, bf16[128,2048]{1,0:T(8,128)(2,1)S(1)} %get-tuple-element.26, bf16[128,2176]{1,0:T(8,128)(2,1)S(1)} %get-tuple-element.23, bf16[128,2048]{1,0:T(8,128)(2,1)S(1)} %get-tuple-element.27, ...), kind=kOutput, calls=%fused_computation.17 | convolution fusion | flops 2245951488 | bytes 14024704 | tf_op jit(solution)/shard_map/dot_general | solution.py:160
  122.4 6.0 %fusion.64 = f32[256,1024]{1,0:T(8,128)S(1)} fusion(bf16[1024,4224]{1,0:T(8,128)(2,1)} %slice_dynamic-update-slice_fusion, bf16[64,4224]{1,0:T(8,128)(2,1)S(1)} %get-tuple-element.5, bf16[64,4224]{1,0:T(8,128)(2,1)S(1)} %get-tuple-element.7, bf16[64,4224]{1,0:T(8,128)(2,1)S(1)} %get-tuple-element.9, bf16[64,4224]{1,0:T(8,128)(2,1)S(1)} %get-tuple-element.11), kind=kOutput, calls=%fused_computation.61 | convolution fusion | flops 2223243264 | bytes 11862016 | tf_op jit(solution)/shard_map/dot_general | solution.py:160
  131.0 1.1 collective-permute-done.23
  134.1 3.0 %collective-permute-done.24 = f32[256]{0:T(256)S(1)} collective-permute-done((f32[256]{0:T(256)S(1)}, f32[256]{0:T(256)S(1)}, u32[]{:S(2)}, u32[]{:S(2)}) %collective-permute-start.24) | collective-permute-done | bytes 1056 | tf_op jit(solution)/shard_map/ppermute | solution.py:118
  137.5 4.5 %collective-permute-done.25 = f32[128]{0:T(128)S(1)} collective-permute-done((f32[128]{0:T(128)S(1)}, f32[128]{0:T(128)S(1)}, u32[]{:S(2)}, u32[]{:S(2)}) %collective-permute-start.25) | collective-permute-done | bytes 544 | tf_op jit(solution)/shard_map/ppermute | solution.py:118
  142.9 4.2 %collective-permute-done.19 = f32[256,512]{1,0:T(8,128)S(1)} collective-permute-done((f32[256,512]{1,0:T(8,128)S(1)}, f32[256,512]{1,0:T(8,128)S(1)}, u32[]{:S(2)}, u32[]{:S(2)}) %collective-permute-start.19) | collective-permute-done | bytes 524320 | tf_op jit(solution)/shard_map/ppermute | solution.py:178
  149.2 2.1 %collective-permute-start.22 = (f32[64,512]{1,0:T(8,128)S(1)}, f32[64,512]{1,0:T(8,128)S(1)}, u32[]{:S(2)}, u32[]{:S(2)}) collective-permute-start(f32[64,512]{1,0:T(8,128)S(1)} %get-tuple-element.66), channel_id=1, source_target_pairs={{0,80},{1,81},{2,82},{3,83},{4,84},{5,85},{6,86},{7,87},{8,88},{9,... | collective-permute-start | bytes 393224 | tf_op jit(solution)/shard_map/ppermute | solution.py:183
  151.9 1.8 %collective-permute-done.20 = f32[64,512]{1,0:T(8,128)S(1)} collective-permute-done((f32[64,512]{1,0:T(8,128)S(1)}, f32[64,512]{1,0:T(8,128)S(1)}, u32[]{:S(2)}, u32[]{:S(2)}) %collective-permute-start.20) | collective-permute-done | bytes 131104 | tf_op jit(solution)/shard_map/ppermute | solution.py:183
  154.2 1.4 collective-permute-done.22
  (117 shorter events, 32.9 us)
Async XLA Ops:
  2.7 1.3 copy-start
  2.8 1.3 copy-start.1
  3.8 1.9 %collective-permute-start.7 = (bf16[64,4224]{1,0:T(8,128)(2,1)S(1)}, bf16[64,4224]{1,0:T(8,128)(2,1)S(1)}, u32[]{:S(2)}, u32[]{:S(2)}) collective-permute-start(bf16[64,4224]{1,0:T(8,128)(2,1)S(1)} %get-tuple-element.48), channel_id=1, source_target_pairs={{0,1},{1,0},{2,3},{3,2},{4,5},{5,4},{6,7},{7,6},{8,9},{9,8},{10,11... | collective-permute-start | bytes 1622024 | tf_op jit(solution)/shard_map/ppermute | solution.py:96
  4.5 11.3 %collective-permute-start = (bf16[64,4224]{1,0:T(8,128)(2,1)S(1)}, bf16[64,4224]{1,0:T(8,128)(2,1)S(1)}, u32[]{:S(2)}, u32[]{:S(2)}) collective-permute-start(bf16[64,4224]{1,0:T(8,128)(2,1)S(1)} %get-tuple-element.44), channel_id=1, source_target_pairs={{0,1},{1,0},{2,3},{3,2},{4,5},{5,4},{6,7},{7,6},{8,9},{9,8},{10,11... | collective-permute-start | bytes 1622024 | tf_op jit(solution)/shard_map/ppermute | solution.py:96
  5.8 11.7 %collective-permute-start.8 = (bf16[128,1408]{1,0:T(8,128)(2,1)S(1)}, bf16[128,1408]{1,0:T(8,128)(2,1)S(1)}, u32[]{:S(2)}, u32[]{:S(2)}) collective-permute-start(bf16[128,1408]{1,0:T(8,128)(2,1)S(1)} %get-tuple-element.45), channel_id=1, source_target_pairs={{0,48},{1,49},{2,50},{3,51},{4,52},{5,53},{6,54},{7,55},{8,56},{9,... | collective-permute-start | bytes 1081352 | tf_op jit(solution)/shard_map/ppermute | solution.py:83
  8.8 12.5 %collective-permute-start.12 = (bf16[128,1408]{1,0:T(8,128)(2,1)S(1)}, bf16[128,1408]{1,0:T(8,128)(2,1)S(1)}, u32[]{:S(2)}, u32[]{:S(2)}) collective-permute-start(bf16[128,1408]{1,0:T(8,128)(2,1)S(1)} %get-tuple-element.46), channel_id=1, source_target_pairs={{0,12},{1,13},{2,14},{3,15},{4,8},{5,9},{6,10},{7,11},{8,4},{9,5},... | collective-permute-start | bytes 1081352 | tf_op jit(solution)/shard_map/ppermute | solution.py:83
  12.8 12.5 %collective-permute-start.9 = (bf16[128,1408]{1,0:T(8,128)(2,1)S(1)}, bf16[128,1408]{1,0:T(8,128)(2,1)S(1)}, u32[]{:S(2)}, u32[]{:S(2)}) collective-permute-start(bf16[128,1408]{1,0:T(8,128)(2,1)S(1)} %get-tuple-element.47), channel_id=1, source_target_pairs={{0,66},{1,67},{2,64},{3,65},{4,70},{5,71},{6,68},{7,69},{8,74},{9,... | collective-permute-start | bytes 1081352 | tf_op jit(solution)/shard_map/ppermute | solution.py:83
  15.9 13.9 %collective-permute-start.2 = (bf16[128,2176]{1,0:T(8,128)(2,1)S(1)}, bf16[128,2176]{1,0:T(8,128)(2,1)S(1)}, u32[]{:S(2)}, u32[]{:S(2)}) collective-permute-start(bf16[128,2176]{1,0:T(8,128)(2,1)S(1)} %pad_maximum_fusion.21), channel_id=1, source_target_pairs={{0,4},{1,5},{2,6},{3,7},{4,0},{5,1},{6,2},{7,3},{8,12},{9,13},{10,... | collective-permute-start | bytes 1671176 | tf_op jit(solution)/shard_map/ppermute | solution.py:83
  16.0 13.2 %collective-permute-start.1 = (bf16[128,2048]{1,0:T(8,128)(2,1)S(1)}, bf16[128,2048]{1,0:T(8,128)(2,1)S(1)}, u32[]{:S(2)}, u32[]{:S(2)}) collective-permute-start(bf16[128,2048]{1,0:T(8,128)(2,1)S(1)} %pad_maximum_fusion.22), channel_id=1, source_target_pairs={{0,16},{1,17},{2,18},{3,19},{4,20},{5,21},{6,22},{7,23},{8,24},{9,... | collective-permute-start | bytes 1572872 | tf_op jit(solution)/shard_map/ppermute | solution.py:83
  17.6 21.8 %collective-permute-start.14 = (bf16[256,1408]{1,0:T(8,128)(2,1)S(1)}, bf16[256,1408]{1,0:T(8,128)(2,1)S(1)}, u32[]{:S(2)}, u32[]{:S(2)}) collective-permute-start(bf16[256,1408]{1,0:T(8,128)(2,1)S(1)} %pad_maximum_fusion.20), channel_id=1, source_target_pairs={{0,66},{1,67},{2,64},{3,65},{4,70},{5,71},{6,68},{7,69},{8,74},{9,... | collective-permute-start | bytes 2162696 | tf_op jit(solution)/shard_map/ppermute | solution.py:83
  21.3 19.4 %collective-permute-start.13 = (bf16[256,1408]{1,0:T(8,128)(2,1)S(1)}, bf16[256,1408]{1,0:T(8,128)(2,1)S(1)}, u32[]{:S(2)}, u32[]{:S(2)}) collective-permute-start(bf16[256,1408]{1,0:T(8,128)(2,1)S(1)} %pad_maximum_fusion.19), channel_id=1, source_target_pairs={{0,48},{1,49},{2,50},{3,51},{4,52},{5,53},{6,54},{7,55},{8,56},{9,... | collective-permute-start | bytes 2162696 | tf_op jit(solution)/shard_map/ppermute | solution.py:83
  25.4 19.1 %collective-permute-start.10 = (bf16[256,1408]{1,0:T(8,128)(2,1)S(1)}, bf16[256,1408]{1,0:T(8,128)(2,1)S(1)}, u32[]{:S(2)}, u32[]{:S(2)}) collective-permute-start(bf16[256,1408]{1,0:T(8,128)(2,1)S(1)} %pad_maximum_fusion.18), channel_id=1, source_target_pairs={{0,12},{1,13},{2,14},{3,15},{4,8},{5,9},{6,10},{7,11},{8,4},{9,5},... | collective-permute-start | bytes 2162696 | tf_op jit(solution)/shard_map/ppermute | solution.py:83
  29.3 23.5 %collective-permute-start.4 = (bf16[256,2048]{1,0:T(8,128)(2,1)S(1)}, bf16[256,2048]{1,0:T(8,128)(2,1)S(1)}, u32[]{:S(2)}, u32[]{:S(2)}) collective-permute-start(bf16[256,2048]{1,0:T(8,128)(2,1)S(1)} %pad_maximum_fusion.17), channel_id=1, source_target_pairs={{0,64},{1,65},{2,66},{3,67},{4,68},{5,69},{6,70},{7,71},{8,72},{9,... | collective-permute-start | bytes 3145736 | tf_op jit(solution)/shard_map/ppermute | solution.py:83
  29.8 24.9 %collective-permute-start.3 = (bf16[256,2176]{1,0:T(8,128)(2,1)S(1)}, bf16[256,2176]{1,0:T(8,128)(2,1)S(1)}, u32[]{:S(2)}, u32[]{:S(2)}) collective-permute-start(bf16[256,2176]{1,0:T(8,128)(2,1)S(1)} %pad_maximum_fusion.7), channel_id=1, source_target_pairs={{0,16},{1,17},{2,18},{3,19},{4,20},{5,21},{6,22},{7,23},{8,24},{9,... | collective-permute-start | bytes 3342344 | tf_op jit(solution)/shard_map/ppermute | solution.py:83
  39.5 40.1 %collective-permute-start.16 = (bf16[512,1408]{1,0:T(8,128)(2,1)S(1)}, bf16[512,1408]{1,0:T(8,128)(2,1)S(1)}, u32[]{:S(2)}, u32[]{:S(2)}) collective-permute-start(bf16[512,1408]{1,0:T(8,128)(2,1)S(1)} %pad_maximum_fusion.6), channel_id=1, source_target_pairs={{0,12},{1,13},{2,14},{3,15},{4,8},{5,9},{6,10},{7,11},{8,4},{9,5},... | collective-permute-start | bytes 4325384 | tf_op jit(solution)/shard_map/ppermute | solution.py:83
  40.8 36.8 %collective-permute-start.15 = (bf16[512,1408]{1,0:T(8,128)(2,1)S(1)}, bf16[512,1408]{1,0:T(8,128)(2,1)S(1)}, u32[]{:S(2)}, u32[]{:S(2)}) collective-permute-start(bf16[512,1408]{1,0:T(8,128)(2,1)S(1)} %pad_maximum_fusion.5), channel_id=1, source_target_pairs={{0,66},{1,67},{2,64},{3,65},{4,70},{5,71},{6,68},{7,69},{8,74},{9,... | collective-permute-start | bytes 4325384 | tf_op jit(solution)/shard_map/ppermute | solution.py:83
  44.6 31.9 %collective-permute-start.11 = (bf16[512,1408]{1,0:T(8,128)(2,1)S(1)}, bf16[512,1408]{1,0:T(8,128)(2,1)S(1)}, u32[]{:S(2)}, u32[]{:S(2)}) collective-permute-start(bf16[512,1408]{1,0:T(8,128)(2,1)S(1)} %pad_maximum_fusion.4), channel_id=1, source_target_pairs={{0,48},{1,49},{2,50},{3,51},{4,52},{5,53},{6,54},{7,55},{8,56},{9,... | collective-permute-start | bytes 4325384 | tf_op jit(solution)/shard_map/ppermute | solution.py:83
  53.0 45.1 %collective-permute-start.6 = (bf16[512,2048]{1,0:T(8,128)(2,1)S(1)}, bf16[512,2048]{1,0:T(8,128)(2,1)S(1)}, u32[]{:S(2)}, u32[]{:S(2)}) collective-permute-start(bf16[512,2048]{1,0:T(8,128)(2,1)S(1)} %pad_maximum_fusion.3), channel_id=1, source_target_pairs={{0,4},{1,5},{2,6},{3,7},{4,0},{5,1},{6,2},{7,3},{8,12},{9,13},{10,... | collective-permute-start | bytes 6291464 | tf_op jit(solution)/shard_map/ppermute | solution.py:83
  54.9 47.9 %collective-permute-start.5 = (bf16[512,2176]{1,0:T(8,128)(2,1)S(1)}, bf16[512,2176]{1,0:T(8,128)(2,1)S(1)}, u32[]{:S(2)}, u32[]{:S(2)}) collective-permute-start(bf16[512,2176]{1,0:T(8,128)(2,1)S(1)} %pad_maximum_fusion), channel_id=1, source_target_pairs={{0,64},{1,65},{2,66},{3,67},{4,68},{5,69},{6,70},{7,71},{8,72},{9,... | collective-permute-start | bytes 6684680 | tf_op jit(solution)/shard_map/ppermute | solution.py:83
  109.0 20.0 %collective-permute-start.17 = (f32[256,1024]{1,0:T(8,128)S(1)}, f32[256,1024]{1,0:T(8,128)S(1)}, u32[]{:S(2)}, u32[]{:S(2)}) collective-permute-start(f32[256,1024]{1,0:T(8,128)S(1)} %fusion.8), channel_id=1, source_target_pairs={{0,1},{1,0},{2,3},{3,2},{4,5},{5,4},{6,7},{7,6},{8,9},{9,8},{10,11... | collective-permute-start | bytes 3145736 | tf_op jit(solution)/shard_map/ppermute | solution.py:171
  121.8 8.1 %collective-permute-start.18 = (f32[256,1024]{1,0:T(8,128)S(1)}, f32[256,1024]{1,0:T(8,128)S(1)}, u32[]{:S(2)}, u32[]{:S(2)}) collective-permute-start(f32[256,1024]{1,0:T(8,128)S(1)} %fusion.13), channel_id=1, source_target_pairs={{0,1},{1,0},{2,3},{3,2},{4,5},{5,4},{6,7},{7,6},{8,9},{9,8},{10,11... | collective-permute-start | bytes 3145736 | tf_op jit(solution)/shard_map/ppermute | solution.py:171
  130.9 1.2 collective-permute-start.23
  132.3 4.8 %collective-permute-start.24 = (f32[256]{0:T(256)S(1)}, f32[256]{0:T(256)S(1)}, u32[]{:S(2)}, u32[]{:S(2)}) collective-permute-start(f32[256]{0:T(256)S(1)} %pad_maximum_fusion.24), channel_id=1, source_target_pairs={{0,48},{1,49},{2,50},{3,51},{4,52},{5,53},{6,54},{7,55},{8,56},{9,... | collective-permute-start | bytes 3080 | tf_op jit(solution)/shard_map/ppermute | solution.py:118
  133.4 13.8 %collective-permute-start.19 = (f32[256,512]{1,0:T(8,128)S(1)}, f32[256,512]{1,0:T(8,128)S(1)}, u32[]{:S(2)}, u32[]{:S(2)}) collective-permute-start(f32[256,512]{1,0:T(8,128)S(1)} %fusion.73), channel_id=1, source_target_pairs={{0,4},{1,5},{2,6},{3,7},{4,0},{5,1},{6,2},{7,3},{8,12},{9,13},{10,... | collective-permute-start | bytes 1572872 | tf_op jit(solution)/shard_map/ppermute | solution.py:178
  137.2 4.8 %collective-permute-start.25 = (f32[128]{0:T(128)S(1)}, f32[128]{0:T(128)S(1)}, u32[]{:S(2)}, u32[]{:S(2)}) collective-permute-start(f32[128]{0:T(128)S(1)} %pad_maximum_fusion.25), channel_id=1, source_target_pairs={{0,66},{1,67},{2,64},{3,65},{4,70},{5,71},{6,68},{7,69},{8,74},{9,... | collective-permute-start | bytes 1544 | tf_op jit(solution)/shard_map/ppermute | solution.py:118
  142.1 9.3 %collective-permute-start.26 = (f32[64]{0:T(128)S(1)}, f32[64]{0:T(128)S(1)}, u32[]{:S(2)}, u32[]{:S(2)}) collective-permute-start(f32[64]{0:T(128)S(1)} %slice_add_fusion.2), channel_id=1, source_target_pairs={{0,12},{1,13},{2,14},{3,15},{4,8},{5,9},{6,10},{7,11},{8,4},{9,5},... | collective-permute-start | bytes 776 | tf_op jit(solution)/shard_map/ppermute | solution.py:118
  147.8 5.9 %collective-permute-start.20 = (f32[64,512]{1,0:T(8,128)S(1)}, f32[64,512]{1,0:T(8,128)S(1)}, u32[]{:S(2)}, u32[]{:S(2)}) collective-permute-start(f32[64,512]{1,0:T(8,128)S(1)} %get-tuple-element.65), channel_id=1, source_target_pairs={{0,16},{1,17},{2,18},{3,19},{4,20},{5,21},{6,22},{7,23},{8,24},{9,... | collective-permute-start | bytes 393224 | tf_op jit(solution)/shard_map/ppermute | solution.py:183
  148.1 6.1 %collective-permute-start.21 = (f32[64,512]{1,0:T(8,128)S(1)}, f32[64,512]{1,0:T(8,128)S(1)}, u32[]{:S(2)}, u32[]{:S(2)}) collective-permute-start(f32[64,512]{1,0:T(8,128)S(1)} %get-tuple-element.67), channel_id=1, source_target_pairs={{0,64},{1,65},{2,66},{3,67},{4,68},{5,69},{6,70},{7,71},{8,72},{9,... | collective-permute-start | bytes 393224 | tf_op jit(solution)/shard_map/ppermute | solution.py:183
  149.2 6.4 %collective-permute-start.22 = (f32[64,512]{1,0:T(8,128)S(1)}, f32[64,512]{1,0:T(8,128)S(1)}, u32[]{:S(2)}, u32[]{:S(2)}) collective-permute-start(f32[64,512]{1,0:T(8,128)S(1)} %get-tuple-element.66), channel_id=1, source_target_pairs={{0,80},{1,81},{2,82},{3,83},{4,84},{5,85},{6,86},{7,87},{8,88},{9,... | collective-permute-start | bytes 393224 | tf_op jit(solution)/shard_map/ppermute | solution.py:183

commit v23 on v20

--- a/solution.py
+++ b/solution.py
@@ -21,8 +21,7 @@
     extra = jnp.zeros((rows, PAD), jnp.bfloat16)
     for j, v in enumerate(side):
         extra = jnp.where(cols == first + j, v[:, None].astype(jnp.bfloat16), extra)
-    h = k // 2
-    return jnp.concatenate([grads[:, :h], extra, grads[:, h:], extra], axis=1)
+    return grads, extra
 
 
 def split_class(c):
@@ -88,11 +87,12 @@
 
 
 def half_gather(shard, mate, n, orders):
-    r, cols = shard.shape
-    h = cols // 2
+    grads, extra = shard
+    r, k = grads.shape
+    h = k // 2 + extra.shape[1]
     c = lax.axis_index(AXES) % 2
-    mine = lax.dynamic_slice_in_dim(shard, c * h, h, axis=1)
-    give = lax.dynamic_slice_in_dim(shard, (1 - c) * h, h, axis=1)
+    mine = jnp.concatenate([lax.dynamic_slice_in_dim(grads, c * (k // 2), k // 2, axis=1), extra], axis=1)
+    give = jnp.concatenate([lax.dynamic_slice_in_dim(grads, (1 - c) * (k // 2), k // 2, axis=1), extra], axis=1)
     unit = jnp.concatenate([mine, lax.ppermute(give, AXES, core_pairs(n))])
     cut = column_cuts(h, len(orders))
     parts = [chain(unit[:, cut[p]:cut[p + 1]], mate, n, order) for p, order in enumerate(orders)]

time: 138 us -> 138 us (level)
  starting transfers between devices: 36 us -> 40.8 us
  waiting for transfers between devices: 76.3 us -> 71.6 us
    ppermute x15, starting transfers between devices: 28.4 us -> 34.2 us  [chain(): got = lax.ppermute(buf, AXES, mate_pairs(n, a, mate))]
    ppermute x15, waiting for transfers between devices: 63.1 us -> 57.5 us  [chain(): got = lax.ppermute(buf, AXES, mate_pairs(n, a, mate))]
    dynamic_slice x0 -> x1, local copies, waits for them, and re-layouts: none -> 1.69 us  [half_gather(): lax.dynamic_slice_in_dim(grads, (1 - c) * (k // 2), k // 2, axis=1)]
  transfers between devices with their start and end apart: 26 -> 26, of which waited for: 18 -> 15; matrix products, arithmetic and copies ran while one was open for 9% -> 9% of each run, Pallas kernels for 0% -> 0%
where the time goes in v23:
time: 138 us; the launch traced here: 137 us
  waiting for transfers between devices  71.6 us (52%)
  starting transfers between devices  40.8 us (30%)
  matrix products  11.2 us (8%)
  other arithmetic  7.5 us (5%)
  local copies, waits for them, and re-layouts  5.09 us (4%)
    ppermute x15, waiting for transfers between devices, chain(): got = lax.ppermute(buf, AXES, mate_pairs(n, a, mate))  57.5 us
    ppermute x15, starting transfers between devices, chain(): got = lax.ppermute(buf, AXES, mate_pairs(n, a, mate))  34.2 us
    dot_general x2, matrix products, partial(): lax.dot_general(t, te_all, (((1,), (1,)), ((), ())), preferred_element_ty...  9.56 us
    ppermute x3, waiting for transfers between devices, cube_reduce(): lax.ppermute(jnp.concatenate([blocks[o] for o in send]), AXES, mate_pairs...  7.67 us
    ppermute x3, starting transfers between devices, cube_reduce_square(): lax.ppermute(jnp.concatenate([blocks[o] for o in send]), AXES, offset_pai...  2.8 us
  transfers between devices with their start and end apart: 26, of which 15 were waited for; matrix products, arithmetic and copies ran while one was open for 9% of the time, Pallas kernels for 0%

profile of v23, /device:TPU:0, one launch (start us, length us, event | category | flops | bytes accessed | tf_op | source)
XLA Modules:
  0.0 137.5 jit_solution(628235997362315300)
XLA Ops:
  1.4 1.7 %constant_dynamic-slice_fusion = (bf16[64,4096]{1,0:T(8,128)(2,1)S(1)}, bf16[64,4096]{1,0:T(8,128)(2,1)S(1)}, bf16[64,4096]{1,0:T(8,128)(2,1)S(1)}, bf16[64,4096]{1,0:T(8,128)(2,1)S(1)}) fusion(bf16[64,8192]{1,0:T(8,128)(2,1)} %param.8, s32[]{:T(128)S(6)} %select_n.58, s32[]{:T(128)S(6)} %select_n.52, bf16[64,8192]{1,0:T(8,128)(2,1)} %param.5), kind=kLoop, calls=%fused_computation.123 | loop fusion | bytes 4194312 | tf_op jit(solution)/shard_map/dynamic_slice | solution.py:95
  4.1 1.1 collective-permute-done.7
  5.5 2.9 %collective-permute-start.8 = (bf16[128,1408]{1,0:T(8,128)(2,1)S(1)}, bf16[128,1408]{1,0:T(8,128)(2,1)S(1)}, u32[]{:S(2)}, u32[]{:S(2)}) collective-permute-start(bf16[128,1408]{1,0:T(8,128)(2,1)S(1)} %get-tuple-element.40), channel_id=1, source_target_pairs={{0,48},{1,49},{2,50},{3,51},{4,52},{5,53},{6,54},{7,55},{8,56},{9,... | collective-permute-start | bytes 1081352 | tf_op jit(solution)/shard_map/ppermute | solution.py:82
  8.4 3.0 %collective-permute-start.9 = (bf16[128,1408]{1,0:T(8,128)(2,1)S(1)}, bf16[128,1408]{1,0:T(8,128)(2,1)S(1)}, u32[]{:S(2)}, u32[]{:S(2)}) collective-permute-start(bf16[128,1408]{1,0:T(8,128)(2,1)S(1)} %get-tuple-element.42), channel_id=1, source_target_pairs={{0,66},{1,67},{2,64},{3,65},{4,70},{5,71},{6,68},{7,69},{8,74},{9,... | collective-permute-start | bytes 1081352 | tf_op jit(solution)/shard_map/ppermute | solution.py:82
  11.4 4.0 %collective-permute-start.12 = (bf16[128,1408]{1,0:T(8,128)(2,1)S(1)}, bf16[128,1408]{1,0:T(8,128)(2,1)S(1)}, u32[]{:S(2)}, u32[]{:S(2)}) collective-permute-start(bf16[128,1408]{1,0:T(8,128)(2,1)S(1)} %get-tuple-element.41), channel_id=1, source_target_pairs={{0,12},{1,13},{2,14},{3,15},{4,8},{5,9},{6,10},{7,11},{8,4},{9,5},... | collective-permute-start | bytes 1081352 | tf_op jit(solution)/shard_map/ppermute | solution.py:82
  17.3 3.2 %collective-permute-start.14 = (bf16[256,1408]{1,0:T(8,128)(2,1)S(1)}, bf16[256,1408]{1,0:T(8,128)(2,1)S(1)}, u32[]{:S(2)}, u32[]{:S(2)}) collective-permute-start(bf16[256,1408]{1,0:T(8,128)(2,1)S(1)} %pad_maximum_fusion.21), channel_id=1, source_target_pairs={{0,66},{1,67},{2,64},{3,65},{4,70},{5,71},{6,68},{7,69},{8,74},{9,... | collective-permute-start | bytes 2162696 | tf_op jit(solution)/shard_map/ppermute | solution.py:82
  20.5 4.1 %collective-permute-start.10 = (bf16[256,1408]{1,0:T(8,128)(2,1)S(1)}, bf16[256,1408]{1,0:T(8,128)(2,1)S(1)}, u32[]{:S(2)}, u32[]{:S(2)}) collective-permute-start(bf16[256,1408]{1,0:T(8,128)(2,1)S(1)} %pad_maximum_fusion.19), channel_id=1, source_target_pairs={{0,12},{1,13},{2,14},{3,15},{4,8},{5,9},{6,10},{7,11},{8,4},{9,5},... | collective-permute-start | bytes 2162696 | tf_op jit(solution)/shard_map/ppermute | solution.py:82
  24.7 2.8 %collective-permute-start.13 = (bf16[256,1408]{1,0:T(8,128)(2,1)S(1)}, bf16[256,1408]{1,0:T(8,128)(2,1)S(1)}, u32[]{:S(2)}, u32[]{:S(2)}) collective-permute-start(bf16[256,1408]{1,0:T(8,128)(2,1)S(1)} %pad_maximum_fusion.20), channel_id=1, source_target_pairs={{0,48},{1,49},{2,50},{3,51},{4,52},{5,53},{6,54},{7,55},{8,56},{9,... | collective-permute-start | bytes 2162696 | tf_op jit(solution)/shard_map/ppermute | solution.py:82
  27.5 1.3 collective-permute-done.1
  29.8 6.3 %collective-permute-done.14 = bf16[256,1408]{1,0:T(8,128)(2,1)S(1)} collective-permute-done((bf16[256,1408]{1,0:T(8,128)(2,1)S(1)}, bf16[256,1408]{1,0:T(8,128)(2,1)S(1)}, u32[]{:S(2)}, u32[]{:S(2)}) %collective-permute-start.14) | collective-permute-done | bytes 720928 | tf_op jit(solution)/shard_map/ppermute | solution.py:82
  36.2 4.1 %collective-permute-start.16 = (bf16[512,1408]{1,0:T(8,128)(2,1)S(1)}, bf16[512,1408]{1,0:T(8,128)(2,1)S(1)}, u32[]{:S(2)}, u32[]{:S(2)}) collective-permute-start(bf16[512,1408]{1,0:T(8,128)(2,1)S(1)} %pad_maximum_fusion.4), channel_id=1, source_target_pairs={{0,12},{1,13},{2,14},{3,15},{4,8},{5,9},{6,10},{7,11},{8,4},{9,5},... | collective-permute-start | bytes 4325384 | tf_op jit(solution)/shard_map/ppermute | solution.py:82
  40.4 2.8 %collective-permute-start.11 = (bf16[512,1408]{1,0:T(8,128)(2,1)S(1)}, bf16[512,1408]{1,0:T(8,128)(2,1)S(1)}, u32[]{:S(2)}, u32[]{:S(2)}) collective-permute-start(bf16[512,1408]{1,0:T(8,128)(2,1)S(1)} %pad_maximum_fusion.2), channel_id=1, source_target_pairs={{0,48},{1,49},{2,50},{3,51},{4,52},{5,53},{6,54},{7,55},{8,56},{9,... | collective-permute-start | bytes 4325384 | tf_op jit(solution)/shard_map/ppermute | solution.py:82
  43.4 3.0 %collective-permute-start.15 = (bf16[512,1408]{1,0:T(8,128)(2,1)S(1)}, bf16[512,1408]{1,0:T(8,128)(2,1)S(1)}, u32[]{:S(2)}, u32[]{:S(2)}) collective-permute-start(bf16[512,1408]{1,0:T(8,128)(2,1)S(1)} %pad_maximum_fusion.3), channel_id=1, source_target_pairs={{0,66},{1,67},{2,64},{3,65},{4,70},{5,71},{6,68},{7,69},{8,74},{9,... | collective-permute-start | bytes 4325384 | tf_op jit(solution)/shard_map/ppermute | solution.py:82
  46.6 5.9 %collective-permute-done.4 = bf16[256,2048]{1,0:T(8,128)(2,1)S(1)} collective-permute-done((bf16[256,2048]{1,0:T(8,128)(2,1)S(1)}, bf16[256,2048]{1,0:T(8,128)(2,1)S(1)}, u32[]{:S(2)}, u32[]{:S(2)}) %collective-permute-start.4) | collective-permute-done | bytes 1048608 | tf_op jit(solution)/shard_map/ppermute | solution.py:82
  52.7 1.5 %collective-permute-start.6 = (bf16[512,2048]{1,0:T(8,128)(2,1)S(1)}, bf16[512,2048]{1,0:T(8,128)(2,1)S(1)}, u32[]{:S(2)}, u32[]{:S(2)}) collective-permute-start(bf16[512,2048]{1,0:T(8,128)(2,1)S(1)} %pad_maximum_fusion.1), channel_id=1, source_target_pairs={{0,4},{1,5},{2,6},{3,7},{4,0},{5,1},{6,2},{7,3},{8,12},{9,13},{10,... | collective-permute-start | bytes 6291464 | tf_op jit(solution)/shard_map/ppermute | solution.py:82
  54.6 1.6 %collective-permute-start.5 = (bf16[512,2176]{1,0:T(8,128)(2,1)S(1)}, bf16[512,2176]{1,0:T(8,128)(2,1)S(1)}, u32[]{:S(2)}, u32[]{:S(2)}) collective-permute-start(bf16[512,2176]{1,0:T(8,128)(2,1)S(1)} %pad_maximum_fusion), channel_id=1, source_target_pairs={{0,64},{1,65},{2,66},{3,67},{4,68},{5,69},{6,70},{7,71},{8,72},{9,... | collective-permute-start | bytes 6684680 | tf_op jit(solution)/shard_map/ppermute | solution.py:82
  56.3 0.9 fusion.28
  57.2 16.5 %collective-permute-done.11 = bf16[512,1408]{1,0:T(8,128)(2,1)S(1)} collective-permute-done((bf16[512,1408]{1,0:T(8,128)(2,1)S(1)}, bf16[512,1408]{1,0:T(8,128)(2,1)S(1)}, u32[]{:S(2)}, u32[]{:S(2)}) %collective-permute-start.11) | collective-permute-done | bytes 1441824 | tf_op jit(solution)/shard_map/ppermute | solution.py:82
  73.9 2.1 %collective-permute-done.15 = bf16[512,1408]{1,0:T(8,128)(2,1)S(1)} collective-permute-done((bf16[512,1408]{1,0:T(8,128)(2,1)S(1)}, bf16[512,1408]{1,0:T(8,128)(2,1)S(1)}, u32[]{:S(2)}, u32[]{:S(2)}) %collective-permute-start.15) | collective-permute-done | bytes 1441824 | tf_op jit(solution)/shard_map/ppermute | solution.py:82
  77.6 20.2 %collective-permute-done.6 = bf16[512,2048]{1,0:T(8,128)(2,1)S(1)} collective-permute-done((bf16[512,2048]{1,0:T(8,128)(2,1)S(1)}, bf16[512,2048]{1,0:T(8,128)(2,1)S(1)}, u32[]{:S(2)}, u32[]{:S(2)}) %collective-permute-start.6) | collective-permute-done | bytes 2097184 | tf_op jit(solution)/shard_map/ppermute | solution.py:82
  98.0 4.6 %collective-permute-done.5 = bf16[512,2176]{1,0:T(8,128)(2,1)S(1)} collective-permute-done((bf16[512,2176]{1,0:T(8,128)(2,1)S(1)}, bf16[512,2176]{1,0:T(8,128)(2,1)S(1)}, u32[]{:S(2)}, u32[]{:S(2)}) %collective-permute-start.5) | collective-permute-done | bytes 2228256 | tf_op jit(solution)/shard_map/ppermute | solution.py:82
  103.7 4.8 %fusion.50 = f32[512,1024]{1,0:T(8,128)S(1)} fusion(bf16[512,4224]{1,0:T(8,128)(2,1)S(1)} %get-tuple-element.26, bf16[1024,4224]{1,0:T(8,128)(2,1)S(1)} %slice_dynamic-update-slice_fusion), kind=kOutput, calls=%fused_computation.156 | convolution fusion | flops 4429185024 | bytes 15073280 | tf_op jit(solution)/shard_map/dot_general | solution.py:160
  109.0 4.8 %fusion.49 = f32[512,1024]{1,0:T(8,128)S(1)} fusion(bf16[512,4224]{1,0:T(8,128)(2,1)S(1)} %get-tuple-element.27, bf16[1024,4224]{1,0:T(8,128)(2,1)S(1)} %slice_dynamic-update-slice_fusion), kind=kOutput, calls=%fused_computation.155 | convolution fusion | flops 4429185024 | bytes 15073280 | tf_op jit(solution)/shard_map/dot_general | solution.py:160
  115.6 0.9 multiply_reduce_fusion
  117.6 1.3 collective-permute-start.19
  119.1 1.0 collective-permute-start.23
  120.0 1.1 collective-permute-start.20
  121.2 2.7 %collective-permute-done.23 = f32[256]{0:T(256)S(1)} collective-permute-done((f32[256]{0:T(256)S(1)}, f32[256]{0:T(256)S(1)}, u32[]{:S(2)}, u32[]{:S(2)}) %collective-permute-start.23) | collective-permute-done | bytes 1056 | tf_op jit(solution)/shard_map/ppermute | solution.py:118
  124.4 4.3 %collective-permute-done.24 = f32[128]{0:T(128)S(1)} collective-permute-done((f32[128]{0:T(128)S(1)}, f32[128]{0:T(128)S(1)}, u32[]{:S(2)}, u32[]{:S(2)}) %collective-permute-start.24) | collective-permute-done | bytes 544 | tf_op jit(solution)/shard_map/ppermute | solution.py:118
  129.0 2.6 %collective-permute-done.20 = f32[128,512]{1,0:T(8,128)S(1)} collective-permute-done((f32[128,512]{1,0:T(8,128)S(1)}, f32[128,512]{1,0:T(8,128)S(1)}, u32[]{:S(2)}, u32[]{:S(2)}) %collective-permute-start.20) | collective-permute-done | bytes 262176 | tf_op jit(solution)/shard_map/ppermute | solution.py:141
  131.7 1.2 collective-permute-start.21
  134.1 2.6 %collective-permute-done.21 = f32[64,512]{1,0:T(8,128)S(1)} collective-permute-done((f32[64,512]{1,0:T(8,128)S(1)}, f32[64,512]{1,0:T(8,128)S(1)}, u32[]{:S(2)}, u32[]{:S(2)}) %collective-permute-start.21) | collective-permute-done | bytes 131104 | tf_op jit(solution)/shard_map/ppermute | solution.py:144
  (113 shorter events, 15.0 us)
Async XLA Ops:
  3.1 0.7 copy-start
  3.3 2.0 %collective-permute-start.7 = (bf16[64,4224]{1,0:T(8,128)(2,1)S(1)}, bf16[64,4224]{1,0:T(8,128)(2,1)S(1)}, u32[]{:S(2)}, u32[]{:S(2)}) collective-permute-start(bf16[64,4224]{1,0:T(8,128)(2,1)S(1)} %get-tuple-element.61), channel_id=1, source_target_pairs={{0,1},{1,0},{2,3},{3,2},{4,5},{5,4},{6,7},{7,6},{8,9},{9,8},{10,11... | collective-permute-start | bytes 1622024 | tf_op jit(solution)/shard_map/ppermute | solution.py:96
  3.9 11.5 %collective-permute-start = (bf16[64,4224]{1,0:T(8,128)(2,1)S(1)}, bf16[64,4224]{1,0:T(8,128)(2,1)S(1)}, u32[]{:S(2)}, u32[]{:S(2)}) collective-permute-start(bf16[64,4224]{1,0:T(8,128)(2,1)S(1)} %get-tuple-element.63), channel_id=1, source_target_pairs={{0,1},{1,0},{2,3},{3,2},{4,5},{5,4},{6,7},{7,6},{8,9},{9,8},{10,11... | collective-permute-start | bytes 1622024 | tf_op jit(solution)/shard_map/ppermute | solution.py:96
  5.5 11.7 %collective-permute-start.8 = (bf16[128,1408]{1,0:T(8,128)(2,1)S(1)}, bf16[128,1408]{1,0:T(8,128)(2,1)S(1)}, u32[]{:S(2)}, u32[]{:S(2)}) collective-permute-start(bf16[128,1408]{1,0:T(8,128)(2,1)S(1)} %get-tuple-element.40), channel_id=1, source_target_pairs={{0,48},{1,49},{2,50},{3,51},{4,52},{5,53},{6,54},{7,55},{8,56},{9,... | collective-permute-start | bytes 1081352 | tf_op jit(solution)/shard_map/ppermute | solution.py:82
  8.4 12.1 %collective-permute-start.9 = (bf16[128,1408]{1,0:T(8,128)(2,1)S(1)}, bf16[128,1408]{1,0:T(8,128)(2,1)S(1)}, u32[]{:S(2)}, u32[]{:S(2)}) collective-permute-start(bf16[128,1408]{1,0:T(8,128)(2,1)S(1)} %get-tuple-element.42), channel_id=1, source_target_pairs={{0,66},{1,67},{2,64},{3,65},{4,70},{5,71},{6,68},{7,69},{8,74},{9,... | collective-permute-start | bytes 1081352 | tf_op jit(solution)/shard_map/ppermute | solution.py:82
  11.4 13.2 %collective-permute-start.12 = (bf16[128,1408]{1,0:T(8,128)(2,1)S(1)}, bf16[128,1408]{1,0:T(8,128)(2,1)S(1)}, u32[]{:S(2)}, u32[]{:S(2)}) collective-permute-start(bf16[128,1408]{1,0:T(8,128)(2,1)S(1)} %get-tuple-element.41), channel_id=1, source_target_pairs={{0,12},{1,13},{2,14},{3,15},{4,8},{5,9},{6,10},{7,11},{8,4},{9,5},... | collective-permute-start | bytes 1081352 | tf_op jit(solution)/shard_map/ppermute | solution.py:82
  15.5 13.9 %collective-permute-start.2 = (bf16[128,2176]{1,0:T(8,128)(2,1)S(1)}, bf16[128,2176]{1,0:T(8,128)(2,1)S(1)}, u32[]{:S(2)}, u32[]{:S(2)}) collective-permute-start(bf16[128,2176]{1,0:T(8,128)(2,1)S(1)} %pad_maximum_fusion.22), channel_id=1, source_target_pairs={{0,4},{1,5},{2,6},{3,7},{4,0},{5,1},{6,2},{7,3},{8,12},{9,13},{10,... | collective-permute-start | bytes 1671176 | tf_op jit(solution)/shard_map/ppermute | solution.py:82
  15.6 13.2 %collective-permute-start.1 = (bf16[128,2048]{1,0:T(8,128)(2,1)S(1)}, bf16[128,2048]{1,0:T(8,128)(2,1)S(1)}, u32[]{:S(2)}, u32[]{:S(2)}) collective-permute-start(bf16[128,2048]{1,0:T(8,128)(2,1)S(1)} %pad_maximum_fusion.31), channel_id=1, source_target_pairs={{0,16},{1,17},{2,18},{3,19},{4,20},{5,21},{6,22},{7,23},{8,24},{9,... | collective-permute-start | bytes 1572872 | tf_op jit(solution)/shard_map/ppermute | solution.py:82
  17.3 18.8 %collective-permute-start.14 = (bf16[256,1408]{1,0:T(8,128)(2,1)S(1)}, bf16[256,1408]{1,0:T(8,128)(2,1)S(1)}, u32[]{:S(2)}, u32[]{:S(2)}) collective-permute-start(bf16[256,1408]{1,0:T(8,128)(2,1)S(1)} %pad_maximum_fusion.21), channel_id=1, source_target_pairs={{0,66},{1,67},{2,64},{3,65},{4,70},{5,71},{6,68},{7,69},{8,74},{9,... | collective-permute-start | bytes 2162696 | tf_op jit(solution)/shard_map/ppermute | solution.py:82
  20.5 19.8 %collective-permute-start.10 = (bf16[256,1408]{1,0:T(8,128)(2,1)S(1)}, bf16[256,1408]{1,0:T(8,128)(2,1)S(1)}, u32[]{:S(2)}, u32[]{:S(2)}) collective-permute-start(bf16[256,1408]{1,0:T(8,128)(2,1)S(1)} %pad_maximum_fusion.19), channel_id=1, source_target_pairs={{0,12},{1,13},{2,14},{3,15},{4,8},{5,9},{6,10},{7,11},{8,4},{9,5},... | collective-permute-start | bytes 2162696 | tf_op jit(solution)/shard_map/ppermute | solution.py:82
  24.7 18.6 %collective-permute-start.13 = (bf16[256,1408]{1,0:T(8,128)(2,1)S(1)}, bf16[256,1408]{1,0:T(8,128)(2,1)S(1)}, u32[]{:S(2)}, u32[]{:S(2)}) collective-permute-start(bf16[256,1408]{1,0:T(8,128)(2,1)S(1)} %pad_maximum_fusion.20), channel_id=1, source_target_pairs={{0,48},{1,49},{2,50},{3,51},{4,52},{5,53},{6,54},{7,55},{8,56},{9,... | collective-permute-start | bytes 2162696 | tf_op jit(solution)/shard_map/ppermute | solution.py:82
  29.0 23.5 %collective-permute-start.4 = (bf16[256,2048]{1,0:T(8,128)(2,1)S(1)}, bf16[256,2048]{1,0:T(8,128)(2,1)S(1)}, u32[]{:S(2)}, u32[]{:S(2)}) collective-permute-start(bf16[256,2048]{1,0:T(8,128)(2,1)S(1)} %pad_maximum_fusion.14), channel_id=1, source_target_pairs={{0,64},{1,65},{2,66},{3,67},{4,68},{5,69},{6,70},{7,71},{8,72},{9,... | collective-permute-start | bytes 3145736 | tf_op jit(solution)/shard_map/ppermute | solution.py:82
  29.5 24.9 %collective-permute-start.3 = (bf16[256,2176]{1,0:T(8,128)(2,1)S(1)}, bf16[256,2176]{1,0:T(8,128)(2,1)S(1)}, u32[]{:S(2)}, u32[]{:S(2)}) collective-permute-start(bf16[256,2176]{1,0:T(8,128)(2,1)S(1)} %pad_maximum_fusion.5), channel_id=1, source_target_pairs={{0,16},{1,17},{2,18},{3,19},{4,20},{5,21},{6,22},{7,23},{8,24},{9,... | collective-permute-start | bytes 3342344 | tf_op jit(solution)/shard_map/ppermute | solution.py:82
  36.2 40.3 %collective-permute-start.16 = (bf16[512,1408]{1,0:T(8,128)(2,1)S(1)}, bf16[512,1408]{1,0:T(8,128)(2,1)S(1)}, u32[]{:S(2)}, u32[]{:S(2)}) collective-permute-start(bf16[512,1408]{1,0:T(8,128)(2,1)S(1)} %pad_maximum_fusion.4), channel_id=1, source_target_pairs={{0,12},{1,13},{2,14},{3,15},{4,8},{5,9},{6,10},{7,11},{8,4},{9,5},... | collective-permute-start | bytes 4325384 | tf_op jit(solution)/shard_map/ppermute | solution.py:82
  40.4 33.3 %collective-permute-start.11 = (bf16[512,1408]{1,0:T(8,128)(2,1)S(1)}, bf16[512,1408]{1,0:T(8,128)(2,1)S(1)}, u32[]{:S(2)}, u32[]{:S(2)}) collective-permute-start(bf16[512,1408]{1,0:T(8,128)(2,1)S(1)} %pad_maximum_fusion.2), channel_id=1, source_target_pairs={{0,48},{1,49},{2,50},{3,51},{4,52},{5,53},{6,54},{7,55},{8,56},{9,... | collective-permute-start | bytes 4325384 | tf_op jit(solution)/shard_map/ppermute | solution.py:82
  43.4 32.7 %collective-permute-start.15 = (bf16[512,1408]{1,0:T(8,128)(2,1)S(1)}, bf16[512,1408]{1,0:T(8,128)(2,1)S(1)}, u32[]{:S(2)}, u32[]{:S(2)}) collective-permute-start(bf16[512,1408]{1,0:T(8,128)(2,1)S(1)} %pad_maximum_fusion.3), channel_id=1, source_target_pairs={{0,66},{1,67},{2,64},{3,65},{4,70},{5,71},{6,68},{7,69},{8,74},{9,... | collective-permute-start | bytes 4325384 | tf_op jit(solution)/shard_map/ppermute | solution.py:82
  52.7 45.1 %collective-permute-start.6 = (bf16[512,2048]{1,0:T(8,128)(2,1)S(1)}, bf16[512,2048]{1,0:T(8,128)(2,1)S(1)}, u32[]{:S(2)}, u32[]{:S(2)}) collective-permute-start(bf16[512,2048]{1,0:T(8,128)(2,1)S(1)} %pad_maximum_fusion.1), channel_id=1, source_target_pairs={{0,4},{1,5},{2,6},{3,7},{4,0},{5,1},{6,2},{7,3},{8,12},{9,13},{10,... | collective-permute-start | bytes 6291464 | tf_op jit(solution)/shard_map/ppermute | solution.py:82
  54.6 48.1 %collective-permute-start.5 = (bf16[512,2176]{1,0:T(8,128)(2,1)S(1)}, bf16[512,2176]{1,0:T(8,128)(2,1)S(1)}, u32[]{:S(2)}, u32[]{:S(2)}) collective-permute-start(bf16[512,2176]{1,0:T(8,128)(2,1)S(1)} %pad_maximum_fusion), channel_id=1, source_target_pairs={{0,64},{1,65},{2,66},{3,67},{4,68},{5,69},{6,70},{7,71},{8,72},{9,... | collective-permute-start | bytes 6684680 | tf_op jit(solution)/shard_map/ppermute | solution.py:82
  77.5 25.2 %slice-start = ((s8[4325376]{0:T(1024)(128)(4,1)}), s8[4194304]{0:T(1024)(128)(4,1)S(1)}, s32[]{:S(2)}) async-start(s8[4325376]{0:T(1024)(128)(4,1)} %bitcast.6), calls=%async_computation | async-start | bytes 8388608
  77.6 25.2 %slice-start.1 = ((s8[4325376]{0:T(1024)(128)(4,1)}), s8[131072]{0:T(1024)(128)(4,1)S(1)}, s32[]{:S(2)}) async-start(s8[4325376]{0:T(1024)(128)(4,1)} %bitcast.6), calls=%async_computation.1 | async-start | bytes 262144
  108.5 5.7 %collective-permute-start.17 = (f32[512,1024]{1,0:T(8,128)S(1)}, f32[512,1024]{1,0:T(8,128)S(1)}, u32[]{:S(2)}, u32[]{:S(2)}) collective-permute-start(f32[512,1024]{1,0:T(8,128)S(1)} %fusion.50), channel_id=1, source_target_pairs={{0,1},{1,0},{2,3},{3,2},{4,5},{5,4},{6,7},{7,6},{8,9},{9,8},{10,11... | collective-permute-start | bytes 6291464 | tf_op jit(solution)/shard_map/ppermute | solution.py:164
  116.5 2.4 %collective-permute-start.22 = (f32[512]{0:T(512)S(1)}, f32[512]{0:T(512)S(1)}, u32[]{:S(2)}, u32[]{:S(2)}) collective-permute-start(f32[512]{0:T(512)S(1)} %slice.398), channel_id=1, source_target_pairs={{0,1},{1,0},{2,3},{3,2},{4,5},{5,4},{6,7},{7,6},{8,9},{9,8},{10,11... | collective-permute-start | bytes 6152 | tf_op jit(solution)/shard_map/ppermute | solution.py:180
  117.2 11.8 %collective-permute-start.18 = (f32[128,512]{1,0:T(8,128)S(1)}, f32[128,512]{1,0:T(8,128)S(1)}, u32[]{:S(2)}, u32[]{:S(2)}) collective-permute-start(f32[128,512]{1,0:T(8,128)S(1)} %pad_maximum_fusion.32), channel_id=1, source_target_pairs={{0,16},{1,17},{2,18},{3,19},{4,20},{5,21},{6,22},{7,23},{8,24},{9,... | collective-permute-start | bytes 786440 | tf_op jit(solution)/shard_map/ppermute | solution.py:141
  117.6 11.4 %collective-permute-start.19 = (f32[128,512]{1,0:T(8,128)S(1)}, f32[128,512]{1,0:T(8,128)S(1)}, u32[]{:S(2)}, u32[]{:S(2)}) collective-permute-start(f32[128,512]{1,0:T(8,128)S(1)} %pad_maximum_fusion.33), channel_id=1, source_target_pairs={{0,64},{1,65},{2,66},{3,67},{4,68},{5,69},{6,70},{7,71},{8,72},{9,... | collective-permute-start | bytes 786440 | tf_op jit(solution)/shard_map/ppermute | solution.py:141
  119.1 4.8 %collective-permute-start.23 = (f32[256]{0:T(256)S(1)}, f32[256]{0:T(256)S(1)}, u32[]{:S(2)}, u32[]{:S(2)}) collective-permute-start(f32[256]{0:T(256)S(1)} %pad_maximum_fusion.35), channel_id=1, source_target_pairs={{0,48},{1,49},{2,50},{3,51},{4,52},{5,53},{6,54},{7,55},{8,56},{9,... | collective-permute-start | bytes 3080 | tf_op jit(solution)/shard_map/ppermute | solution.py:118
  120.0 11.6 %collective-permute-start.20 = (f32[128,512]{1,0:T(8,128)S(1)}, f32[128,512]{1,0:T(8,128)S(1)}, u32[]{:S(2)}, u32[]{:S(2)}) collective-permute-start(f32[128,512]{1,0:T(8,128)S(1)} %pad_maximum_fusion.34), channel_id=1, source_target_pairs={{0,80},{1,81},{2,82},{3,83},{4,84},{5,85},{6,86},{7,87},{8,88},{9,... | collective-permute-start | bytes 786440 | tf_op jit(solution)/shard_map/ppermute | solution.py:141
  124.0 4.8 %collective-permute-start.24 = (f32[128]{0:T(128)S(1)}, f32[128]{0:T(128)S(1)}, u32[]{:S(2)}, u32[]{:S(2)}) collective-permute-start(f32[128]{0:T(128)S(1)} %pad_maximum_fusion.36), channel_id=1, source_target_pairs={{0,66},{1,67},{2,64},{3,65},{4,70},{5,71},{6,68},{7,69},{8,74},{9,... | collective-permute-start | bytes 1544 | tf_op jit(solution)/shard_map/ppermute | solution.py:118
  128.8 4.8 %collective-permute-start.25 = (f32[64]{0:T(128)S(1)}, f32[64]{0:T(128)S(1)}, u32[]{:S(2)}, u32[]{:S(2)}) collective-permute-start(f32[64]{0:T(128)S(1)} %slice_add_fusion.7), channel_id=1, source_target_pairs={{0,12},{1,13},{2,14},{3,15},{4,8},{5,9},{6,10},{7,11},{8,4},{9,5},... | collective-permute-start | bytes 776 | tf_op jit(solution)/shard_map/ppermute | solution.py:118
  131.7 5.0 %collective-permute-start.21 = (f32[64,512]{1,0:T(8,128)S(1)}, f32[64,512]{1,0:T(8,128)S(1)}, u32[]{:S(2)}, u32[]{:S(2)}) collective-permute-start(f32[64,512]{1,0:T(8,128)S(1)} %slice_add_fusion), channel_id=1, source_target_pairs={{0,4},{1,5},{2,6},{3,7},{4,0},{5,1},{6,2},{7,3},{8,12},{9,13},{10,... | collective-permute-start | bytes 393224 | tf_op jit(solution)/shard_map/ppermute | solution.py:144
